TPU v7x, 512 devices: a whole 4x4x16 slice. The times are simulated.
512 devices in a mesh: row: 64 (over x_lo, z, core), col: 8 (over y, x_hi).
Axes of the slice: x: 4 (x_hi: 2, x_lo: 2; x = x_hi * 2 + x_lo), y: 4, z: 16, core: 2. Of those that a mesh axis runs over, the one named last changes fastest.
Arguments:
- features: bfloat16 [128, 131072], P(None, 'row'), may hold values from -6 to 6
- weight_in: bfloat16 [128, 512], P(None, 'col'), may hold values from -0.5 to 0.5
- weight_out: bfloat16 [512, 64], replicated, may hold values from -0.25 to 0.25
- score_grad: bfloat16 [64, 131072], P('col', 'row'), may hold values from -0.011962891 to 0.011962891
- band_blocks: bfloat16 [1024, 3, 128, 128], P('row'), may hold values from -0.25 to 0.25
- long_blocks: bfloat16 [768, 128, 128], P('row'), may hold values from -0.25 to 0.25
- long_rows: int32 [64, 12], P('row'), may hold values from 0 to 15
- long_sources: int32 [64, 12], replicated, may hold values from 0 to 1023, as said below
- long_counts: int32 [64], replicated, may hold values from 1 to 12, as said below
Outputs:
- scores: bfloat16 [64, 131072], P('col', 'row')
- first_grad: float32 [128, 512], P(None, 'col')
- second_grad: float32 [512, 64], P('col')
Inputs may be any that keep to these rules, and one draw needn't show every extreme that they name: `long_sources`: every slot's block column lies on a partition at cycle distance 1 to 3 from the slot's own partition (either direction, indices taken mod the number of partitions); over ALL 12 slots of a partition each of the 6 such partitions is read by exactly 2 slots. Slots s < long_counts[p] are live, the others are ignored; some partition has all 12 live.
All inputs are finite; a program needn't handle non-finite values.
Results may differ from a plain program's by a relative error of at most 0.0065.
Values may be sent and summed in bfloat16 or wider, within the bound.
No kernel may reach another device: no remote copies, remote signals or barrier semaphores. Data moves between devices by JAX's collectives and lax.ppermute only.
A program may use at most 64 MiB of HBM per device.

v0:
```python
import jax
import jax.numpy as jnp
from jax import lax
from jax.sharding import PartitionSpec as P

BLK = 128
NB = 16
REACH = 3
SLOTS = 12


def passed_along(x, axis, by):
    devices = lax.axis_size(axis)
    return lax.ppermute(x, axis, [(i, (i + by) % devices) for i in range(devices)])


def signed_offset(owner_part, partition, row_devices):
    offset = jnp.mod(owner_part - partition, row_devices)
    return jnp.where(offset > row_devices // 2, offset - row_devices, offset)


def slot_table(long_sources, long_counts, partition, row_devices):
    source = lax.dynamic_index_in_dim(long_sources, partition, 0, keepdims=False)
    live_count = lax.dynamic_index_in_dim(long_counts, partition, 0, keepdims=False)
    slot_order = jnp.arange(SLOTS, dtype=jnp.int32)
    is_live = slot_order < live_count
    owner_part = source // NB
    local_block = source - owner_part * NB
    offset = signed_offset(owner_part, partition, row_devices)
    same_offset = (
        (offset[:, None] == offset[None, :])
        & is_live[None, :]
        & (slot_order[None, :] < slot_order[:, None])
    )
    slot_rank = jnp.sum(same_offset.astype(jnp.int32), axis=1)
    return (is_live, offset, local_block, slot_rank)


def distances():
    return [distance for distance in range(-REACH, REACH + 1) if distance != 0]


def aggregate(values, band_blocks, long_blocks, row_ids, long_sources, long_counts):
    feature_rows = values.shape[0]
    row_devices = lax.axis_size("row")
    my_index = lax.axis_index("row")
    blocks = values.reshape(feature_rows, NB, BLK)
    is_live, offset, local_block, slot_rank = slot_table(
        long_sources, long_counts, my_index, row_devices
    )
    position = jnp.where(offset < 0, offset + REACH, offset + REACH - 1)
    received = {}
    for distance in distances():
        arrived = passed_along(values, "row", -distance)
        received[distance] = arrived.reshape(feature_rows, NB, BLK)
    panel_pool = jnp.stack([received[distance] for distance in distances()], 0)
    panel_pool = panel_pool.transpose(0, 2, 1, 3).reshape(2 * REACH * NB, feature_rows, BLK)
    slot_index = position * NB + local_block
    before = received[-1][:, NB - 1]
    beyond = received[1][:, 0]
    slot_index = jnp.clip(slot_index, 0, panel_pool.shape[0] - 1)
    panels = jnp.take(panel_pool, slot_index, axis=0)
    contrib = jnp.einsum("kfm,knm->kfn", panels, long_blocks, preferred_element_type=jnp.float32)
    contrib = contrib * is_live.astype(jnp.float32)[:, None, None]
    targets = (
        (row_ids[:, None] == jnp.arange(NB, dtype=jnp.int32)[None, :]) & is_live[:, None]
    ).astype(jnp.float32)
    far_sum = jnp.einsum("kb,kfn->fbn", targets, contrib, precision=lax.Precision.HIGHEST)
    earlier = jnp.concatenate([before[:, None], blocks[:, :-1]], 1)
    onward = jnp.concatenate([blocks[:, 1:], beyond[:, None]], 1)
    near_sum = jnp.einsum(
        "fbm,bnm->fbn", earlier, band_blocks[:, 0], preferred_element_type=jnp.float32
    )
    near_sum = near_sum + jnp.einsum(
        "fbm,bnm->fbn", blocks, band_blocks[:, 1], preferred_element_type=jnp.float32
    )
    near_sum = near_sum + jnp.einsum(
        "fbm,bnm->fbn", onward, band_blocks[:, 2], preferred_element_type=jnp.float32
    )
    return (near_sum + far_sum).reshape(feature_rows, NB * BLK)


def aggregate_back(values, band_blocks, long_blocks, row_ids, long_sources, long_counts):
    feature_rows = values.shape[0]
    row_devices = lax.axis_size("row")
    my_index = lax.axis_index("row")
    blocks = values.reshape(feature_rows, NB, BLK)
    is_live, offset, local_block, slot_rank = slot_table(
        long_sources, long_counts, my_index, row_devices
    )
    to_prior = jnp.einsum(
        "fbn,bnm->fbm", blocks, band_blocks[:, 0], preferred_element_type=jnp.float32
    )
    middle = jnp.einsum(
        "fbn,bnm->fbm", blocks, band_blocks[:, 1], preferred_element_type=jnp.float32
    )
    to_later = jnp.einsum(
        "fbn,bnm->fbm", blocks, band_blocks[:, 2], preferred_element_type=jnp.float32
    )
    zero_block = jnp.zeros((feature_rows, 1, BLK), jnp.float32)
    summed = (
        middle
        + jnp.concatenate([to_prior[:, 1:], zero_block], 1)
        + jnp.concatenate([zero_block, to_later[:, :-1]], 1)
    )
    edge_prior = to_prior[:, 0]
    edge_later = to_later[:, NB - 1]
    gathered_rows = jnp.take(blocks, row_ids, axis=1)
    contrib = jnp.einsum(
        "fkn,knm->kfm", gathered_rows, long_blocks, preferred_element_type=jnp.float32
    )
    contrib = contrib * is_live.astype(jnp.float32)[:, None, None]
    block_hot = local_block[:, None] == jnp.arange(NB, dtype=jnp.int32)[None, :]
    for distance in distances():
        placing = ((is_live & (offset == distance))[:, None] & block_hot).astype(jnp.float32)
        outgoing = jnp.einsum("kb,kfm->fbm", placing, contrib, precision=lax.Precision.HIGHEST)
        if distance == -1:
            outgoing = outgoing.at[:, NB - 1].add(edge_prior)
        if distance == 1:
            outgoing = outgoing.at[:, 0].add(edge_later)
        summed = summed + passed_along(outgoing, "row", distance)
    return summed.reshape(feature_rows, NB * BLK)


def local(
    features,
    weight_in,
    weight_out,
    score_grad,
    band_blocks,
    long_blocks,
    long_rows,
    long_sources,
    long_counts,
):
    row_ids = long_rows[0]
    hidden_count = weight_in.shape[1]
    class_count = score_grad.shape[0]
    col_index = lax.axis_index("col")
    my_rows = lax.dynamic_slice_in_dim(weight_out, col_index * hidden_count, hidden_count, 0)
    hidden_in = jnp.einsum(
        "ih,in->hn", weight_in, features, preferred_element_type=jnp.float32
    ).astype(jnp.bfloat16)
    hidden_sum = aggregate(hidden_in, band_blocks, long_blocks, row_ids, long_sources, long_counts)
    hidden_act = jax.nn.silu(hidden_sum).astype(jnp.bfloat16)
    out_cols = lax.dynamic_slice_in_dim(weight_out, col_index * class_count, class_count, 1)
    class_sum = jnp.einsum(
        "hc,hn->cn",
        out_cols,
        lax.all_gather(hidden_act, "col", axis=0, tiled=True),
        preferred_element_type=jnp.float32,
    )
    class_in = class_sum.astype(jnp.bfloat16)
    scores = aggregate(
        class_in, band_blocks, long_blocks, row_ids, long_sources, long_counts
    ).astype(jnp.bfloat16)
    class_back = aggregate_back(
        score_grad, band_blocks, long_blocks, row_ids, long_sources, long_counts
    ).astype(jnp.bfloat16)
    shard_piece = lax.all_gather(class_back, "col", axis=0, tiled=True)
    hidden_back = jnp.einsum("hc,cn->hn", my_rows, shard_piece, preferred_element_type=jnp.float32)
    block_grad = jnp.einsum(
        "hn,cn->hc", hidden_act, shard_piece, preferred_element_type=jnp.float32
    )
    second_part = block_grad
    hidden_back, second_part = (hidden_back, second_part)
    sigmoid_val = jax.nn.sigmoid(hidden_sum)
    slope_back = (hidden_back * sigmoid_val * (1.0 + hidden_sum * (1.0 - sigmoid_val))).astype(
        jnp.bfloat16
    )
    input_back = aggregate_back(
        slope_back, band_blocks, long_blocks, row_ids, long_sources, long_counts
    ).astype(jnp.bfloat16)
    first_part = jnp.einsum("in,hn->ih", features, input_back, preferred_element_type=jnp.float32)
    first_grad, second_grad = lax.psum((first_part, second_part), "row")
    return (scores, first_grad, second_grad)


def solution(mesh):
    return jax.shard_map(
        local,
        mesh=mesh,
        in_specs=(
            P(None, "row"),
            P(None, "col"),
            P(),
            P("col", "row"),
            P("row", None, None, None),
            P("row", None, None),
            P("row", None),
            P(),
            P(),
        ),
        out_specs=(P("col", "row"), P(None, "col"), P("col", None)),
        check_vma=False,
    )
```

profile of v0, /device:TPU:1, one launch (start us, length us, event | category | flops | bytes accessed | tf_op | source)
XLA Modules:
  0.0 422.9 jit_solution(10532549555107713151)
XLA Ops:
  15.8 6.3 %collective-permute-start.17 = (f32[8,16,128]{2,0,1:T(8,128)S(1)}, f32[8,16,128]{2,0,1:T(8,128)S(1)}, u32[]{:S(2)}, u32[]{:S(2)}) collective-permute-start(f32[8,16,128]{2,0,1:T(8,128)S(1)} %bitcast.346), channel_id=1, source_target_pairs={{0,24},{8,32},{16,40},{24,48},{32,56},{40,64},{48,72},{56,80},{64,... | collective-permute-start | bytes 196616 | tf_op jit(solution)/shard_map/ppermute | solution.py:14
  22.3 3.5 collective-permute-start.16
  28.6 2.2 collective-permute-start.15
  32.5 2.5 collective-permute-start.14
  35.2 6.7 %collective-permute-start.13 = (f32[8,16,128]{2,0,1:T(8,128)S(1)}, f32[8,16,128]{2,0,1:T(8,128)S(1)}, u32[]{:S(2)}, u32[]{:S(2)}) collective-permute-start(f32[8,16,128]{2,0,1:T(8,128)S(1)} %bitcast.347), channel_id=1, source_target_pairs={{0,496},{8,504},{16,0},{24,8},{32,16},{40,24},{48,32},{56,40},{64,... | collective-permute-start | bytes 196616 | tf_op jit(solution)/shard_map/ppermute | solution.py:14
  43.3 5.5 %collective-permute-start.12 = (f32[8,16,128]{2,0,1:T(8,128)S(1)}, f32[8,16,128]{2,0,1:T(8,128)S(1)}, u32[]{:S(2)}, u32[]{:S(2)}) collective-permute-start(f32[8,16,128]{2,0,1:T(8,128)S(1)} %bitcast.348), channel_id=1, source_target_pairs={{0,488},{8,496},{16,504},{24,0},{32,8},{40,16},{48,24},{56,32},{64... | collective-permute-start | bytes 196616 | tf_op jit(solution)/shard_map/ppermute | solution.py:14
  54.7 2.4 collective-permute-start.1
  57.1 5.8 %collective-permute-start.4 = (bf16[64,2048]{1,0:T(8,128)(2,1)S(1)}, bf16[64,2048]{1,0:T(8,128)(2,1)S(1)}, u32[]{:S(2)}, u32[]{:S(2)}) collective-permute-start(bf16[64,2048]{1,0:T(8,128)(2,1)S(1)} %convolution_convert_fusion), channel_id=1, source_target_pairs={{0,496},{8,504},{16,0},{24,8},{32,16},{40,24},{48,32},{56,40},{64,... | collective-permute-start | bytes 786440 | tf_op jit(solution)/shard_map/ppermute | solution.py:14
  63.1 36.6 %all_gather.7 = bf16[64,2048]{1,0:T(8,128)(2,1)} all-gather(bf16[8,2048]{1,0:T(8,128)(2,1)S(1)} %fusion.27), channel_id=1, replica_groups=mesh['row'=64,'col'=8] {'col'}, dimensions={0}, use_global_device_ids=true | all-gather | bytes 294912 | tf_op jit(solution)/shard_map/all_gather | solution.py:160
  99.7 9.1 %collective-permute-start.5 = (bf16[64,2048]{1,0:T(8,128)(2,1)S(1)}, bf16[64,2048]{1,0:T(8,128)(2,1)S(1)}, u32[]{:S(2)}, u32[]{:S(2)}) collective-permute-start(bf16[64,2048]{1,0:T(8,128)(2,1)S(1)} %convolution_convert_fusion), channel_id=1, source_target_pairs={{0,488},{8,496},{16,504},{24,0},{32,8},{40,16},{48,24},{56,32},{64... | collective-permute-start | bytes 786440 | tf_op jit(solution)/shard_map/ppermute | solution.py:14
  110.1 4.4 %collective-permute-done.5 = bf16[64,2048]{1,0:T(8,128)(2,1)S(1)} collective-permute-done((bf16[64,2048]{1,0:T(8,128)(2,1)S(1)}, bf16[64,2048]{1,0:T(8,128)(2,1)S(1)}, u32[]{:S(2)}, u32[]{:S(2)}) %collective-permute-start.5) | collective-permute-done | bytes 262176 | tf_op jit(solution)/shard_map/ppermute | solution.py:14
  116.8 2.0 gather_fusion
  134.4 2.6 collective-permute-start.21
  143.9 6.0 %collective-permute-start.19 = (f32[64,16,128]{2,0,1:T(8,128)}, f32[64,16,128]{2,0,1:T(8,128)}, u32[]{:S(2)}, u32[]{:S(2)}) collective-permute-start(f32[64,16,128]{2,0,1:T(8,128)} %bitcast.315), channel_id=1, source_target_pairs={{0,496},{8,504},{16,0},{24,8},{32,16},{40,24},{48,32},{56,40},{64,... | collective-permute-start | bytes 1572872 | tf_op jit(solution)/shard_map/ppermute | solution.py:14
  151.2 5.6 %collective-permute-start.18 = (f32[64,16,128]{2,0,1:T(8,128)}, f32[64,16,128]{2,0,1:T(8,128)}, u32[]{:S(2)}, u32[]{:S(2)}) collective-permute-start(f32[64,16,128]{2,0,1:T(8,128)} %bitcast.316), channel_id=1, source_target_pairs={{0,488},{8,496},{16,504},{24,0},{32,8},{40,16},{48,24},{56,32},{64... | collective-permute-start | bytes 1572872 | tf_op jit(solution)/shard_map/ppermute | solution.py:14
  157.9 4.5 %collective-permute-done.21 = f32[64,16,128]{2,0,1:T(8,128)} collective-permute-done((f32[64,16,128]{2,0,1:T(8,128)}, f32[64,16,128]{2,0,1:T(8,128)}, u32[]{:S(2)}, u32[]{:S(2)}) %collective-permute-start.21) | collective-permute-done | bytes 524320 | tf_op jit(solution)/shard_map/ppermute | solution.py:14
  162.5 16.8 %collective-permute-done.18 = f32[64,16,128]{2,0,1:T(8,128)} collective-permute-done((f32[64,16,128]{2,0,1:T(8,128)}, f32[64,16,128]{2,0,1:T(8,128)}, u32[]{:S(2)}, u32[]{:S(2)}) %collective-permute-start.18) | collective-permute-done | bytes 524320 | tf_op jit(solution)/shard_map/ppermute | solution.py:14
  179.3 2.2 fusion.14
  181.8 204.9 %all-reduce.4 = (f32[128,64]{0,1:T(8,128)}, f32[64,64]{1,0:T(8,128)}) all-reduce(f32[128,64]{0,1:T(8,128)S(1)} %convolution_bitcast_fusion.6, f32[64,64]{1,0:T(8,128)S(1)} %fusion.208), channel_id=1, replica_groups=mesh['row'=64,'col'=8] {'row'}, use_global_device_ids=true, to_apply=%region_0.1 | all-reduce | flops 12288 | bytes 98304 | tf_op jit(solution)/shard_map/psum | solution.py:175
  386.7 2.0 convolution_convert_fusion.1
  389.1 3.6 collective-permute-start.6
  396.6 4.7 %collective-permute-start.7 = (bf16[8,2048]{1,0:T(8,128)(2,1)S(1)}, bf16[8,2048]{1,0:T(8,128)(2,1)S(1)}, u32[]{:S(2)}, u32[]{:S(2)}) collective-permute-start(bf16[8,2048]{1,0:T(8,128)(2,1)S(1)} %convolution_convert_fusion.1), channel_id=1, source_target_pairs={{0,504},{8,0},{16,8},{24,16},{32,24},{40,32},{48,40},{56,48},{64,5... | collective-permute-start | bytes 98312 | tf_op jit(solution)/shard_map/ppermute | solution.py:14
  401.2 5.8 %collective-permute-start.10 = (bf16[8,2048]{1,0:T(8,128)(2,1)S(1)}, bf16[8,2048]{1,0:T(8,128)(2,1)S(1)}, u32[]{:S(2)}, u32[]{:S(2)}) collective-permute-start(bf16[8,2048]{1,0:T(8,128)(2,1)S(1)} %convolution_convert_fusion.1), channel_id=1, source_target_pairs={{0,496},{8,504},{16,0},{24,8},{32,16},{40,24},{48,32},{56,40},{64,... | collective-permute-start | bytes 98312 | tf_op jit(solution)/shard_map/ppermute | solution.py:14
  407.0 4.7 %collective-permute-start.11 = (bf16[8,2048]{1,0:T(8,128)(2,1)S(1)}, bf16[8,2048]{1,0:T(8,128)(2,1)S(1)}, u32[]{:S(2)}, u32[]{:S(2)}) collective-permute-start(bf16[8,2048]{1,0:T(8,128)(2,1)S(1)} %convolution_convert_fusion.1), channel_id=1, source_target_pairs={{0,488},{8,496},{16,504},{24,0},{32,8},{40,16},{48,24},{56,32},{64... | collective-permute-start | bytes 98312 | tf_op jit(solution)/shard_map/ppermute | solution.py:14
  (189 shorter events, 57.3 us)
Async XLA Ops:
  7.2 379.5 %all-gather.2.cloned.1.call-start = ((), (), s32[]{:S(2)}) async-start(), calls=%async_computation | async-start | bytes 2359296 | tf_op jit(solution)/shard_map/all_gather | solution.py:150
  15.8 27.5 %collective-permute-start.17 = (f32[8,16,128]{2,0,1:T(8,128)S(1)}, f32[8,16,128]{2,0,1:T(8,128)S(1)}, u32[]{:S(2)}, u32[]{:S(2)}) collective-permute-start(f32[8,16,128]{2,0,1:T(8,128)S(1)} %bitcast.346), channel_id=1, source_target_pairs={{0,24},{8,32},{16,40},{24,48},{32,56},{40,64},{48,72},{56,80},{64,... | collective-permute-start | bytes 196616 | tf_op jit(solution)/shard_map/ppermute | solution.py:14
  22.3 26.6 %collective-permute-start.16 = (f32[8,16,128]{2,0,1:T(8,128)S(1)}, f32[8,16,128]{2,0,1:T(8,128)S(1)}, u32[]{:S(2)}, u32[]{:S(2)}) collective-permute-start(f32[8,16,128]{2,0,1:T(8,128)S(1)} %bitcast.345), channel_id=1, source_target_pairs={{0,16},{8,24},{16,32},{24,40},{32,48},{40,56},{48,64},{56,72},{64,... | collective-permute-start | bytes 196616 | tf_op jit(solution)/shard_map/ppermute | solution.py:14
  28.6 22.2 %collective-permute-start.15 = (f32[8,16,128]{2,0,1:T(8,128)}, f32[8,16,128]{2,0,1:T(8,128)S(1)}, u32[]{:S(2)}, u32[]{:S(2)}) collective-permute-start(f32[8,16,128]{2,0,1:T(8,128)} %fusion.149), channel_id=1, source_target_pairs={{0,8},{8,16},{16,24},{24,32},{32,40},{40,48},{48,56},{56,64},{64,7... | collective-permute-start | bytes 196616 | tf_op jit(solution)/shard_map/ppermute | solution.py:14
  32.5 20.2 %collective-permute-start.14 = (f32[8,16,128]{2,0,1:T(8,128)}, f32[8,16,128]{2,0,1:T(8,128)S(1)}, u32[]{:S(2)}, u32[]{:S(2)}) collective-permute-start(f32[8,16,128]{2,0,1:T(8,128)} %fusion.150), channel_id=1, source_target_pairs={{0,504},{8,0},{16,8},{24,16},{32,24},{40,32},{48,40},{56,48},{64,5... | collective-permute-start | bytes 196616 | tf_op jit(solution)/shard_map/ppermute | solution.py:14
  35.2 19.4 %collective-permute-start.13 = (f32[8,16,128]{2,0,1:T(8,128)S(1)}, f32[8,16,128]{2,0,1:T(8,128)S(1)}, u32[]{:S(2)}, u32[]{:S(2)}) collective-permute-start(f32[8,16,128]{2,0,1:T(8,128)S(1)} %bitcast.347), channel_id=1, source_target_pairs={{0,496},{8,504},{16,0},{24,8},{32,16},{40,24},{48,32},{56,40},{64,... | collective-permute-start | bytes 196616 | tf_op jit(solution)/shard_map/ppermute | solution.py:14
  43.3 13.8 %collective-permute-start.12 = (f32[8,16,128]{2,0,1:T(8,128)S(1)}, f32[8,16,128]{2,0,1:T(8,128)S(1)}, u32[]{:S(2)}, u32[]{:S(2)}) collective-permute-start(f32[8,16,128]{2,0,1:T(8,128)S(1)} %bitcast.348), channel_id=1, source_target_pairs={{0,488},{8,496},{16,504},{24,0},{32,8},{40,16},{48,24},{56,32},{64... | collective-permute-start | bytes 196616 | tf_op jit(solution)/shard_map/ppermute | solution.py:14
  48.9 50.8 %collective-permute-start = (bf16[64,2048]{1,0:T(8,128)(2,1)S(1)}, bf16[64,2048]{1,0:T(8,128)(2,1)S(1)}, u32[]{:S(2)}, u32[]{:S(2)}) collective-permute-start(bf16[64,2048]{1,0:T(8,128)(2,1)S(1)} %convolution_convert_fusion), channel_id=1, source_target_pairs={{0,8},{8,16},{16,24},{24,32},{32,40},{40,48},{48,56},{56,64},{64,7... | collective-permute-start | bytes 786440 | tf_op jit(solution)/shard_map/ppermute | solution.py:14
  50.8 58.1 %collective-permute-start.2 = (bf16[64,2048]{1,0:T(8,128)(2,1)S(1)}, bf16[64,2048]{1,0:T(8,128)(2,1)S(1)}, u32[]{:S(2)}, u32[]{:S(2)}) collective-permute-start(bf16[64,2048]{1,0:T(8,128)(2,1)S(1)} %convolution_convert_fusion), channel_id=1, source_target_pairs={{0,24},{8,32},{16,40},{24,48},{32,56},{40,64},{48,72},{56,80},{64,... | collective-permute-start | bytes 786440 | tf_op jit(solution)/shard_map/ppermute | solution.py:14
  52.7 56.2 %collective-permute-start.3 = (bf16[64,2048]{1,0:T(8,128)(2,1)S(1)}, bf16[64,2048]{1,0:T(8,128)(2,1)S(1)}, u32[]{:S(2)}, u32[]{:S(2)}) collective-permute-start(bf16[64,2048]{1,0:T(8,128)(2,1)S(1)} %convolution_convert_fusion), channel_id=1, source_target_pairs={{0,16},{8,24},{16,32},{24,40},{32,48},{40,56},{48,64},{56,72},{64,... | collective-permute-start | bytes 786440 | tf_op jit(solution)/shard_map/ppermute | solution.py:14
  54.7 54.4 %collective-permute-start.1 = (bf16[64,2048]{1,0:T(8,128)(2,1)S(1)}, bf16[64,2048]{1,0:T(8,128)(2,1)S(1)}, u32[]{:S(2)}, u32[]{:S(2)}) collective-permute-start(bf16[64,2048]{1,0:T(8,128)(2,1)S(1)} %convolution_convert_fusion), channel_id=1, source_target_pairs={{0,504},{8,0},{16,8},{24,16},{32,24},{40,32},{48,40},{56,48},{64,5... | collective-permute-start | bytes 786440 | tf_op jit(solution)/shard_map/ppermute | solution.py:14
  57.1 52.1 %collective-permute-start.4 = (bf16[64,2048]{1,0:T(8,128)(2,1)S(1)}, bf16[64,2048]{1,0:T(8,128)(2,1)S(1)}, u32[]{:S(2)}, u32[]{:S(2)}) collective-permute-start(bf16[64,2048]{1,0:T(8,128)(2,1)S(1)} %convolution_convert_fusion), channel_id=1, source_target_pairs={{0,496},{8,504},{16,0},{24,8},{32,16},{40,24},{48,32},{56,40},{64,... | collective-permute-start | bytes 786440 | tf_op jit(solution)/shard_map/ppermute | solution.py:14
  99.7 14.8 %collective-permute-start.5 = (bf16[64,2048]{1,0:T(8,128)(2,1)S(1)}, bf16[64,2048]{1,0:T(8,128)(2,1)S(1)}, u32[]{:S(2)}, u32[]{:S(2)}) collective-permute-start(bf16[64,2048]{1,0:T(8,128)(2,1)S(1)} %convolution_convert_fusion), channel_id=1, source_target_pairs={{0,488},{8,496},{16,504},{24,0},{32,8},{40,16},{48,24},{56,32},{64... | collective-permute-start | bytes 786440 | tf_op jit(solution)/shard_map/ppermute | solution.py:14
  126.2 24.9 %collective-permute-start.23 = (f32[64,16,128]{2,0,1:T(8,128)S(1)}, f32[64,16,128]{2,0,1:T(8,128)}, u32[]{:S(2)}, u32[]{:S(2)}) collective-permute-start(f32[64,16,128]{2,0,1:T(8,128)S(1)} %bitcast.333), channel_id=1, source_target_pairs={{0,24},{8,32},{16,40},{24,48},{32,56},{40,64},{48,72},{56,80},{64,... | collective-permute-start | bytes 1572872 | tf_op jit(solution)/shard_map/ppermute | solution.py:14
  129.8 28.1 %collective-permute-start.22 = (f32[64,16,128]{2,0,1:T(8,128)}, f32[64,16,128]{2,0,1:T(8,128)}, u32[]{:S(2)}, u32[]{:S(2)}) collective-permute-start(f32[64,16,128]{2,0,1:T(8,128)} %bitcast.314), channel_id=1, source_target_pairs={{0,16},{8,24},{16,32},{24,40},{32,48},{40,56},{48,64},{56,72},{64,... | collective-permute-start | bytes 1572872 | tf_op jit(solution)/shard_map/ppermute | solution.py:14
  134.4 28.0 %collective-permute-start.21 = (f32[64,16,128]{2,0,1:T(8,128)}, f32[64,16,128]{2,0,1:T(8,128)}, u32[]{:S(2)}, u32[]{:S(2)}) collective-permute-start(f32[64,16,128]{2,0,1:T(8,128)} %fusion.104), channel_id=1, source_target_pairs={{0,8},{8,16},{16,24},{24,32},{32,40},{40,48},{48,56},{56,64},{64,7... | collective-permute-start | bytes 1572872 | tf_op jit(solution)/shard_map/ppermute | solution.py:14
  139.6 22.8 %collective-permute-start.20 = (f32[64,16,128]{2,0,1:T(8,128)}, f32[64,16,128]{2,0,1:T(8,128)}, u32[]{:S(2)}, u32[]{:S(2)}) collective-permute-start(f32[64,16,128]{2,0,1:T(8,128)} %fusion.105), channel_id=1, source_target_pairs={{0,504},{8,0},{16,8},{24,16},{32,24},{40,32},{48,40},{56,48},{64,5... | collective-permute-start | bytes 1572872 | tf_op jit(solution)/shard_map/ppermute | solution.py:14
  143.9 18.5 %collective-permute-start.19 = (f32[64,16,128]{2,0,1:T(8,128)}, f32[64,16,128]{2,0,1:T(8,128)}, u32[]{:S(2)}, u32[]{:S(2)}) collective-permute-start(f32[64,16,128]{2,0,1:T(8,128)} %bitcast.315), channel_id=1, source_target_pairs={{0,496},{8,504},{16,0},{24,8},{32,16},{40,24},{48,32},{56,40},{64,... | collective-permute-start | bytes 1572872 | tf_op jit(solution)/shard_map/ppermute | solution.py:14
  151.2 28.1 %collective-permute-start.18 = (f32[64,16,128]{2,0,1:T(8,128)}, f32[64,16,128]{2,0,1:T(8,128)}, u32[]{:S(2)}, u32[]{:S(2)}) collective-permute-start(f32[64,16,128]{2,0,1:T(8,128)} %bitcast.316), channel_id=1, source_target_pairs={{0,488},{8,496},{16,504},{24,0},{32,8},{40,16},{48,24},{56,32},{64... | collective-permute-start | bytes 1572872 | tf_op jit(solution)/shard_map/ppermute | solution.py:14
  389.1 22.7 %collective-permute-start.6 = (bf16[8,2048]{1,0:T(8,128)(2,1)S(1)}, bf16[8,2048]{1,0:T(8,128)(2,1)S(1)}, u32[]{:S(2)}, u32[]{:S(2)}) collective-permute-start(bf16[8,2048]{1,0:T(8,128)(2,1)S(1)} %convolution_convert_fusion.1), channel_id=1, source_target_pairs={{0,8},{8,16},{16,24},{24,32},{32,40},{40,48},{48,56},{56,64},{64,7... | collective-permute-start | bytes 98312 | tf_op jit(solution)/shard_map/ppermute | solution.py:14
  392.7 14.3 %collective-permute-start.8 = (bf16[8,2048]{1,0:T(8,128)(2,1)S(1)}, bf16[8,2048]{1,0:T(8,128)(2,1)S(1)}, u32[]{:S(2)}, u32[]{:S(2)}) collective-permute-start(bf16[8,2048]{1,0:T(8,128)(2,1)S(1)} %convolution_convert_fusion.1), channel_id=1, source_target_pairs={{0,24},{8,32},{16,40},{24,48},{32,56},{40,64},{48,72},{56,80},{64,... | collective-permute-start | bytes 98312 | tf_op jit(solution)/shard_map/ppermute | solution.py:14
  394.6 17.1 %collective-permute-start.9 = (bf16[8,2048]{1,0:T(8,128)(2,1)S(1)}, bf16[8,2048]{1,0:T(8,128)(2,1)S(1)}, u32[]{:S(2)}, u32[]{:S(2)}) collective-permute-start(bf16[8,2048]{1,0:T(8,128)(2,1)S(1)} %convolution_convert_fusion.1), channel_id=1, source_target_pairs={{0,16},{8,24},{16,32},{24,40},{32,48},{40,56},{48,64},{56,72},{64,... | collective-permute-start | bytes 98312 | tf_op jit(solution)/shard_map/ppermute | solution.py:14
  396.6 15.2 %collective-permute-start.7 = (bf16[8,2048]{1,0:T(8,128)(2,1)S(1)}, bf16[8,2048]{1,0:T(8,128)(2,1)S(1)}, u32[]{:S(2)}, u32[]{:S(2)}) collective-permute-start(bf16[8,2048]{1,0:T(8,128)(2,1)S(1)} %convolution_convert_fusion.1), channel_id=1, source_target_pairs={{0,504},{8,0},{16,8},{24,16},{32,24},{40,32},{48,40},{56,48},{64,5... | collective-permute-start | bytes 98312 | tf_op jit(solution)/shard_map/ppermute | solution.py:14
  401.2 10.6 %collective-permute-start.10 = (bf16[8,2048]{1,0:T(8,128)(2,1)S(1)}, bf16[8,2048]{1,0:T(8,128)(2,1)S(1)}, u32[]{:S(2)}, u32[]{:S(2)}) collective-permute-start(bf16[8,2048]{1,0:T(8,128)(2,1)S(1)} %convolution_convert_fusion.1), channel_id=1, source_target_pairs={{0,496},{8,504},{16,0},{24,8},{32,16},{40,24},{48,32},{56,40},{64,... | collective-permute-start | bytes 98312 | tf_op jit(solution)/shard_map/ppermute | solution.py:14
  (32 other events, 671.4 us)
Sparse Core Ops, SparseCore 0:
  122.4 77.6 all-gather.1
where the time goes:
time: 425 us; the launch traced here: 423 us
  blocking collectives  241 us (57%)
  starting transfers between devices  92.3 us (22%)
  waiting for transfers between devices  27.5 us (6%)
  matrix products  21.6 us (5%)
  local copies, waits for them, and re-layouts  18 us (4%)
  between operations  15.3 us (4%)
  other arithmetic  6.68 us (2%)
    psum x1, blocking collectives, local(): first_grad, second_grad = lax.psum((first_part, second_part), 'row')  205 us
    ppermute x24, starting transfers between devices, passed_along(): lax.ppermute(x, axis, [(i, (i + by) % devices) for i in range(devices)])  92.3 us
    all_gather x1, blocking collectives, local(): shard_piece = lax.all_gather(class_back, 'col', axis=0, tiled=True)  36.6 us
    ppermute x24, waiting for transfers between devices, passed_along(): lax.ppermute(x, axis, [(i, (i + by) % devices) for i in range(devices)])  27.5 us
  transfers between devices with their start and end apart: 25, of which 5 were waited for; matrix products, arithmetic and copies ran while one was open for 6% of the time, Pallas kernels for 0%

commit v1 on v0

v1 whole, which is shorter than its diff:
```python
import jax
import jax.numpy as jnp
from jax import lax
from jax.sharding import PartitionSpec as P

BLK = 128
NB = 16
REACH = 3
SLOTS = 12
HI = lax.Precision.HIGHEST


def shifts():
    return [e for e in range(-REACH, REACH + 1) if e != 0]


def shift_index(e):
    return e + REACH if e < 0 else e + REACH - 1


def send_by(x, axis, by):
    devices = lax.axis_size(axis)
    return lax.ppermute(x, axis, [(i, (i + by) % devices) for i in range(devices)])


def swap_with(x, axis, mask):
    devices = lax.axis_size(axis)
    return lax.ppermute(x, axis, [(i, i ^ mask) for i in range(devices)])


def reading_blocks(long_sources, reader, owner):
    source = lax.dynamic_index_in_dim(long_sources, reader, 0, keepdims=False)
    hit = (source // NB) == owner
    rank = jnp.cumsum(hit.astype(jnp.int32)) - 1
    local = source % NB
    return [jnp.sum(jnp.where(hit & (rank == q), local, 0)) for q in range(2)]


def own_slot_pairs(long_sources, me, row_devices):
    source = lax.dynamic_index_in_dim(long_sources, me, 0, keepdims=False)
    owner = source // NB
    offset = jnp.mod(owner - me, row_devices)
    offset = jnp.where(offset > row_devices // 2, offset - row_devices, offset)
    same = (owner[:, None] == owner[None, :]) & (
        jnp.arange(SLOTS)[None, :] < jnp.arange(SLOTS)[:, None]
    )
    rank = jnp.sum(same.astype(jnp.int32), axis=1)
    position = jnp.where(offset < 0, offset + REACH, offset + REACH - 1)
    return offset, position * 2 + rank


def block(v, b):
    return lax.dynamic_slice_in_dim(v, b * BLK, BLK, axis=1)


def forward_sum(blocks, prev_edge, next_edge, panels, band_blocks, long_blocks, targets):
    earlier = jnp.concatenate([prev_edge[:, None], blocks[:, :-1]], 1)
    onward = jnp.concatenate([blocks[:, 1:], next_edge[:, None]], 1)
    near = jnp.einsum("fbm,bnm->fbn", earlier, band_blocks[:, 0], preferred_element_type=jnp.float32)
    near = near + jnp.einsum("fbm,bnm->fbn", blocks, band_blocks[:, 1], preferred_element_type=jnp.float32)
    near = near + jnp.einsum("fbm,bnm->fbn", onward, band_blocks[:, 2], preferred_element_type=jnp.float32)
    contrib = jnp.einsum("kfm,knm->kfn", panels, long_blocks, preferred_element_type=jnp.float32)
    far = jnp.einsum("kb,kfn->fbn", targets, contrib, precision=HI)
    return near + far


def local(
    features,
    weight_in,
    weight_out,
    score_grad,
    band_blocks,
    long_blocks,
    long_rows,
    long_sources,
    long_counts,
):
    row_devices = lax.axis_size("row")
    col_devices = lax.axis_size("col")
    me = lax.axis_index("row")
    col_index = lax.axis_index("col")
    row_ids = long_rows[0]
    hidden_count = weight_in.shape[1]
    class_count = score_grad.shape[0]
    nodes = features.shape[1]

    live_count = lax.dynamic_index_in_dim(long_counts, me, 0, keepdims=False)
    is_live = jnp.arange(SLOTS, dtype=jnp.int32) < live_count
    live = is_live.astype(jnp.float32)
    targets = (
        (row_ids[:, None] == jnp.arange(NB, dtype=jnp.int32)[None, :]) & is_live[:, None]
    ).astype(jnp.float32)
    offset, pair = own_slot_pairs(long_sources, me, row_devices)
    slot_of_pair = jnp.sum(
        jnp.where(pair[None, :] == jnp.arange(SLOTS)[:, None], jnp.arange(SLOTS)[None, :], 0), axis=1
    )

    hidden_in = jnp.einsum(
        "ih,in->hn", weight_in, features, preferred_element_type=jnp.float32
    ).astype(jnp.bfloat16)

    sg_blocks = score_grad.reshape(class_count, NB, BLK)
    sg_prior = jnp.einsum("fbn,bnm->fbm", sg_blocks, band_blocks[:, 0], preferred_element_type=jnp.float32)
    sg_middle = jnp.einsum("fbn,bnm->fbm", sg_blocks, band_blocks[:, 1], preferred_element_type=jnp.float32)
    sg_later = jnp.einsum("fbn,bnm->fbm", sg_blocks, band_blocks[:, 2], preferred_element_type=jnp.float32)
    sg_rows = jnp.take(sg_blocks, row_ids, axis=1)
    sg_contrib = jnp.einsum("fkn,knm->kfm", sg_rows, long_blocks, preferred_element_type=jnp.float32)
    sg_contrib = sg_contrib * live[:, None, None]
    sg_out = jnp.take(sg_contrib, slot_of_pair, axis=0)

    payloads = {}
    for e in shifts():
        reader = jnp.mod(me + e, row_devices)
        wanted = reading_blocks(long_sources, reader, me)
        parts = [block(hidden_in, b).astype(jnp.float32) for b in wanted]
        parts += [block(features, b).astype(jnp.float32) for b in wanted]
        t = shift_index(e) * 2
        parts += [sg_out[t], sg_out[t + 1]]
        if e == 1:
            parts += [
                hidden_in[:, nodes - BLK:].astype(jnp.float32),
                features[:, nodes - BLK:].astype(jnp.float32),
                sg_later[:, NB - 1],
            ]
        if e == -1:
            parts += [
                hidden_in[:, :BLK].astype(jnp.float32),
                features[:, :BLK].astype(jnp.float32),
                sg_prior[:, 0],
            ]
        payloads[e] = send_by(jnp.concatenate(parts, 0), "row", e)

    h_rows = hidden_count
    f_rows = features.shape[0]
    c_rows = class_count

    def unpack(x):
        i = 0
        out = []
        for size in (h_rows, h_rows, f_rows, f_rows, c_rows, c_rows, h_rows, f_rows, c_rows):
            if i >= x.shape[0]:
                break
            out.append(x[i:i + size])
            i += size
        return out

    arrived = {e: unpack(payloads[e]) for e in shifts()}
    hid_pool = jnp.stack([arrived[e][q] for e in shifts() for q in range(2)], 0)
    feat_pool = jnp.stack([arrived[e][2 + q] for e in shifts() for q in range(2)], 0)
    read_position = jnp.where(-offset < 0, -offset + REACH, -offset + REACH - 1)
    own_rank = pair % 2
    read_index = read_position * 2 + own_rank
    hid_panels = jnp.take(hid_pool, read_index, axis=0).astype(jnp.bfloat16)
    feat_panels = jnp.take(feat_pool, read_index, axis=0).astype(jnp.bfloat16)

    hid_blocks = hidden_in.reshape(h_rows, NB, BLK)
    hidden_sum = forward_sum(
        hid_blocks,
        arrived[1][6].astype(jnp.bfloat16),
        arrived[-1][6].astype(jnp.bfloat16),
        hid_panels,
        band_blocks,
        long_blocks,
        targets,
    ).reshape(h_rows, nodes)
    feat_blocks = features.reshape(f_rows, NB, BLK)
    feat_sum = forward_sum(
        feat_blocks,
        arrived[1][7].astype(jnp.bfloat16),
        arrived[-1][7].astype(jnp.bfloat16),
        feat_panels,
        band_blocks,
        long_blocks,
        targets,
    ).reshape(f_rows, nodes)

    zero_block = jnp.zeros((c_rows, 1, BLK), jnp.float32)
    sg_sum = (
        sg_middle
        + jnp.concatenate([sg_prior[:, 1:], zero_block], 1)
        + jnp.concatenate([zero_block, sg_later[:, :-1]], 1)
    )
    sg_in = jnp.stack([arrived[e][4 + q] for e in shifts() for q in range(2)], 0)
    land = []
    for e in shifts():
        sender = jnp.mod(me - e, row_devices)
        land += reading_blocks(long_sources, sender, me)
    land = jnp.stack(land)
    landing = (land[:, None] == jnp.arange(NB, dtype=jnp.int32)[None, :]).astype(jnp.float32)
    sg_sum = sg_sum + jnp.einsum("kb,kfm->fbm", landing, sg_in, precision=HI)
    sg_sum = sg_sum.at[:, 0].add(arrived[1][8])
    sg_sum = sg_sum.at[:, NB - 1].add(arrived[-1][8])
    class_back = sg_sum.reshape(c_rows, nodes).astype(jnp.bfloat16)

    hidden_act = jax.nn.silu(hidden_sum).astype(jnp.bfloat16)

    my_rows = lax.dynamic_slice_in_dim(weight_out, col_index * hidden_count, hidden_count, 0)
    class_part = jnp.einsum("hc,hn->cn", my_rows, hidden_act, preferred_element_type=jnp.float32)
    reduced = class_part.reshape(col_devices, c_rows, nodes)
    gathered = class_back.reshape(1, c_rows, nodes)
    mask = col_devices // 2
    while mask >= 1:
        bit = (col_index // mask) % 2
        halves = reduced.reshape(2, -1, c_rows, nodes)
        keep = lax.dynamic_index_in_dim(halves, bit, 0, keepdims=False)
        away = lax.dynamic_index_in_dim(halves, 1 - bit, 0, keepdims=False)
        count = away.shape[0]
        both = swap_with(jnp.concatenate([away, gathered.astype(jnp.float32)], 0), "col", mask)
        reduced = keep + both[:count]
        other = both[count:].astype(jnp.bfloat16)
        gathered = jnp.where(
            bit == 0,
            jnp.concatenate([gathered, other], 0),
            jnp.concatenate([other, gathered], 0),
        )
        mask //= 2
    class_in = reduced.reshape(c_rows, nodes).astype(jnp.bfloat16)
    order = []
    for j in range(col_devices):
        rev = 0
        bits = col_devices.bit_length() - 1
        for k in range(bits):
            if j & (1 << k):
                rev |= 1 << (bits - 1 - k)
        order.append(rev)
    all_back = gathered.reshape(col_devices * c_rows, nodes)
    out_order = jnp.array(
        [order[j] * c_rows + k for j in range(col_devices) for k in range(c_rows)], jnp.int32
    )
    rows_in_order = jnp.take(my_rows, out_order, axis=1)

    hidden_back = jnp.einsum("hc,cn->hn", rows_in_order, all_back, preferred_element_type=jnp.float32)
    block_grad = jnp.einsum("hn,cn->hc", hidden_act, all_back, preferred_element_type=jnp.float32)
    inverse = [0] * (col_devices * c_rows)
    for pos in range(col_devices * c_rows):
        inverse[int(order[pos // c_rows]) * c_rows + pos % c_rows] = pos
    second_part = jnp.take(block_grad, jnp.array(inverse, jnp.int32), axis=1)

    sigmoid_val = jax.nn.sigmoid(hidden_sum)
    slope_back = (hidden_back * sigmoid_val * (1.0 + hidden_sum * (1.0 - sigmoid_val))).astype(
        jnp.bfloat16
    )
    first_part = jnp.einsum(
        "in,hn->ih", feat_sum, slope_back.astype(jnp.float32), precision=HI
    )

    class_sent = {}
    for e in shifts():
        reader = jnp.mod(me + e, row_devices)
        wanted = reading_blocks(long_sources, reader, me)
        parts = [block(class_in, b) for b in wanted]
        if e == 1:
            parts.append(class_in[:, nodes - BLK:])
        if e == -1:
            parts.append(class_in[:, :BLK])
        class_sent[e] = send_by(jnp.concatenate(parts, 0), "row", e)
    cls_pool = jnp.stack(
        [class_sent[e][q * c_rows:(q + 1) * c_rows] for e in shifts() for q in range(2)], 0
    )
    cls_panels = jnp.take(cls_pool, read_index, axis=0)
    scores = forward_sum(
        class_in.reshape(c_rows, NB, BLK),
        class_sent[1][2 * c_rows:],
        class_sent[-1][2 * c_rows:],
        cls_panels,
        band_blocks,
        long_blocks,
        targets,
    ).reshape(c_rows, nodes).astype(jnp.bfloat16)

    flat = jnp.concatenate([first_part.reshape(-1), second_part.reshape(-1)])
    for mask in [1, row_devices // 2] + [m for m in (2, 4, 8, 16, 32) if m < row_devices // 2]:
        if mask < row_devices:
            flat = flat + swap_with(flat, "row", mask)
    first_grad = flat[: first_part.size].reshape(first_part.shape)
    second_grad = flat[first_part.size:].reshape(second_part.shape)
    return (scores, first_grad, second_grad)


def solution(mesh):
    return jax.shard_map(
        local,
        mesh=mesh,
        in_specs=(
            P(None, "row"),
            P(None, "col"),
            P(),
            P("col", "row"),
            P("row", None, None, None),
            P("row", None, None),
            P("row", None),
            P(),
            P(),
        ),
        out_specs=(P("col", "row"), P(None, "col"), P("col", None)),
        check_vma=False,
    )
```

time: 425 us -> 254 us (0.60)
  the two profiles are of different devices: /device:TPU:1 before, /device:TPU:4 now
where the time goes in v1:
time: 254 us; the launch traced here: 250 us
  local copies, waits for them, and re-layouts  83.7 us (33%)
  starting transfers between devices  74.1 us (29%)
  waiting for transfers between devices  42.1 us (17%)
  other arithmetic  22.4 us (9%)
  matrix products  18.8 us (7%)
  between operations  9.34 us (4%)
    unnamed x133, local copies, waits for them, and re-layouts  50.8 us
    ppermute x12, starting transfers between devices, send_by(): lax.ppermute(x, axis, [(i, (i + by) % devices) for i in range(devices)])  45.7 us
    ppermute x9, waiting for transfers between devices, swap_with(): return lax.ppermute(x, axis, [(i, i ^ mask) for i in range(devices)])  34.4 us
    ppermute x9, starting transfers between devices, swap_with(): return lax.ppermute(x, axis, [(i, i ^ mask) for i in range(devices)])  28.3 us
    another operation x1, local copies, waits for them, and re-layouts, local(): land = jnp.stack(land)  8.13 us
    ppermute x12, waiting for transfers between devices, send_by(): lax.ppermute(x, axis, [(i, (i + by) % devices) for i in range(devices)])  7.68 us
  transfers between devices with their start and end apart: 21, of which 10 were waited for; matrix products, arithmetic and copies ran while one was open for 30% of the time, Pallas kernels for 0%

profile of v1, /device:TPU:4, one launch (start us, length us, event | category | flops | bytes accessed | tf_op | source)
XLA Modules:
  0.0 250.4 jit_solution(2395458167548198639)
XLA Ops:
  28.7 11.9 %collective-permute-start.2 = (f32[400,128]{1,0:T(8,128)}, f32[400,128]{1,0:T(8,128)}, u32[]{:S(2)}, u32[]{:S(2)}) collective-permute-start(f32[400,128]{1,0:T(8,128)} %get-tuple-element.92), channel_id=1, source_target_pairs={{0,488},{8,496},{16,504},{24,0},{32,8},{40,16},{48,24},{56,32},{64... | collective-permute-start | bytes 614408 | tf_op jit(solution)/shard_map/ppermute | solution.py:23
  40.6 2.9 %collective-permute-start.3 = (f32[400,128]{1,0:T(8,128)}, f32[400,128]{1,0:T(8,128)}, u32[]{:S(2)}, u32[]{:S(2)}) collective-permute-start(f32[400,128]{1,0:T(8,128)} %get-tuple-element.91), channel_id=1, source_target_pairs={{0,496},{8,504},{16,0},{24,8},{32,16},{40,24},{48,32},{56,40},{64,... | collective-permute-start | bytes 614408 | tf_op jit(solution)/shard_map/ppermute | solution.py:23
  44.4 2.5 collective-permute-start.1
  49.7 2.9 %collective-permute-start.4 = (f32[400,128]{1,0:T(8,128)}, f32[400,128]{1,0:T(8,128)}, u32[]{:S(2)}, u32[]{:S(2)}) collective-permute-start(f32[400,128]{1,0:T(8,128)} %get-tuple-element.90), channel_id=1, source_target_pairs={{0,16},{8,24},{16,32},{24,40},{32,48},{40,56},{48,64},{56,72},{64,... | collective-permute-start | bytes 614408 | tf_op jit(solution)/shard_map/ppermute | solution.py:23
  62.6 8.1 %stack.233 = s32[12]{0:T(128)} concatenate(s32[1]{0:T(128)} %bitcast.81, s32[1]{0:T(128)} %bitcast.82, s32[1]{0:T(128)} %bitcast.83, s32[1]{0:T(128)} %bitcast.84, s32[1]{0:T(128)} %bitcast.85, s32[1]{0:T(128)} %bitcast.86, s32[1]{0:T(128)} %bitcast.87, s32[1]{0:T(128)} %bitcast.88, s32[1]{0:T(128)} %bitcast.89, s32[1]{0:T(128)} %bitcast.90, s32[1]{0:T(128)} %bitcast.91, s32[1]{0:T(128)} %bitcast.92), dimensions={0} | concatenate | bytes 96 | tf_op jit(solution)/shard_map/stack | solution.py:188
  71.3 2.6 %collective-permute-start.5 = (f32[400,128]{1,0:T(8,128)}, f32[400,128]{1,0:T(8,128)S(1)}, u32[]{:S(2)}, u32[]{:S(2)}) collective-permute-start(f32[400,128]{1,0:T(8,128)} %copy-done.31), channel_id=1, source_target_pairs={{0,24},{8,32},{16,40},{24,48},{32,56},{40,64},{48,72},{56,80},{64,... | collective-permute-start | bytes 614408 | tf_op jit(solution)/shard_map/ppermute | solution.py:23
  121.1 5.2 %collective-permute-start.6 = (f32[5,8,2048]{2,1,0:T(8,128)}, f32[5,8,2048]{2,1,0:T(8,128)}, u32[]{:S(2)}, u32[]{:S(2)}) collective-permute-start(f32[5,8,2048]{2,1,0:T(8,128)} %pad_maximum_fusion), channel_id=1, source_target_pairs={{0,4},{1,5},{2,6},{3,7},{4,0},{5,1},{6,2},{7,3},{8,12},{9,13},{10,... | collective-permute-start | bytes 983048 | tf_op jit(solution)/shard_map/ppermute | solution.py:28
  143.6 2.6 %collective-permute-start.7 = (f32[4,8,2048]{2,1,0:T(8,128)S(1)}, f32[4,8,2048]{2,1,0:T(8,128)S(1)}, u32[]{:S(2)}, u32[]{:S(2)}) collective-permute-start(f32[4,8,2048]{2,1,0:T(8,128)S(1)} %pad_maximum_fusion.2), channel_id=1, source_target_pairs={{0,2},{1,3},{2,0},{3,1},{4,6},{5,7},{6,4},{7,5},{8,10},{9,11},{10,... | collective-permute-start | bytes 786440 | tf_op jit(solution)/shard_map/ppermute | solution.py:28
  148.4 5.1 %collective-permute-done.7 = f32[4,8,2048]{2,1,0:T(8,128)S(1)} collective-permute-done((f32[4,8,2048]{2,1,0:T(8,128)S(1)}, f32[4,8,2048]{2,1,0:T(8,128)S(1)}, u32[]{:S(2)}, u32[]{:S(2)}) %collective-permute-start.7) | collective-permute-done | bytes 262176 | tf_op jit(solution)/shard_map/ppermute | solution.py:28
  155.7 2.9 %collective-permute-start.8 = (f32[5,8,2048]{2,1,0:T(8,128)}, f32[5,8,2048]{2,1,0:T(8,128)}, u32[]{:S(2)}, u32[]{:S(2)}) collective-permute-start(f32[5,8,2048]{2,1,0:T(8,128)} %pad_maximum_fusion.1), channel_id=1, source_target_pairs={{0,1},{1,0},{2,3},{3,2},{4,5},{5,4},{6,7},{7,6},{8,9},{9,8},{10,11... | collective-permute-start | bytes 983048 | tf_op jit(solution)/shard_map/ppermute | solution.py:28
  159.3 2.5 %copy.68 = f32[128,128,16]{0,1,2:T(8,128)} copy(f32[128,128,16]{1,2,0:T(8,128)} %fusion.14) | data formatting | bytes 2097152 | tf_op jit(solution)/shard_map/kb,kfn->fbn/dot_general | solution.py:63
  161.9 2.7 %fusion.3 = f32[128,16,128]{0,2,1:T(8,128)} fusion(f32[128,16,128]{0,2,1:T(8,128)S(1)} %fusion.4, f32[128,128,16]{0,1,2:T(8,128)} %copy.68, bf16[128,1,128]{2,0,1:T(8,128)(2,1)S(1)} %slice_bitcast_fusion.12, bf16[128,15,128]{2,0,1:T(8,128)(2,1)S(1)} %copy-done.7, bf16[16,3,128,128]{3,2,1,0:T(8,128)(2,1)S(1)} %copy-done.1), kind=kOutput, calls=%fused_computation.13 | convolution fusion | flops 67895296 | bytes 4194304 | tf_op jit(solution)/shard_map/fbm,bnm->fbn/dot_general | solution.py:61
  164.6 3.3 %collective-permute-done.8 = f32[5,8,2048]{2,1,0:T(8,128)} collective-permute-done((f32[5,8,2048]{2,1,0:T(8,128)}, f32[5,8,2048]{2,1,0:T(8,128)}, u32[]{:S(2)}, u32[]{:S(2)}) %collective-permute-start.8) | collective-permute-done | bytes 327712 | tf_op jit(solution)/shard_map/ppermute | solution.py:28
  179.8 5.5 %collective-permute-start.10 = (bf16[24,128]{1,0:T(8,128)(2,1)S(1)}, bf16[24,128]{1,0:T(8,128)(2,1)S(1)}, u32[]{:S(2)}, u32[]{:S(2)}) collective-permute-start(bf16[24,128]{1,0:T(8,128)(2,1)S(1)} %pad_maximum_fusion.4), channel_id=1, source_target_pairs={{0,504},{8,0},{16,8},{24,16},{32,24},{40,32},{48,40},{56,48},{64,5... | collective-permute-start | bytes 18440 | tf_op jit(solution)/shard_map/ppermute | solution.py:23
  185.3 3.7 %collective-permute-start.11 = (bf16[16,128]{1,0:T(8,128)(2,1)S(1)}, bf16[16,128]{1,0:T(8,128)(2,1)S(1)}, u32[]{:S(2)}, u32[]{:S(2)}) collective-permute-start(bf16[16,128]{1,0:T(8,128)(2,1)S(1)} %pad_maximum_fusion.5), channel_id=1, source_target_pairs={{0,488},{8,496},{16,504},{24,0},{32,8},{40,16},{48,24},{56,32},{64... | collective-permute-start | bytes 12296 | tf_op jit(solution)/shard_map/ppermute | solution.py:23
  190.4 5.6 %collective-permute-start.12 = (bf16[16,128]{1,0:T(8,128)(2,1)S(1)}, bf16[16,128]{1,0:T(8,128)(2,1)S(1)}, u32[]{:S(2)}, u32[]{:S(2)}) collective-permute-start(bf16[16,128]{1,0:T(8,128)(2,1)S(1)} %pad_maximum_fusion.6), channel_id=1, source_target_pairs={{0,496},{8,504},{16,0},{24,8},{32,16},{40,24},{48,32},{56,40},{64,... | collective-permute-start | bytes 12296 | tf_op jit(solution)/shard_map/ppermute | solution.py:23
  199.3 5.1 %collective-permute-done.9 = bf16[24,128]{1,0:T(8,128)(2,1)S(1)} collective-permute-done((bf16[24,128]{1,0:T(8,128)(2,1)S(1)}, bf16[24,128]{1,0:T(8,128)(2,1)S(1)}, u32[]{:S(2)}, u32[]{:S(2)}) %collective-permute-start.9) | collective-permute-done | bytes 6176 | tf_op jit(solution)/shard_map/ppermute | solution.py:23
  204.9 2.7 %collective-permute-start.16 = (f32[12288]{0:T(1024)S(1)}, f32[12288]{0:T(1024)S(1)}, u32[]{:S(2)}, u32[]{:S(2)}) collective-permute-start(f32[12288]{0:T(1024)S(1)} %add.735), channel_id=1, source_target_pairs={{0,256},{8,264},{16,272},{24,280},{32,288},{40,296},{48,304},{56,3... | collective-permute-start | bytes 147464 | tf_op jit(solution)/shard_map/ppermute | solution.py:28
  208.3 2.5 %collective-permute-done.16 = f32[12288]{0:T(1024)S(1)} collective-permute-done((f32[12288]{0:T(1024)S(1)}, f32[12288]{0:T(1024)S(1)}, u32[]{:S(2)}, u32[]{:S(2)}) %collective-permute-start.16) | collective-permute-done | bytes 49184 | tf_op jit(solution)/shard_map/ppermute | solution.py:28
  213.1 4.2 %collective-permute-done.17 = f32[12288]{0:T(1024)S(1)} collective-permute-done((f32[12288]{0:T(1024)S(1)}, f32[12288]{0:T(1024)S(1)}, u32[]{:S(2)}, u32[]{:S(2)}) %collective-permute-start.17) | collective-permute-done | bytes 49184 | tf_op jit(solution)/shard_map/ppermute | solution.py:28
  219.4 4.8 %collective-permute-done.18 = f32[12288]{0:T(1024)S(1)} collective-permute-done((f32[12288]{0:T(1024)S(1)}, f32[12288]{0:T(1024)S(1)}, u32[]{:S(2)}, u32[]{:S(2)}) %collective-permute-start.18) | collective-permute-done | bytes 49184 | tf_op jit(solution)/shard_map/ppermute | solution.py:28
  226.6 7.6 %collective-permute-done.19 = f32[12288]{0:T(1024)S(1)} collective-permute-done((f32[12288]{0:T(1024)S(1)}, f32[12288]{0:T(1024)S(1)}, u32[]{:S(2)}, u32[]{:S(2)}) %collective-permute-start.19) | collective-permute-done | bytes 49184 | tf_op jit(solution)/shard_map/ppermute | solution.py:28
  234.2 6.8 %collective-permute-start.20 = (f32[12288]{0:T(1024)S(1)}, f32[12288]{0:T(1024)S(1)}, u32[]{:S(2)}, u32[]{:S(2)}) collective-permute-start(f32[12288]{0:T(1024)S(1)} %add.739), channel_id=1, source_target_pairs={{0,128},{8,136},{16,144},{24,152},{32,160},{40,168},{48,176},{56,1... | collective-permute-start | bytes 147464 | tf_op jit(solution)/shard_map/ppermute | solution.py:28
  242.0 6.9 %collective-permute-done.20 = f32[12288]{0:T(1024)S(1)} collective-permute-done((f32[12288]{0:T(1024)S(1)}, f32[12288]{0:T(1024)S(1)}, u32[]{:S(2)}, u32[]{:S(2)}) %collective-permute-start.20) | collective-permute-done | bytes 49184 | tf_op jit(solution)/shard_map/ppermute | solution.py:28
  (287 shorter events, 130.3 us)
Async XLA Ops:
  28.7 42.6 %collective-permute-start.2 = (f32[400,128]{1,0:T(8,128)}, f32[400,128]{1,0:T(8,128)}, u32[]{:S(2)}, u32[]{:S(2)}) collective-permute-start(f32[400,128]{1,0:T(8,128)} %get-tuple-element.92), channel_id=1, source_target_pairs={{0,488},{8,496},{16,504},{24,0},{32,8},{40,16},{48,24},{56,32},{64... | collective-permute-start | bytes 614408 | tf_op jit(solution)/shard_map/ppermute | solution.py:23
  40.6 38.8 %collective-permute-start.3 = (f32[400,128]{1,0:T(8,128)}, f32[400,128]{1,0:T(8,128)}, u32[]{:S(2)}, u32[]{:S(2)}) collective-permute-start(f32[400,128]{1,0:T(8,128)} %get-tuple-element.91), channel_id=1, source_target_pairs={{0,496},{8,504},{16,0},{24,8},{32,16},{40,24},{48,32},{56,40},{64,... | collective-permute-start | bytes 614408 | tf_op jit(solution)/shard_map/ppermute | solution.py:23
  44.4 49.2 %collective-permute-start.1 = (f32[600,128]{1,0:T(8,128)}, f32[600,128]{1,0:T(8,128)}, u32[]{:S(2)}, u32[]{:S(2)}) collective-permute-start(f32[600,128]{1,0:T(8,128)} %constant_dynamic-update-slice_fusion.9), channel_id=1, source_target_pairs={{0,504},{8,0},{16,8},{24,16},{32,24},{40,32},{48,40},{56,48},{64,5... | collective-permute-start | bytes 921608 | tf_op jit(solution)/shard_map/ppermute | solution.py:23
  47.7 42.6 %collective-permute-start = (f32[600,128]{1,0:T(8,128)}, f32[600,128]{1,0:T(8,128)}, u32[]{:S(2)}, u32[]{:S(2)}) collective-permute-start(f32[600,128]{1,0:T(8,128)} %constant_dynamic-update-slice_fusion), channel_id=1, source_target_pairs={{0,8},{8,16},{16,24},{24,32},{32,40},{40,48},{48,56},{56,64},{64,7... | collective-permute-start | bytes 921608 | tf_op jit(solution)/shard_map/ppermute | solution.py:23
  49.7 50.5 %collective-permute-start.4 = (f32[400,128]{1,0:T(8,128)}, f32[400,128]{1,0:T(8,128)}, u32[]{:S(2)}, u32[]{:S(2)}) collective-permute-start(f32[400,128]{1,0:T(8,128)} %get-tuple-element.90), channel_id=1, source_target_pairs={{0,16},{8,24},{16,32},{24,40},{32,48},{40,56},{48,64},{56,72},{64,... | collective-permute-start | bytes 614408 | tf_op jit(solution)/shard_map/ppermute | solution.py:23
  71.3 31.6 %collective-permute-start.5 = (f32[400,128]{1,0:T(8,128)}, f32[400,128]{1,0:T(8,128)S(1)}, u32[]{:S(2)}, u32[]{:S(2)}) collective-permute-start(f32[400,128]{1,0:T(8,128)} %copy-done.31), channel_id=1, source_target_pairs={{0,24},{8,32},{16,40},{24,48},{32,56},{40,64},{48,72},{56,80},{64,... | collective-permute-start | bytes 614408 | tf_op jit(solution)/shard_map/ppermute | solution.py:23
  121.1 19.9 %collective-permute-start.6 = (f32[5,8,2048]{2,1,0:T(8,128)}, f32[5,8,2048]{2,1,0:T(8,128)}, u32[]{:S(2)}, u32[]{:S(2)}) collective-permute-start(f32[5,8,2048]{2,1,0:T(8,128)} %pad_maximum_fusion), channel_id=1, source_target_pairs={{0,4},{1,5},{2,6},{3,7},{4,0},{5,1},{6,2},{7,3},{8,12},{9,13},{10,... | collective-permute-start | bytes 983048 | tf_op jit(solution)/shard_map/ppermute | solution.py:28
  143.6 9.9 %collective-permute-start.7 = (f32[4,8,2048]{2,1,0:T(8,128)S(1)}, f32[4,8,2048]{2,1,0:T(8,128)S(1)}, u32[]{:S(2)}, u32[]{:S(2)}) collective-permute-start(f32[4,8,2048]{2,1,0:T(8,128)S(1)} %pad_maximum_fusion.2), channel_id=1, source_target_pairs={{0,2},{1,3},{2,0},{3,1},{4,6},{5,7},{6,4},{7,5},{8,10},{9,11},{10,... | collective-permute-start | bytes 786440 | tf_op jit(solution)/shard_map/ppermute | solution.py:28
  155.7 12.3 %collective-permute-start.8 = (f32[5,8,2048]{2,1,0:T(8,128)}, f32[5,8,2048]{2,1,0:T(8,128)}, u32[]{:S(2)}, u32[]{:S(2)}) collective-permute-start(f32[5,8,2048]{2,1,0:T(8,128)} %pad_maximum_fusion.1), channel_id=1, source_target_pairs={{0,1},{1,0},{2,3},{3,2},{4,5},{5,4},{6,7},{7,6},{8,9},{9,8},{10,11... | collective-permute-start | bytes 983048 | tf_op jit(solution)/shard_map/ppermute | solution.py:28
  171.6 41.2 %copy-start.27 = (pred[12]{0:T(512)(128)(4,1)S(1)}, pred[12]{0:T(512)(128)(4,1)}, u32[]{:S(2)}) copy-start(pred[12]{0:T(512)(128)(4,1)} %compare_and_fusion) | copy-start | bytes 40
  172.5 46.7 %copy-start.25 = (s32[1,12]{1,0:T(1,128)S(1)}, s32[1,12]{1,0:T(1,128)}, u32[]{:S(2)}) copy-start(s32[1,12]{1,0:T(1,128)} %param.21) | copy-start | bytes 148
  172.5 46.7 %copy-start.36 = (pred[12]{0:T(512)(128)(4,1)S(1)}, pred[12]{0:T(512)(128)(4,1)}, u32[]{:S(2)}) copy-start(pred[12]{0:T(512)(128)(4,1)} %iota_compare_fusion.4) | copy-start | bytes 40
  173.6 31.2 %collective-permute-start.15 = (f32[12288]{0:T(1024)S(1)}, f32[12288]{0:T(1024)S(1)}, u32[]{:S(2)}, u32[]{:S(2)}) collective-permute-start(f32[12288]{0:T(1024)S(1)} %constant_dynamic-update-slice_fusion.93), channel_id=1, source_target_pairs={{0,8},{8,0},{16,24},{24,16},{32,40},{40,32},{48,56},{56,48},{64,72... | collective-permute-start | bytes 147464 | tf_op jit(solution)/shard_map/ppermute | solution.py:28
  175.6 29.3 %collective-permute-start.14 = (bf16[16,128]{1,0:T(8,128)(2,1)S(1)}, bf16[16,128]{1,0:T(8,128)(2,1)S(1)}, u32[]{:S(2)}, u32[]{:S(2)}) collective-permute-start(bf16[16,128]{1,0:T(8,128)(2,1)S(1)} %pad_maximum_fusion.8), channel_id=1, source_target_pairs={{0,24},{8,32},{16,40},{24,48},{32,56},{40,64},{48,72},{56,80},{64,... | collective-permute-start | bytes 12296 | tf_op jit(solution)/shard_map/ppermute | solution.py:23
  177.9 26.9 %collective-permute-start.13 = (bf16[16,128]{1,0:T(8,128)(2,1)S(1)}, bf16[16,128]{1,0:T(8,128)(2,1)S(1)}, u32[]{:S(2)}, u32[]{:S(2)}) collective-permute-start(bf16[16,128]{1,0:T(8,128)(2,1)S(1)} %pad_maximum_fusion.7), channel_id=1, source_target_pairs={{0,16},{8,24},{16,32},{24,40},{32,48},{40,56},{48,64},{56,72},{64,... | collective-permute-start | bytes 12296 | tf_op jit(solution)/shard_map/ppermute | solution.py:23
  179.8 24.9 %collective-permute-start.10 = (bf16[24,128]{1,0:T(8,128)(2,1)S(1)}, bf16[24,128]{1,0:T(8,128)(2,1)S(1)}, u32[]{:S(2)}, u32[]{:S(2)}) collective-permute-start(bf16[24,128]{1,0:T(8,128)(2,1)S(1)} %pad_maximum_fusion.4), channel_id=1, source_target_pairs={{0,504},{8,0},{16,8},{24,16},{32,24},{40,32},{48,40},{56,48},{64,5... | collective-permute-start | bytes 18440 | tf_op jit(solution)/shard_map/ppermute | solution.py:23
  185.3 5.1 %collective-permute-start.11 = (bf16[16,128]{1,0:T(8,128)(2,1)S(1)}, bf16[16,128]{1,0:T(8,128)(2,1)S(1)}, u32[]{:S(2)}, u32[]{:S(2)}) collective-permute-start(bf16[16,128]{1,0:T(8,128)(2,1)S(1)} %pad_maximum_fusion.5), channel_id=1, source_target_pairs={{0,488},{8,496},{16,504},{24,0},{32,8},{40,16},{48,24},{56,32},{64... | collective-permute-start | bytes 12296 | tf_op jit(solution)/shard_map/ppermute | solution.py:23
  190.4 6.9 %collective-permute-start.12 = (bf16[16,128]{1,0:T(8,128)(2,1)S(1)}, bf16[16,128]{1,0:T(8,128)(2,1)S(1)}, u32[]{:S(2)}, u32[]{:S(2)}) collective-permute-start(bf16[16,128]{1,0:T(8,128)(2,1)S(1)} %pad_maximum_fusion.6), channel_id=1, source_target_pairs={{0,496},{8,504},{16,0},{24,8},{32,16},{40,24},{48,32},{56,40},{64,... | collective-permute-start | bytes 12296 | tf_op jit(solution)/shard_map/ppermute | solution.py:23
  197.3 7.0 %collective-permute-start.9 = (bf16[24,128]{1,0:T(8,128)(2,1)S(1)}, bf16[24,128]{1,0:T(8,128)(2,1)S(1)}, u32[]{:S(2)}, u32[]{:S(2)}) collective-permute-start(bf16[24,128]{1,0:T(8,128)(2,1)S(1)} %pad_maximum_fusion.3), channel_id=1, source_target_pairs={{0,8},{8,16},{16,24},{24,32},{32,40},{40,48},{48,56},{56,64},{64,7... | collective-permute-start | bytes 18440 | tf_op jit(solution)/shard_map/ppermute | solution.py:23
  204.9 6.0 %collective-permute-start.16 = (f32[12288]{0:T(1024)S(1)}, f32[12288]{0:T(1024)S(1)}, u32[]{:S(2)}, u32[]{:S(2)}) collective-permute-start(f32[12288]{0:T(1024)S(1)} %add.735), channel_id=1, source_target_pairs={{0,256},{8,264},{16,272},{24,280},{32,288},{40,296},{48,304},{56,3... | collective-permute-start | bytes 147464 | tf_op jit(solution)/shard_map/ppermute | solution.py:28
  210.9 6.4 %collective-permute-start.17 = (f32[12288]{0:T(1024)S(1)}, f32[12288]{0:T(1024)S(1)}, u32[]{:S(2)}, u32[]{:S(2)}) collective-permute-start(f32[12288]{0:T(1024)S(1)} %add.736), channel_id=1, source_target_pairs={{0,16},{8,24},{16,0},{24,8},{32,48},{40,56},{48,32},{56,40},{64,80... | collective-permute-start | bytes 147464 | tf_op jit(solution)/shard_map/ppermute | solution.py:28
  217.3 6.9 %collective-permute-start.18 = (f32[12288]{0:T(1024)S(1)}, f32[12288]{0:T(1024)S(1)}, u32[]{:S(2)}, u32[]{:S(2)}) collective-permute-start(f32[12288]{0:T(1024)S(1)} %add.737), channel_id=1, source_target_pairs={{0,32},{8,40},{16,48},{24,56},{32,0},{40,8},{48,16},{56,24},{64,96... | collective-permute-start | bytes 147464 | tf_op jit(solution)/shard_map/ppermute | solution.py:28
  224.2 10.0 %collective-permute-start.19 = (f32[12288]{0:T(1024)S(1)}, f32[12288]{0:T(1024)S(1)}, u32[]{:S(2)}, u32[]{:S(2)}) collective-permute-start(f32[12288]{0:T(1024)S(1)} %add.738), channel_id=1, source_target_pairs={{0,64},{8,72},{16,80},{24,88},{32,96},{40,104},{48,112},{56,120},{... | collective-permute-start | bytes 147464 | tf_op jit(solution)/shard_map/ppermute | solution.py:28
  234.2 14.7 %collective-permute-start.20 = (f32[12288]{0:T(1024)S(1)}, f32[12288]{0:T(1024)S(1)}, u32[]{:S(2)}, u32[]{:S(2)}) collective-permute-start(f32[12288]{0:T(1024)S(1)} %add.739), channel_id=1, source_target_pairs={{0,128},{8,136},{16,144},{24,152},{32,160},{40,168},{48,176},{56,1... | collective-permute-start | bytes 147464 | tf_op jit(solution)/shard_map/ppermute | solution.py:28
  (37 other events, 451.0 us)

commit v2 on v1

v2 whole, which is shorter than its diff:
```python
import jax
import jax.numpy as jnp
from jax import lax
from jax.sharding import PartitionSpec as P

BLK = 128
NB = 16
REACH = 3
SLOTS = 12
HI = lax.Precision.HIGHEST


def shifts():
    return [e for e in range(-REACH, REACH + 1) if e != 0]


def shift_index(e):
    return e + REACH if e < 0 else e + REACH - 1


def send_by(x, axis, by):
    devices = lax.axis_size(axis)
    return lax.ppermute(x, axis, [(i, (i + by) % devices) for i in range(devices)])


def swap_with(x, axis, mask):
    devices = lax.axis_size(axis)
    return lax.ppermute(x, axis, [(i, i ^ mask) for i in range(devices)])


def slot_tables(long_sources, me, row_devices):
    steps = jnp.array(shifts(), jnp.int32)
    partners = jnp.concatenate([jnp.mod(me + steps, row_devices), jnp.mod(me - steps, row_devices)])
    rows = jnp.take(long_sources, partners, axis=0)
    hit = (rows // NB) == me
    earlier = jnp.arange(SLOTS)[None, :] < jnp.arange(SLOTS)[:, None]
    rank = jnp.sum((hit[:, None, :] & earlier[None]).astype(jnp.int32), axis=2)
    local = rows % NB
    picks = [jnp.sum(jnp.where(hit & (rank == q), local, 0), axis=1) for q in range(2)]
    table = jnp.stack(picks, 1)
    return table[: len(shifts())], table[len(shifts()):]


def own_slot_pairs(long_sources, me, row_devices):
    source = lax.dynamic_index_in_dim(long_sources, me, 0, keepdims=False)
    owner = source // NB
    offset = jnp.mod(owner - me, row_devices)
    offset = jnp.where(offset > row_devices // 2, offset - row_devices, offset)
    same = (owner[:, None] == owner[None, :]) & (
        jnp.arange(SLOTS)[None, :] < jnp.arange(SLOTS)[:, None]
    )
    rank = jnp.sum(same.astype(jnp.int32), axis=1)
    send_position = jnp.where(offset < 0, offset + REACH, offset + REACH - 1)
    read_position = jnp.where(offset > 0, -offset + REACH, -offset + REACH - 1)
    return send_position * 2 + rank, read_position * 2 + rank


def inverse_of(pairs):
    return jnp.sum(
        jnp.where(pairs[None, :] == jnp.arange(SLOTS)[:, None], jnp.arange(SLOTS)[None, :], 0), axis=1
    )


def forward_sum(blocks, prev_edge, next_edge, panels, band_blocks, long_in_order, targets_in_order):
    earlier = jnp.concatenate([prev_edge[:, None], blocks[:, :-1]], 1)
    onward = jnp.concatenate([blocks[:, 1:], next_edge[:, None]], 1)
    near = jnp.einsum("fbm,bnm->fbn", earlier, band_blocks[:, 0], preferred_element_type=jnp.float32)
    near = near + jnp.einsum("fbm,bnm->fbn", blocks, band_blocks[:, 1], preferred_element_type=jnp.float32)
    near = near + jnp.einsum("fbm,bnm->fbn", onward, band_blocks[:, 2], preferred_element_type=jnp.float32)
    contrib = jnp.einsum("kfm,knm->kfn", panels, long_in_order, preferred_element_type=jnp.float32)
    far = jnp.einsum("kb,kfn->fbn", targets_in_order, contrib, precision=HI)
    return near + far


def local(
    features,
    weight_in,
    weight_out,
    score_grad,
    band_blocks,
    long_blocks,
    long_rows,
    long_sources,
    long_counts,
):
    row_devices = lax.axis_size("row")
    col_devices = lax.axis_size("col")
    me = lax.axis_index("row")
    col_index = lax.axis_index("col")
    row_ids = long_rows[0]
    hidden_count = weight_in.shape[1]
    class_count = score_grad.shape[0]
    nodes = features.shape[1]
    h_rows = hidden_count
    f_rows = features.shape[0]
    c_rows = class_count
    hf_rows = h_rows + f_rows
    up = shift_index(1)
    down = shift_index(-1)

    live_count = lax.dynamic_index_in_dim(long_counts, me, 0, keepdims=False)
    is_live = jnp.arange(SLOTS, dtype=jnp.int32) < live_count
    live = is_live.astype(jnp.float32)
    targets = (
        (row_ids[:, None] == jnp.arange(NB, dtype=jnp.int32)[None, :]) & is_live[:, None]
    ).astype(jnp.float32)
    send_pair, read_pair = own_slot_pairs(long_sources, me, row_devices)
    sending_slot = inverse_of(send_pair)
    reading_slot = inverse_of(read_pair)
    long_read = jnp.take(long_blocks, reading_slot, axis=0)
    targets_read = jnp.take(targets, reading_slot, axis=0)
    wanted, landing_blocks = slot_tables(long_sources, me, row_devices)
    edge_block = jnp.array([[NB - 1 if e == 1 else 0] for e in shifts()], jnp.int32)
    pick = jnp.concatenate([wanted, edge_block], 1).reshape(-1)

    hidden_in = jnp.einsum(
        "ih,in->hn", weight_in, features, preferred_element_type=jnp.float32
    ).astype(jnp.bfloat16)
    both_in = jnp.concatenate([hidden_in, features], 0)
    both_blocks = both_in.reshape(hf_rows, NB, BLK)

    sg_blocks = score_grad.reshape(class_count, NB, BLK)
    sg_prior = jnp.einsum("fbn,bnm->fbm", sg_blocks, band_blocks[:, 0], preferred_element_type=jnp.float32)
    sg_middle = jnp.einsum("fbn,bnm->fbm", sg_blocks, band_blocks[:, 1], preferred_element_type=jnp.float32)
    sg_later = jnp.einsum("fbn,bnm->fbm", sg_blocks, band_blocks[:, 2], preferred_element_type=jnp.float32)
    sg_rows = jnp.take(sg_blocks, jnp.take(row_ids, sending_slot), axis=1)
    sg_out = jnp.einsum(
        "fkn,knm->kfm", sg_rows, jnp.take(long_blocks, sending_slot, axis=0),
        preferred_element_type=jnp.float32,
    )
    sg_out = sg_out * jnp.take(live, sending_slot)[:, None, None]
    sg_edges = jnp.zeros((len(shifts()), 1, c_rows, BLK), jnp.float32)
    sg_edges = sg_edges.at[up, 0].set(sg_later[:, NB - 1]).at[down, 0].set(sg_prior[:, 0])
    sg_send = jnp.concatenate([sg_out.reshape(len(shifts()), 2, c_rows, BLK), sg_edges], 1)

    picked = jnp.take(both_blocks.transpose(1, 0, 2), pick, axis=0)
    picked = picked.reshape(len(shifts()), 3, hf_rows, BLK).astype(jnp.float32)
    send_all = jnp.concatenate([picked, sg_send], 2)
    arrived = [send_by(send_all[i], "row", e) for i, e in enumerate(shifts())]
    pairs_in = jnp.concatenate([a[:2] for a in arrived], 0)

    both_sum = forward_sum(
        both_blocks,
        arrived[up][2, :hf_rows].astype(jnp.bfloat16),
        arrived[down][2, :hf_rows].astype(jnp.bfloat16),
        pairs_in[:, :hf_rows].astype(jnp.bfloat16),
        band_blocks,
        long_read,
        targets_read,
    )
    hidden_sum = both_sum[:h_rows].reshape(h_rows, nodes)
    feat_sum = both_sum[h_rows:].reshape(f_rows, nodes)

    landing = (
        landing_blocks.reshape(-1)[:, None] == jnp.arange(NB, dtype=jnp.int32)[None, :]
    ).astype(jnp.float32)
    sg_sum = (
        sg_middle
        + jnp.concatenate([sg_prior[:, 1:], arrived[down][2, hf_rows:][:, None]], 1)
        + jnp.concatenate([arrived[up][2, hf_rows:][:, None], sg_later[:, :-1]], 1)
        + jnp.einsum("kb,kfm->fbm", landing, pairs_in[:, hf_rows:], precision=HI)
    )
    class_back = sg_sum.reshape(c_rows, nodes).astype(jnp.bfloat16)

    hidden_act = jax.nn.silu(hidden_sum).astype(jnp.bfloat16)

    my_rows = lax.dynamic_slice_in_dim(weight_out, col_index * hidden_count, hidden_count, 0)
    class_part = jnp.einsum("hc,hn->cn", my_rows, hidden_act, preferred_element_type=jnp.float32)
    reduced = class_part.reshape(col_devices, c_rows, nodes)
    gathered = class_back.reshape(1, c_rows, nodes)
    mask = col_devices // 2
    while mask >= 1:
        bit = (col_index // mask) % 2
        halves = reduced.reshape(2, -1, c_rows, nodes)
        keep = lax.dynamic_index_in_dim(halves, bit, 0, keepdims=False)
        away = lax.dynamic_index_in_dim(halves, 1 - bit, 0, keepdims=False)
        count = away.shape[0]
        both = swap_with(jnp.concatenate([away, gathered.astype(jnp.float32)], 0), "col", mask)
        reduced = keep + both[:count]
        other = both[count:].astype(jnp.bfloat16)
        gathered = jnp.where(
            bit == 0,
            jnp.concatenate([gathered, other], 0),
            jnp.concatenate([other, gathered], 0),
        )
        mask //= 2
    class_in = reduced.reshape(c_rows, nodes).astype(jnp.bfloat16)
    order = []
    for j in range(col_devices):
        rev = 0
        bits = col_devices.bit_length() - 1
        for k in range(bits):
            if j & (1 << k):
                rev |= 1 << (bits - 1 - k)
        order.append(rev)
    all_back = gathered.reshape(col_devices * c_rows, nodes)
    out_order = jnp.array(
        [order[j] * c_rows + k for j in range(col_devices) for k in range(c_rows)], jnp.int32
    )
    rows_in_order = jnp.take(my_rows, out_order, axis=1)

    hidden_back = jnp.einsum("hc,cn->hn", rows_in_order, all_back, preferred_element_type=jnp.float32)
    block_grad = jnp.einsum("hn,cn->hc", hidden_act, all_back, preferred_element_type=jnp.float32)
    inverse = [0] * (col_devices * c_rows)
    for pos in range(col_devices * c_rows):
        inverse[int(order[pos // c_rows]) * c_rows + pos % c_rows] = pos
    second_part = jnp.take(block_grad, jnp.array(inverse, jnp.int32), axis=1)

    sigmoid_val = jax.nn.sigmoid(hidden_sum)
    slope_back = (hidden_back * sigmoid_val * (1.0 + hidden_sum * (1.0 - sigmoid_val))).astype(
        jnp.bfloat16
    )
    first_part = jnp.einsum(
        "in,hn->ih", feat_sum, slope_back.astype(jnp.float32), precision=HI
    )

    class_blocks = class_in.reshape(c_rows, NB, BLK)
    class_pick = jnp.take(class_blocks.transpose(1, 0, 2), pick, axis=0)
    class_pick = class_pick.reshape(len(shifts()), 3, c_rows, BLK)
    class_arrived = [send_by(class_pick[i], "row", e) for i, e in enumerate(shifts())]
    class_pairs = jnp.concatenate([a[:2] for a in class_arrived], 0)
    scores = forward_sum(
        class_blocks,
        class_arrived[up][2],
        class_arrived[down][2],
        class_pairs,
        band_blocks,
        long_read,
        targets_read,
    ).reshape(c_rows, nodes).astype(jnp.bfloat16)

    flat = jnp.concatenate([first_part.reshape(-1), second_part.reshape(-1)])
    for mask in [1, row_devices // 2] + [m for m in (2, 4, 8, 16, 32) if m < row_devices // 2]:
        if mask < row_devices:
            flat = flat + swap_with(flat, "row", mask)
    first_grad = flat[: first_part.size].reshape(first_part.shape)
    second_grad = flat[first_part.size:].reshape(second_part.shape)
    return (scores, first_grad, second_grad)


def solution(mesh):
    return jax.shard_map(
        local,
        mesh=mesh,
        in_specs=(
            P(None, "row"),
            P(None, "col"),
            P(),
            P("col", "row"),
            P("row", None, None, None),
            P("row", None, None),
            P("row", None),
            P(),
            P(),
        ),
        out_specs=(P("col", "row"), P(None, "col"), P("col", None)),
        check_vma=False,
    )
```

time: 254 us -> 214 us (0.84)
  the two profiles are of different devices: /device:TPU:4 before, /device:TPU:8 now
where the time goes in v2:
time: 214 us; the launch traced here: 212 us
  starting transfers between devices  68.8 us (32%)
  waiting for transfers between devices  56.3 us (26%)
  local copies, waits for them, and re-layouts  47.2 us (22%)
  matrix products  21.5 us (10%)
  other arithmetic  16.8 us (8%)
    ppermute x9, waiting for transfers between devices, swap_with(): return lax.ppermute(x, axis, [(i, i ^ mask) for i in range(devices)])  46.2 us
    ppermute x12, starting transfers between devices, send_by(): lax.ppermute(x, axis, [(i, (i + by) % devices) for i in range(devices)])  43.7 us
    ppermute x9, starting transfers between devices, swap_with(): return lax.ppermute(x, axis, [(i, i ^ mask) for i in range(devices)])  25.1 us
    unnamed x87, local copies, waits for them, and re-layouts  12.6 us
    ppermute x12, waiting for transfers between devices, send_by(): lax.ppermute(x, axis, [(i, (i + by) % devices) for i in range(devices)])  10.1 us
  transfers between devices with their start and end apart: 21, of which 9 were waited for; matrix products, arithmetic and copies ran while one was open for 16% of the time, Pallas kernels for 0%

profile of v2, /device:TPU:8, one launch (start us, length us, event | category | flops | bytes accessed | tf_op | source)
XLA Modules:
  0.0 212.2 jit_solution(1823436740611125267)
XLA Ops:
  20.0 12.2 %collective-permute-start.2 = (f32[3,200,128]{2,1,0:T(8,128)}, f32[3,200,128]{2,1,0:T(8,128)}, u32[]{:S(2)}, u32[]{:S(2)}) collective-permute-start(f32[3,200,128]{2,1,0:T(8,128)} %get-tuple-element.50), channel_id=1, source_target_pairs={{0,488},{8,496},{16,504},{24,0},{32,8},{40,16},{48,24},{56,32},{64... | collective-permute-start | bytes 921608 | tf_op jit(solution)/shard_map/ppermute | solution.py:23
  32.2 2.9 %collective-permute-start.3 = (f32[3,200,128]{2,1,0:T(8,128)}, f32[3,200,128]{2,1,0:T(8,128)}, u32[]{:S(2)}, u32[]{:S(2)}) collective-permute-start(f32[3,200,128]{2,1,0:T(8,128)} %get-tuple-element.49), channel_id=1, source_target_pairs={{0,496},{8,504},{16,0},{24,8},{32,16},{40,24},{48,32},{56,40},{64,... | collective-permute-start | bytes 921608 | tf_op jit(solution)/shard_map/ppermute | solution.py:23
  35.1 2.5 %collective-permute-start.1 = (f32[3,200,128]{2,1,0:T(8,128)}, f32[3,200,128]{2,1,0:T(8,128)}, u32[]{:S(2)}, u32[]{:S(2)}) collective-permute-start(f32[3,200,128]{2,1,0:T(8,128)} %get-tuple-element.51), channel_id=1, source_target_pairs={{0,504},{8,0},{16,8},{24,16},{32,24},{40,32},{48,40},{56,48},{64,5... | collective-permute-start | bytes 921608 | tf_op jit(solution)/shard_map/ppermute | solution.py:23
  39.6 2.9 %collective-permute-start.4 = (f32[3,200,128]{2,1,0:T(8,128)}, f32[3,200,128]{2,1,0:T(8,128)}, u32[]{:S(2)}, u32[]{:S(2)}) collective-permute-start(f32[3,200,128]{2,1,0:T(8,128)} %get-tuple-element.48), channel_id=1, source_target_pairs={{0,16},{8,24},{16,32},{24,40},{32,48},{40,56},{48,64},{56,72},{64,... | collective-permute-start | bytes 921608 | tf_op jit(solution)/shard_map/ppermute | solution.py:23
  49.9 2.6 %collective-permute-start.5 = (f32[3,200,128]{2,1,0:T(8,128)}, f32[3,200,128]{2,1,0:T(8,128)S(1)}, u32[]{:S(2)}, u32[]{:S(2)}) collective-permute-start(f32[3,200,128]{2,1,0:T(8,128)} %get-tuple-element.47), channel_id=1, source_target_pairs={{0,24},{8,32},{16,40},{24,48},{32,56},{40,64},{48,72},{56,80},{64,... | collective-permute-start | bytes 921608 | tf_op jit(solution)/shard_map/ppermute | solution.py:23
  57.4 10.1 %collective-permute-done.5 = f32[3,200,128]{2,1,0:T(8,128)S(1)} collective-permute-done((f32[3,200,128]{2,1,0:T(8,128)}, f32[3,200,128]{2,1,0:T(8,128)S(1)}, u32[]{:S(2)}, u32[]{:S(2)}) %collective-permute-start.5) | collective-permute-done | bytes 307232 | tf_op jit(solution)/shard_map/ppermute | solution.py:23
  68.6 2.4 %fusion.2 = f32[192,128,16]{1,2,0:T(8,128)S(1)} fusion(f32[12,192,128]{2,1,0:T(8,128)S(1)} %fusion.15, f32[12,16]{1,0:T(8,128)S(1)} %gather_fusion.5, pred[12]{0:T(512)(128)(4,1)S(1)} %compare_and_fusion), kind=kOutput, calls=%fused_computation.17 | convolution fusion | flops 56623296 | bytes 2753292 | tf_op jit(solution)/shard_map/kb,kfn->fbn/dot_general | solution.py:71
  86.3 4.2 %collective-permute-start.6 = (f32[5,8,2048]{2,1,0:T(8,128)}, f32[5,8,2048]{2,1,0:T(8,128)}, u32[]{:S(2)}, u32[]{:S(2)}) collective-permute-start(f32[5,8,2048]{2,1,0:T(8,128)} %pad_maximum_fusion), channel_id=1, source_target_pairs={{0,4},{1,5},{2,6},{3,7},{4,0},{5,1},{6,2},{7,3},{8,12},{9,13},{10,... | collective-permute-start | bytes 983048 | tf_op jit(solution)/shard_map/ppermute | solution.py:28
  90.6 9.2 %collective-permute-done.6 = f32[5,8,2048]{2,1,0:T(8,128)} collective-permute-done((f32[5,8,2048]{2,1,0:T(8,128)}, f32[5,8,2048]{2,1,0:T(8,128)}, u32[]{:S(2)}, u32[]{:S(2)}) %collective-permute-start.6) | collective-permute-done | bytes 327712 | tf_op jit(solution)/shard_map/ppermute | solution.py:28
  104.6 2.3 %collective-permute-start.7 = (f32[4,8,2048]{2,1,0:T(8,128)}, f32[4,8,2048]{2,1,0:T(8,128)}, u32[]{:S(2)}, u32[]{:S(2)}) collective-permute-start(f32[4,8,2048]{2,1,0:T(8,128)} %pad_maximum_fusion.2), channel_id=1, source_target_pairs={{0,2},{1,3},{2,0},{3,1},{4,6},{5,7},{6,4},{7,5},{8,10},{9,11},{10,... | collective-permute-start | bytes 786440 | tf_op jit(solution)/shard_map/ppermute | solution.py:28
  108.2 6.0 %collective-permute-done.7 = f32[4,8,2048]{2,1,0:T(8,128)} collective-permute-done((f32[4,8,2048]{2,1,0:T(8,128)}, f32[4,8,2048]{2,1,0:T(8,128)}, u32[]{:S(2)}, u32[]{:S(2)}) %collective-permute-start.7) | collective-permute-done | bytes 262176 | tf_op jit(solution)/shard_map/ppermute | solution.py:28
  118.6 4.6 %collective-permute-start.8 = (f32[5,8,2048]{2,1,0:T(8,128)}, f32[5,8,2048]{2,1,0:T(8,128)}, u32[]{:S(2)}, u32[]{:S(2)}) collective-permute-start(f32[5,8,2048]{2,1,0:T(8,128)} %pad_maximum_fusion.1), channel_id=1, source_target_pairs={{0,1},{1,0},{2,3},{3,2},{4,5},{5,4},{6,7},{7,6},{8,9},{9,8},{10,11... | collective-permute-start | bytes 983048 | tf_op jit(solution)/shard_map/ppermute | solution.py:28
  135.5 4.7 %collective-permute-start.11 = (bf16[3,8,128]{2,1,0:T(8,128)(2,1)}, bf16[3,8,128]{2,1,0:T(8,128)(2,1)}, u32[]{:S(2)}, u32[]{:S(2)}) collective-permute-start(bf16[3,8,128]{2,1,0:T(8,128)(2,1)} %get-tuple-element.62), channel_id=1, source_target_pairs={{0,488},{8,496},{16,504},{24,0},{32,8},{40,16},{48,24},{56,32},{64... | collective-permute-start | bytes 18440 | tf_op jit(solution)/shard_map/ppermute | solution.py:23
  142.2 2.9 %collective-permute-start.10 = (bf16[3,8,128]{2,1,0:T(8,128)(2,1)}, bf16[3,8,128]{2,1,0:T(8,128)(2,1)}, u32[]{:S(2)}, u32[]{:S(2)}) collective-permute-start(bf16[3,8,128]{2,1,0:T(8,128)(2,1)} %get-tuple-element.63), channel_id=1, source_target_pairs={{0,504},{8,0},{16,8},{24,16},{32,24},{40,32},{48,40},{56,48},{64,5... | collective-permute-start | bytes 18440 | tf_op jit(solution)/shard_map/ppermute | solution.py:23
  145.1 3.6 %collective-permute-start.13 = (bf16[3,8,128]{2,1,0:T(8,128)(2,1)}, bf16[3,8,128]{2,1,0:T(8,128)(2,1)}, u32[]{:S(2)}, u32[]{:S(2)}) collective-permute-start(bf16[3,8,128]{2,1,0:T(8,128)(2,1)} %get-tuple-element.60), channel_id=1, source_target_pairs={{0,16},{8,24},{16,32},{24,40},{32,48},{40,56},{48,64},{56,72},{64,... | collective-permute-start | bytes 18440 | tf_op jit(solution)/shard_map/ppermute | solution.py:23
  155.7 3.5 %collective-permute-start.14 = (bf16[3,8,128]{2,1,0:T(8,128)(2,1)S(1)}, bf16[3,8,128]{2,1,0:T(8,128)(2,1)S(1)}, u32[]{:S(2)}, u32[]{:S(2)}) collective-permute-start(bf16[3,8,128]{2,1,0:T(8,128)(2,1)S(1)} %get-tuple-element.59), channel_id=1, source_target_pairs={{0,24},{8,32},{16,40},{24,48},{32,56},{40,64},{48,72},{56,80},{64,... | collective-permute-start | bytes 18440 | tf_op jit(solution)/shard_map/ppermute | solution.py:23
  166.4 2.4 %collective-permute-start.16 = (f32[12288]{0:T(1024)S(1)}, f32[12288]{0:T(1024)S(1)}, u32[]{:S(2)}, u32[]{:S(2)}) collective-permute-start(f32[12288]{0:T(1024)S(1)} %add.359), channel_id=1, source_target_pairs={{0,256},{8,264},{16,272},{24,280},{32,288},{40,296},{48,304},{56,3... | collective-permute-start | bytes 147464 | tf_op jit(solution)/shard_map/ppermute | solution.py:28
  168.9 3.6 %collective-permute-done.16 = f32[12288]{0:T(1024)S(1)} collective-permute-done((f32[12288]{0:T(1024)S(1)}, f32[12288]{0:T(1024)S(1)}, u32[]{:S(2)}, u32[]{:S(2)}) %collective-permute-start.16) | collective-permute-done | bytes 49184 | tf_op jit(solution)/shard_map/ppermute | solution.py:28
  172.4 2.3 %collective-permute-start.17 = (f32[12288]{0:T(1024)S(1)}, f32[12288]{0:T(1024)S(1)}, u32[]{:S(2)}, u32[]{:S(2)}) collective-permute-start(f32[12288]{0:T(1024)S(1)} %add.360), channel_id=1, source_target_pairs={{0,16},{8,24},{16,0},{24,8},{32,48},{40,56},{48,32},{56,40},{64,80... | collective-permute-start | bytes 147464 | tf_op jit(solution)/shard_map/ppermute | solution.py:28
  175.8 2.7 %collective-permute-done.17 = f32[12288]{0:T(1024)S(1)} collective-permute-done((f32[12288]{0:T(1024)S(1)}, f32[12288]{0:T(1024)S(1)}, u32[]{:S(2)}, u32[]{:S(2)}) %collective-permute-start.17) | collective-permute-done | bytes 49184 | tf_op jit(solution)/shard_map/ppermute | solution.py:28
  180.8 4.9 %collective-permute-done.18 = f32[12288]{0:T(1024)S(1)} collective-permute-done((f32[12288]{0:T(1024)S(1)}, f32[12288]{0:T(1024)S(1)}, u32[]{:S(2)}, u32[]{:S(2)}) %collective-permute-start.18) | collective-permute-done | bytes 49184 | tf_op jit(solution)/shard_map/ppermute | solution.py:28
  188.3 7.8 %collective-permute-done.19 = f32[12288]{0:T(1024)S(1)} collective-permute-done((f32[12288]{0:T(1024)S(1)}, f32[12288]{0:T(1024)S(1)}, u32[]{:S(2)}, u32[]{:S(2)}) %collective-permute-start.19) | collective-permute-done | bytes 49184 | tf_op jit(solution)/shard_map/ppermute | solution.py:28
  196.0 3.4 %collective-permute-start.20 = (f32[12288]{0:T(1024)S(1)}, f32[12288]{0:T(1024)S(1)}, u32[]{:S(2)}, u32[]{:S(2)}) collective-permute-start(f32[12288]{0:T(1024)S(1)} %add.363), channel_id=1, source_target_pairs={{0,128},{8,136},{16,144},{24,152},{32,160},{40,168},{48,176},{56,1... | collective-permute-start | bytes 147464 | tf_op jit(solution)/shard_map/ppermute | solution.py:28
  200.5 10.3 %collective-permute-done.20 = f32[12288]{0:T(1024)S(1)} collective-permute-done((f32[12288]{0:T(1024)S(1)}, f32[12288]{0:T(1024)S(1)}, u32[]{:S(2)}, u32[]{:S(2)}) %collective-permute-start.20) | collective-permute-done | bytes 49184 | tf_op jit(solution)/shard_map/ppermute | solution.py:28
  (237 shorter events, 96.6 us)
Async XLA Ops:
  20.0 29.9 %collective-permute-start.2 = (f32[3,200,128]{2,1,0:T(8,128)}, f32[3,200,128]{2,1,0:T(8,128)}, u32[]{:S(2)}, u32[]{:S(2)}) collective-permute-start(f32[3,200,128]{2,1,0:T(8,128)} %get-tuple-element.50), channel_id=1, source_target_pairs={{0,488},{8,496},{16,504},{24,0},{32,8},{40,16},{48,24},{56,32},{64... | collective-permute-start | bytes 921608 | tf_op jit(solution)/shard_map/ppermute | solution.py:23
  32.2 21.3 %collective-permute-start.3 = (f32[3,200,128]{2,1,0:T(8,128)}, f32[3,200,128]{2,1,0:T(8,128)}, u32[]{:S(2)}, u32[]{:S(2)}) collective-permute-start(f32[3,200,128]{2,1,0:T(8,128)} %get-tuple-element.49), channel_id=1, source_target_pairs={{0,496},{8,504},{16,0},{24,8},{32,16},{40,24},{48,32},{56,40},{64,... | collective-permute-start | bytes 921608 | tf_op jit(solution)/shard_map/ppermute | solution.py:23
  35.1 19.4 %collective-permute-start.1 = (f32[3,200,128]{2,1,0:T(8,128)}, f32[3,200,128]{2,1,0:T(8,128)}, u32[]{:S(2)}, u32[]{:S(2)}) collective-permute-start(f32[3,200,128]{2,1,0:T(8,128)} %get-tuple-element.51), channel_id=1, source_target_pairs={{0,504},{8,0},{16,8},{24,16},{32,24},{40,32},{48,40},{56,48},{64,5... | collective-permute-start | bytes 921608 | tf_op jit(solution)/shard_map/ppermute | solution.py:23
  37.6 17.8 %collective-permute-start = (f32[3,200,128]{2,1,0:T(8,128)}, f32[3,200,128]{2,1,0:T(8,128)}, u32[]{:S(2)}, u32[]{:S(2)}) collective-permute-start(f32[3,200,128]{2,1,0:T(8,128)} %get-tuple-element.52), channel_id=1, source_target_pairs={{0,8},{8,16},{16,24},{24,32},{32,40},{40,48},{48,56},{56,64},{64,7... | collective-permute-start | bytes 921608 | tf_op jit(solution)/shard_map/ppermute | solution.py:23
  39.6 16.9 %collective-permute-start.4 = (f32[3,200,128]{2,1,0:T(8,128)}, f32[3,200,128]{2,1,0:T(8,128)}, u32[]{:S(2)}, u32[]{:S(2)}) collective-permute-start(f32[3,200,128]{2,1,0:T(8,128)} %get-tuple-element.48), channel_id=1, source_target_pairs={{0,16},{8,24},{16,32},{24,40},{32,48},{40,56},{48,64},{56,72},{64,... | collective-permute-start | bytes 921608 | tf_op jit(solution)/shard_map/ppermute | solution.py:23
  49.9 17.5 %collective-permute-start.5 = (f32[3,200,128]{2,1,0:T(8,128)}, f32[3,200,128]{2,1,0:T(8,128)S(1)}, u32[]{:S(2)}, u32[]{:S(2)}) collective-permute-start(f32[3,200,128]{2,1,0:T(8,128)} %get-tuple-element.47), channel_id=1, source_target_pairs={{0,24},{8,32},{16,40},{24,48},{32,56},{40,64},{48,72},{56,80},{64,... | collective-permute-start | bytes 921608 | tf_op jit(solution)/shard_map/ppermute | solution.py:23
  86.3 13.4 %collective-permute-start.6 = (f32[5,8,2048]{2,1,0:T(8,128)}, f32[5,8,2048]{2,1,0:T(8,128)}, u32[]{:S(2)}, u32[]{:S(2)}) collective-permute-start(f32[5,8,2048]{2,1,0:T(8,128)} %pad_maximum_fusion), channel_id=1, source_target_pairs={{0,4},{1,5},{2,6},{3,7},{4,0},{5,1},{6,2},{7,3},{8,12},{9,13},{10,... | collective-permute-start | bytes 983048 | tf_op jit(solution)/shard_map/ppermute | solution.py:28
  104.6 9.7 %collective-permute-start.7 = (f32[4,8,2048]{2,1,0:T(8,128)}, f32[4,8,2048]{2,1,0:T(8,128)}, u32[]{:S(2)}, u32[]{:S(2)}) collective-permute-start(f32[4,8,2048]{2,1,0:T(8,128)} %pad_maximum_fusion.2), channel_id=1, source_target_pairs={{0,2},{1,3},{2,0},{3,1},{4,6},{5,7},{6,4},{7,5},{8,10},{9,11},{10,... | collective-permute-start | bytes 786440 | tf_op jit(solution)/shard_map/ppermute | solution.py:28
  118.6 11.7 %collective-permute-start.8 = (f32[5,8,2048]{2,1,0:T(8,128)}, f32[5,8,2048]{2,1,0:T(8,128)}, u32[]{:S(2)}, u32[]{:S(2)}) collective-permute-start(f32[5,8,2048]{2,1,0:T(8,128)} %pad_maximum_fusion.1), channel_id=1, source_target_pairs={{0,1},{1,0},{2,3},{3,2},{4,5},{5,4},{6,7},{7,6},{8,9},{9,8},{10,11... | collective-permute-start | bytes 983048 | tf_op jit(solution)/shard_map/ppermute | solution.py:28
  133.6 22.1 %collective-permute-start.9 = (bf16[3,8,128]{2,1,0:T(8,128)(2,1)}, bf16[3,8,128]{2,1,0:T(8,128)(2,1)}, u32[]{:S(2)}, u32[]{:S(2)}) collective-permute-start(bf16[3,8,128]{2,1,0:T(8,128)(2,1)} %get-tuple-element.64), channel_id=1, source_target_pairs={{0,8},{8,16},{16,24},{24,32},{32,40},{40,48},{48,56},{56,64},{64,7... | collective-permute-start | bytes 18440 | tf_op jit(solution)/shard_map/ppermute | solution.py:23
  135.5 25.5 %collective-permute-start.11 = (bf16[3,8,128]{2,1,0:T(8,128)(2,1)}, bf16[3,8,128]{2,1,0:T(8,128)(2,1)}, u32[]{:S(2)}, u32[]{:S(2)}) collective-permute-start(bf16[3,8,128]{2,1,0:T(8,128)(2,1)} %get-tuple-element.62), channel_id=1, source_target_pairs={{0,488},{8,496},{16,504},{24,0},{32,8},{40,16},{48,24},{56,32},{64... | collective-permute-start | bytes 18440 | tf_op jit(solution)/shard_map/ppermute | solution.py:23
  140.2 23.4 %collective-permute-start.12 = (bf16[3,8,128]{2,1,0:T(8,128)(2,1)}, bf16[3,8,128]{2,1,0:T(8,128)(2,1)}, u32[]{:S(2)}, u32[]{:S(2)}) collective-permute-start(bf16[3,8,128]{2,1,0:T(8,128)(2,1)} %get-tuple-element.61), channel_id=1, source_target_pairs={{0,496},{8,504},{16,0},{24,8},{32,16},{40,24},{48,32},{56,40},{64,... | collective-permute-start | bytes 18440 | tf_op jit(solution)/shard_map/ppermute | solution.py:23
  142.2 22.1 %collective-permute-start.10 = (bf16[3,8,128]{2,1,0:T(8,128)(2,1)}, bf16[3,8,128]{2,1,0:T(8,128)(2,1)}, u32[]{:S(2)}, u32[]{:S(2)}) collective-permute-start(bf16[3,8,128]{2,1,0:T(8,128)(2,1)} %get-tuple-element.63), channel_id=1, source_target_pairs={{0,504},{8,0},{16,8},{24,16},{32,24},{40,32},{48,40},{56,48},{64,5... | collective-permute-start | bytes 18440 | tf_op jit(solution)/shard_map/ppermute | solution.py:23
  145.1 20.6 %collective-permute-start.13 = (bf16[3,8,128]{2,1,0:T(8,128)(2,1)}, bf16[3,8,128]{2,1,0:T(8,128)(2,1)}, u32[]{:S(2)}, u32[]{:S(2)}) collective-permute-start(bf16[3,8,128]{2,1,0:T(8,128)(2,1)} %get-tuple-element.60), channel_id=1, source_target_pairs={{0,16},{8,24},{16,32},{24,40},{32,48},{40,56},{48,64},{56,72},{64,... | collective-permute-start | bytes 18440 | tf_op jit(solution)/shard_map/ppermute | solution.py:23
  152.3 28.1 %copy-start.19 = (f32[12,16]{1,0:T(8,128)S(1)}, f32[12,16]{1,0:T(8,128)}, u32[]{:S(2)}) copy-start(f32[12,16]{1,0:T(8,128)} %copy-done.18) | copy-start | bytes 2308
  153.9 26.5 %copy-start.27 = (pred[12]{0:T(512)(128)(4,1)S(1)}, pred[12]{0:T(512)(128)(4,1)}, u32[]{:S(2)}) copy-start(pred[12]{0:T(512)(128)(4,1)} %copy-done.26) | copy-start | bytes 40
  153.9 45.6 %copy-start.17 = (bf16[8,15,128]{2,0,1:T(8,128)(2,1)S(1)}, bf16[8,15,128]{2,0,1:T(8,128)(2,1)}, u32[]{:S(2)}) copy-start(bf16[8,15,128]{2,0,1:T(8,128)(2,1)} %get-tuple-element.65) | copy-start | bytes 92164
  155.7 13.1 %collective-permute-start.14 = (bf16[3,8,128]{2,1,0:T(8,128)(2,1)S(1)}, bf16[3,8,128]{2,1,0:T(8,128)(2,1)S(1)}, u32[]{:S(2)}, u32[]{:S(2)}) collective-permute-start(bf16[3,8,128]{2,1,0:T(8,128)(2,1)S(1)} %get-tuple-element.59), channel_id=1, source_target_pairs={{0,24},{8,32},{16,40},{24,48},{32,56},{40,64},{48,72},{56,80},{64,... | collective-permute-start | bytes 18440 | tf_op jit(solution)/shard_map/ppermute | solution.py:23
  161.0 5.4 %collective-permute-start.15 = (f32[12288]{0:T(1024)S(1)}, f32[12288]{0:T(1024)S(1)}, u32[]{:S(2)}, u32[]{:S(2)}) collective-permute-start(f32[12288]{0:T(1024)S(1)} %constant_dynamic-update-slice_fusion.7), channel_id=1, source_target_pairs={{0,8},{8,0},{16,24},{24,16},{32,40},{40,32},{48,56},{56,48},{64,72... | collective-permute-start | bytes 147464 | tf_op jit(solution)/shard_map/ppermute | solution.py:28
  166.4 6.0 %collective-permute-start.16 = (f32[12288]{0:T(1024)S(1)}, f32[12288]{0:T(1024)S(1)}, u32[]{:S(2)}, u32[]{:S(2)}) collective-permute-start(f32[12288]{0:T(1024)S(1)} %add.359), channel_id=1, source_target_pairs={{0,256},{8,264},{16,272},{24,280},{32,288},{40,296},{48,304},{56,3... | collective-permute-start | bytes 147464 | tf_op jit(solution)/shard_map/ppermute | solution.py:28
  172.4 6.0 %collective-permute-start.17 = (f32[12288]{0:T(1024)S(1)}, f32[12288]{0:T(1024)S(1)}, u32[]{:S(2)}, u32[]{:S(2)}) collective-permute-start(f32[12288]{0:T(1024)S(1)} %add.360), channel_id=1, source_target_pairs={{0,16},{8,24},{16,0},{24,8},{32,48},{40,56},{48,32},{56,40},{64,80... | collective-permute-start | bytes 147464 | tf_op jit(solution)/shard_map/ppermute | solution.py:28
  178.4 7.2 %collective-permute-start.18 = (f32[12288]{0:T(1024)S(1)}, f32[12288]{0:T(1024)S(1)}, u32[]{:S(2)}, u32[]{:S(2)}) collective-permute-start(f32[12288]{0:T(1024)S(1)} %add.361), channel_id=1, source_target_pairs={{0,32},{8,40},{16,48},{24,56},{32,0},{40,8},{48,16},{56,24},{64,96... | collective-permute-start | bytes 147464 | tf_op jit(solution)/shard_map/ppermute | solution.py:28
  185.6 10.4 %collective-permute-start.19 = (f32[12288]{0:T(1024)S(1)}, f32[12288]{0:T(1024)S(1)}, u32[]{:S(2)}, u32[]{:S(2)}) collective-permute-start(f32[12288]{0:T(1024)S(1)} %add.362), channel_id=1, source_target_pairs={{0,64},{8,72},{16,80},{24,88},{32,96},{40,104},{48,112},{56,120},{... | collective-permute-start | bytes 147464 | tf_op jit(solution)/shard_map/ppermute | solution.py:28
  196.0 14.7 %collective-permute-start.20 = (f32[12288]{0:T(1024)S(1)}, f32[12288]{0:T(1024)S(1)}, u32[]{:S(2)}, u32[]{:S(2)}) collective-permute-start(f32[12288]{0:T(1024)S(1)} %add.363), channel_id=1, source_target_pairs={{0,128},{8,136},{16,144},{24,152},{32,160},{40,168},{48,176},{56,1... | collective-permute-start | bytes 147464 | tf_op jit(solution)/shard_map/ppermute | solution.py:28
  (34 other events, 313.8 us)

commit v3 on v2

--- a/solution.py
+++ b/solution.py
@@ -166,45 +166,26 @@
 
     my_rows = lax.dynamic_slice_in_dim(weight_out, col_index * hidden_count, hidden_count, 0)
     class_part = jnp.einsum("hc,hn->cn", my_rows, hidden_act, preferred_element_type=jnp.float32)
-    reduced = class_part.reshape(col_devices, c_rows, nodes)
-    gathered = class_back.reshape(1, c_rows, nodes)
-    mask = col_devices // 2
-    while mask >= 1:
-        bit = (col_index // mask) % 2
-        halves = reduced.reshape(2, -1, c_rows, nodes)
-        keep = lax.dynamic_index_in_dim(halves, bit, 0, keepdims=False)
-        away = lax.dynamic_index_in_dim(halves, 1 - bit, 0, keepdims=False)
-        count = away.shape[0]
-        both = swap_with(jnp.concatenate([away, gathered.astype(jnp.float32)], 0), "col", mask)
-        reduced = keep + both[:count]
-        other = both[count:].astype(jnp.bfloat16)
-        gathered = jnp.where(
-            bit == 0,
-            jnp.concatenate([gathered, other], 0),
-            jnp.concatenate([other, gathered], 0),
-        )
-        mask //= 2
-    class_in = reduced.reshape(c_rows, nodes).astype(jnp.bfloat16)
-    order = []
-    for j in range(col_devices):
-        rev = 0
-        bits = col_devices.bit_length() - 1
-        for k in range(bits):
-            if j & (1 << k):
-                rev |= 1 << (bits - 1 - k)
-        order.append(rev)
-    all_back = gathered.reshape(col_devices * c_rows, nodes)
-    out_order = jnp.array(
-        [order[j] * c_rows + k for j in range(col_devices) for k in range(c_rows)], jnp.int32
-    )
-    rows_in_order = jnp.take(my_rows, out_order, axis=1)
+    part_blocks = class_part.reshape(col_devices, c_rows, nodes)
+    xor_order = jnp.bitwise_xor(col_index, jnp.arange(col_devices, dtype=jnp.int32))
+    away = jnp.take(part_blocks, xor_order[1:], axis=0)
+    mine = jnp.broadcast_to(class_back.astype(jnp.float32)[None], away.shape)
+    outgoing = jnp.stack([away, mine], 1)
+    incoming = [swap_with(outgoing[m - 1], "col", m) for m in range(1, col_devices)]
+    own_part = lax.dynamic_index_in_dim(part_blocks, col_index, 0, keepdims=False)
+    class_in = (own_part + sum(x[0] for x in incoming)).astype(jnp.bfloat16)
+    all_back = jnp.concatenate(
+        [class_back] + [x[1].astype(jnp.bfloat16) for x in incoming], 0
+    )
+    rows_in_order = jnp.take(
+        my_rows.reshape(hidden_count, col_devices, c_rows), xor_order, axis=1
+    ).reshape(hidden_count, col_devices * c_rows)
 
     hidden_back = jnp.einsum("hc,cn->hn", rows_in_order, all_back, preferred_element_type=jnp.float32)
     block_grad = jnp.einsum("hn,cn->hc", hidden_act, all_back, preferred_element_type=jnp.float32)
-    inverse = [0] * (col_devices * c_rows)
-    for pos in range(col_devices * c_rows):
-        inverse[int(order[pos // c_rows]) * c_rows + pos % c_rows] = pos
-    second_part = jnp.take(block_grad, jnp.array(inverse, jnp.int32), axis=1)
+    second_part = jnp.take(
+        block_grad.reshape(hidden_count, col_devices, c_rows), xor_order, axis=1
+    ).reshape(hidden_count, col_devices * c_rows)
 
     sigmoid_val = jax.nn.sigmoid(hidden_sum)
     slope_back = (hidden_back * sigmoid_val * (1.0 + hidden_sum * (1.0 - sigmoid_val))).astype(

time: 214 us -> 221 us (1.033)
  the two profiles are of different devices: /device:TPU:8 before, /device:TPU:2 now
where the time goes in v3:
time: 221 us; the launch traced here: 219 us
  starting transfers between devices  80.5 us (36%)
  waiting for transfers between devices  50 us (23%)
  local copies, waits for them, and re-layouts  49.5 us (22%)
  matrix products  21.5 us (10%)
  other arithmetic  15.9 us (7%)
    ppermute x13, starting transfers between devices, swap_with(): return lax.ppermute(x, axis, [(i, i ^ mask) for i in range(devices)])  41.2 us
    ppermute x12, starting transfers between devices, send_by(): lax.ppermute(x, axis, [(i, (i + by) % devices) for i in range(devices)])  39.4 us
    ppermute x13, waiting for transfers between devices, swap_with(): return lax.ppermute(x, axis, [(i, i ^ mask) for i in range(devices)])  31.8 us
    ppermute x12, waiting for transfers between devices, send_by(): lax.ppermute(x, axis, [(i, (i + by) % devices) for i in range(devices)])  18.2 us
    unnamed x90, local copies, waits for them, and re-layouts  15.1 us
  transfers between devices with their start and end apart: 25, of which 10 were waited for; matrix products, arithmetic and copies ran while one was open for 14% of the time, Pallas kernels for 0%

profile of v3, /device:TPU:2, one launch (start us, length us, event | category | flops | bytes accessed | tf_op | source)
XLA Modules:
  0.0 219.0 jit_solution(11597230452589129470)
XLA Ops:
  28.4 11.2 %collective-permute-start.2 = (f32[3,200,128]{2,1,0:T(8,128)}, f32[3,200,128]{2,1,0:T(8,128)}, u32[]{:S(2)}, u32[]{:S(2)}) collective-permute-start(f32[3,200,128]{2,1,0:T(8,128)} %get-tuple-element.48), channel_id=1, source_target_pairs={{0,488},{8,496},{16,504},{24,0},{32,8},{40,16},{48,24},{56,32},{64... | collective-permute-start | bytes 921608 | tf_op jit(solution)/shard_map/ppermute | solution.py:23
  39.6 2.9 %collective-permute-start.3 = (f32[3,200,128]{2,1,0:T(8,128)}, f32[3,200,128]{2,1,0:T(8,128)}, u32[]{:S(2)}, u32[]{:S(2)}) collective-permute-start(f32[3,200,128]{2,1,0:T(8,128)} %get-tuple-element.47), channel_id=1, source_target_pairs={{0,496},{8,504},{16,0},{24,8},{32,16},{40,24},{48,32},{56,40},{64,... | collective-permute-start | bytes 921608 | tf_op jit(solution)/shard_map/ppermute | solution.py:23
  47.0 2.9 %collective-permute-start.4 = (f32[3,200,128]{2,1,0:T(8,128)}, f32[3,200,128]{2,1,0:T(8,128)}, u32[]{:S(2)}, u32[]{:S(2)}) collective-permute-start(f32[3,200,128]{2,1,0:T(8,128)} %get-tuple-element.46), channel_id=1, source_target_pairs={{0,16},{8,24},{16,32},{24,40},{32,48},{40,56},{48,64},{56,72},{64,... | collective-permute-start | bytes 921608 | tf_op jit(solution)/shard_map/ppermute | solution.py:23
  60.8 2.6 %collective-permute-start.5 = (f32[3,200,128]{2,1,0:T(8,128)}, f32[3,200,128]{2,1,0:T(8,128)S(1)}, u32[]{:S(2)}, u32[]{:S(2)}) collective-permute-start(f32[3,200,128]{2,1,0:T(8,128)} %get-tuple-element.45), channel_id=1, source_target_pairs={{0,24},{8,32},{16,40},{24,48},{32,56},{40,64},{48,72},{56,80},{64,... | collective-permute-start | bytes 921608 | tf_op jit(solution)/shard_map/ppermute | solution.py:23
  68.2 10.1 %collective-permute-done.5 = f32[3,200,128]{2,1,0:T(8,128)S(1)} collective-permute-done((f32[3,200,128]{2,1,0:T(8,128)}, f32[3,200,128]{2,1,0:T(8,128)S(1)}, u32[]{:S(2)}, u32[]{:S(2)}) %collective-permute-start.5) | collective-permute-done | bytes 307232 | tf_op jit(solution)/shard_map/ppermute | solution.py:23
  92.5 2.5 %gather_fusion.6 = f32[7,8,2048]{2,1,0:T(8,128)} fusion(f32[8,8,2048]{2,1,0:T(8,128)} %fusion.86, s32[1024]{0:T(1024)} %pad_clamp_fusion.1), kind=kCustom, calls=%fused_computation.8 | custom fusion | bytes 917532 | tf_op jit(solution)/shard_map/jit(_take)/gather | solution.py:171
  99.7 4.3 %collective-permute-start.6 = (f32[2,8,2048]{2,1,0:T(8,128)}, f32[2,8,2048]{2,1,0:T(8,128)}, u32[]{:S(2)}, u32[]{:S(2)}) collective-permute-start(f32[2,8,2048]{2,1,0:T(8,128)} %get-tuple-element.53), channel_id=1, source_target_pairs={{0,1},{1,0},{2,3},{3,2},{4,5},{5,4},{6,7},{7,6},{8,9},{9,8},{10,11... | collective-permute-start | bytes 393224 | tf_op jit(solution)/shard_map/ppermute | solution.py:28
  105.7 3.6 %collective-permute-start.7 = (f32[2,8,2048]{2,1,0:T(8,128)}, f32[2,8,2048]{2,1,0:T(8,128)}, u32[]{:S(2)}, u32[]{:S(2)}) collective-permute-start(f32[2,8,2048]{2,1,0:T(8,128)} %get-tuple-element.54), channel_id=1, source_target_pairs={{0,2},{1,3},{2,0},{3,1},{4,6},{5,7},{6,4},{7,5},{8,10},{9,11},{10,... | collective-permute-start | bytes 393224 | tf_op jit(solution)/shard_map/ppermute | solution.py:28
  109.4 2.9 %collective-permute-start.8 = (f32[2,8,2048]{2,1,0:T(8,128)}, f32[2,8,2048]{2,1,0:T(8,128)}, u32[]{:S(2)}, u32[]{:S(2)}) collective-permute-start(f32[2,8,2048]{2,1,0:T(8,128)} %get-tuple-element.55), channel_id=1, source_target_pairs={{0,3},{1,2},{2,1},{3,0},{4,7},{5,6},{6,5},{7,4},{8,11},{9,10},{10,... | collective-permute-start | bytes 393224 | tf_op jit(solution)/shard_map/ppermute | solution.py:28
  112.3 5.1 %collective-permute-start.9 = (f32[2,8,2048]{2,1,0:T(8,128)}, f32[2,8,2048]{2,1,0:T(8,128)}, u32[]{:S(2)}, u32[]{:S(2)}) collective-permute-start(f32[2,8,2048]{2,1,0:T(8,128)} %get-tuple-element.56), channel_id=1, source_target_pairs={{0,4},{1,5},{2,6},{3,7},{4,0},{5,1},{6,2},{7,3},{8,12},{9,13},{10,... | collective-permute-start | bytes 393224 | tf_op jit(solution)/shard_map/ppermute | solution.py:28
  117.4 4.1 %collective-permute-start.10 = (f32[2,8,2048]{2,1,0:T(8,128)}, f32[2,8,2048]{2,1,0:T(8,128)}, u32[]{:S(2)}, u32[]{:S(2)}) collective-permute-start(f32[2,8,2048]{2,1,0:T(8,128)} %get-tuple-element.57), channel_id=1, source_target_pairs={{0,5},{1,4},{2,7},{3,6},{4,1},{5,0},{6,3},{7,2},{8,13},{9,12},{10,... | collective-permute-start | bytes 393224 | tf_op jit(solution)/shard_map/ppermute | solution.py:28
  123.1 4.9 %collective-permute-start.11 = (f32[2,8,2048]{2,1,0:T(8,128)}, f32[2,8,2048]{2,1,0:T(8,128)S(1)}, u32[]{:S(2)}, u32[]{:S(2)}) collective-permute-start(f32[2,8,2048]{2,1,0:T(8,128)} %get-tuple-element.59), channel_id=1, source_target_pairs={{0,6},{1,7},{2,4},{3,5},{4,2},{5,3},{6,0},{7,1},{8,14},{9,15},{10,... | collective-permute-start | bytes 393224 | tf_op jit(solution)/shard_map/ppermute | solution.py:28
  129.5 2.7 %collective-permute-start.12 = (f32[2,8,2048]{2,1,0:T(8,128)S(1)}, f32[2,8,2048]{2,1,0:T(8,128)S(1)}, u32[]{:S(2)}, u32[]{:S(2)}) collective-permute-start(f32[2,8,2048]{2,1,0:T(8,128)S(1)} %copy-done.13), channel_id=1, source_target_pairs={{0,7},{1,6},{2,5},{3,4},{4,3},{5,2},{6,1},{7,0},{8,15},{9,14},{10,... | collective-permute-start | bytes 393224 | tf_op jit(solution)/shard_map/ppermute | solution.py:28
  149.8 2.7 %collective-permute-start.15 = (bf16[3,8,128]{2,1,0:T(8,128)(2,1)S(1)}, bf16[3,8,128]{2,1,0:T(8,128)(2,1)S(1)}, u32[]{:S(2)}, u32[]{:S(2)}) collective-permute-start(bf16[3,8,128]{2,1,0:T(8,128)(2,1)S(1)} %get-tuple-element.67), channel_id=1, source_target_pairs={{0,488},{8,496},{16,504},{24,0},{32,8},{40,16},{48,24},{56,32},{64... | collective-permute-start | bytes 18440 | tf_op jit(solution)/shard_map/ppermute | solution.py:23
  152.5 4.4 %collective-permute-start.16 = (bf16[3,8,128]{2,1,0:T(8,128)(2,1)S(1)}, bf16[3,8,128]{2,1,0:T(8,128)(2,1)S(1)}, u32[]{:S(2)}, u32[]{:S(2)}) collective-permute-start(bf16[3,8,128]{2,1,0:T(8,128)(2,1)S(1)} %get-tuple-element.66), channel_id=1, source_target_pairs={{0,496},{8,504},{16,0},{24,8},{32,16},{40,24},{48,32},{56,40},{64,... | collective-permute-start | bytes 18440 | tf_op jit(solution)/shard_map/ppermute | solution.py:23
  161.2 4.6 %collective-permute-done.13 = bf16[3,8,128]{2,1,0:T(8,128)(2,1)S(1)} collective-permute-done((bf16[3,8,128]{2,1,0:T(8,128)(2,1)S(1)}, bf16[3,8,128]{2,1,0:T(8,128)(2,1)S(1)}, u32[]{:S(2)}, u32[]{:S(2)}) %collective-permute-start.13) | collective-permute-done | bytes 6176 | tf_op jit(solution)/shard_map/ppermute | solution.py:23
  170.2 3.3 %collective-permute-done.17 = bf16[3,8,128]{2,1,0:T(8,128)(2,1)S(1)} collective-permute-done((bf16[3,8,128]{2,1,0:T(8,128)(2,1)S(1)}, bf16[3,8,128]{2,1,0:T(8,128)(2,1)S(1)}, u32[]{:S(2)}, u32[]{:S(2)}) %collective-permute-start.17) | collective-permute-done | bytes 6176 | tf_op jit(solution)/shard_map/ppermute | solution.py:23
  176.1 3.4 %collective-permute-done.20 = f32[12288]{0:T(1024)S(1)} collective-permute-done((f32[12288]{0:T(1024)S(1)}, f32[12288]{0:T(1024)S(1)}, u32[]{:S(2)}, u32[]{:S(2)}) %collective-permute-start.20) | collective-permute-done | bytes 49184 | tf_op jit(solution)/shard_map/ppermute | solution.py:28
  181.8 3.7 %collective-permute-done.21 = f32[12288]{0:T(1024)S(1)} collective-permute-done((f32[12288]{0:T(1024)S(1)}, f32[12288]{0:T(1024)S(1)}, u32[]{:S(2)}, u32[]{:S(2)}) %collective-permute-start.21) | collective-permute-done | bytes 49184 | tf_op jit(solution)/shard_map/ppermute | solution.py:28
  187.7 4.6 %collective-permute-done.22 = f32[12288]{0:T(1024)S(1)} collective-permute-done((f32[12288]{0:T(1024)S(1)}, f32[12288]{0:T(1024)S(1)}, u32[]{:S(2)}, u32[]{:S(2)}) %collective-permute-start.22) | collective-permute-done | bytes 49184 | tf_op jit(solution)/shard_map/ppermute | solution.py:28
  192.4 2.7 %collective-permute-start.23 = (f32[12288]{0:T(1024)S(1)}, f32[12288]{0:T(1024)S(1)}, u32[]{:S(2)}, u32[]{:S(2)}) collective-permute-start(f32[12288]{0:T(1024)S(1)} %add.358), channel_id=1, source_target_pairs={{0,64},{8,72},{16,80},{24,88},{32,96},{40,104},{48,112},{56,120},{... | collective-permute-start | bytes 147464 | tf_op jit(solution)/shard_map/ppermute | solution.py:28
  195.1 7.7 %collective-permute-done.23 = f32[12288]{0:T(1024)S(1)} collective-permute-done((f32[12288]{0:T(1024)S(1)}, f32[12288]{0:T(1024)S(1)}, u32[]{:S(2)}, u32[]{:S(2)}) %collective-permute-start.23) | collective-permute-done | bytes 49184 | tf_op jit(solution)/shard_map/ppermute | solution.py:28
  202.8 2.5 %collective-permute-start.24 = (f32[12288]{0:T(1024)S(1)}, f32[12288]{0:T(1024)S(1)}, u32[]{:S(2)}, u32[]{:S(2)}) collective-permute-start(f32[12288]{0:T(1024)S(1)} %add.359), channel_id=1, source_target_pairs={{0,128},{8,136},{16,144},{24,152},{32,160},{40,168},{48,176},{56,1... | collective-permute-start | bytes 147464 | tf_op jit(solution)/shard_map/ppermute | solution.py:28
  206.3 11.2 %collective-permute-done.24 = f32[12288]{0:T(1024)S(1)} collective-permute-done((f32[12288]{0:T(1024)S(1)}, f32[12288]{0:T(1024)S(1)}, u32[]{:S(2)}, u32[]{:S(2)}) %collective-permute-start.24) | collective-permute-done | bytes 49184 | tf_op jit(solution)/shard_map/ppermute | solution.py:28
  (248 shorter events, 106.7 us)
Async XLA Ops:
  28.4 32.4 %collective-permute-start.2 = (f32[3,200,128]{2,1,0:T(8,128)}, f32[3,200,128]{2,1,0:T(8,128)}, u32[]{:S(2)}, u32[]{:S(2)}) collective-permute-start(f32[3,200,128]{2,1,0:T(8,128)} %get-tuple-element.48), channel_id=1, source_target_pairs={{0,488},{8,496},{16,504},{24,0},{32,8},{40,16},{48,24},{56,32},{64... | collective-permute-start | bytes 921608 | tf_op jit(solution)/shard_map/ppermute | solution.py:23
  39.6 24.8 %collective-permute-start.3 = (f32[3,200,128]{2,1,0:T(8,128)}, f32[3,200,128]{2,1,0:T(8,128)}, u32[]{:S(2)}, u32[]{:S(2)}) collective-permute-start(f32[3,200,128]{2,1,0:T(8,128)} %get-tuple-element.47), channel_id=1, source_target_pairs={{0,496},{8,504},{16,0},{24,8},{32,16},{40,24},{48,32},{56,40},{64,... | collective-permute-start | bytes 921608 | tf_op jit(solution)/shard_map/ppermute | solution.py:23
  42.5 22.8 %collective-permute-start.1 = (f32[3,200,128]{2,1,0:T(8,128)}, f32[3,200,128]{2,1,0:T(8,128)}, u32[]{:S(2)}, u32[]{:S(2)}) collective-permute-start(f32[3,200,128]{2,1,0:T(8,128)} %get-tuple-element.49), channel_id=1, source_target_pairs={{0,504},{8,0},{16,8},{24,16},{32,24},{40,32},{48,40},{56,48},{64,5... | collective-permute-start | bytes 921608 | tf_op jit(solution)/shard_map/ppermute | solution.py:23
  45.0 21.3 %collective-permute-start = (f32[3,200,128]{2,1,0:T(8,128)}, f32[3,200,128]{2,1,0:T(8,128)}, u32[]{:S(2)}, u32[]{:S(2)}) collective-permute-start(f32[3,200,128]{2,1,0:T(8,128)} %get-tuple-element.50), channel_id=1, source_target_pairs={{0,8},{8,16},{16,24},{24,32},{32,40},{40,48},{48,56},{56,64},{64,7... | collective-permute-start | bytes 921608 | tf_op jit(solution)/shard_map/ppermute | solution.py:23
  47.0 20.3 %collective-permute-start.4 = (f32[3,200,128]{2,1,0:T(8,128)}, f32[3,200,128]{2,1,0:T(8,128)}, u32[]{:S(2)}, u32[]{:S(2)}) collective-permute-start(f32[3,200,128]{2,1,0:T(8,128)} %get-tuple-element.46), channel_id=1, source_target_pairs={{0,16},{8,24},{16,32},{24,40},{32,48},{40,56},{48,64},{56,72},{64,... | collective-permute-start | bytes 921608 | tf_op jit(solution)/shard_map/ppermute | solution.py:23
  60.8 17.5 %collective-permute-start.5 = (f32[3,200,128]{2,1,0:T(8,128)}, f32[3,200,128]{2,1,0:T(8,128)S(1)}, u32[]{:S(2)}, u32[]{:S(2)}) collective-permute-start(f32[3,200,128]{2,1,0:T(8,128)} %get-tuple-element.45), channel_id=1, source_target_pairs={{0,24},{8,32},{16,40},{24,48},{32,56},{40,64},{48,72},{56,80},{64,... | collective-permute-start | bytes 921608 | tf_op jit(solution)/shard_map/ppermute | solution.py:23
  99.7 23.4 %collective-permute-start.6 = (f32[2,8,2048]{2,1,0:T(8,128)}, f32[2,8,2048]{2,1,0:T(8,128)}, u32[]{:S(2)}, u32[]{:S(2)}) collective-permute-start(f32[2,8,2048]{2,1,0:T(8,128)} %get-tuple-element.53), channel_id=1, source_target_pairs={{0,1},{1,0},{2,3},{3,2},{4,5},{5,4},{6,7},{7,6},{8,9},{9,8},{10,11... | collective-permute-start | bytes 393224 | tf_op jit(solution)/shard_map/ppermute | solution.py:28
  105.7 23.8 %collective-permute-start.7 = (f32[2,8,2048]{2,1,0:T(8,128)}, f32[2,8,2048]{2,1,0:T(8,128)}, u32[]{:S(2)}, u32[]{:S(2)}) collective-permute-start(f32[2,8,2048]{2,1,0:T(8,128)} %get-tuple-element.54), channel_id=1, source_target_pairs={{0,2},{1,3},{2,0},{3,1},{4,6},{5,7},{6,4},{7,5},{8,10},{9,11},{10,... | collective-permute-start | bytes 393224 | tf_op jit(solution)/shard_map/ppermute | solution.py:28
  109.4 24.3 %collective-permute-start.8 = (f32[2,8,2048]{2,1,0:T(8,128)}, f32[2,8,2048]{2,1,0:T(8,128)}, u32[]{:S(2)}, u32[]{:S(2)}) collective-permute-start(f32[2,8,2048]{2,1,0:T(8,128)} %get-tuple-element.55), channel_id=1, source_target_pairs={{0,3},{1,2},{2,1},{3,0},{4,7},{5,6},{6,5},{7,4},{8,11},{9,10},{10,... | collective-permute-start | bytes 393224 | tf_op jit(solution)/shard_map/ppermute | solution.py:28
  112.3 22.8 %collective-permute-start.9 = (f32[2,8,2048]{2,1,0:T(8,128)}, f32[2,8,2048]{2,1,0:T(8,128)}, u32[]{:S(2)}, u32[]{:S(2)}) collective-permute-start(f32[2,8,2048]{2,1,0:T(8,128)} %get-tuple-element.56), channel_id=1, source_target_pairs={{0,4},{1,5},{2,6},{3,7},{4,0},{5,1},{6,2},{7,3},{8,12},{9,13},{10,... | collective-permute-start | bytes 393224 | tf_op jit(solution)/shard_map/ppermute | solution.py:28
  117.4 19.1 %collective-permute-start.10 = (f32[2,8,2048]{2,1,0:T(8,128)}, f32[2,8,2048]{2,1,0:T(8,128)}, u32[]{:S(2)}, u32[]{:S(2)}) collective-permute-start(f32[2,8,2048]{2,1,0:T(8,128)} %get-tuple-element.57), channel_id=1, source_target_pairs={{0,5},{1,4},{2,7},{3,6},{4,1},{5,0},{6,3},{7,2},{8,13},{9,12},{10,... | collective-permute-start | bytes 393224 | tf_op jit(solution)/shard_map/ppermute | solution.py:28
  123.1 14.9 %collective-permute-start.11 = (f32[2,8,2048]{2,1,0:T(8,128)}, f32[2,8,2048]{2,1,0:T(8,128)S(1)}, u32[]{:S(2)}, u32[]{:S(2)}) collective-permute-start(f32[2,8,2048]{2,1,0:T(8,128)} %get-tuple-element.59), channel_id=1, source_target_pairs={{0,6},{1,7},{2,4},{3,5},{4,2},{5,3},{6,0},{7,1},{8,14},{9,15},{10,... | collective-permute-start | bytes 393224 | tf_op jit(solution)/shard_map/ppermute | solution.py:28
  129.5 10.5 %collective-permute-start.12 = (f32[2,8,2048]{2,1,0:T(8,128)S(1)}, f32[2,8,2048]{2,1,0:T(8,128)S(1)}, u32[]{:S(2)}, u32[]{:S(2)}) collective-permute-start(f32[2,8,2048]{2,1,0:T(8,128)S(1)} %copy-done.13), channel_id=1, source_target_pairs={{0,7},{1,6},{2,5},{3,4},{4,3},{5,2},{6,1},{7,0},{8,15},{9,14},{10,... | collective-permute-start | bytes 393224 | tf_op jit(solution)/shard_map/ppermute | solution.py:28
  145.5 28.0 %collective-permute-start.19 = (f32[12288]{0:T(1024)S(1)}, f32[12288]{0:T(1024)S(1)}, u32[]{:S(2)}, u32[]{:S(2)}) collective-permute-start(f32[12288]{0:T(1024)S(1)} %constant_dynamic-update-slice_fusion.15), channel_id=1, source_target_pairs={{0,8},{8,0},{16,24},{24,16},{32,40},{40,32},{48,56},{56,48},{64,72... | collective-permute-start | bytes 147464 | tf_op jit(solution)/shard_map/ppermute | solution.py:28
  149.8 18.4 %collective-permute-start.15 = (bf16[3,8,128]{2,1,0:T(8,128)(2,1)S(1)}, bf16[3,8,128]{2,1,0:T(8,128)(2,1)S(1)}, u32[]{:S(2)}, u32[]{:S(2)}) collective-permute-start(bf16[3,8,128]{2,1,0:T(8,128)(2,1)S(1)} %get-tuple-element.67), channel_id=1, source_target_pairs={{0,488},{8,496},{16,504},{24,0},{32,8},{40,16},{48,24},{56,32},{64... | collective-permute-start | bytes 18440 | tf_op jit(solution)/shard_map/ppermute | solution.py:23
  152.5 17.6 %collective-permute-start.16 = (bf16[3,8,128]{2,1,0:T(8,128)(2,1)S(1)}, bf16[3,8,128]{2,1,0:T(8,128)(2,1)S(1)}, u32[]{:S(2)}, u32[]{:S(2)}) collective-permute-start(bf16[3,8,128]{2,1,0:T(8,128)(2,1)S(1)} %get-tuple-element.66), channel_id=1, source_target_pairs={{0,496},{8,504},{16,0},{24,8},{32,16},{40,24},{48,32},{56,40},{64,... | collective-permute-start | bytes 18440 | tf_op jit(solution)/shard_map/ppermute | solution.py:23
  156.9 13.3 %collective-permute-start.14 = (bf16[3,8,128]{2,1,0:T(8,128)(2,1)S(1)}, bf16[3,8,128]{2,1,0:T(8,128)(2,1)S(1)}, u32[]{:S(2)}, u32[]{:S(2)}) collective-permute-start(bf16[3,8,128]{2,1,0:T(8,128)(2,1)S(1)} %get-tuple-element.68), channel_id=1, source_target_pairs={{0,504},{8,0},{16,8},{24,16},{32,24},{40,32},{48,40},{56,48},{64,5... | collective-permute-start | bytes 18440 | tf_op jit(solution)/shard_map/ppermute | solution.py:23
  158.8 7.1 %collective-permute-start.13 = (bf16[3,8,128]{2,1,0:T(8,128)(2,1)S(1)}, bf16[3,8,128]{2,1,0:T(8,128)(2,1)S(1)}, u32[]{:S(2)}, u32[]{:S(2)}) collective-permute-start(bf16[3,8,128]{2,1,0:T(8,128)(2,1)S(1)} %get-tuple-element.69), channel_id=1, source_target_pairs={{0,8},{8,16},{16,24},{24,32},{32,40},{40,48},{48,56},{56,64},{64,7... | collective-permute-start | bytes 18440 | tf_op jit(solution)/shard_map/ppermute | solution.py:23
  165.9 7.6 %collective-permute-start.17 = (bf16[3,8,128]{2,1,0:T(8,128)(2,1)S(1)}, bf16[3,8,128]{2,1,0:T(8,128)(2,1)S(1)}, u32[]{:S(2)}, u32[]{:S(2)}) collective-permute-start(bf16[3,8,128]{2,1,0:T(8,128)(2,1)S(1)} %get-tuple-element.65), channel_id=1, source_target_pairs={{0,16},{8,24},{16,32},{24,40},{32,48},{40,56},{48,64},{56,72},{64,... | collective-permute-start | bytes 18440 | tf_op jit(solution)/shard_map/ppermute | solution.py:23
  168.2 8.0 %collective-permute-start.18 = (bf16[3,8,128]{2,1,0:T(8,128)(2,1)S(1)}, bf16[3,8,128]{2,1,0:T(8,128)(2,1)S(1)}, u32[]{:S(2)}, u32[]{:S(2)}) collective-permute-start(bf16[3,8,128]{2,1,0:T(8,128)(2,1)S(1)} %get-tuple-element.64), channel_id=1, source_target_pairs={{0,24},{8,32},{16,40},{24,48},{32,56},{40,64},{48,72},{56,80},{64,... | collective-permute-start | bytes 18440 | tf_op jit(solution)/shard_map/ppermute | solution.py:23
  173.5 6.0 %collective-permute-start.20 = (f32[12288]{0:T(1024)S(1)}, f32[12288]{0:T(1024)S(1)}, u32[]{:S(2)}, u32[]{:S(2)}) collective-permute-start(f32[12288]{0:T(1024)S(1)} %add.355), channel_id=1, source_target_pairs={{0,256},{8,264},{16,272},{24,280},{32,288},{40,296},{48,304},{56,3... | collective-permute-start | bytes 147464 | tf_op jit(solution)/shard_map/ppermute | solution.py:28
  185.5 6.9 %collective-permute-start.22 = (f32[12288]{0:T(1024)S(1)}, f32[12288]{0:T(1024)S(1)}, u32[]{:S(2)}, u32[]{:S(2)}) collective-permute-start(f32[12288]{0:T(1024)S(1)} %add.357), channel_id=1, source_target_pairs={{0,32},{8,40},{16,48},{24,56},{32,0},{40,8},{48,16},{56,24},{64,96... | collective-permute-start | bytes 147464 | tf_op jit(solution)/shard_map/ppermute | solution.py:28
  192.4 10.4 %collective-permute-start.23 = (f32[12288]{0:T(1024)S(1)}, f32[12288]{0:T(1024)S(1)}, u32[]{:S(2)}, u32[]{:S(2)}) collective-permute-start(f32[12288]{0:T(1024)S(1)} %add.358), channel_id=1, source_target_pairs={{0,64},{8,72},{16,80},{24,88},{32,96},{40,104},{48,112},{56,120},{... | collective-permute-start | bytes 147464 | tf_op jit(solution)/shard_map/ppermute | solution.py:28
  202.8 14.7 %collective-permute-start.24 = (f32[12288]{0:T(1024)S(1)}, f32[12288]{0:T(1024)S(1)}, u32[]{:S(2)}, u32[]{:S(2)}) collective-permute-start(f32[12288]{0:T(1024)S(1)} %add.359), channel_id=1, source_target_pairs={{0,128},{8,136},{16,144},{24,152},{32,160},{40,168},{48,176},{56,1... | collective-permute-start | bytes 147464 | tf_op jit(solution)/shard_map/ppermute | solution.py:28
  (36 other events, 449.7 us)

commit v4 on v3

--- a/solution.py
+++ b/solution.py
@@ -167,25 +167,14 @@
     my_rows = lax.dynamic_slice_in_dim(weight_out, col_index * hidden_count, hidden_count, 0)
     class_part = jnp.einsum("hc,hn->cn", my_rows, hidden_act, preferred_element_type=jnp.float32)
     part_blocks = class_part.reshape(col_devices, c_rows, nodes)
-    xor_order = jnp.bitwise_xor(col_index, jnp.arange(col_devices, dtype=jnp.int32))
-    away = jnp.take(part_blocks, xor_order[1:], axis=0)
-    mine = jnp.broadcast_to(class_back.astype(jnp.float32)[None], away.shape)
-    outgoing = jnp.stack([away, mine], 1)
-    incoming = [swap_with(outgoing[m - 1], "col", m) for m in range(1, col_devices)]
-    own_part = lax.dynamic_index_in_dim(part_blocks, col_index, 0, keepdims=False)
-    class_in = (own_part + sum(x[0] for x in incoming)).astype(jnp.bfloat16)
-    all_back = jnp.concatenate(
-        [class_back] + [x[1].astype(jnp.bfloat16) for x in incoming], 0
-    )
-    rows_in_order = jnp.take(
-        my_rows.reshape(hidden_count, col_devices, c_rows), xor_order, axis=1
-    ).reshape(hidden_count, col_devices * c_rows)
-
-    hidden_back = jnp.einsum("hc,cn->hn", rows_in_order, all_back, preferred_element_type=jnp.float32)
-    block_grad = jnp.einsum("hn,cn->hc", hidden_act, all_back, preferred_element_type=jnp.float32)
-    second_part = jnp.take(
-        block_grad.reshape(hidden_count, col_devices, c_rows), xor_order, axis=1
-    ).reshape(hidden_count, col_devices * c_rows)
+    mine = jnp.broadcast_to(class_back.astype(jnp.float32)[None], part_blocks.shape)
+    outgoing = jnp.stack([part_blocks, mine], 1)
+    incoming = lax.all_to_all(outgoing, "col", 0, 0, tiled=True)
+    class_in = jnp.sum(incoming[:, 0], axis=0).astype(jnp.bfloat16)
+    all_back = incoming[:, 1].astype(jnp.bfloat16).reshape(col_devices * c_rows, nodes)
+
+    hidden_back = jnp.einsum("hc,cn->hn", my_rows, all_back, preferred_element_type=jnp.float32)
+    second_part = jnp.einsum("hn,cn->hc", hidden_act, all_back, preferred_element_type=jnp.float32)
 
     sigmoid_val = jax.nn.sigmoid(hidden_sum)
     slope_back = (hidden_back * sigmoid_val * (1.0 + hidden_sum * (1.0 - sigmoid_val))).astype(

time: 221 us -> 182 us (0.82)
  local copies, waits for them, and re-layouts: 49.5 us -> 32.8 us
  starting transfers between devices: 80.5 us -> 64.8 us
  matrix products: 21.5 us -> 16.7 us
  other arithmetic: 15.9 us -> 11.2 us
  waiting for transfers between devices: 50 us -> 53.2 us
    ppermute x13 -> x6, starting transfers between devices: 41.2 us -> 15.7 us  [swap_with(): return lax.ppermute(x, axis, [(i, i ^ mask) for i in range(devices)])]
    all_to_all x0 -> x1, waiting for transfers between devices: none -> 15.1 us  [local(): incoming = lax.all_to_all(outgoing, 'col', 0, 0, tiled=True)]
    ppermute x12, waiting for transfers between devices: 18.2 us -> 10.1 us  [send_by(): lax.ppermute(x, axis, [(i, (i + by) % devices) for i in range(devices)])]
    all_to_all x0 -> x1, starting transfers between devices: none -> 6.33 us  [local(): incoming = lax.all_to_all(outgoing, 'col', 0, 0, tiled=True)]
    gather x3 -> x0, local copies, waits for them, and re-layouts: 4.23 us -> none  [the longest x1 2.52 us: local(): away = jnp.take(part_blocks, xor_order[1:], axis=0)]
    unnamed x90 -> x55, local copies, waits for them, and re-layouts: 15.1 us -> 10.9 us
    ppermute x13 -> x6, waiting for transfers between devices: 31.8 us -> 28 us  [swap_with(): return lax.ppermute(x, axis, [(i, i ^ mask) for i in range(devices)])]
    ppermute x12, starting transfers between devices: 39.4 us -> 42.7 us  [send_by(): lax.ppermute(x, axis, [(i, (i + by) % devices) for i in range(devices)])]
  transfers between devices with their start and end apart: 25 -> 19, of which waited for: 10 -> 7; matrix products, arithmetic and copies ran while one was open for 14% -> 13% of each run, Pallas kernels for 0% -> 0%
where the time goes in v4:
time: 182 us; the launch traced here: 180 us
  starting transfers between devices  64.8 us (36%)
  waiting for transfers between devices  53.2 us (29%)
  local copies, waits for them, and re-layouts  32.8 us (18%)
  matrix products  16.7 us (9%)
  other arithmetic  11.2 us (6%)
    ppermute x12, starting transfers between devices, send_by(): lax.ppermute(x, axis, [(i, (i + by) % devices) for i in range(devices)])  42.7 us
    ppermute x6, waiting for transfers between devices, swap_with(): return lax.ppermute(x, axis, [(i, i ^ mask) for i in range(devices)])  28 us
    ppermute x6, starting transfers between devices, swap_with(): return lax.ppermute(x, axis, [(i, i ^ mask) for i in range(devices)])  15.7 us
    all_to_all x1, waiting for transfers between devices, local(): incoming = lax.all_to_all(outgoing, 'col', 0, 0, tiled=True)  15.1 us
    unnamed x55, local copies, waits for them, and re-layouts  10.9 us
    ppermute x12, waiting for transfers between devices, send_by(): lax.ppermute(x, axis, [(i, (i + by) % devices) for i in range(devices)])  10.1 us
    all_to_all x1, starting transfers between devices, local(): incoming = lax.all_to_all(outgoing, 'col', 0, 0, tiled=True)  6.33 us
  transfers between devices with their start and end apart: 19, of which 7 were waited for; matrix products, arithmetic and copies ran while one was open for 13% of the time, Pallas kernels for 0%

profile of v4, /device:TPU:2, one launch (start us, length us, event | category | flops | bytes accessed | tf_op | source)
XLA Modules:
  0.0 180.2 jit_solution(9936697604669087079)
XLA Ops:
  20.0 11.2 %collective-permute-start.2 = (f32[3,200,128]{2,1,0:T(8,128)}, f32[3,200,128]{2,1,0:T(8,128)}, u32[]{:S(2)}, u32[]{:S(2)}) collective-permute-start(f32[3,200,128]{2,1,0:T(8,128)} %get-tuple-element.49), channel_id=1, source_target_pairs={{0,488},{8,496},{16,504},{24,0},{32,8},{40,16},{48,24},{56,32},{64... | collective-permute-start | bytes 921608 | tf_op jit(solution)/shard_map/ppermute | solution.py:23
  31.2 2.9 %collective-permute-start.3 = (f32[3,200,128]{2,1,0:T(8,128)}, f32[3,200,128]{2,1,0:T(8,128)}, u32[]{:S(2)}, u32[]{:S(2)}) collective-permute-start(f32[3,200,128]{2,1,0:T(8,128)} %get-tuple-element.48), channel_id=1, source_target_pairs={{0,496},{8,504},{16,0},{24,8},{32,16},{40,24},{48,32},{56,40},{64,... | collective-permute-start | bytes 921608 | tf_op jit(solution)/shard_map/ppermute | solution.py:23
  34.1 2.5 %collective-permute-start.1 = (f32[3,200,128]{2,1,0:T(8,128)}, f32[3,200,128]{2,1,0:T(8,128)}, u32[]{:S(2)}, u32[]{:S(2)}) collective-permute-start(f32[3,200,128]{2,1,0:T(8,128)} %get-tuple-element.50), channel_id=1, source_target_pairs={{0,504},{8,0},{16,8},{24,16},{32,24},{40,32},{48,40},{56,48},{64,5... | collective-permute-start | bytes 921608 | tf_op jit(solution)/shard_map/ppermute | solution.py:23
  36.6 1.9 %collective-permute-start = (f32[3,200,128]{2,1,0:T(8,128)}, f32[3,200,128]{2,1,0:T(8,128)}, u32[]{:S(2)}, u32[]{:S(2)}) collective-permute-start(f32[3,200,128]{2,1,0:T(8,128)} %get-tuple-element.51), channel_id=1, source_target_pairs={{0,8},{8,16},{16,24},{24,32},{32,40},{40,48},{48,56},{56,64},{64,7... | collective-permute-start | bytes 921608 | tf_op jit(solution)/shard_map/ppermute | solution.py:23
  38.6 2.9 %collective-permute-start.4 = (f32[3,200,128]{2,1,0:T(8,128)}, f32[3,200,128]{2,1,0:T(8,128)}, u32[]{:S(2)}, u32[]{:S(2)}) collective-permute-start(f32[3,200,128]{2,1,0:T(8,128)} %get-tuple-element.47), channel_id=1, source_target_pairs={{0,16},{8,24},{16,32},{24,40},{32,48},{40,56},{48,64},{56,72},{64,... | collective-permute-start | bytes 921608 | tf_op jit(solution)/shard_map/ppermute | solution.py:23
  48.4 2.6 %collective-permute-start.5 = (f32[3,200,128]{2,1,0:T(8,128)}, f32[3,200,128]{2,1,0:T(8,128)S(1)}, u32[]{:S(2)}, u32[]{:S(2)}) collective-permute-start(f32[3,200,128]{2,1,0:T(8,128)} %get-tuple-element.46), channel_id=1, source_target_pairs={{0,24},{8,32},{16,40},{24,48},{32,56},{40,64},{48,72},{56,80},{64,... | collective-permute-start | bytes 921608 | tf_op jit(solution)/shard_map/ppermute | solution.py:23
  55.8 10.1 %collective-permute-done.5 = f32[3,200,128]{2,1,0:T(8,128)S(1)} collective-permute-done((f32[3,200,128]{2,1,0:T(8,128)}, f32[3,200,128]{2,1,0:T(8,128)S(1)}, u32[]{:S(2)}, u32[]{:S(2)}) %collective-permute-start.5) | collective-permute-done | bytes 307232 | tf_op jit(solution)/shard_map/ppermute | solution.py:23
  66.4 2.4 %fusion.2 = f32[192,128,16]{1,2,0:T(8,128)S(1)} fusion(f32[12,192,128]{2,1,0:T(8,128)S(1)} %fusion.15, f32[12,16]{1,0:T(8,128)S(1)} %gather_fusion.5, pred[12]{0:T(512)(128)(4,1)S(1)} %compare_and_fusion), kind=kOutput, calls=%fused_computation.16 | convolution fusion | flops 56623296 | bytes 2753292 | tf_op jit(solution)/shard_map/kb,kfn->fbn/dot_general | solution.py:71
  78.4 6.3 %all-to-all-start = ((f32[8,2,8,2048]{3,2,1,0:T(8,128)}), f32[8,2,8,2048]{3,2,1,0:T(8,128)}, u32[]{:S(2)}, u32[]{:S(2)}) async-start(f32[8,2,8,2048]{3,2,1,0:T(8,128)} %copy.125), calls=%async_computation | async-start | bytes 2097152 | tf_op jit(solution)/shard_map/all_to_all | solution.py:172
  87.3 15.1 %all-to-all-done = f32[8,2,8,2048]{3,2,1,0:T(8,128)} async-done(((f32[8,2,8,2048]{3,2,1,0:T(8,128)}), f32[8,2,8,2048]{3,2,1,0:T(8,128)}, u32[]{:S(2)}, u32[]{:S(2)}) %all-to-all-start) | async-done | bytes 1048608 | tf_op jit(solution)/shard_map/all_to_all | solution.py:172
  107.1 4.4 %collective-permute-start.8 = (bf16[3,8,128]{2,1,0:T(8,128)(2,1)S(1)}, bf16[3,8,128]{2,1,0:T(8,128)(2,1)}, u32[]{:S(2)}, u32[]{:S(2)}) collective-permute-start(bf16[3,8,128]{2,1,0:T(8,128)(2,1)S(1)} %get-tuple-element.61), channel_id=1, source_target_pairs={{0,488},{8,496},{16,504},{24,0},{32,8},{40,16},{48,24},{56,32},{64... | collective-permute-start | bytes 18440 | tf_op jit(solution)/shard_map/ppermute | solution.py:23
  111.5 2.1 %collective-permute-start.9 = (bf16[3,8,128]{2,1,0:T(8,128)(2,1)S(1)}, bf16[3,8,128]{2,1,0:T(8,128)(2,1)}, u32[]{:S(2)}, u32[]{:S(2)}) collective-permute-start(bf16[3,8,128]{2,1,0:T(8,128)(2,1)S(1)} %get-tuple-element.60), channel_id=1, source_target_pairs={{0,496},{8,504},{16,0},{24,8},{32,16},{40,24},{48,32},{56,40},{64,... | collective-permute-start | bytes 18440 | tf_op jit(solution)/shard_map/ppermute | solution.py:23
  113.6 3.1 %collective-permute-start.7 = (bf16[3,8,128]{2,1,0:T(8,128)(2,1)S(1)}, bf16[3,8,128]{2,1,0:T(8,128)(2,1)}, u32[]{:S(2)}, u32[]{:S(2)}) collective-permute-start(bf16[3,8,128]{2,1,0:T(8,128)(2,1)S(1)} %get-tuple-element.62), channel_id=1, source_target_pairs={{0,504},{8,0},{16,8},{24,16},{32,24},{40,32},{48,40},{56,48},{64,5... | collective-permute-start | bytes 18440 | tf_op jit(solution)/shard_map/ppermute | solution.py:23
  116.7 3.6 %collective-permute-start.10 = (bf16[3,8,128]{2,1,0:T(8,128)(2,1)S(1)}, bf16[3,8,128]{2,1,0:T(8,128)(2,1)}, u32[]{:S(2)}, u32[]{:S(2)}) collective-permute-start(bf16[3,8,128]{2,1,0:T(8,128)(2,1)S(1)} %get-tuple-element.59), channel_id=1, source_target_pairs={{0,16},{8,24},{16,32},{24,40},{32,48},{40,56},{48,64},{56,72},{64,... | collective-permute-start | bytes 18440 | tf_op jit(solution)/shard_map/ppermute | solution.py:23
  124.4 3.5 %collective-permute-start.11 = (bf16[3,8,128]{2,1,0:T(8,128)(2,1)S(1)}, bf16[3,8,128]{2,1,0:T(8,128)(2,1)S(1)}, u32[]{:S(2)}, u32[]{:S(2)}) collective-permute-start(bf16[3,8,128]{2,1,0:T(8,128)(2,1)S(1)} %get-tuple-element.58), channel_id=1, source_target_pairs={{0,24},{8,32},{16,40},{24,48},{32,56},{40,64},{48,72},{56,80},{64,... | collective-permute-start | bytes 18440 | tf_op jit(solution)/shard_map/ppermute | solution.py:23
  129.0 1.9 %collective-permute-start.12 = (f32[12288]{0:T(1024)S(1)}, f32[12288]{0:T(1024)S(1)}, u32[]{:S(2)}, u32[]{:S(2)}) collective-permute-start(f32[12288]{0:T(1024)S(1)} %constant_dynamic-update-slice_fusion.7), channel_id=1, source_target_pairs={{0,8},{8,0},{16,24},{24,16},{32,40},{40,32},{48,56},{56,48},{64,72... | collective-permute-start | bytes 147464 | tf_op jit(solution)/shard_map/ppermute | solution.py:28
  134.3 3.7 %collective-permute-start.13 = (f32[12288]{0:T(1024)S(1)}, f32[12288]{0:T(1024)S(1)}, u32[]{:S(2)}, u32[]{:S(2)}) collective-permute-start(f32[12288]{0:T(1024)S(1)} %add.284), channel_id=1, source_target_pairs={{0,256},{8,264},{16,272},{24,280},{32,288},{40,296},{48,304},{56,3... | collective-permute-start | bytes 147464 | tf_op jit(solution)/shard_map/ppermute | solution.py:28
  138.1 2.4 %collective-permute-done.13 = f32[12288]{0:T(1024)S(1)} collective-permute-done((f32[12288]{0:T(1024)S(1)}, f32[12288]{0:T(1024)S(1)}, u32[]{:S(2)}, u32[]{:S(2)}) %collective-permute-start.13) | collective-permute-done | bytes 49184 | tf_op jit(solution)/shard_map/ppermute | solution.py:28
  140.5 2.2 %collective-permute-start.14 = (f32[12288]{0:T(1024)S(1)}, f32[12288]{0:T(1024)S(1)}, u32[]{:S(2)}, u32[]{:S(2)}) collective-permute-start(f32[12288]{0:T(1024)S(1)} %add.285), channel_id=1, source_target_pairs={{0,16},{8,24},{16,0},{24,8},{32,48},{40,56},{48,32},{56,40},{64,80... | collective-permute-start | bytes 147464 | tf_op jit(solution)/shard_map/ppermute | solution.py:28
  143.1 3.4 %collective-permute-done.14 = f32[12288]{0:T(1024)S(1)} collective-permute-done((f32[12288]{0:T(1024)S(1)}, f32[12288]{0:T(1024)S(1)}, u32[]{:S(2)}, u32[]{:S(2)}) %collective-permute-start.14) | collective-permute-done | bytes 49184 | tf_op jit(solution)/shard_map/ppermute | solution.py:28
  148.7 4.9 %collective-permute-done.15 = f32[12288]{0:T(1024)S(1)} collective-permute-done((f32[12288]{0:T(1024)S(1)}, f32[12288]{0:T(1024)S(1)}, u32[]{:S(2)}, u32[]{:S(2)}) %collective-permute-start.15) | collective-permute-done | bytes 49184 | tf_op jit(solution)/shard_map/ppermute | solution.py:28
  156.2 7.8 %collective-permute-done.16 = f32[12288]{0:T(1024)S(1)} collective-permute-done((f32[12288]{0:T(1024)S(1)}, f32[12288]{0:T(1024)S(1)}, u32[]{:S(2)}, u32[]{:S(2)}) %collective-permute-start.16) | collective-permute-done | bytes 49184 | tf_op jit(solution)/shard_map/ppermute | solution.py:28
  164.0 4.1 %collective-permute-start.17 = (f32[12288]{0:T(1024)S(1)}, f32[12288]{0:T(1024)S(1)}, u32[]{:S(2)}, u32[]{:S(2)}) collective-permute-start(f32[12288]{0:T(1024)S(1)} %add.288), channel_id=1, source_target_pairs={{0,128},{8,136},{16,144},{24,152},{32,160},{40,168},{48,176},{56,1... | collective-permute-start | bytes 147464 | tf_op jit(solution)/shard_map/ppermute | solution.py:28
  169.1 9.6 %collective-permute-done.17 = f32[12288]{0:T(1024)S(1)} collective-permute-done((f32[12288]{0:T(1024)S(1)}, f32[12288]{0:T(1024)S(1)}, u32[]{:S(2)}, u32[]{:S(2)}) %collective-permute-start.17) | collective-permute-done | bytes 49184 | tf_op jit(solution)/shard_map/ppermute | solution.py:28
  (189 shorter events, 64.1 us)
Async XLA Ops:
  2.1 39.4 %copy-start.11 = (f32[8,16,128]{2,0,1:T(8,128)}, f32[8,16,128]{2,0,1:T(8,128)S(1)}, u32[]{:S(2)}) copy-start(f32[8,16,128]{2,0,1:T(8,128)S(1)} %convolution_bitcast_fusion.3) | copy-start | bytes 196612
  3.4 38.1 %copy-start.10 = (f32[8,16,128]{2,0,1:T(8,128)}, f32[8,16,128]{2,0,1:T(8,128)S(1)}, u32[]{:S(2)}) copy-start(f32[8,16,128]{2,0,1:T(8,128)S(1)} %convolution_bitcast_fusion.2) | copy-start | bytes 196612
  10.0 31.5 %copy-start.18 = (s32[12]{0:T(128)}, s32[12]{0:T(128)S(1)}, u32[]{:S(2)}) copy-start(s32[12]{0:T(128)S(1)} %select_reduce_fusion) | copy-start | bytes 148
  20.0 28.4 %collective-permute-start.2 = (f32[3,200,128]{2,1,0:T(8,128)}, f32[3,200,128]{2,1,0:T(8,128)}, u32[]{:S(2)}, u32[]{:S(2)}) collective-permute-start(f32[3,200,128]{2,1,0:T(8,128)} %get-tuple-element.49), channel_id=1, source_target_pairs={{0,488},{8,496},{16,504},{24,0},{32,8},{40,16},{48,24},{56,32},{64... | collective-permute-start | bytes 921608 | tf_op jit(solution)/shard_map/ppermute | solution.py:23
  31.2 20.7 %collective-permute-start.3 = (f32[3,200,128]{2,1,0:T(8,128)}, f32[3,200,128]{2,1,0:T(8,128)}, u32[]{:S(2)}, u32[]{:S(2)}) collective-permute-start(f32[3,200,128]{2,1,0:T(8,128)} %get-tuple-element.48), channel_id=1, source_target_pairs={{0,496},{8,504},{16,0},{24,8},{32,16},{40,24},{48,32},{56,40},{64,... | collective-permute-start | bytes 921608 | tf_op jit(solution)/shard_map/ppermute | solution.py:23
  34.1 18.8 %collective-permute-start.1 = (f32[3,200,128]{2,1,0:T(8,128)}, f32[3,200,128]{2,1,0:T(8,128)}, u32[]{:S(2)}, u32[]{:S(2)}) collective-permute-start(f32[3,200,128]{2,1,0:T(8,128)} %get-tuple-element.50), channel_id=1, source_target_pairs={{0,504},{8,0},{16,8},{24,16},{32,24},{40,32},{48,40},{56,48},{64,5... | collective-permute-start | bytes 921608 | tf_op jit(solution)/shard_map/ppermute | solution.py:23
  36.6 17.3 %collective-permute-start = (f32[3,200,128]{2,1,0:T(8,128)}, f32[3,200,128]{2,1,0:T(8,128)}, u32[]{:S(2)}, u32[]{:S(2)}) collective-permute-start(f32[3,200,128]{2,1,0:T(8,128)} %get-tuple-element.51), channel_id=1, source_target_pairs={{0,8},{8,16},{16,24},{24,32},{32,40},{40,48},{48,56},{56,64},{64,7... | collective-permute-start | bytes 921608 | tf_op jit(solution)/shard_map/ppermute | solution.py:23
  38.6 16.3 %collective-permute-start.4 = (f32[3,200,128]{2,1,0:T(8,128)}, f32[3,200,128]{2,1,0:T(8,128)}, u32[]{:S(2)}, u32[]{:S(2)}) collective-permute-start(f32[3,200,128]{2,1,0:T(8,128)} %get-tuple-element.47), channel_id=1, source_target_pairs={{0,16},{8,24},{16,32},{24,40},{32,48},{40,56},{48,64},{56,72},{64,... | collective-permute-start | bytes 921608 | tf_op jit(solution)/shard_map/ppermute | solution.py:23
  41.5 24.9 %copy-start.15 = (pred[12]{0:T(512)(128)(4,1)}, pred[12]{0:T(512)(128)(4,1)S(1)}, u32[]{:S(2)}) copy-start(pred[12]{0:T(512)(128)(4,1)S(1)} %compare_and_fusion) | copy-start | bytes 40
  48.4 17.5 %collective-permute-start.5 = (f32[3,200,128]{2,1,0:T(8,128)}, f32[3,200,128]{2,1,0:T(8,128)S(1)}, u32[]{:S(2)}, u32[]{:S(2)}) collective-permute-start(f32[3,200,128]{2,1,0:T(8,128)} %get-tuple-element.46), channel_id=1, source_target_pairs={{0,24},{8,32},{16,40},{24,48},{32,56},{40,64},{48,72},{56,80},{64,... | collective-permute-start | bytes 921608 | tf_op jit(solution)/shard_map/ppermute | solution.py:23
  78.4 24.0 %all-to-all-start = ((f32[8,2,8,2048]{3,2,1,0:T(8,128)}), f32[8,2,8,2048]{3,2,1,0:T(8,128)}, u32[]{:S(2)}, u32[]{:S(2)}) async-start(f32[8,2,8,2048]{3,2,1,0:T(8,128)} %copy.125), calls=%async_computation | async-start | bytes 2097152 | tf_op jit(solution)/shard_map/all_to_all | solution.py:172
  105.1 19.3 %collective-permute-start.6 = (bf16[3,8,128]{2,1,0:T(8,128)(2,1)}, bf16[3,8,128]{2,1,0:T(8,128)(2,1)}, u32[]{:S(2)}, u32[]{:S(2)}) collective-permute-start(bf16[3,8,128]{2,1,0:T(8,128)(2,1)} %get-tuple-element.63), channel_id=1, source_target_pairs={{0,8},{8,16},{16,24},{24,32},{32,40},{40,48},{48,56},{56,64},{64,7... | collective-permute-start | bytes 18440 | tf_op jit(solution)/shard_map/ppermute | solution.py:23
  107.1 21.9 %collective-permute-start.8 = (bf16[3,8,128]{2,1,0:T(8,128)(2,1)S(1)}, bf16[3,8,128]{2,1,0:T(8,128)(2,1)}, u32[]{:S(2)}, u32[]{:S(2)}) collective-permute-start(bf16[3,8,128]{2,1,0:T(8,128)(2,1)S(1)} %get-tuple-element.61), channel_id=1, source_target_pairs={{0,488},{8,496},{16,504},{24,0},{32,8},{40,16},{48,24},{56,32},{64... | collective-permute-start | bytes 18440 | tf_op jit(solution)/shard_map/ppermute | solution.py:23
  111.5 20.1 %collective-permute-start.9 = (bf16[3,8,128]{2,1,0:T(8,128)(2,1)S(1)}, bf16[3,8,128]{2,1,0:T(8,128)(2,1)}, u32[]{:S(2)}, u32[]{:S(2)}) collective-permute-start(bf16[3,8,128]{2,1,0:T(8,128)(2,1)S(1)} %get-tuple-element.60), channel_id=1, source_target_pairs={{0,496},{8,504},{16,0},{24,8},{32,16},{40,24},{48,32},{56,40},{64,... | collective-permute-start | bytes 18440 | tf_op jit(solution)/shard_map/ppermute | solution.py:23
  113.6 18.7 %collective-permute-start.7 = (bf16[3,8,128]{2,1,0:T(8,128)(2,1)S(1)}, bf16[3,8,128]{2,1,0:T(8,128)(2,1)}, u32[]{:S(2)}, u32[]{:S(2)}) collective-permute-start(bf16[3,8,128]{2,1,0:T(8,128)(2,1)S(1)} %get-tuple-element.62), channel_id=1, source_target_pairs={{0,504},{8,0},{16,8},{24,16},{32,24},{40,32},{48,40},{56,48},{64,5... | collective-permute-start | bytes 18440 | tf_op jit(solution)/shard_map/ppermute | solution.py:23
  116.7 17.0 %collective-permute-start.10 = (bf16[3,8,128]{2,1,0:T(8,128)(2,1)S(1)}, bf16[3,8,128]{2,1,0:T(8,128)(2,1)}, u32[]{:S(2)}, u32[]{:S(2)}) collective-permute-start(bf16[3,8,128]{2,1,0:T(8,128)(2,1)S(1)} %get-tuple-element.59), channel_id=1, source_target_pairs={{0,16},{8,24},{16,32},{24,40},{32,48},{40,56},{48,64},{56,72},{64,... | collective-permute-start | bytes 18440 | tf_op jit(solution)/shard_map/ppermute | solution.py:23
  122.9 19.7 %copy-start.9 = (bf16[12,128,128]{2,1,0:T(8,128)(2,1)S(1)}, bf16[12,128,128]{2,1,0:T(8,128)(2,1)}, u32[]{:S(2)}) copy-start(bf16[12,128,128]{2,1,0:T(8,128)(2,1)} %gather_fusion.8) | copy-start | bytes 1179652
  124.4 13.6 %collective-permute-start.11 = (bf16[3,8,128]{2,1,0:T(8,128)(2,1)S(1)}, bf16[3,8,128]{2,1,0:T(8,128)(2,1)S(1)}, u32[]{:S(2)}, u32[]{:S(2)}) collective-permute-start(bf16[3,8,128]{2,1,0:T(8,128)(2,1)S(1)} %get-tuple-element.58), channel_id=1, source_target_pairs={{0,24},{8,32},{16,40},{24,48},{32,56},{40,64},{48,72},{56,80},{64,... | collective-permute-start | bytes 18440 | tf_op jit(solution)/shard_map/ppermute | solution.py:23
  129.0 5.4 %collective-permute-start.12 = (f32[12288]{0:T(1024)S(1)}, f32[12288]{0:T(1024)S(1)}, u32[]{:S(2)}, u32[]{:S(2)}) collective-permute-start(f32[12288]{0:T(1024)S(1)} %constant_dynamic-update-slice_fusion.7), channel_id=1, source_target_pairs={{0,8},{8,0},{16,24},{24,16},{32,40},{40,32},{48,56},{56,48},{64,72... | collective-permute-start | bytes 147464 | tf_op jit(solution)/shard_map/ppermute | solution.py:28
  134.3 6.1 %collective-permute-start.13 = (f32[12288]{0:T(1024)S(1)}, f32[12288]{0:T(1024)S(1)}, u32[]{:S(2)}, u32[]{:S(2)}) collective-permute-start(f32[12288]{0:T(1024)S(1)} %add.284), channel_id=1, source_target_pairs={{0,256},{8,264},{16,272},{24,280},{32,288},{40,296},{48,304},{56,3... | collective-permute-start | bytes 147464 | tf_op jit(solution)/shard_map/ppermute | solution.py:28
  140.5 6.0 %collective-permute-start.14 = (f32[12288]{0:T(1024)S(1)}, f32[12288]{0:T(1024)S(1)}, u32[]{:S(2)}, u32[]{:S(2)}) collective-permute-start(f32[12288]{0:T(1024)S(1)} %add.285), channel_id=1, source_target_pairs={{0,16},{8,24},{16,0},{24,8},{32,48},{40,56},{48,32},{56,40},{64,80... | collective-permute-start | bytes 147464 | tf_op jit(solution)/shard_map/ppermute | solution.py:28
  146.5 7.1 %collective-permute-start.15 = (f32[12288]{0:T(1024)S(1)}, f32[12288]{0:T(1024)S(1)}, u32[]{:S(2)}, u32[]{:S(2)}) collective-permute-start(f32[12288]{0:T(1024)S(1)} %add.286), channel_id=1, source_target_pairs={{0,32},{8,40},{16,48},{24,56},{32,0},{40,8},{48,16},{56,24},{64,96... | collective-permute-start | bytes 147464 | tf_op jit(solution)/shard_map/ppermute | solution.py:28
  153.6 10.4 %collective-permute-start.16 = (f32[12288]{0:T(1024)S(1)}, f32[12288]{0:T(1024)S(1)}, u32[]{:S(2)}, u32[]{:S(2)}) collective-permute-start(f32[12288]{0:T(1024)S(1)} %add.287), channel_id=1, source_target_pairs={{0,64},{8,72},{16,80},{24,88},{32,96},{40,104},{48,112},{56,120},{... | collective-permute-start | bytes 147464 | tf_op jit(solution)/shard_map/ppermute | solution.py:28
  164.0 14.7 %collective-permute-start.17 = (f32[12288]{0:T(1024)S(1)}, f32[12288]{0:T(1024)S(1)}, u32[]{:S(2)}, u32[]{:S(2)}) collective-permute-start(f32[12288]{0:T(1024)S(1)} %add.288), channel_id=1, source_target_pairs={{0,128},{8,136},{16,144},{24,152},{32,160},{40,168},{48,176},{56,1... | collective-permute-start | bytes 147464 | tf_op jit(solution)/shard_map/ppermute | solution.py:28
  (19 other events, 146.9 us)

commit v5 on v4

--- a/solution.py
+++ b/solution.py
@@ -200,9 +200,10 @@
     ).reshape(c_rows, nodes).astype(jnp.bfloat16)
 
     flat = jnp.concatenate([first_part.reshape(-1), second_part.reshape(-1)])
-    for mask in [1, row_devices // 2] + [m for m in (2, 4, 8, 16, 32) if m < row_devices // 2]:
-        if mask < row_devices:
-            flat = flat + swap_with(flat, "row", mask)
+    pieces = lax.all_to_all(flat.reshape(row_devices, -1), "row", 0, 0, tiled=True)
+    summed = jnp.sum(pieces, axis=0, keepdims=True)
+    spread = jnp.broadcast_to(summed, (row_devices, summed.shape[1]))
+    flat = lax.all_to_all(spread, "row", 0, 0, tiled=True).reshape(-1)
     first_grad = flat[: first_part.size].reshape(first_part.shape)
     second_grad = flat[first_part.size:].reshape(second_part.shape)
     return (scores, first_grad, second_grad)

time: 182 us -> 177 us (0.973)
  the two profiles are of different devices: /device:TPU:2 before, /device:TPU:1 now
where the time goes in v5:
time: 177 us; the launch traced here: 175 us
  starting transfers between devices  67.5 us (38%)
  waiting for transfers between devices  40.7 us (23%)
  local copies, waits for them, and re-layouts  34.8 us (20%)
  matrix products  18.1 us (10%)
  other arithmetic  12.6 us (7%)
    ppermute x12, starting transfers between devices, send_by(): lax.ppermute(x, axis, [(i, (i + by) % devices) for i in range(devices)])  47 us
    all_to_all x1, waiting for transfers between devices, local(): incoming = lax.all_to_all(outgoing, 'col', 0, 0, tiled=True)  14.2 us
    all_to_all x1, waiting for transfers between devices, local(): flat = lax.all_to_all(spread, 'row', 0, 0, tiled=True).reshape(-1)  12.9 us
    unnamed x58, local copies, waits for them, and re-layouts  10.9 us
    ppermute x12, waiting for transfers between devices, send_by(): lax.ppermute(x, axis, [(i, (i + by) % devices) for i in range(devices)])  10.1 us
    all_to_all x1, starting transfers between devices, local(): flat = lax.all_to_all(spread, 'row', 0, 0, tiled=True).reshape(-1)  9.31 us
    all_to_all x1, starting transfers between devices, local(): incoming = lax.all_to_all(outgoing, 'col', 0, 0, tiled=True)  6.35 us
    all_to_all x1, starting transfers between devices, local(): lax.all_to_all(flat.reshape(row_devices, -1), 'row', 0, 0, tiled=True)  4.86 us
  transfers between devices with their start and end apart: 15, of which 4 were waited for; matrix products, arithmetic and copies ran while one was open for 15% of the time, Pallas kernels for 0%

profile of v5, /device:TPU:1, one launch (start us, length us, event | category | flops | bytes accessed | tf_op | source)
XLA Modules:
  0.0 174.9 jit_solution(10562736952777963628)
XLA Ops:
  0.7 1.4 convolution_bitcast_fusion.3
  15.2 1.6 gather_fusion.1
  19.9 13.6 %collective-permute-start.2 = (f32[3,200,128]{2,1,0:T(8,128)}, f32[3,200,128]{2,1,0:T(8,128)}, u32[]{:S(2)}, u32[]{:S(2)}) collective-permute-start(f32[3,200,128]{2,1,0:T(8,128)} %get-tuple-element.55), channel_id=1, source_target_pairs={{0,488},{8,496},{16,504},{24,0},{32,8},{40,16},{48,24},{56,32},{64... | collective-permute-start | bytes 921608 | tf_op jit(solution)/shard_map/ppermute | solution.py:23
  33.5 2.6 %collective-permute-start.3 = (f32[3,200,128]{2,1,0:T(8,128)}, f32[3,200,128]{2,1,0:T(8,128)}, u32[]{:S(2)}, u32[]{:S(2)}) collective-permute-start(f32[3,200,128]{2,1,0:T(8,128)} %get-tuple-element.54), channel_id=1, source_target_pairs={{0,496},{8,504},{16,0},{24,8},{32,16},{40,24},{48,32},{56,40},{64,... | collective-permute-start | bytes 921608 | tf_op jit(solution)/shard_map/ppermute | solution.py:23
  36.1 2.5 %collective-permute-start.1 = (f32[3,200,128]{2,1,0:T(8,128)}, f32[3,200,128]{2,1,0:T(8,128)}, u32[]{:S(2)}, u32[]{:S(2)}) collective-permute-start(f32[3,200,128]{2,1,0:T(8,128)} %get-tuple-element.56), channel_id=1, source_target_pairs={{0,504},{8,0},{16,8},{24,16},{32,24},{40,32},{48,40},{56,48},{64,5... | collective-permute-start | bytes 921608 | tf_op jit(solution)/shard_map/ppermute | solution.py:23
  38.6 3.1 %collective-permute-start = (f32[3,200,128]{2,1,0:T(8,128)}, f32[3,200,128]{2,1,0:T(8,128)}, u32[]{:S(2)}, u32[]{:S(2)}) collective-permute-start(f32[3,200,128]{2,1,0:T(8,128)} %get-tuple-element.57), channel_id=1, source_target_pairs={{0,8},{8,16},{16,24},{24,32},{32,40},{40,48},{48,56},{56,64},{64,7... | collective-permute-start | bytes 921608 | tf_op jit(solution)/shard_map/ppermute | solution.py:23
  41.7 2.6 %collective-permute-start.4 = (f32[3,200,128]{2,1,0:T(8,128)}, f32[3,200,128]{2,1,0:T(8,128)}, u32[]{:S(2)}, u32[]{:S(2)}) collective-permute-start(f32[3,200,128]{2,1,0:T(8,128)} %get-tuple-element.53), channel_id=1, source_target_pairs={{0,16},{8,24},{16,32},{24,40},{32,48},{40,56},{48,64},{56,72},{64,... | collective-permute-start | bytes 921608 | tf_op jit(solution)/shard_map/ppermute | solution.py:23
  44.9 1.5 fusion.23
  51.0 1.9 %collective-permute-start.5 = (f32[3,200,128]{2,1,0:T(8,128)}, f32[3,200,128]{2,1,0:T(8,128)S(1)}, u32[]{:S(2)}, u32[]{:S(2)}) collective-permute-start(f32[3,200,128]{2,1,0:T(8,128)} %get-tuple-element.52), channel_id=1, source_target_pairs={{0,24},{8,32},{16,40},{24,48},{32,56},{40,64},{48,72},{56,80},{64,... | collective-permute-start | bytes 921608 | tf_op jit(solution)/shard_map/ppermute | solution.py:23
  57.8 10.1 %collective-permute-done.5 = f32[3,200,128]{2,1,0:T(8,128)S(1)} collective-permute-done((f32[3,200,128]{2,1,0:T(8,128)}, f32[3,200,128]{2,1,0:T(8,128)S(1)}, u32[]{:S(2)}, u32[]{:S(2)}) %collective-permute-start.5) | collective-permute-done | bytes 307232 | tf_op jit(solution)/shard_map/ppermute | solution.py:23
  68.4 2.4 %fusion.2 = f32[192,128,16]{1,2,0:T(8,128)S(1)} fusion(f32[12,192,128]{2,1,0:T(8,128)S(1)} %fusion.15, f32[12,16]{1,0:T(8,128)S(1)} %gather_fusion.5, pred[12]{0:T(512)(128)(4,1)S(1)} %copy-done.16), kind=kOutput, calls=%fused_computation.16 | convolution fusion | flops 56623296 | bytes 2753292 | tf_op jit(solution)/shard_map/kb,kfn->fbn/dot_general | solution.py:71
  80.5 6.3 %all-to-all-start = ((f32[8,2,8,2048]{3,2,1,0:T(8,128)}), f32[8,2,8,2048]{3,2,1,0:T(8,128)}, u32[]{:S(2)}, u32[]{:S(2)}) async-start(f32[8,2,8,2048]{3,2,1,0:T(8,128)} %copy.153), calls=%async_computation | async-start | bytes 2097152 | tf_op jit(solution)/shard_map/all_to_all | solution.py:172
  89.3 14.2 %all-to-all-done = f32[8,2,8,2048]{3,2,1,0:T(8,128)} async-done(((f32[8,2,8,2048]{3,2,1,0:T(8,128)}), f32[8,2,8,2048]{3,2,1,0:T(8,128)}, u32[]{:S(2)}, u32[]{:S(2)}) %all-to-all-start) | async-done | bytes 1048608 | tf_op jit(solution)/shard_map/all_to_all | solution.py:172
  106.9 1.9 %collective-permute-start.6 = (bf16[3,8,128]{2,1,0:T(8,128)(2,1)}, bf16[3,8,128]{2,1,0:T(8,128)(2,1)}, u32[]{:S(2)}, u32[]{:S(2)}) collective-permute-start(bf16[3,8,128]{2,1,0:T(8,128)(2,1)} %get-tuple-element.69), channel_id=1, source_target_pairs={{0,8},{8,16},{16,24},{24,32},{32,40},{40,48},{48,56},{56,64},{64,7... | collective-permute-start | bytes 18440 | tf_op jit(solution)/shard_map/ppermute | solution.py:23
  108.8 3.2 %collective-permute-start.8 = (bf16[3,8,128]{2,1,0:T(8,128)(2,1)}, bf16[3,8,128]{2,1,0:T(8,128)(2,1)}, u32[]{:S(2)}, u32[]{:S(2)}) collective-permute-start(bf16[3,8,128]{2,1,0:T(8,128)(2,1)} %get-tuple-element.67), channel_id=1, source_target_pairs={{0,488},{8,496},{16,504},{24,0},{32,8},{40,16},{48,24},{56,32},{64... | collective-permute-start | bytes 18440 | tf_op jit(solution)/shard_map/ppermute | solution.py:23
  112.1 5.6 %collective-permute-start.9 = (bf16[3,8,128]{2,1,0:T(8,128)(2,1)}, bf16[3,8,128]{2,1,0:T(8,128)(2,1)}, u32[]{:S(2)}, u32[]{:S(2)}) collective-permute-start(bf16[3,8,128]{2,1,0:T(8,128)(2,1)} %get-tuple-element.66), channel_id=1, source_target_pairs={{0,496},{8,504},{16,0},{24,8},{32,16},{40,24},{48,32},{56,40},{64,... | collective-permute-start | bytes 18440 | tf_op jit(solution)/shard_map/ppermute | solution.py:23
  117.7 1.9 %collective-permute-start.7 = (bf16[3,8,128]{2,1,0:T(8,128)(2,1)}, bf16[3,8,128]{2,1,0:T(8,128)(2,1)}, u32[]{:S(2)}, u32[]{:S(2)}) collective-permute-start(bf16[3,8,128]{2,1,0:T(8,128)(2,1)} %get-tuple-element.68), channel_id=1, source_target_pairs={{0,504},{8,0},{16,8},{24,16},{32,24},{40,32},{48,40},{56,48},{64,5... | collective-permute-start | bytes 18440 | tf_op jit(solution)/shard_map/ppermute | solution.py:23
  119.6 3.5 %collective-permute-start.10 = (bf16[3,8,128]{2,1,0:T(8,128)(2,1)}, bf16[3,8,128]{2,1,0:T(8,128)(2,1)}, u32[]{:S(2)}, u32[]{:S(2)}) collective-permute-start(bf16[3,8,128]{2,1,0:T(8,128)(2,1)} %get-tuple-element.65), channel_id=1, source_target_pairs={{0,16},{8,24},{16,32},{24,40},{32,48},{40,56},{48,64},{56,72},{64,... | collective-permute-start | bytes 18440 | tf_op jit(solution)/shard_map/ppermute | solution.py:23
  125.1 1.6 fusion.1
  129.3 4.9 %all-to-all-start.1 = ((f32[64,1,192]{2,1,0:T(1,128)}), f32[64,1,192]{2,1,0:T(1,128)S(1)}, u32[]{:S(2)}, u32[]{:S(2)}) async-start(f32[64,1,192]{2,1,0:T(1,128)} %all_to_all.14), calls=%async_computation.1 | async-start | bytes 131072 | tf_op jit(solution)/shard_map/all_to_all | solution.py:203
  134.1 4.4 %collective-permute-start.11 = (bf16[3,8,128]{2,1,0:T(8,128)(2,1)S(1)}, bf16[3,8,128]{2,1,0:T(8,128)(2,1)S(1)}, u32[]{:S(2)}, u32[]{:S(2)}) collective-permute-start(bf16[3,8,128]{2,1,0:T(8,128)(2,1)S(1)} %get-tuple-element.64), channel_id=1, source_target_pairs={{0,24},{8,32},{16,40},{24,48},{32,56},{40,64},{48,72},{56,80},{64,... | collective-permute-start | bytes 18440 | tf_op jit(solution)/shard_map/ppermute | solution.py:23
  145.2 3.6 %all-to-all-done.1 = f32[64,1,192]{2,1,0:T(1,128)S(1)} async-done(((f32[64,1,192]{2,1,0:T(1,128)}), f32[64,1,192]{2,1,0:T(1,128)S(1)}, u32[]{:S(2)}, u32[]{:S(2)}) %all-to-all-start.1) | async-done | bytes 49184 | tf_op jit(solution)/shard_map/all_to_all | solution.py:203
  149.5 9.3 %all-to-all-start.2 = ((f32[64,1,192]{2,1,0:T(1,128)}), f32[64,1,192]{2,1,0:T(1,128)S(1)}, u32[]{:S(2)}, u32[]{:S(2)}) async-start(f32[64,1,192]{2,1,0:T(1,128)} %broadcast_in_dim.116), calls=%async_computation.2 | async-start | bytes 131072 | tf_op jit(solution)/shard_map/all_to_all | solution.py:206
  160.5 12.9 %all-to-all-done.2 = f32[64,1,192]{2,1,0:T(1,128)S(1)} async-done(((f32[64,1,192]{2,1,0:T(1,128)}), f32[64,1,192]{2,1,0:T(1,128)S(1)}, u32[]{:S(2)}, u32[]{:S(2)}) %all-to-all-start.2) | async-done | bytes 49184 | tf_op jit(solution)/shard_map/all_to_all | solution.py:206
  (181 shorter events, 56.9 us)
Async XLA Ops:
  2.1 42.3 %copy-start.12 = (f32[8,16,128]{2,0,1:T(8,128)}, f32[8,16,128]{2,0,1:T(8,128)S(1)}, u32[]{:S(2)}) copy-start(f32[8,16,128]{2,0,1:T(8,128)S(1)} %convolution_bitcast_fusion.3) | copy-start | bytes 196612
  3.4 41.0 %copy-start.11 = (f32[8,16,128]{2,0,1:T(8,128)}, f32[8,16,128]{2,0,1:T(8,128)S(1)}, u32[]{:S(2)}) copy-start(f32[8,16,128]{2,0,1:T(8,128)S(1)} %convolution_bitcast_fusion.2) | copy-start | bytes 196612
  10.0 34.3 %copy-start.20 = (s32[12]{0:T(128)}, s32[12]{0:T(128)S(1)}, u32[]{:S(2)}) copy-start(s32[12]{0:T(128)S(1)} %select_reduce_fusion) | copy-start | bytes 148
  19.9 26.5 %copy-start.18 = (s32[6,2]{0,1:T(2,128)S(1)}, s32[6,2]{0,1:T(2,128)}, u32[]{:S(2)}) copy-start(s32[6,2]{0,1:T(2,128)} %get-tuple-element.72) | copy-start | bytes 148
  19.9 31.1 %collective-permute-start.2 = (f32[3,200,128]{2,1,0:T(8,128)}, f32[3,200,128]{2,1,0:T(8,128)}, u32[]{:S(2)}, u32[]{:S(2)}) collective-permute-start(f32[3,200,128]{2,1,0:T(8,128)} %get-tuple-element.55), channel_id=1, source_target_pairs={{0,488},{8,496},{16,504},{24,0},{32,8},{40,16},{48,24},{56,32},{64... | collective-permute-start | bytes 921608 | tf_op jit(solution)/shard_map/ppermute | solution.py:23
  33.5 20.4 %collective-permute-start.3 = (f32[3,200,128]{2,1,0:T(8,128)}, f32[3,200,128]{2,1,0:T(8,128)}, u32[]{:S(2)}, u32[]{:S(2)}) collective-permute-start(f32[3,200,128]{2,1,0:T(8,128)} %get-tuple-element.54), channel_id=1, source_target_pairs={{0,496},{8,504},{16,0},{24,8},{32,16},{40,24},{48,32},{56,40},{64,... | collective-permute-start | bytes 921608 | tf_op jit(solution)/shard_map/ppermute | solution.py:23
  36.1 18.8 %collective-permute-start.1 = (f32[3,200,128]{2,1,0:T(8,128)}, f32[3,200,128]{2,1,0:T(8,128)}, u32[]{:S(2)}, u32[]{:S(2)}) collective-permute-start(f32[3,200,128]{2,1,0:T(8,128)} %get-tuple-element.56), channel_id=1, source_target_pairs={{0,504},{8,0},{16,8},{24,16},{32,24},{40,32},{48,40},{56,48},{64,5... | collective-permute-start | bytes 921608 | tf_op jit(solution)/shard_map/ppermute | solution.py:23
  38.6 17.2 %collective-permute-start = (f32[3,200,128]{2,1,0:T(8,128)}, f32[3,200,128]{2,1,0:T(8,128)}, u32[]{:S(2)}, u32[]{:S(2)}) collective-permute-start(f32[3,200,128]{2,1,0:T(8,128)} %get-tuple-element.57), channel_id=1, source_target_pairs={{0,8},{8,16},{16,24},{24,32},{32,40},{40,48},{48,56},{56,64},{64,7... | collective-permute-start | bytes 921608 | tf_op jit(solution)/shard_map/ppermute | solution.py:23
  41.7 15.1 %collective-permute-start.4 = (f32[3,200,128]{2,1,0:T(8,128)}, f32[3,200,128]{2,1,0:T(8,128)}, u32[]{:S(2)}, u32[]{:S(2)}) collective-permute-start(f32[3,200,128]{2,1,0:T(8,128)} %get-tuple-element.53), channel_id=1, source_target_pairs={{0,16},{8,24},{16,32},{24,40},{32,48},{40,56},{48,64},{56,72},{64,... | collective-permute-start | bytes 921608 | tf_op jit(solution)/shard_map/ppermute | solution.py:23
  50.4 17.4 %copy-start.8 = (bf16[12,128,128]{2,1,0:T(8,128)(2,1)S(1)}, bf16[12,128,128]{2,1,0:T(8,128)(2,1)}, u32[]{:S(2)}) copy-start(bf16[12,128,128]{2,1,0:T(8,128)(2,1)} %gather_fusion.8) | copy-start | bytes 1179652
  50.5 17.4 %copy-start.16 = (pred[12]{0:T(512)(128)(4,1)S(1)}, pred[12]{0:T(512)(128)(4,1)}, u32[]{:S(2)}) copy-start(pred[12]{0:T(512)(128)(4,1)} %compare_and_fusion) | copy-start | bytes 40
  51.0 16.8 %collective-permute-start.5 = (f32[3,200,128]{2,1,0:T(8,128)}, f32[3,200,128]{2,1,0:T(8,128)S(1)}, u32[]{:S(2)}, u32[]{:S(2)}) collective-permute-start(f32[3,200,128]{2,1,0:T(8,128)} %get-tuple-element.52), channel_id=1, source_target_pairs={{0,24},{8,32},{16,40},{24,48},{32,56},{40,64},{48,72},{56,80},{64,... | collective-permute-start | bytes 921608 | tf_op jit(solution)/shard_map/ppermute | solution.py:23
  80.5 23.0 %all-to-all-start = ((f32[8,2,8,2048]{3,2,1,0:T(8,128)}), f32[8,2,8,2048]{3,2,1,0:T(8,128)}, u32[]{:S(2)}, u32[]{:S(2)}) async-start(f32[8,2,8,2048]{3,2,1,0:T(8,128)} %copy.153), calls=%async_computation | async-start | bytes 2097152 | tf_op jit(solution)/shard_map/all_to_all | solution.py:172
  106.9 33.8 %collective-permute-start.6 = (bf16[3,8,128]{2,1,0:T(8,128)(2,1)}, bf16[3,8,128]{2,1,0:T(8,128)(2,1)}, u32[]{:S(2)}, u32[]{:S(2)}) collective-permute-start(bf16[3,8,128]{2,1,0:T(8,128)(2,1)} %get-tuple-element.69), channel_id=1, source_target_pairs={{0,8},{8,16},{16,24},{24,32},{32,40},{40,48},{48,56},{56,64},{64,7... | collective-permute-start | bytes 18440 | tf_op jit(solution)/shard_map/ppermute | solution.py:23
  108.8 25.3 %collective-permute-start.8 = (bf16[3,8,128]{2,1,0:T(8,128)(2,1)}, bf16[3,8,128]{2,1,0:T(8,128)(2,1)}, u32[]{:S(2)}, u32[]{:S(2)}) collective-permute-start(bf16[3,8,128]{2,1,0:T(8,128)(2,1)} %get-tuple-element.67), channel_id=1, source_target_pairs={{0,488},{8,496},{16,504},{24,0},{32,8},{40,16},{48,24},{56,32},{64... | collective-permute-start | bytes 18440 | tf_op jit(solution)/shard_map/ppermute | solution.py:23
  112.1 27.2 %collective-permute-start.9 = (bf16[3,8,128]{2,1,0:T(8,128)(2,1)}, bf16[3,8,128]{2,1,0:T(8,128)(2,1)}, u32[]{:S(2)}, u32[]{:S(2)}) collective-permute-start(bf16[3,8,128]{2,1,0:T(8,128)(2,1)} %get-tuple-element.66), channel_id=1, source_target_pairs={{0,496},{8,504},{16,0},{24,8},{32,16},{40,24},{48,32},{56,40},{64,... | collective-permute-start | bytes 18440 | tf_op jit(solution)/shard_map/ppermute | solution.py:23
  117.7 22.2 %collective-permute-start.7 = (bf16[3,8,128]{2,1,0:T(8,128)(2,1)}, bf16[3,8,128]{2,1,0:T(8,128)(2,1)}, u32[]{:S(2)}, u32[]{:S(2)}) collective-permute-start(bf16[3,8,128]{2,1,0:T(8,128)(2,1)} %get-tuple-element.68), channel_id=1, source_target_pairs={{0,504},{8,0},{16,8},{24,16},{32,24},{40,32},{48,40},{56,48},{64,5... | collective-permute-start | bytes 18440 | tf_op jit(solution)/shard_map/ppermute | solution.py:23
  119.6 21.7 %collective-permute-start.10 = (bf16[3,8,128]{2,1,0:T(8,128)(2,1)}, bf16[3,8,128]{2,1,0:T(8,128)(2,1)}, u32[]{:S(2)}, u32[]{:S(2)}) collective-permute-start(bf16[3,8,128]{2,1,0:T(8,128)(2,1)} %get-tuple-element.65), channel_id=1, source_target_pairs={{0,16},{8,24},{16,32},{24,40},{32,48},{40,56},{48,64},{56,72},{64,... | collective-permute-start | bytes 18440 | tf_op jit(solution)/shard_map/ppermute | solution.py:23
  126.7 15.4 %copy-start.9 = (bf16[12,128,128]{2,1,0:T(8,128)(2,1)S(1)}, bf16[12,128,128]{2,1,0:T(8,128)(2,1)}, u32[]{:S(2)}) copy-start(bf16[12,128,128]{2,1,0:T(8,128)(2,1)} %gather_fusion.8) | copy-start | bytes 1179652
  127.7 17.1 %copy-start.17 = (pred[12]{0:T(512)(128)(4,1)S(1)}, pred[12]{0:T(512)(128)(4,1)}, u32[]{:S(2)}) copy-start(pred[12]{0:T(512)(128)(4,1)} %compare_and_fusion) | copy-start | bytes 40
  127.7 31.8 %copy-start.10 = (bf16[8,15,128]{2,0,1:T(8,128)(2,1)S(1)}, bf16[8,15,128]{2,0,1:T(8,128)(2,1)}, u32[]{:S(2)}) copy-start(bf16[8,15,128]{2,0,1:T(8,128)(2,1)} %get-tuple-element.70) | copy-start | bytes 92164
  129.3 19.4 %all-to-all-start.1 = ((f32[64,1,192]{2,1,0:T(1,128)}), f32[64,1,192]{2,1,0:T(1,128)S(1)}, u32[]{:S(2)}, u32[]{:S(2)}) async-start(f32[64,1,192]{2,1,0:T(1,128)} %all_to_all.14), calls=%async_computation.1 | async-start | bytes 131072 | tf_op jit(solution)/shard_map/all_to_all | solution.py:203
  134.1 7.9 %collective-permute-start.11 = (bf16[3,8,128]{2,1,0:T(8,128)(2,1)S(1)}, bf16[3,8,128]{2,1,0:T(8,128)(2,1)S(1)}, u32[]{:S(2)}, u32[]{:S(2)}) collective-permute-start(bf16[3,8,128]{2,1,0:T(8,128)(2,1)S(1)} %get-tuple-element.64), channel_id=1, source_target_pairs={{0,24},{8,32},{16,40},{24,48},{32,56},{40,64},{48,72},{56,80},{64,... | collective-permute-start | bytes 18440 | tf_op jit(solution)/shard_map/ppermute | solution.py:23
  149.5 23.9 %all-to-all-start.2 = ((f32[64,1,192]{2,1,0:T(1,128)}), f32[64,1,192]{2,1,0:T(1,128)S(1)}, u32[]{:S(2)}, u32[]{:S(2)}) async-start(f32[64,1,192]{2,1,0:T(1,128)} %broadcast_in_dim.116), calls=%async_computation.2 | async-start | bytes 131072 | tf_op jit(solution)/shard_map/all_to_all | solution.py:206
  (17 other events, 93.2 us)

commit v6 on v5

--- a/solution.py
+++ b/solution.py
@@ -187,7 +187,15 @@
     class_blocks = class_in.reshape(c_rows, NB, BLK)
     class_pick = jnp.take(class_blocks.transpose(1, 0, 2), pick, axis=0)
     class_pick = class_pick.reshape(len(shifts()), 3, c_rows, BLK)
-    class_arrived = [send_by(class_pick[i], "row", e) for i, e in enumerate(shifts())]
+    lanes = jnp.zeros((row_devices,) + class_pick.shape[1:], class_pick.dtype)
+    for i, e in enumerate(shifts()):
+        lanes = lanes.at[e % row_devices].set(class_pick[i])
+    doubled = jnp.concatenate([lanes, lanes], 0)
+    outgoing = lax.dynamic_slice_in_dim(doubled, jnp.mod(row_devices - me, row_devices), row_devices, 0)
+    incoming = lax.all_to_all(outgoing, "row", 0, 0, tiled=True)
+    doubled = jnp.concatenate([incoming, incoming], 0)
+    near = lax.dynamic_slice_in_dim(doubled, jnp.mod(me - REACH, row_devices), 2 * REACH + 1, 0)
+    class_arrived = [near[REACH - e] for e in shifts()]
     class_pairs = jnp.concatenate([a[:2] for a in class_arrived], 0)
     scores = forward_sum(
         class_blocks,

time: 177 us -> 190 us (1.073)
  waiting for transfers between devices: 40.7 us -> 76.2 us
  starting transfers between devices: 67.5 us -> 48.1 us
    all_to_all x0 -> x1, waiting for transfers between devices: none -> 25.7 us  [local(): incoming = lax.all_to_all(outgoing, 'row', 0, 0, tiled=True)]
    ppermute x12 -> x6, starting transfers between devices: 47 us -> 26.2 us  [send_by(): lax.ppermute(x, axis, [(i, (i + by) % devices) for i in range(devices)])]
    all_to_all x1, waiting for transfers between devices: 3.56 us -> 14 us  [local(): lax.all_to_all(flat.reshape(row_devices, -1), 'row', 0, 0, tiled=True)]
    all_to_all x1, starting transfers between devices: 9.31 us -> 4.61 us  [local(): flat = lax.all_to_all(spread, 'row', 0, 0, tiled=True).reshape(-1)]
    all_to_all x0 -> x1, starting transfers between devices: none -> 4.45 us  [local(): incoming = lax.all_to_all(outgoing, 'row', 0, 0, tiled=True)]
    scatter x0 -> x6, local copies, waits for them, and re-layouts: none -> 3.76 us  [local(): lanes = lanes.at[e % row_devices].set(class_pick[i])]
    unnamed x58 -> x52, local copies, waits for them, and re-layouts: 10.9 us -> 7.5 us
    concatenate x0 -> x2, other arithmetic: none -> 1.99 us  [the longest x1 1.94 us: local(): doubled = jnp.concatenate([lanes, lanes], 0)]
  transfers between devices with their start and end apart: 15 -> 10, of which waited for: 4 -> 5; matrix products, arithmetic and copies ran while one was open for 15% -> 10% of each run, Pallas kernels for 0% -> 0%
where the time goes in v6:
time: 190 us; the launch traced here: 189 us
  waiting for transfers between devices  76.2 us (40%)
  starting transfers between devices  48.1 us (25%)
  local copies, waits for them, and re-layouts  33.2 us (17%)
  matrix products  16.8 us (9%)
  other arithmetic  13.3 us (7%)
    ppermute x6, starting transfers between devices, send_by(): lax.ppermute(x, axis, [(i, (i + by) % devices) for i in range(devices)])  26.2 us
    all_to_all x1, waiting for transfers between devices, local(): incoming = lax.all_to_all(outgoing, 'row', 0, 0, tiled=True)  25.7 us
    all_to_all x1, waiting for transfers between devices, local(): incoming = lax.all_to_all(outgoing, 'col', 0, 0, tiled=True)  14.2 us
    all_to_all x1, waiting for transfers between devices, local(): lax.all_to_all(flat.reshape(row_devices, -1), 'row', 0, 0, tiled=True)  14 us
    all_to_all x1, waiting for transfers between devices, local(): flat = lax.all_to_all(spread, 'row', 0, 0, tiled=True).reshape(-1)  12.2 us
    ppermute x6, waiting for transfers between devices, send_by(): lax.ppermute(x, axis, [(i, (i + by) % devices) for i in range(devices)])  10.1 us
    unnamed x52, local copies, waits for them, and re-layouts  7.5 us
    all_to_all x1, starting transfers between devices, local(): lax.all_to_all(flat.reshape(row_devices, -1), 'row', 0, 0, tiled=True)  6.51 us
  transfers between devices with their start and end apart: 10, of which 5 were waited for; matrix products, arithmetic and copies ran while one was open for 10% of the time, Pallas kernels for 0%

profile of v6, /device:TPU:1, one launch (start us, length us, event | category | flops | bytes accessed | tf_op | source)
XLA Modules:
  0.0 188.8 jit_solution(10756957532683933726)
XLA Ops:
  0.7 1.4 convolution_bitcast_fusion.3
  15.1 1.7 gather_fusion.1
  16.8 1.3 select_convert_fusion
  19.9 13.4 %collective-permute-start.2 = (f32[3,200,128]{2,1,0:T(8,128)}, f32[3,200,128]{2,1,0:T(8,128)}, u32[]{:S(2)}, u32[]{:S(2)}) collective-permute-start(f32[3,200,128]{2,1,0:T(8,128)} %get-tuple-element.127), channel_id=1, source_target_pairs={{0,488},{8,496},{16,504},{24,0},{32,8},{40,16},{48,24},{56,32},{64... | collective-permute-start | bytes 921608 | tf_op jit(solution)/shard_map/ppermute | solution.py:23
  33.3 2.6 %collective-permute-start.3 = (f32[3,200,128]{2,1,0:T(8,128)}, f32[3,200,128]{2,1,0:T(8,128)}, u32[]{:S(2)}, u32[]{:S(2)}) collective-permute-start(f32[3,200,128]{2,1,0:T(8,128)} %get-tuple-element.126), channel_id=1, source_target_pairs={{0,496},{8,504},{16,0},{24,8},{32,16},{40,24},{48,32},{56,40},{64,... | collective-permute-start | bytes 921608 | tf_op jit(solution)/shard_map/ppermute | solution.py:23
  36.0 2.5 %collective-permute-start.1 = (f32[3,200,128]{2,1,0:T(8,128)}, f32[3,200,128]{2,1,0:T(8,128)}, u32[]{:S(2)}, u32[]{:S(2)}) collective-permute-start(f32[3,200,128]{2,1,0:T(8,128)} %get-tuple-element.128), channel_id=1, source_target_pairs={{0,504},{8,0},{16,8},{24,16},{32,24},{40,32},{48,40},{56,48},{64,5... | collective-permute-start | bytes 921608 | tf_op jit(solution)/shard_map/ppermute | solution.py:23
  38.5 3.1 %collective-permute-start = (f32[3,200,128]{2,1,0:T(8,128)}, f32[3,200,128]{2,1,0:T(8,128)}, u32[]{:S(2)}, u32[]{:S(2)}) collective-permute-start(f32[3,200,128]{2,1,0:T(8,128)} %get-tuple-element.129), channel_id=1, source_target_pairs={{0,8},{8,16},{16,24},{24,32},{32,40},{40,48},{48,56},{56,64},{64,7... | collective-permute-start | bytes 921608 | tf_op jit(solution)/shard_map/ppermute | solution.py:23
  41.6 2.6 %collective-permute-start.4 = (f32[3,200,128]{2,1,0:T(8,128)}, f32[3,200,128]{2,1,0:T(8,128)}, u32[]{:S(2)}, u32[]{:S(2)}) collective-permute-start(f32[3,200,128]{2,1,0:T(8,128)} %get-tuple-element.125), channel_id=1, source_target_pairs={{0,16},{8,24},{16,32},{24,40},{32,48},{40,56},{48,64},{56,72},{64,... | collective-permute-start | bytes 921608 | tf_op jit(solution)/shard_map/ppermute | solution.py:23
  44.3 1.5 fusion.22
  47.8 1.4 gather_fusion.8
  51.5 1.9 %collective-permute-start.5 = (f32[3,200,128]{2,1,0:T(8,128)}, f32[3,200,128]{2,1,0:T(8,128)S(1)}, u32[]{:S(2)}, u32[]{:S(2)}) collective-permute-start(f32[3,200,128]{2,1,0:T(8,128)} %get-tuple-element.124), channel_id=1, source_target_pairs={{0,24},{8,32},{16,40},{24,48},{32,56},{40,64},{48,72},{56,80},{64,... | collective-permute-start | bytes 921608 | tf_op jit(solution)/shard_map/ppermute | solution.py:23
  58.2 10.1 %collective-permute-done.5 = f32[3,200,128]{2,1,0:T(8,128)S(1)} collective-permute-done((f32[3,200,128]{2,1,0:T(8,128)}, f32[3,200,128]{2,1,0:T(8,128)S(1)}, u32[]{:S(2)}, u32[]{:S(2)}) %collective-permute-start.5) | collective-permute-done | bytes 307232 | tf_op jit(solution)/shard_map/ppermute | solution.py:23
  68.8 2.4 %fusion.2 = f32[192,128,16]{1,2,0:T(8,128)S(1)} fusion(f32[12,192,128]{2,1,0:T(8,128)S(1)} %fusion.15, f32[12,16]{1,0:T(8,128)S(1)} %gather_fusion.5, pred[12]{0:T(512)(128)(4,1)S(1)} %compare_and_fusion), kind=kOutput, calls=%fused_computation.16 | convolution fusion | flops 56623296 | bytes 2753292 | tf_op jit(solution)/shard_map/kb,kfn->fbn/dot_general | solution.py:71
  80.9 6.4 %all-to-all-start = ((f32[8,2,8,2048]{3,2,1,0:T(8,128)}), f32[8,2,8,2048]{3,2,1,0:T(8,128)}, u32[]{:S(2)}, u32[]{:S(2)}) async-start(f32[8,2,8,2048]{3,2,1,0:T(8,128)} %copy.153), calls=%async_computation | async-start | bytes 2097152 | tf_op jit(solution)/shard_map/all_to_all | solution.py:172
  88.5 1.3 copy.157
  89.8 14.2 %all-to-all-done = f32[8,2,8,2048]{3,2,1,0:T(8,128)} async-done(((f32[8,2,8,2048]{3,2,1,0:T(8,128)}), f32[8,2,8,2048]{3,2,1,0:T(8,128)}, u32[]{:S(2)}, u32[]{:S(2)}) %all-to-all-start) | async-done | bytes 1048608 | tf_op jit(solution)/shard_map/all_to_all | solution.py:172
  109.7 1.7 fusion.1
  113.2 6.5 %all-to-all-start.2 = ((f32[64,1,192]{2,1,0:T(1,128)}), f32[64,1,192]{2,1,0:T(1,128)S(1)}, u32[]{:S(2)}, u32[]{:S(2)}) async-start(f32[64,1,192]{2,1,0:T(1,128)} %all_to_all.18), calls=%async_computation.2 | async-start | bytes 131072 | tf_op jit(solution)/shard_map/all_to_all | solution.py:211
  120.3 14.0 %all-to-all-done.2 = f32[64,1,192]{2,1,0:T(1,128)S(1)} async-done(((f32[64,1,192]{2,1,0:T(1,128)}), f32[64,1,192]{2,1,0:T(1,128)S(1)}, u32[]{:S(2)}, u32[]{:S(2)}) %all-to-all-start.2) | async-done | bytes 49184 | tf_op jit(solution)/shard_map/all_to_all | solution.py:211
  135.1 4.6 %all-to-all-start.3 = ((f32[64,1,192]{2,1,0:T(1,128)}), f32[64,1,192]{2,1,0:T(1,128)S(1)}, u32[]{:S(2)}, u32[]{:S(2)}) async-start(f32[64,1,192]{2,1,0:T(1,128)} %broadcast_in_dim.117), calls=%async_computation.3 | async-start | bytes 131072 | tf_op jit(solution)/shard_map/all_to_all | solution.py:214
  140.3 1.9 %fusion.40 = bf16[64,3,8,128]{3,2,1,0:T(8,128)(2,1)} fusion(s32[]{:T(128)S(6)} %select_n.283, bf16[64,3,8,128]{3,2,1,0:T(8,128)(2,1)} %fusion.84), kind=kLoop, calls=%fused_computation.75 | loop fusion | flops 196608 | bytes 786436 | tf_op jit(solution)/shard_map/concatenate | solution.py:193
  142.2 12.2 %all-to-all-done.3 = f32[64,1,192]{2,1,0:T(1,128)S(1)} async-done(((f32[64,1,192]{2,1,0:T(1,128)}), f32[64,1,192]{2,1,0:T(1,128)S(1)}, u32[]{:S(2)}, u32[]{:S(2)}) %all-to-all-start.3) | async-done | bytes 49184 | tf_op jit(solution)/shard_map/all_to_all | solution.py:214
  154.4 4.5 %all-to-all-start.1 = ((bf16[64,3,8,128]{3,2,1,0:T(8,128)(2,1)}), bf16[64,3,8,128]{3,2,1,0:T(8,128)(2,1)S(1)}, u32[]{:S(2)}, u32[]{:S(2)}) async-start(bf16[64,3,8,128]{3,2,1,0:T(8,128)(2,1)} %fusion.40), calls=%async_computation.1 | async-start | bytes 786432 | tf_op jit(solution)/shard_map/all_to_all | solution.py:195
  160.5 25.7 %all-to-all-done.1 = bf16[64,3,8,128]{3,2,1,0:T(8,128)(2,1)S(1)} async-done(((bf16[64,3,8,128]{3,2,1,0:T(8,128)(2,1)}), bf16[64,3,8,128]{3,2,1,0:T(8,128)(2,1)S(1)}, u32[]{:S(2)}, u32[]{:S(2)}) %all-to-all-start.1) | async-done | bytes 393248 | tf_op jit(solution)/shard_map/all_to_all | solution.py:195
  (172 shorter events, 48.6 us)
Async XLA Ops:
  0.6 13.3 %copy-start = (bf16[12,128,128]{2,1,0:T(8,128)(2,1)S(1)}, bf16[12,128,128]{2,1,0:T(8,128)(2,1)}, u32[]{:S(2)}) copy-start(bf16[12,128,128]{2,1,0:T(8,128)(2,1)} %param.34) | copy-start | bytes 1179652
  0.6 9.2 %copy-start.16 = (s32[6,1]{0,1:T(1,128)S(1)}, s32[6,1]{0,1:T(1,128)}, u32[]{:S(2)}) copy-start(s32[6,1]{0,1:T(1,128)} %constant.448.clone) | copy-start | bytes 76
  0.7 6.6 %copy-start.1 = (s32[1,12]{1,0:T(1,128)S(1)}, s32[1,12]{1,0:T(1,128)}, u32[]{:S(2)}) copy-start(s32[1,12]{1,0:T(1,128)} %param.35) | copy-start | bytes 148
  0.7 9.9 %copy-start.19 = (s32[64]{0:T(128)S(1)}, s32[64]{0:T(128)}, u32[]{:S(2)}) copy-start(s32[64]{0:T(128)} %param.37) | copy-start | bytes 772
  0.7 12.3 %copy-start.5 = (bf16[128,2048]{1,0:T(8,128)(2,1)S(1)}, bf16[128,2048]{1,0:T(8,128)(2,1)}, u32[]{:S(2)}) copy-start(bf16[128,2048]{1,0:T(8,128)(2,1)} %param.29) | copy-start | bytes 1572868
  0.7 12.3 %copy-start.14 = (bf16[128,64]{0,1:T(8,128)(2,1)S(1)}, bf16[128,64]{0,1:T(8,128)(2,1)}, u32[]{:S(2)}) copy-start(bf16[128,64]{0,1:T(8,128)(2,1)} %param.30) | copy-start | bytes 49156
  2.1 42.2 %copy-start.11 = (f32[8,16,128]{2,0,1:T(8,128)}, f32[8,16,128]{2,0,1:T(8,128)S(1)}, u32[]{:S(2)}) copy-start(f32[8,16,128]{2,0,1:T(8,128)S(1)} %convolution_bitcast_fusion.3) | copy-start | bytes 196612
  3.4 40.8 %copy-start.10 = (f32[8,16,128]{2,0,1:T(8,128)}, f32[8,16,128]{2,0,1:T(8,128)S(1)}, u32[]{:S(2)}) copy-start(f32[8,16,128]{2,0,1:T(8,128)S(1)} %convolution_bitcast_fusion.2) | copy-start | bytes 196612
  10.0 34.2 %copy-start.17 = (s32[12]{0:T(128)}, s32[12]{0:T(128)S(1)}, u32[]{:S(2)}) copy-start(s32[12]{0:T(128)S(1)} %select_reduce_fusion) | copy-start | bytes 148
  19.9 31.6 %collective-permute-start.2 = (f32[3,200,128]{2,1,0:T(8,128)}, f32[3,200,128]{2,1,0:T(8,128)}, u32[]{:S(2)}, u32[]{:S(2)}) collective-permute-start(f32[3,200,128]{2,1,0:T(8,128)} %get-tuple-element.127), channel_id=1, source_target_pairs={{0,488},{8,496},{16,504},{24,0},{32,8},{40,16},{48,24},{56,32},{64... | collective-permute-start | bytes 921608 | tf_op jit(solution)/shard_map/ppermute | solution.py:23
  33.3 21.0 %collective-permute-start.3 = (f32[3,200,128]{2,1,0:T(8,128)}, f32[3,200,128]{2,1,0:T(8,128)}, u32[]{:S(2)}, u32[]{:S(2)}) collective-permute-start(f32[3,200,128]{2,1,0:T(8,128)} %get-tuple-element.126), channel_id=1, source_target_pairs={{0,496},{8,504},{16,0},{24,8},{32,16},{40,24},{48,32},{56,40},{64,... | collective-permute-start | bytes 921608 | tf_op jit(solution)/shard_map/ppermute | solution.py:23
  36.0 19.4 %collective-permute-start.1 = (f32[3,200,128]{2,1,0:T(8,128)}, f32[3,200,128]{2,1,0:T(8,128)}, u32[]{:S(2)}, u32[]{:S(2)}) collective-permute-start(f32[3,200,128]{2,1,0:T(8,128)} %get-tuple-element.128), channel_id=1, source_target_pairs={{0,504},{8,0},{16,8},{24,16},{32,24},{40,32},{48,40},{56,48},{64,5... | collective-permute-start | bytes 921608 | tf_op jit(solution)/shard_map/ppermute | solution.py:23
  38.5 17.8 %collective-permute-start = (f32[3,200,128]{2,1,0:T(8,128)}, f32[3,200,128]{2,1,0:T(8,128)}, u32[]{:S(2)}, u32[]{:S(2)}) collective-permute-start(f32[3,200,128]{2,1,0:T(8,128)} %get-tuple-element.129), channel_id=1, source_target_pairs={{0,8},{8,16},{16,24},{24,32},{32,40},{40,48},{48,56},{56,64},{64,7... | collective-permute-start | bytes 921608 | tf_op jit(solution)/shard_map/ppermute | solution.py:23
  41.6 15.7 %collective-permute-start.4 = (f32[3,200,128]{2,1,0:T(8,128)}, f32[3,200,128]{2,1,0:T(8,128)}, u32[]{:S(2)}, u32[]{:S(2)}) collective-permute-start(f32[3,200,128]{2,1,0:T(8,128)} %get-tuple-element.125), channel_id=1, source_target_pairs={{0,16},{8,24},{16,32},{24,40},{32,48},{40,56},{48,64},{56,72},{64,... | collective-permute-start | bytes 921608 | tf_op jit(solution)/shard_map/ppermute | solution.py:23
  50.9 17.4 %copy-start.8 = (bf16[12,128,128]{2,1,0:T(8,128)(2,1)S(1)}, bf16[12,128,128]{2,1,0:T(8,128)(2,1)}, u32[]{:S(2)}) copy-start(bf16[12,128,128]{2,1,0:T(8,128)(2,1)} %gather_fusion.8) | copy-start | bytes 1179652
  51.5 16.8 %collective-permute-start.5 = (f32[3,200,128]{2,1,0:T(8,128)}, f32[3,200,128]{2,1,0:T(8,128)S(1)}, u32[]{:S(2)}, u32[]{:S(2)}) collective-permute-start(f32[3,200,128]{2,1,0:T(8,128)} %get-tuple-element.124), channel_id=1, source_target_pairs={{0,24},{8,32},{16,40},{24,48},{32,56},{40,64},{48,72},{56,80},{64,... | collective-permute-start | bytes 921608 | tf_op jit(solution)/shard_map/ppermute | solution.py:23
  75.7 3.8 %slice-start.1 = ((f32[8,16,128]{2,0,1:T(8,128)}), f32[8,15,128]{2,0,1:T(8,128)S(1)}, s32[]{:S(2)}) async-start(f32[8,16,128]{2,0,1:T(8,128)} %copy-done.10), calls=%async_computation.5 | async-start | bytes 122880 | tf_op jit(solution)/shard_map/slice | solution.py:159
  75.7 3.8 %slice-start.2 = ((f32[8,16,128]{2,0,1:T(8,128)}), f32[8,15,128]{2,0,1:T(8,128)S(1)}, s32[]{:S(2)}) async-start(f32[8,16,128]{2,0,1:T(8,128)} %copy-done.11), calls=%async_computation.6 | async-start | bytes 122880 | tf_op jit(solution)/shard_map/slice | solution.py:160
  75.7 3.8 %copy-start.13 = (bf16[8,2048]{1,0:T(8,128)(2,1)S(1)}, bf16[8,2048]{1,0:T(8,128)(2,1)}, u32[]{:S(2)}) copy-start(bf16[8,2048]{1,0:T(8,128)(2,1)} %param.32) | copy-start | bytes 98308
  80.9 23.1 %all-to-all-start = ((f32[8,2,8,2048]{3,2,1,0:T(8,128)}), f32[8,2,8,2048]{3,2,1,0:T(8,128)}, u32[]{:S(2)}, u32[]{:S(2)}) async-start(f32[8,2,8,2048]{3,2,1,0:T(8,128)} %copy.153), calls=%async_computation | async-start | bytes 2097152 | tf_op jit(solution)/shard_map/all_to_all | solution.py:172
  113.2 21.1 %all-to-all-start.2 = ((f32[64,1,192]{2,1,0:T(1,128)}), f32[64,1,192]{2,1,0:T(1,128)S(1)}, u32[]{:S(2)}, u32[]{:S(2)}) async-start(f32[64,1,192]{2,1,0:T(1,128)} %all_to_all.18), calls=%async_computation.2 | async-start | bytes 131072 | tf_op jit(solution)/shard_map/all_to_all | solution.py:211
  135.1 19.3 %all-to-all-start.3 = ((f32[64,1,192]{2,1,0:T(1,128)}), f32[64,1,192]{2,1,0:T(1,128)S(1)}, u32[]{:S(2)}, u32[]{:S(2)}) async-start(f32[64,1,192]{2,1,0:T(1,128)} %broadcast_in_dim.117), calls=%async_computation.3 | async-start | bytes 131072 | tf_op jit(solution)/shard_map/all_to_all | solution.py:214
  142.2 44.9 %copy-start.9 = (bf16[12,128,128]{2,1,0:T(8,128)(2,1)S(1)}, bf16[12,128,128]{2,1,0:T(8,128)(2,1)}, u32[]{:S(2)}) copy-start(bf16[12,128,128]{2,1,0:T(8,128)(2,1)} %gather_fusion.8) | copy-start | bytes 1179652
  154.4 31.8 %all-to-all-start.1 = ((bf16[64,3,8,128]{3,2,1,0:T(8,128)(2,1)}), bf16[64,3,8,128]{3,2,1,0:T(8,128)(2,1)S(1)}, u32[]{:S(2)}, u32[]{:S(2)}) async-start(bf16[64,3,8,128]{3,2,1,0:T(8,128)(2,1)} %fusion.40), calls=%async_computation.1 | async-start | bytes 786432 | tf_op jit(solution)/shard_map/all_to_all | solution.py:195
  (9 other events, 18.9 us)

commit v7 on v5

--- a/solution.py
+++ b/solution.py
@@ -184,9 +184,12 @@
         "in,hn->ih", feat_sum, slope_back.astype(jnp.float32), precision=HI
     )
 
+    flat = jnp.concatenate([first_part.reshape(-1), second_part.reshape(-1)])
+    pieces = lax.all_to_all(flat.reshape(row_devices, -1), "row", 0, 0, tiled=True)
     class_blocks = class_in.reshape(c_rows, NB, BLK)
     class_pick = jnp.take(class_blocks.transpose(1, 0, 2), pick, axis=0)
     class_pick = class_pick.reshape(len(shifts()), 3, c_rows, BLK)
+    class_pick, pieces = lax.optimization_barrier((class_pick, pieces))
     class_arrived = [send_by(class_pick[i], "row", e) for i, e in enumerate(shifts())]
     class_pairs = jnp.concatenate([a[:2] for a in class_arrived], 0)
     scores = forward_sum(
@@ -199,8 +202,6 @@
         targets_read,
     ).reshape(c_rows, nodes).astype(jnp.bfloat16)
 
-    flat = jnp.concatenate([first_part.reshape(-1), second_part.reshape(-1)])
-    pieces = lax.all_to_all(flat.reshape(row_devices, -1), "row", 0, 0, tiled=True)
     summed = jnp.sum(pieces, axis=0, keepdims=True)
     spread = jnp.broadcast_to(summed, (row_devices, summed.shape[1]))
     flat = lax.all_to_all(spread, "row", 0, 0, tiled=True).reshape(-1)

time: 177 us -> 173 us (0.977)
  waiting for transfers between devices: 40.7 us -> 45.9 us
  local copies, waits for them, and re-layouts: 34.8 us -> 29.7 us
  starting transfers between devices: 67.5 us -> 64.4 us
    all_to_all x1, waiting for transfers between devices: 3.56 us -> 13.8 us  [local(): lax.all_to_all(flat.reshape(row_devices, -1), 'row', 0, 0, tiled=True)]
    all_to_all x1, waiting for transfers between devices: 12.9 us -> 4.75 us  [local(): flat = lax.all_to_all(spread, 'row', 0, 0, tiled=True).reshape(-1)]
    unnamed x58 -> x61, local copies, waits for them, and re-layouts: 10.9 us -> 7.55 us
    ppermute x12, waiting for transfers between devices: 10.1 us -> 13.2 us  [send_by(): lax.ppermute(x, axis, [(i, (i + by) % devices) for i in range(devices)])]
    all_to_all x1, starting transfers between devices: 9.31 us -> 6.65 us  [local(): flat = lax.all_to_all(spread, 'row', 0, 0, tiled=True).reshape(-1)]
    ppermute x12, starting transfers between devices: 47 us -> 44.8 us  [send_by(): lax.ppermute(x, axis, [(i, (i + by) % devices) for i in range(devices)])]
  transfers between devices with their start and end apart: 15 -> 15, of which waited for: 4 -> 5; matrix products, arithmetic and copies ran while one was open for 15% -> 9% of each run, Pallas kernels for 0% -> 0%
where the time goes in v7:
time: 173 us; the launch traced here: 171 us
  starting transfers between devices  64.4 us (37%)
  waiting for transfers between devices  45.9 us (27%)
  local copies, waits for them, and re-layouts  29.7 us (17%)
  matrix products  17.3 us (10%)
  other arithmetic  12.6 us (7%)
    ppermute x12, starting transfers between devices, send_by(): lax.ppermute(x, axis, [(i, (i + by) % devices) for i in range(devices)])  44.8 us
    all_to_all x1, waiting for transfers between devices, local(): incoming = lax.all_to_all(outgoing, 'col', 0, 0, tiled=True)  14.1 us
    all_to_all x1, waiting for transfers between devices, local(): lax.all_to_all(flat.reshape(row_devices, -1), 'row', 0, 0, tiled=True)  13.8 us
    ppermute x12, waiting for transfers between devices, send_by(): lax.ppermute(x, axis, [(i, (i + by) % devices) for i in range(devices)])  13.2 us
    unnamed x61, local copies, waits for them, and re-layouts  7.55 us
    all_to_all x1, starting transfers between devices, local(): flat = lax.all_to_all(spread, 'row', 0, 0, tiled=True).reshape(-1)  6.65 us
    all_to_all x1, starting transfers between devices, local(): lax.all_to_all(flat.reshape(row_devices, -1), 'row', 0, 0, tiled=True)  6.53 us
    all_to_all x1, starting transfers between devices, local(): incoming = lax.all_to_all(outgoing, 'col', 0, 0, tiled=True)  6.35 us
  transfers between devices with their start and end apart: 15, of which 5 were waited for; matrix products, arithmetic and copies ran while one was open for 9% of the time, Pallas kernels for 0%

profile of v7, /device:TPU:1, one launch (start us, length us, event | category | flops | bytes accessed | tf_op | source)
XLA Modules:
  0.0 171.3 jit_solution(9750978457839425914)
XLA Ops:
  15.2 1.6 gather_fusion.1
  19.9 13.6 %collective-permute-start.2 = (f32[3,200,128]{2,1,0:T(8,128)}, f32[3,200,128]{2,1,0:T(8,128)}, u32[]{:S(2)}, u32[]{:S(2)}) collective-permute-start(f32[3,200,128]{2,1,0:T(8,128)} %get-tuple-element.56), channel_id=1, source_target_pairs={{0,488},{8,496},{16,504},{24,0},{32,8},{40,16},{48,24},{56,32},{64... | collective-permute-start | bytes 921608 | tf_op jit(solution)/shard_map/ppermute | solution.py:23
  33.5 2.6 %collective-permute-start.3 = (f32[3,200,128]{2,1,0:T(8,128)}, f32[3,200,128]{2,1,0:T(8,128)}, u32[]{:S(2)}, u32[]{:S(2)}) collective-permute-start(f32[3,200,128]{2,1,0:T(8,128)} %get-tuple-element.55), channel_id=1, source_target_pairs={{0,496},{8,504},{16,0},{24,8},{32,16},{40,24},{48,32},{56,40},{64,... | collective-permute-start | bytes 921608 | tf_op jit(solution)/shard_map/ppermute | solution.py:23
  36.1 2.5 %collective-permute-start.1 = (f32[3,200,128]{2,1,0:T(8,128)}, f32[3,200,128]{2,1,0:T(8,128)}, u32[]{:S(2)}, u32[]{:S(2)}) collective-permute-start(f32[3,200,128]{2,1,0:T(8,128)} %get-tuple-element.57), channel_id=1, source_target_pairs={{0,504},{8,0},{16,8},{24,16},{32,24},{40,32},{48,40},{56,48},{64,5... | collective-permute-start | bytes 921608 | tf_op jit(solution)/shard_map/ppermute | solution.py:23
  38.6 3.1 %collective-permute-start = (f32[3,200,128]{2,1,0:T(8,128)}, f32[3,200,128]{2,1,0:T(8,128)}, u32[]{:S(2)}, u32[]{:S(2)}) collective-permute-start(f32[3,200,128]{2,1,0:T(8,128)} %get-tuple-element.58), channel_id=1, source_target_pairs={{0,8},{8,16},{16,24},{24,32},{32,40},{40,48},{48,56},{56,64},{64,7... | collective-permute-start | bytes 921608 | tf_op jit(solution)/shard_map/ppermute | solution.py:23
  41.7 2.6 %collective-permute-start.4 = (f32[3,200,128]{2,1,0:T(8,128)}, f32[3,200,128]{2,1,0:T(8,128)}, u32[]{:S(2)}, u32[]{:S(2)}) collective-permute-start(f32[3,200,128]{2,1,0:T(8,128)} %get-tuple-element.54), channel_id=1, source_target_pairs={{0,16},{8,24},{16,32},{24,40},{32,48},{40,56},{48,64},{56,72},{64,... | collective-permute-start | bytes 921608 | tf_op jit(solution)/shard_map/ppermute | solution.py:23
  50.5 1.9 %collective-permute-start.5 = (f32[3,200,128]{2,1,0:T(8,128)}, f32[3,200,128]{2,1,0:T(8,128)S(1)}, u32[]{:S(2)}, u32[]{:S(2)}) collective-permute-start(f32[3,200,128]{2,1,0:T(8,128)} %get-tuple-element.53), channel_id=1, source_target_pairs={{0,24},{8,32},{16,40},{24,48},{32,56},{40,64},{48,72},{56,80},{64,... | collective-permute-start | bytes 921608 | tf_op jit(solution)/shard_map/ppermute | solution.py:23
  57.2 10.1 %collective-permute-done.5 = f32[3,200,128]{2,1,0:T(8,128)S(1)} collective-permute-done((f32[3,200,128]{2,1,0:T(8,128)}, f32[3,200,128]{2,1,0:T(8,128)S(1)}, u32[]{:S(2)}, u32[]{:S(2)}) %collective-permute-start.5) | collective-permute-done | bytes 307232 | tf_op jit(solution)/shard_map/ppermute | solution.py:23
  67.8 2.4 %fusion.2 = f32[192,128,16]{1,2,0:T(8,128)S(1)} fusion(f32[12,192,128]{2,1,0:T(8,128)S(1)} %fusion.15, f32[12,16]{1,0:T(8,128)S(1)} %gather_fusion.5, pred[12]{0:T(512)(128)(4,1)S(1)} %copy-done.15), kind=kOutput, calls=%fused_computation.16 | convolution fusion | flops 56623296 | bytes 2753292 | tf_op jit(solution)/shard_map/kb,kfn->fbn/dot_general | solution.py:71
  79.9 6.3 %all-to-all-start = ((f32[8,2,8,2048]{3,2,1,0:T(8,128)}), f32[8,2,8,2048]{3,2,1,0:T(8,128)}, u32[]{:S(2)}, u32[]{:S(2)}) async-start(f32[8,2,8,2048]{3,2,1,0:T(8,128)} %copy.126), calls=%async_computation | async-start | bytes 2097152 | tf_op jit(solution)/shard_map/all_to_all | solution.py:172
  88.8 14.1 %all-to-all-done = f32[8,2,8,2048]{3,2,1,0:T(8,128)} async-done(((f32[8,2,8,2048]{3,2,1,0:T(8,128)}), f32[8,2,8,2048]{3,2,1,0:T(8,128)}, u32[]{:S(2)}, u32[]{:S(2)}) %all-to-all-start) | async-done | bytes 1048608 | tf_op jit(solution)/shard_map/all_to_all | solution.py:172
  106.9 1.6 fusion.1
  108.5 1.6 fusion.126
  112.6 6.5 %all-to-all-start.1 = ((f32[64,1,192]{2,1,0:T(1,128)}), f32[64,1,192]{2,1,0:T(1,128)S(1)}, u32[]{:S(2)}, u32[]{:S(2)}) async-start(f32[64,1,192]{2,1,0:T(1,128)} %all_to_all.16), calls=%async_computation.1 | async-start | bytes 131072 | tf_op jit(solution)/shard_map/all_to_all | solution.py:188
  119.9 13.8 %all-to-all-done.1 = f32[64,1,192]{2,1,0:T(1,128)S(1)} async-done(((f32[64,1,192]{2,1,0:T(1,128)}), f32[64,1,192]{2,1,0:T(1,128)S(1)}, u32[]{:S(2)}, u32[]{:S(2)}) %all-to-all-start.1) | async-done | bytes 49184 | tf_op jit(solution)/shard_map/all_to_all | solution.py:188
  133.7 2.2 %collective-permute-start.8 = (bf16[3,8,128]{2,1,0:T(8,128)(2,1)S(1)}, bf16[3,8,128]{2,1,0:T(8,128)(2,1)S(1)}, u32[]{:S(2)}, u32[]{:S(2)}) collective-permute-start(bf16[3,8,128]{2,1,0:T(8,128)(2,1)S(1)} %get-tuple-element.68), channel_id=1, source_target_pairs={{0,488},{8,496},{16,504},{24,0},{32,8},{40,16},{48,24},{56,32},{64... | collective-permute-start | bytes 18440 | tf_op jit(solution)/shard_map/ppermute | solution.py:23
  135.9 3.1 %collective-permute-start.6 = (bf16[3,8,128]{2,1,0:T(8,128)(2,1)S(1)}, bf16[3,8,128]{2,1,0:T(8,128)(2,1)S(1)}, u32[]{:S(2)}, u32[]{:S(2)}) collective-permute-start(bf16[3,8,128]{2,1,0:T(8,128)(2,1)S(1)} %get-tuple-element.70), channel_id=1, source_target_pairs={{0,8},{8,16},{16,24},{24,32},{32,40},{40,48},{48,56},{56,64},{64,7... | collective-permute-start | bytes 18440 | tf_op jit(solution)/shard_map/ppermute | solution.py:23
  139.0 4.9 %collective-permute-start.9 = (bf16[3,8,128]{2,1,0:T(8,128)(2,1)S(1)}, bf16[3,8,128]{2,1,0:T(8,128)(2,1)S(1)}, u32[]{:S(2)}, u32[]{:S(2)}) collective-permute-start(bf16[3,8,128]{2,1,0:T(8,128)(2,1)S(1)} %get-tuple-element.67), channel_id=1, source_target_pairs={{0,496},{8,504},{16,0},{24,8},{32,16},{40,24},{48,32},{56,40},{64,... | collective-permute-start | bytes 18440 | tf_op jit(solution)/shard_map/ppermute | solution.py:23
  144.0 1.9 %collective-permute-start.7 = (bf16[3,8,128]{2,1,0:T(8,128)(2,1)S(1)}, bf16[3,8,128]{2,1,0:T(8,128)(2,1)S(1)}, u32[]{:S(2)}, u32[]{:S(2)}) collective-permute-start(bf16[3,8,128]{2,1,0:T(8,128)(2,1)S(1)} %get-tuple-element.69), channel_id=1, source_target_pairs={{0,504},{8,0},{16,8},{24,16},{32,24},{40,32},{48,40},{56,48},{64,5... | collective-permute-start | bytes 18440 | tf_op jit(solution)/shard_map/ppermute | solution.py:23
  145.9 1.9 %collective-permute-start.10 = (bf16[3,8,128]{2,1,0:T(8,128)(2,1)S(1)}, bf16[3,8,128]{2,1,0:T(8,128)(2,1)S(1)}, u32[]{:S(2)}, u32[]{:S(2)}) collective-permute-start(bf16[3,8,128]{2,1,0:T(8,128)(2,1)S(1)} %get-tuple-element.66), channel_id=1, source_target_pairs={{0,16},{8,24},{16,32},{24,40},{32,48},{40,56},{48,64},{56,72},{64,... | collective-permute-start | bytes 18440 | tf_op jit(solution)/shard_map/ppermute | solution.py:23
  148.5 6.7 %all-to-all-start.2 = ((f32[64,1,192]{2,1,0:T(1,128)}), f32[64,1,192]{2,1,0:T(1,128)S(1)}, u32[]{:S(2)}, u32[]{:S(2)}) async-start(f32[64,1,192]{2,1,0:T(1,128)} %broadcast_in_dim.116), calls=%async_computation.2 | async-start | bytes 131072 | tf_op jit(solution)/shard_map/all_to_all | solution.py:207
  155.2 4.4 %collective-permute-start.11 = (bf16[3,8,128]{2,1,0:T(8,128)(2,1)S(1)}, bf16[3,8,128]{2,1,0:T(8,128)(2,1)S(1)}, u32[]{:S(2)}, u32[]{:S(2)}) collective-permute-start(bf16[3,8,128]{2,1,0:T(8,128)(2,1)S(1)} %get-tuple-element.65), channel_id=1, source_target_pairs={{0,24},{8,32},{16,40},{24,48},{32,56},{40,64},{48,72},{56,80},{64,... | collective-permute-start | bytes 18440 | tf_op jit(solution)/shard_map/ppermute | solution.py:23
  159.7 3.1 %collective-permute-done.11 = bf16[3,8,128]{2,1,0:T(8,128)(2,1)S(1)} collective-permute-done((bf16[3,8,128]{2,1,0:T(8,128)(2,1)S(1)}, bf16[3,8,128]{2,1,0:T(8,128)(2,1)S(1)}, u32[]{:S(2)}, u32[]{:S(2)}) %collective-permute-start.11) | collective-permute-done | bytes 6176 | tf_op jit(solution)/shard_map/ppermute | solution.py:23
  165.0 4.7 %all-to-all-done.2 = f32[64,1,192]{2,1,0:T(1,128)S(1)} async-done(((f32[64,1,192]{2,1,0:T(1,128)}), f32[64,1,192]{2,1,0:T(1,128)S(1)}, u32[]{:S(2)}, u32[]{:S(2)}) %all-to-all-start.2) | async-done | bytes 49184 | tf_op jit(solution)/shard_map/all_to_all | solution.py:207
  (182 shorter events, 52.4 us)
Async XLA Ops:
  0.6 13.4 %copy-start = (bf16[12,128,128]{2,1,0:T(8,128)(2,1)S(1)}, bf16[12,128,128]{2,1,0:T(8,128)(2,1)}, u32[]{:S(2)}) copy-start(bf16[12,128,128]{2,1,0:T(8,128)(2,1)} %param.22) | copy-start | bytes 1179652
  2.1 42.3 %copy-start.11 = (f32[8,16,128]{2,0,1:T(8,128)}, f32[8,16,128]{2,0,1:T(8,128)S(1)}, u32[]{:S(2)}) copy-start(f32[8,16,128]{2,0,1:T(8,128)S(1)} %convolution_bitcast_fusion.3) | copy-start | bytes 196612
  3.4 41.0 %copy-start.10 = (f32[8,16,128]{2,0,1:T(8,128)}, f32[8,16,128]{2,0,1:T(8,128)S(1)}, u32[]{:S(2)}) copy-start(f32[8,16,128]{2,0,1:T(8,128)S(1)} %convolution_bitcast_fusion.2) | copy-start | bytes 196612
  10.0 34.4 %copy-start.21 = (s32[12]{0:T(128)}, s32[12]{0:T(128)S(1)}, u32[]{:S(2)}) copy-start(s32[12]{0:T(128)S(1)} %select_reduce_fusion) | copy-start | bytes 148
  19.9 26.6 %copy-start.18 = (s32[6,2]{0,1:T(2,128)S(1)}, s32[6,2]{0,1:T(2,128)}, u32[]{:S(2)}) copy-start(s32[6,2]{0,1:T(2,128)} %get-tuple-element.73) | copy-start | bytes 148
  19.9 30.6 %collective-permute-start.2 = (f32[3,200,128]{2,1,0:T(8,128)}, f32[3,200,128]{2,1,0:T(8,128)}, u32[]{:S(2)}, u32[]{:S(2)}) collective-permute-start(f32[3,200,128]{2,1,0:T(8,128)} %get-tuple-element.56), channel_id=1, source_target_pairs={{0,488},{8,496},{16,504},{24,0},{32,8},{40,16},{48,24},{56,32},{64... | collective-permute-start | bytes 921608 | tf_op jit(solution)/shard_map/ppermute | solution.py:23
  33.5 19.9 %collective-permute-start.3 = (f32[3,200,128]{2,1,0:T(8,128)}, f32[3,200,128]{2,1,0:T(8,128)}, u32[]{:S(2)}, u32[]{:S(2)}) collective-permute-start(f32[3,200,128]{2,1,0:T(8,128)} %get-tuple-element.55), channel_id=1, source_target_pairs={{0,496},{8,504},{16,0},{24,8},{32,16},{40,24},{48,32},{56,40},{64,... | collective-permute-start | bytes 921608 | tf_op jit(solution)/shard_map/ppermute | solution.py:23
  36.1 18.2 %collective-permute-start.1 = (f32[3,200,128]{2,1,0:T(8,128)}, f32[3,200,128]{2,1,0:T(8,128)}, u32[]{:S(2)}, u32[]{:S(2)}) collective-permute-start(f32[3,200,128]{2,1,0:T(8,128)} %get-tuple-element.57), channel_id=1, source_target_pairs={{0,504},{8,0},{16,8},{24,16},{32,24},{40,32},{48,40},{56,48},{64,5... | collective-permute-start | bytes 921608 | tf_op jit(solution)/shard_map/ppermute | solution.py:23
  38.6 16.7 %collective-permute-start = (f32[3,200,128]{2,1,0:T(8,128)}, f32[3,200,128]{2,1,0:T(8,128)}, u32[]{:S(2)}, u32[]{:S(2)}) collective-permute-start(f32[3,200,128]{2,1,0:T(8,128)} %get-tuple-element.58), channel_id=1, source_target_pairs={{0,8},{8,16},{16,24},{24,32},{32,40},{40,48},{48,56},{56,64},{64,7... | collective-permute-start | bytes 921608 | tf_op jit(solution)/shard_map/ppermute | solution.py:23
  41.7 14.5 %collective-permute-start.4 = (f32[3,200,128]{2,1,0:T(8,128)}, f32[3,200,128]{2,1,0:T(8,128)}, u32[]{:S(2)}, u32[]{:S(2)}) collective-permute-start(f32[3,200,128]{2,1,0:T(8,128)} %get-tuple-element.54), channel_id=1, source_target_pairs={{0,16},{8,24},{16,32},{24,40},{32,48},{40,56},{48,64},{56,72},{64,... | collective-permute-start | bytes 921608 | tf_op jit(solution)/shard_map/ppermute | solution.py:23
  49.9 17.4 %copy-start.8 = (bf16[12,128,128]{2,1,0:T(8,128)(2,1)S(1)}, bf16[12,128,128]{2,1,0:T(8,128)(2,1)}, u32[]{:S(2)}) copy-start(bf16[12,128,128]{2,1,0:T(8,128)(2,1)} %gather_fusion.8) | copy-start | bytes 1179652
  49.9 17.4 %copy-start.15 = (pred[12]{0:T(512)(128)(4,1)S(1)}, pred[12]{0:T(512)(128)(4,1)}, u32[]{:S(2)}) copy-start(pred[12]{0:T(512)(128)(4,1)} %compare_and_fusion) | copy-start | bytes 40
  50.5 16.8 %collective-permute-start.5 = (f32[3,200,128]{2,1,0:T(8,128)}, f32[3,200,128]{2,1,0:T(8,128)S(1)}, u32[]{:S(2)}, u32[]{:S(2)}) collective-permute-start(f32[3,200,128]{2,1,0:T(8,128)} %get-tuple-element.53), channel_id=1, source_target_pairs={{0,24},{8,32},{16,40},{24,48},{32,56},{40,64},{48,72},{56,80},{64,... | collective-permute-start | bytes 921608 | tf_op jit(solution)/shard_map/ppermute | solution.py:23
  79.9 23.0 %all-to-all-start = ((f32[8,2,8,2048]{3,2,1,0:T(8,128)}), f32[8,2,8,2048]{3,2,1,0:T(8,128)}, u32[]{:S(2)}, u32[]{:S(2)}) async-start(f32[8,2,8,2048]{3,2,1,0:T(8,128)} %copy.126), calls=%async_computation | async-start | bytes 2097152 | tf_op jit(solution)/shard_map/all_to_all | solution.py:172
  108.5 54.4 %copy-start.9 = (bf16[12,128,128]{2,1,0:T(8,128)(2,1)S(1)}, bf16[12,128,128]{2,1,0:T(8,128)(2,1)}, u32[]{:S(2)}) copy-start(bf16[12,128,128]{2,1,0:T(8,128)(2,1)} %gather_fusion.8) | copy-start | bytes 1179652
  108.5 54.3 %copy-start.16 = (pred[12]{0:T(512)(128)(4,1)S(1)}, pred[12]{0:T(512)(128)(4,1)}, u32[]{:S(2)}) copy-start(pred[12]{0:T(512)(128)(4,1)} %compare_and_fusion) | copy-start | bytes 40
  112.6 21.1 %all-to-all-start.1 = ((f32[64,1,192]{2,1,0:T(1,128)}), f32[64,1,192]{2,1,0:T(1,128)S(1)}, u32[]{:S(2)}, u32[]{:S(2)}) async-start(f32[64,1,192]{2,1,0:T(1,128)} %all_to_all.16), calls=%async_computation.1 | async-start | bytes 131072 | tf_op jit(solution)/shard_map/all_to_all | solution.py:188
  133.7 21.5 %collective-permute-start.8 = (bf16[3,8,128]{2,1,0:T(8,128)(2,1)S(1)}, bf16[3,8,128]{2,1,0:T(8,128)(2,1)S(1)}, u32[]{:S(2)}, u32[]{:S(2)}) collective-permute-start(bf16[3,8,128]{2,1,0:T(8,128)(2,1)S(1)} %get-tuple-element.68), channel_id=1, source_target_pairs={{0,488},{8,496},{16,504},{24,0},{32,8},{40,16},{48,24},{56,32},{64... | collective-permute-start | bytes 18440 | tf_op jit(solution)/shard_map/ppermute | solution.py:23
  135.9 23.7 %collective-permute-start.6 = (bf16[3,8,128]{2,1,0:T(8,128)(2,1)S(1)}, bf16[3,8,128]{2,1,0:T(8,128)(2,1)S(1)}, u32[]{:S(2)}, u32[]{:S(2)}) collective-permute-start(bf16[3,8,128]{2,1,0:T(8,128)(2,1)S(1)} %get-tuple-element.70), channel_id=1, source_target_pairs={{0,8},{8,16},{16,24},{24,32},{32,40},{40,48},{48,56},{56,64},{64,7... | collective-permute-start | bytes 18440 | tf_op jit(solution)/shard_map/ppermute | solution.py:23
  139.0 20.6 %collective-permute-start.9 = (bf16[3,8,128]{2,1,0:T(8,128)(2,1)S(1)}, bf16[3,8,128]{2,1,0:T(8,128)(2,1)S(1)}, u32[]{:S(2)}, u32[]{:S(2)}) collective-permute-start(bf16[3,8,128]{2,1,0:T(8,128)(2,1)S(1)} %get-tuple-element.67), channel_id=1, source_target_pairs={{0,496},{8,504},{16,0},{24,8},{32,16},{40,24},{48,32},{56,40},{64,... | collective-permute-start | bytes 18440 | tf_op jit(solution)/shard_map/ppermute | solution.py:23
  144.0 15.7 %collective-permute-start.7 = (bf16[3,8,128]{2,1,0:T(8,128)(2,1)S(1)}, bf16[3,8,128]{2,1,0:T(8,128)(2,1)S(1)}, u32[]{:S(2)}, u32[]{:S(2)}) collective-permute-start(bf16[3,8,128]{2,1,0:T(8,128)(2,1)S(1)} %get-tuple-element.69), channel_id=1, source_target_pairs={{0,504},{8,0},{16,8},{24,16},{32,24},{40,32},{48,40},{56,48},{64,5... | collective-permute-start | bytes 18440 | tf_op jit(solution)/shard_map/ppermute | solution.py:23
  145.9 13.8 %collective-permute-start.10 = (bf16[3,8,128]{2,1,0:T(8,128)(2,1)S(1)}, bf16[3,8,128]{2,1,0:T(8,128)(2,1)S(1)}, u32[]{:S(2)}, u32[]{:S(2)}) collective-permute-start(bf16[3,8,128]{2,1,0:T(8,128)(2,1)S(1)} %get-tuple-element.66), channel_id=1, source_target_pairs={{0,16},{8,24},{16,32},{24,40},{32,48},{40,56},{48,64},{56,72},{64,... | collective-permute-start | bytes 18440 | tf_op jit(solution)/shard_map/ppermute | solution.py:23
  148.5 21.2 %all-to-all-start.2 = ((f32[64,1,192]{2,1,0:T(1,128)}), f32[64,1,192]{2,1,0:T(1,128)S(1)}, u32[]{:S(2)}, u32[]{:S(2)}) async-start(f32[64,1,192]{2,1,0:T(1,128)} %broadcast_in_dim.116), calls=%async_computation.2 | async-start | bytes 131072 | tf_op jit(solution)/shard_map/all_to_all | solution.py:207
  155.2 7.7 %collective-permute-start.11 = (bf16[3,8,128]{2,1,0:T(8,128)(2,1)S(1)}, bf16[3,8,128]{2,1,0:T(8,128)(2,1)S(1)}, u32[]{:S(2)}, u32[]{:S(2)}) collective-permute-start(bf16[3,8,128]{2,1,0:T(8,128)(2,1)S(1)} %get-tuple-element.65), channel_id=1, source_target_pairs={{0,24},{8,32},{16,40},{24,48},{32,56},{40,64},{48,72},{56,80},{64,... | collective-permute-start | bytes 18440 | tf_op jit(solution)/shard_map/ppermute | solution.py:23
  (18 other events, 89.1 us)

commit v8 on v7

--- a/solution.py
+++ b/solution.py
@@ -134,16 +134,24 @@
     sg_send = jnp.concatenate([sg_out.reshape(len(shifts()), 2, c_rows, BLK), sg_edges], 1)
 
     picked = jnp.take(both_blocks.transpose(1, 0, 2), pick, axis=0)
-    picked = picked.reshape(len(shifts()), 3, hf_rows, BLK).astype(jnp.float32)
-    send_all = jnp.concatenate([picked, sg_send], 2)
+    picked = picked.reshape(len(shifts()), 3, hf_rows, BLK)
+    sg_high = sg_send.astype(jnp.bfloat16)
+    sg_low = (sg_send - sg_high.astype(jnp.float32)).astype(jnp.bfloat16)
+    send_all = jnp.concatenate([picked, sg_high, sg_low], 2)
     arrived = [send_by(send_all[i], "row", e) for i, e in enumerate(shifts())]
-    pairs_in = jnp.concatenate([a[:2] for a in arrived], 0)
+    arrived = [
+        (a[:, :hf_rows], a[:, hf_rows:hf_rows + c_rows].astype(jnp.float32)
+         + a[:, hf_rows + c_rows:].astype(jnp.float32))
+        for a in arrived
+    ]
+    pairs_in = jnp.concatenate([a[0][:2] for a in arrived], 0)
+    sg_pairs = jnp.concatenate([a[1][:2] for a in arrived], 0)
 
     both_sum = forward_sum(
         both_blocks,
-        arrived[up][2, :hf_rows].astype(jnp.bfloat16),
-        arrived[down][2, :hf_rows].astype(jnp.bfloat16),
-        pairs_in[:, :hf_rows].astype(jnp.bfloat16),
+        arrived[up][0][2],
+        arrived[down][0][2],
+        pairs_in,
         band_blocks,
         long_read,
         targets_read,
@@ -156,9 +164,9 @@
     ).astype(jnp.float32)
     sg_sum = (
         sg_middle
-        + jnp.concatenate([sg_prior[:, 1:], arrived[down][2, hf_rows:][:, None]], 1)
-        + jnp.concatenate([arrived[up][2, hf_rows:][:, None], sg_later[:, :-1]], 1)
-        + jnp.einsum("kb,kfm->fbm", landing, pairs_in[:, hf_rows:], precision=HI)
+        + jnp.concatenate([sg_prior[:, 1:], arrived[down][1][2][:, None]], 1)
+        + jnp.concatenate([arrived[up][1][2][:, None], sg_later[:, :-1]], 1)
+        + jnp.einsum("kb,kfm->fbm", landing, sg_pairs, precision=HI)
     )
     class_back = sg_sum.reshape(c_rows, nodes).astype(jnp.bfloat16)
 

time: 173 us -> 176 us (1.017)
  waiting for transfers between devices: 45.9 us -> 35.1 us
  local copies, waits for them, and re-layouts: 29.7 us -> 35.1 us
  starting transfers between devices: 64.4 us -> 68.4 us
  other arithmetic: 12.6 us -> 15.6 us
  matrix products: 17.3 us -> 19.2 us
    ppermute x12, waiting for transfers between devices: 13.2 us -> 3.16 us  [send_by(): lax.ppermute(x, axis, [(i, (i + by) % devices) for i in range(devices)])]
    ppermute x12, starting transfers between devices: 44.8 us -> 47.7 us  [send_by(): lax.ppermute(x, axis, [(i, (i + by) % devices) for i in range(devices)])]
    slice x1 -> x4, local copies, waits for them, and re-layouts: 0.01 us -> 2.84 us  [local(): a[:, hf_rows:hf_rows + c_rows].astype(jnp.float32)]
    convert_element_type x2, local copies, waits for them, and re-layouts: 0.29 us -> 2.65 us  [local(): hidden_act = jax.nn.silu(hidden_sum).astype(jnp.bfloat16)]
    convert_element_type x2 -> x0, local copies, waits for them, and re-layouts: 1.8 us -> none  [the longest x1 0.9 us: local(): arrived[down][2, :hf_rows].astype(jnp.bfloat16)]
  transfers between devices with their start and end apart: 15 -> 15, of which waited for: 5 -> 4; matrix products, arithmetic and copies ran while one was open for 9% -> 13% of each run, Pallas kernels for 0% -> 0%
where the time goes in v8:
time: 176 us; the launch traced here: 175 us
  starting transfers between devices  68.4 us (39%)
  local copies, waits for them, and re-layouts  35.1 us (20%)
  waiting for transfers between devices  35.1 us (20%)
  matrix products  19.2 us (11%)
  other arithmetic  15.6 us (9%)
    ppermute x12, starting transfers between devices, send_by(): lax.ppermute(x, axis, [(i, (i + by) % devices) for i in range(devices)])  47.7 us
    all_to_all x1, waiting for transfers between devices, local(): lax.all_to_all(flat.reshape(row_devices, -1), 'row', 0, 0, tiled=True)  13.8 us
    all_to_all x1, waiting for transfers between devices, local(): incoming = lax.all_to_all(outgoing, 'col', 0, 0, tiled=True)  13.4 us
    all_to_all x1, starting transfers between devices, local(): lax.all_to_all(flat.reshape(row_devices, -1), 'row', 0, 0, tiled=True)  7.7 us
    unnamed x61, local copies, waits for them, and re-layouts  6.98 us
    all_to_all x1, starting transfers between devices, local(): flat = lax.all_to_all(spread, 'row', 0, 0, tiled=True).reshape(-1)  6.64 us
    all_to_all x1, starting transfers between devices, local(): incoming = lax.all_to_all(outgoing, 'col', 0, 0, tiled=True)  6.35 us
    all_to_all x1, waiting for transfers between devices, local(): flat = lax.all_to_all(spread, 'row', 0, 0, tiled=True).reshape(-1)  4.76 us
  transfers between devices with their start and end apart: 15, of which 4 were waited for; matrix products, arithmetic and copies ran while one was open for 13% of the time, Pallas kernels for 0%

profile of v8, /device:TPU:1, one launch (start us, length us, event | category | flops | bytes accessed | tf_op | source)
XLA Modules:
  0.0 174.7 jit_solution(12768378128785015351)
XLA Ops:
  14.9 1.6 gather_fusion.1
  18.9 8.8 %collective-permute-start.1 = (bf16[3,208,128]{2,1,0:T(8,128)(2,1)}, bf16[3,208,128]{2,1,0:T(8,128)(2,1)}, u32[]{:S(2)}, u32[]{:S(2)}) collective-permute-start(bf16[3,208,128]{2,1,0:T(8,128)(2,1)} %get-tuple-element.59), channel_id=1, source_target_pairs={{0,504},{8,0},{16,8},{24,16},{32,24},{40,32},{48,40},{56,48},{64,5... | collective-permute-start | bytes 479240 | tf_op jit(solution)/shard_map/ppermute | solution.py:23
  27.7 1.9 %collective-permute-start = (bf16[3,208,128]{2,1,0:T(8,128)(2,1)}, bf16[3,208,128]{2,1,0:T(8,128)(2,1)}, u32[]{:S(2)}, u32[]{:S(2)}) collective-permute-start(bf16[3,208,128]{2,1,0:T(8,128)(2,1)} %get-tuple-element.60), channel_id=1, source_target_pairs={{0,8},{8,16},{16,24},{24,32},{32,40},{40,48},{48,56},{56,64},{64,7... | collective-permute-start | bytes 479240 | tf_op jit(solution)/shard_map/ppermute | solution.py:23
  29.6 7.1 %collective-permute-start.2 = (bf16[3,208,128]{2,1,0:T(8,128)(2,1)}, bf16[3,208,128]{2,1,0:T(8,128)(2,1)}, u32[]{:S(2)}, u32[]{:S(2)}) collective-permute-start(bf16[3,208,128]{2,1,0:T(8,128)(2,1)} %get-tuple-element.58), channel_id=1, source_target_pairs={{0,488},{8,496},{16,504},{24,0},{32,8},{40,16},{48,24},{56,32},{64... | collective-permute-start | bytes 479240 | tf_op jit(solution)/shard_map/ppermute | solution.py:23
  36.7 4.7 %collective-permute-start.3 = (bf16[3,208,128]{2,1,0:T(8,128)(2,1)}, bf16[3,208,128]{2,1,0:T(8,128)(2,1)}, u32[]{:S(2)}, u32[]{:S(2)}) collective-permute-start(bf16[3,208,128]{2,1,0:T(8,128)(2,1)} %get-tuple-element.57), channel_id=1, source_target_pairs={{0,496},{8,504},{16,0},{24,8},{32,16},{40,24},{48,32},{56,40},{64,... | collective-permute-start | bytes 479240 | tf_op jit(solution)/shard_map/ppermute | solution.py:23
  41.4 1.9 %collective-permute-start.4 = (bf16[3,208,128]{2,1,0:T(8,128)(2,1)}, bf16[3,208,128]{2,1,0:T(8,128)(2,1)}, u32[]{:S(2)}, u32[]{:S(2)}) collective-permute-start(bf16[3,208,128]{2,1,0:T(8,128)(2,1)} %get-tuple-element.56), channel_id=1, source_target_pairs={{0,16},{8,24},{16,32},{24,40},{32,48},{40,56},{48,64},{56,72},{64,... | collective-permute-start | bytes 479240 | tf_op jit(solution)/shard_map/ppermute | solution.py:23
  51.7 4.8 %collective-permute-start.5 = (bf16[3,208,128]{2,1,0:T(8,128)(2,1)}, bf16[3,208,128]{2,1,0:T(8,128)(2,1)S(1)}, u32[]{:S(2)}, u32[]{:S(2)}) collective-permute-start(bf16[3,208,128]{2,1,0:T(8,128)(2,1)} %get-tuple-element.55), channel_id=1, source_target_pairs={{0,24},{8,32},{16,40},{24,48},{32,56},{40,64},{48,72},{56,80},{64,... | collective-permute-start | bytes 479240 | tf_op jit(solution)/shard_map/ppermute | solution.py:23
  65.8 2.4 %fusion.2 = f32[192,128,16]{1,2,0:T(8,128)S(1)} fusion(f32[12,192,128]{2,1,0:T(8,128)S(1)} %fusion.53, f32[12,16]{1,0:T(8,128)S(1)} %gather_fusion.5, pred[12]{0:T(512)(128)(4,1)S(1)} %compare_and_fusion), kind=kOutput, calls=%fused_computation.15 | convolution fusion | flops 56623296 | bytes 2753292 | tf_op jit(solution)/shard_map/kb,kfn->fbn/dot_general | solution.py:71
  73.8 1.8 %reshape.540 = bf16[64,2048,1]{1,0,2:T(8,128)(2,1)} reshape(bf16[64,16,128]{2,1,0:T(8,128)(2,1)} %copy.122) | data formatting | bytes 524288 | tf_op jit(solution)/shard_map/convert_element_type | solution.py:173
  82.8 6.4 %all-to-all-start = ((f32[8,2,8,2048]{3,2,1,0:T(8,128)}), f32[8,2,8,2048]{3,2,1,0:T(8,128)}, u32[]{:S(2)}, u32[]{:S(2)}) async-start(f32[8,2,8,2048]{3,2,1,0:T(8,128)} %copy.126), calls=%async_computation | async-start | bytes 2097152 | tf_op jit(solution)/shard_map/all_to_all | solution.py:180
  90.2 1.6 copy.127
  91.8 13.4 %all-to-all-done = f32[8,2,8,2048]{3,2,1,0:T(8,128)} async-done(((f32[8,2,8,2048]{3,2,1,0:T(8,128)}), f32[8,2,8,2048]{3,2,1,0:T(8,128)}, u32[]{:S(2)}, u32[]{:S(2)}) %all-to-all-start) | async-done | bytes 1048608 | tf_op jit(solution)/shard_map/all_to_all | solution.py:180
  110.8 1.6 fusion.128
  114.8 7.7 %all-to-all-start.1 = ((f32[64,1,192]{2,1,0:T(1,128)}), f32[64,1,192]{2,1,0:T(1,128)S(1)}, u32[]{:S(2)}, u32[]{:S(2)}) async-start(f32[64,1,192]{2,1,0:T(1,128)} %all_to_all.16), calls=%async_computation.1 | async-start | bytes 131072 | tf_op jit(solution)/shard_map/all_to_all | solution.py:196
  123.3 13.8 %all-to-all-done.1 = f32[64,1,192]{2,1,0:T(1,128)S(1)} async-done(((f32[64,1,192]{2,1,0:T(1,128)}), f32[64,1,192]{2,1,0:T(1,128)S(1)}, u32[]{:S(2)}, u32[]{:S(2)}) %all-to-all-start.1) | async-done | bytes 49184 | tf_op jit(solution)/shard_map/all_to_all | solution.py:196
  137.1 2.2 %collective-permute-start.8 = (bf16[3,8,128]{2,1,0:T(8,128)(2,1)S(1)}, bf16[3,8,128]{2,1,0:T(8,128)(2,1)S(1)}, u32[]{:S(2)}, u32[]{:S(2)}) collective-permute-start(bf16[3,8,128]{2,1,0:T(8,128)(2,1)S(1)} %get-tuple-element.76), channel_id=1, source_target_pairs={{0,488},{8,496},{16,504},{24,0},{32,8},{40,16},{48,24},{56,32},{64... | collective-permute-start | bytes 18440 | tf_op jit(solution)/shard_map/ppermute | solution.py:23
  139.3 3.1 %collective-permute-start.6 = (bf16[3,8,128]{2,1,0:T(8,128)(2,1)S(1)}, bf16[3,8,128]{2,1,0:T(8,128)(2,1)S(1)}, u32[]{:S(2)}, u32[]{:S(2)}) collective-permute-start(bf16[3,8,128]{2,1,0:T(8,128)(2,1)S(1)} %get-tuple-element.78), channel_id=1, source_target_pairs={{0,8},{8,16},{16,24},{24,32},{32,40},{40,48},{48,56},{56,64},{64,7... | collective-permute-start | bytes 18440 | tf_op jit(solution)/shard_map/ppermute | solution.py:23
  142.4 4.9 %collective-permute-start.9 = (bf16[3,8,128]{2,1,0:T(8,128)(2,1)S(1)}, bf16[3,8,128]{2,1,0:T(8,128)(2,1)S(1)}, u32[]{:S(2)}, u32[]{:S(2)}) collective-permute-start(bf16[3,8,128]{2,1,0:T(8,128)(2,1)S(1)} %get-tuple-element.75), channel_id=1, source_target_pairs={{0,496},{8,504},{16,0},{24,8},{32,16},{40,24},{48,32},{56,40},{64,... | collective-permute-start | bytes 18440 | tf_op jit(solution)/shard_map/ppermute | solution.py:23
  147.3 1.9 %collective-permute-start.7 = (bf16[3,8,128]{2,1,0:T(8,128)(2,1)S(1)}, bf16[3,8,128]{2,1,0:T(8,128)(2,1)S(1)}, u32[]{:S(2)}, u32[]{:S(2)}) collective-permute-start(bf16[3,8,128]{2,1,0:T(8,128)(2,1)S(1)} %get-tuple-element.77), channel_id=1, source_target_pairs={{0,504},{8,0},{16,8},{24,16},{32,24},{40,32},{48,40},{56,48},{64,5... | collective-permute-start | bytes 18440 | tf_op jit(solution)/shard_map/ppermute | solution.py:23
  149.3 1.9 %collective-permute-start.10 = (bf16[3,8,128]{2,1,0:T(8,128)(2,1)S(1)}, bf16[3,8,128]{2,1,0:T(8,128)(2,1)S(1)}, u32[]{:S(2)}, u32[]{:S(2)}) collective-permute-start(bf16[3,8,128]{2,1,0:T(8,128)(2,1)S(1)} %get-tuple-element.74), channel_id=1, source_target_pairs={{0,16},{8,24},{16,32},{24,40},{32,48},{40,56},{48,64},{56,72},{64,... | collective-permute-start | bytes 18440 | tf_op jit(solution)/shard_map/ppermute | solution.py:23
  151.9 6.6 %all-to-all-start.2 = ((f32[64,1,192]{2,1,0:T(1,128)}), f32[64,1,192]{2,1,0:T(1,128)S(1)}, u32[]{:S(2)}, u32[]{:S(2)}) async-start(f32[64,1,192]{2,1,0:T(1,128)} %broadcast_in_dim.114), calls=%async_computation.2 | async-start | bytes 131072 | tf_op jit(solution)/shard_map/all_to_all | solution.py:215
  158.6 4.4 %collective-permute-start.11 = (bf16[3,8,128]{2,1,0:T(8,128)(2,1)S(1)}, bf16[3,8,128]{2,1,0:T(8,128)(2,1)S(1)}, u32[]{:S(2)}, u32[]{:S(2)}) collective-permute-start(bf16[3,8,128]{2,1,0:T(8,128)(2,1)S(1)} %get-tuple-element.73), channel_id=1, source_target_pairs={{0,24},{8,32},{16,40},{24,48},{32,56},{40,64},{48,72},{56,80},{64,... | collective-permute-start | bytes 18440 | tf_op jit(solution)/shard_map/ppermute | solution.py:23
  163.1 3.1 %collective-permute-done.11 = bf16[3,8,128]{2,1,0:T(8,128)(2,1)S(1)} collective-permute-done((bf16[3,8,128]{2,1,0:T(8,128)(2,1)S(1)}, bf16[3,8,128]{2,1,0:T(8,128)(2,1)S(1)}, u32[]{:S(2)}, u32[]{:S(2)}) %collective-permute-start.11) | collective-permute-done | bytes 6176 | tf_op jit(solution)/shard_map/ppermute | solution.py:23
  168.4 4.8 %all-to-all-done.2 = f32[64,1,192]{2,1,0:T(1,128)S(1)} async-done(((f32[64,1,192]{2,1,0:T(1,128)}), f32[64,1,192]{2,1,0:T(1,128)S(1)}, u32[]{:S(2)}, u32[]{:S(2)}) %all-to-all-start.2) | async-done | bytes 49184 | tf_op jit(solution)/shard_map/all_to_all | solution.py:215
  (190 shorter events, 60.8 us)
Async XLA Ops:
  0.6 11.1 %copy-start.12 = (bf16[8,2048]{1,0:T(8,128)(2,1)S(1)}, bf16[8,2048]{1,0:T(8,128)(2,1)}, u32[]{:S(2)}) copy-start(bf16[8,2048]{1,0:T(8,128)(2,1)} %param.20) | copy-start | bytes 98308
  3.3 10.6 %copy-start.4 = (bf16[128,2048]{1,0:T(8,128)(2,1)S(1)}, bf16[128,2048]{1,0:T(8,128)(2,1)}, u32[]{:S(2)}) copy-start(bf16[128,2048]{1,0:T(8,128)(2,1)} %param.17) | copy-start | bytes 1572868
  3.3 10.7 %copy-start.13 = (bf16[128,64]{0,1:T(8,128)(2,1)S(1)}, bf16[128,64]{0,1:T(8,128)(2,1)}, u32[]{:S(2)}) copy-start(bf16[128,64]{0,1:T(8,128)(2,1)} %param.18) | copy-start | bytes 49156
  7.2 37.4 %copy-start.20 = (s32[12]{0:T(128)}, s32[12]{0:T(128)S(1)}, u32[]{:S(2)}) copy-start(s32[12]{0:T(128)S(1)} %select_reduce_fusion) | copy-start | bytes 148
  18.9 39.1 %collective-permute-start.1 = (bf16[3,208,128]{2,1,0:T(8,128)(2,1)}, bf16[3,208,128]{2,1,0:T(8,128)(2,1)}, u32[]{:S(2)}, u32[]{:S(2)}) collective-permute-start(bf16[3,208,128]{2,1,0:T(8,128)(2,1)} %get-tuple-element.59), channel_id=1, source_target_pairs={{0,504},{8,0},{16,8},{24,16},{32,24},{40,32},{48,40},{56,48},{64,5... | collective-permute-start | bytes 479240 | tf_op jit(solution)/shard_map/ppermute | solution.py:23
  27.7 31.1 %collective-permute-start = (bf16[3,208,128]{2,1,0:T(8,128)(2,1)}, bf16[3,208,128]{2,1,0:T(8,128)(2,1)}, u32[]{:S(2)}, u32[]{:S(2)}) collective-permute-start(bf16[3,208,128]{2,1,0:T(8,128)(2,1)} %get-tuple-element.60), channel_id=1, source_target_pairs={{0,8},{8,16},{16,24},{24,32},{32,40},{40,48},{48,56},{56,64},{64,7... | collective-permute-start | bytes 479240 | tf_op jit(solution)/shard_map/ppermute | solution.py:23
  29.6 22.1 %collective-permute-start.2 = (bf16[3,208,128]{2,1,0:T(8,128)(2,1)}, bf16[3,208,128]{2,1,0:T(8,128)(2,1)}, u32[]{:S(2)}, u32[]{:S(2)}) collective-permute-start(bf16[3,208,128]{2,1,0:T(8,128)(2,1)} %get-tuple-element.58), channel_id=1, source_target_pairs={{0,488},{8,496},{16,504},{24,0},{32,8},{40,16},{48,24},{56,32},{64... | collective-permute-start | bytes 479240 | tf_op jit(solution)/shard_map/ppermute | solution.py:23
  36.7 20.6 %collective-permute-start.3 = (bf16[3,208,128]{2,1,0:T(8,128)(2,1)}, bf16[3,208,128]{2,1,0:T(8,128)(2,1)}, u32[]{:S(2)}, u32[]{:S(2)}) collective-permute-start(bf16[3,208,128]{2,1,0:T(8,128)(2,1)} %get-tuple-element.57), channel_id=1, source_target_pairs={{0,496},{8,504},{16,0},{24,8},{32,16},{40,24},{48,32},{56,40},{64,... | collective-permute-start | bytes 479240 | tf_op jit(solution)/shard_map/ppermute | solution.py:23
  41.4 22.3 %collective-permute-start.4 = (bf16[3,208,128]{2,1,0:T(8,128)(2,1)}, bf16[3,208,128]{2,1,0:T(8,128)(2,1)}, u32[]{:S(2)}, u32[]{:S(2)}) collective-permute-start(bf16[3,208,128]{2,1,0:T(8,128)(2,1)} %get-tuple-element.56), channel_id=1, source_target_pairs={{0,16},{8,24},{16,32},{24,40},{32,48},{40,56},{48,64},{56,72},{64,... | collective-permute-start | bytes 479240 | tf_op jit(solution)/shard_map/ppermute | solution.py:23
  51.1 14.1 %copy-start.8 = (bf16[12,128,128]{2,1,0:T(8,128)(2,1)S(1)}, bf16[12,128,128]{2,1,0:T(8,128)(2,1)}, u32[]{:S(2)}) copy-start(bf16[12,128,128]{2,1,0:T(8,128)(2,1)} %gather_fusion.8) | copy-start | bytes 1179652
  51.7 14.0 %copy-start.14 = (pred[12]{0:T(512)(128)(4,1)}, pred[12]{0:T(512)(128)(4,1)S(1)}, u32[]{:S(2)}) copy-start(pred[12]{0:T(512)(128)(4,1)S(1)} %compare_and_fusion) | copy-start | bytes 40
  51.7 13.5 %collective-permute-start.5 = (bf16[3,208,128]{2,1,0:T(8,128)(2,1)}, bf16[3,208,128]{2,1,0:T(8,128)(2,1)S(1)}, u32[]{:S(2)}, u32[]{:S(2)}) collective-permute-start(bf16[3,208,128]{2,1,0:T(8,128)(2,1)} %get-tuple-element.55), channel_id=1, source_target_pairs={{0,24},{8,32},{16,40},{24,48},{32,56},{40,64},{48,72},{56,80},{64,... | collective-permute-start | bytes 479240 | tf_op jit(solution)/shard_map/ppermute | solution.py:23
  82.8 22.4 %all-to-all-start = ((f32[8,2,8,2048]{3,2,1,0:T(8,128)}), f32[8,2,8,2048]{3,2,1,0:T(8,128)}, u32[]{:S(2)}, u32[]{:S(2)}) async-start(f32[8,2,8,2048]{3,2,1,0:T(8,128)} %copy.126), calls=%async_computation | async-start | bytes 2097152 | tf_op jit(solution)/shard_map/all_to_all | solution.py:180
  90.2 17.0 %copy-start.7 = (bf16[64,16,128]{2,0,1:T(8,128)(2,1)S(1)}, bf16[64,16,128]{2,0,1:T(8,128)(2,1)}, u32[]{:S(2)}) copy-start(bf16[64,16,128]{2,0,1:T(8,128)(2,1)} %copy-done.6) | copy-start | bytes 786436
  110.8 55.5 %copy-start.9 = (bf16[12,128,128]{2,1,0:T(8,128)(2,1)S(1)}, bf16[12,128,128]{2,1,0:T(8,128)(2,1)}, u32[]{:S(2)}) copy-start(bf16[12,128,128]{2,1,0:T(8,128)(2,1)} %gather_fusion.8) | copy-start | bytes 1179652
  110.8 55.5 %copy-start.15 = (pred[12]{0:T(512)(128)(4,1)S(1)}, pred[12]{0:T(512)(128)(4,1)}, u32[]{:S(2)}) copy-start(pred[12]{0:T(512)(128)(4,1)} %copy-done.14) | copy-start | bytes 40
  114.8 22.3 %all-to-all-start.1 = ((f32[64,1,192]{2,1,0:T(1,128)}), f32[64,1,192]{2,1,0:T(1,128)S(1)}, u32[]{:S(2)}, u32[]{:S(2)}) async-start(f32[64,1,192]{2,1,0:T(1,128)} %all_to_all.16), calls=%async_computation.1 | async-start | bytes 131072 | tf_op jit(solution)/shard_map/all_to_all | solution.py:196
  137.1 21.5 %collective-permute-start.8 = (bf16[3,8,128]{2,1,0:T(8,128)(2,1)S(1)}, bf16[3,8,128]{2,1,0:T(8,128)(2,1)S(1)}, u32[]{:S(2)}, u32[]{:S(2)}) collective-permute-start(bf16[3,8,128]{2,1,0:T(8,128)(2,1)S(1)} %get-tuple-element.76), channel_id=1, source_target_pairs={{0,488},{8,496},{16,504},{24,0},{32,8},{40,16},{48,24},{56,32},{64... | collective-permute-start | bytes 18440 | tf_op jit(solution)/shard_map/ppermute | solution.py:23
  139.3 23.7 %collective-permute-start.6 = (bf16[3,8,128]{2,1,0:T(8,128)(2,1)S(1)}, bf16[3,8,128]{2,1,0:T(8,128)(2,1)S(1)}, u32[]{:S(2)}, u32[]{:S(2)}) collective-permute-start(bf16[3,8,128]{2,1,0:T(8,128)(2,1)S(1)} %get-tuple-element.78), channel_id=1, source_target_pairs={{0,8},{8,16},{16,24},{24,32},{32,40},{40,48},{48,56},{56,64},{64,7... | collective-permute-start | bytes 18440 | tf_op jit(solution)/shard_map/ppermute | solution.py:23
  142.4 20.6 %collective-permute-start.9 = (bf16[3,8,128]{2,1,0:T(8,128)(2,1)S(1)}, bf16[3,8,128]{2,1,0:T(8,128)(2,1)S(1)}, u32[]{:S(2)}, u32[]{:S(2)}) collective-permute-start(bf16[3,8,128]{2,1,0:T(8,128)(2,1)S(1)} %get-tuple-element.75), channel_id=1, source_target_pairs={{0,496},{8,504},{16,0},{24,8},{32,16},{40,24},{48,32},{56,40},{64,... | collective-permute-start | bytes 18440 | tf_op jit(solution)/shard_map/ppermute | solution.py:23
  147.3 15.7 %collective-permute-start.7 = (bf16[3,8,128]{2,1,0:T(8,128)(2,1)S(1)}, bf16[3,8,128]{2,1,0:T(8,128)(2,1)S(1)}, u32[]{:S(2)}, u32[]{:S(2)}) collective-permute-start(bf16[3,8,128]{2,1,0:T(8,128)(2,1)S(1)} %get-tuple-element.77), channel_id=1, source_target_pairs={{0,504},{8,0},{16,8},{24,16},{32,24},{40,32},{48,40},{56,48},{64,5... | collective-permute-start | bytes 18440 | tf_op jit(solution)/shard_map/ppermute | solution.py:23
  149.3 13.8 %collective-permute-start.10 = (bf16[3,8,128]{2,1,0:T(8,128)(2,1)S(1)}, bf16[3,8,128]{2,1,0:T(8,128)(2,1)S(1)}, u32[]{:S(2)}, u32[]{:S(2)}) collective-permute-start(bf16[3,8,128]{2,1,0:T(8,128)(2,1)S(1)} %get-tuple-element.74), channel_id=1, source_target_pairs={{0,16},{8,24},{16,32},{24,40},{32,48},{40,56},{48,64},{56,72},{64,... | collective-permute-start | bytes 18440 | tf_op jit(solution)/shard_map/ppermute | solution.py:23
  151.9 21.2 %all-to-all-start.2 = ((f32[64,1,192]{2,1,0:T(1,128)}), f32[64,1,192]{2,1,0:T(1,128)S(1)}, u32[]{:S(2)}, u32[]{:S(2)}) async-start(f32[64,1,192]{2,1,0:T(1,128)} %broadcast_in_dim.114), calls=%async_computation.2 | async-start | bytes 131072 | tf_op jit(solution)/shard_map/all_to_all | solution.py:215
  158.6 7.7 %collective-permute-start.11 = (bf16[3,8,128]{2,1,0:T(8,128)(2,1)S(1)}, bf16[3,8,128]{2,1,0:T(8,128)(2,1)S(1)}, u32[]{:S(2)}, u32[]{:S(2)}) collective-permute-start(bf16[3,8,128]{2,1,0:T(8,128)(2,1)S(1)} %get-tuple-element.73), channel_id=1, source_target_pairs={{0,24},{8,32},{16,40},{24,48},{32,56},{40,64},{48,72},{56,80},{64,... | collective-permute-start | bytes 18440 | tf_op jit(solution)/shard_map/ppermute | solution.py:23
  (14 other events, 81.8 us)

commit v9 on v7

--- a/solution.py
+++ b/solution.py
@@ -139,17 +139,24 @@
     arrived = [send_by(send_all[i], "row", e) for i, e in enumerate(shifts())]
     pairs_in = jnp.concatenate([a[:2] for a in arrived], 0)
 
-    both_sum = forward_sum(
-        both_blocks,
-        arrived[up][2, :hf_rows].astype(jnp.bfloat16),
-        arrived[down][2, :hf_rows].astype(jnp.bfloat16),
-        pairs_in[:, :hf_rows].astype(jnp.bfloat16),
+    hidden_sum = forward_sum(
+        both_blocks[:h_rows],
+        arrived[up][2, :h_rows].astype(jnp.bfloat16),
+        arrived[down][2, :h_rows].astype(jnp.bfloat16),
+        pairs_in[:, :h_rows].astype(jnp.bfloat16),
         band_blocks,
         long_read,
         targets_read,
-    )
-    hidden_sum = both_sum[:h_rows].reshape(h_rows, nodes)
-    feat_sum = both_sum[h_rows:].reshape(f_rows, nodes)
+    ).reshape(h_rows, nodes)
+    feat_sum = forward_sum(
+        both_blocks[h_rows:],
+        arrived[up][2, h_rows:hf_rows].astype(jnp.bfloat16),
+        arrived[down][2, h_rows:hf_rows].astype(jnp.bfloat16),
+        pairs_in[:, h_rows:hf_rows].astype(jnp.bfloat16),
+        band_blocks,
+        long_read,
+        targets_read,
+    ).reshape(f_rows, nodes)
 
     landing = (
         landing_blocks.reshape(-1)[:, None] == jnp.arange(NB, dtype=jnp.int32)[None, :]

time: 173 us -> 175 us (1.012)
  waiting for transfers between devices: 45.9 us -> 39.7 us
  local copies, waits for them, and re-layouts: 29.7 us -> 35.7 us
  matrix products: 17.3 us -> 23.1 us
  starting transfers between devices: 64.4 us -> 62.4 us
    all_to_all x1, waiting for transfers between devices: 14.1 us -> 8.39 us  [local(): incoming = lax.all_to_all(outgoing, 'col', 0, 0, tiled=True)]
    dot_general x0 -> x1, local copies, waits for them, and re-layouts: none -> 2.54 us  [forward_sum(): far = jnp.einsum('kb,kfn->fbn', targets_in_order, contrib, precision=HI)]
    slice x3 -> x1, local copies, waits for them, and re-layouts: 2.54 us -> 0.06 us  [local(): both_blocks[:h_rows]]
    convert_element_type x2, local copies, waits for them, and re-layouts: 0.29 us -> 2.65 us  [local(): hidden_act = jax.nn.silu(hidden_sum).astype(jnp.bfloat16)]
    unnamed x61 -> x66, local copies, waits for them, and re-layouts: 7.55 us -> 9.57 us
    dot_general x2 -> x3, matrix products: 2.73 us -> 3.87 us  [forward_sum(): far = jnp.einsum('kb,kfn->fbn', targets_in_order, contrib, precision=HI)]
  transfers between devices with their start and end apart: 15 -> 15, of which waited for: 5 -> 5; matrix products, arithmetic and copies ran while one was open for 9% -> 13% of each run, Pallas kernels for 0% -> 0%
where the time goes in v9:
time: 175 us; the launch traced here: 174 us
  starting transfers between devices  62.4 us (36%)
  waiting for transfers between devices  39.7 us (23%)
  local copies, waits for them, and re-layouts  35.7 us (20%)
  matrix products  23.1 us (13%)
  other arithmetic  11.7 us (7%)
    ppermute x12, starting transfers between devices, send_by(): lax.ppermute(x, axis, [(i, (i + by) % devices) for i in range(devices)])  43.9 us
    ppermute x12, waiting for transfers between devices, send_by(): lax.ppermute(x, axis, [(i, (i + by) % devices) for i in range(devices)])  14.1 us
    all_to_all x1, waiting for transfers between devices, local(): lax.all_to_all(flat.reshape(row_devices, -1), 'row', 0, 0, tiled=True)  12.4 us
    unnamed x66, local copies, waits for them, and re-layouts  9.57 us
    all_to_all x1, waiting for transfers between devices, local(): incoming = lax.all_to_all(outgoing, 'col', 0, 0, tiled=True)  8.39 us
    all_to_all x1, starting transfers between devices, local(): lax.all_to_all(flat.reshape(row_devices, -1), 'row', 0, 0, tiled=True)  6.68 us
    all_to_all x1, starting transfers between devices, local(): incoming = lax.all_to_all(outgoing, 'col', 0, 0, tiled=True)  6.35 us
    all_to_all x1, starting transfers between devices, local(): flat = lax.all_to_all(spread, 'row', 0, 0, tiled=True).reshape(-1)  5.47 us
  transfers between devices with their start and end apart: 15, of which 5 were waited for; matrix products, arithmetic and copies ran while one was open for 13% of the time, Pallas kernels for 0%

profile of v9, /device:TPU:1, one launch (start us, length us, event | category | flops | bytes accessed | tf_op | source)
XLA Modules:
  0.0 173.9 jit_solution(14077213214299897474)
XLA Ops:
  15.5 1.7 gather_fusion.1
  22.9 13.6 %collective-permute-start.2 = (f32[3,200,128]{2,1,0:T(8,128)}, f32[3,200,128]{2,1,0:T(8,128)}, u32[]{:S(2)}, u32[]{:S(2)}) collective-permute-start(f32[3,200,128]{2,1,0:T(8,128)} %get-tuple-element.56), channel_id=1, source_target_pairs={{0,488},{8,496},{16,504},{24,0},{32,8},{40,16},{48,24},{56,32},{64... | collective-permute-start | bytes 921608 | tf_op jit(solution)/shard_map/ppermute | solution.py:23
  36.5 2.6 %collective-permute-start.3 = (f32[3,200,128]{2,1,0:T(8,128)}, f32[3,200,128]{2,1,0:T(8,128)}, u32[]{:S(2)}, u32[]{:S(2)}) collective-permute-start(f32[3,200,128]{2,1,0:T(8,128)} %get-tuple-element.55), channel_id=1, source_target_pairs={{0,496},{8,504},{16,0},{24,8},{32,16},{40,24},{48,32},{56,40},{64,... | collective-permute-start | bytes 921608 | tf_op jit(solution)/shard_map/ppermute | solution.py:23
  39.2 2.5 %collective-permute-start.1 = (f32[3,200,128]{2,1,0:T(8,128)}, f32[3,200,128]{2,1,0:T(8,128)S(1)}, u32[]{:S(2)}, u32[]{:S(2)}) collective-permute-start(f32[3,200,128]{2,1,0:T(8,128)} %get-tuple-element.57), channel_id=1, source_target_pairs={{0,504},{8,0},{16,8},{24,16},{32,24},{40,32},{48,40},{56,48},{64,5... | collective-permute-start | bytes 921608 | tf_op jit(solution)/shard_map/ppermute | solution.py:23
  41.6 3.1 %collective-permute-start = (f32[3,200,128]{2,1,0:T(8,128)}, f32[3,200,128]{2,1,0:T(8,128)}, u32[]{:S(2)}, u32[]{:S(2)}) collective-permute-start(f32[3,200,128]{2,1,0:T(8,128)} %get-tuple-element.58), channel_id=1, source_target_pairs={{0,8},{8,16},{16,24},{24,32},{32,40},{40,48},{48,56},{56,64},{64,7... | collective-permute-start | bytes 921608 | tf_op jit(solution)/shard_map/ppermute | solution.py:23
  44.7 2.6 %collective-permute-start.4 = (f32[3,200,128]{2,1,0:T(8,128)}, f32[3,200,128]{2,1,0:T(8,128)}, u32[]{:S(2)}, u32[]{:S(2)}) collective-permute-start(f32[3,200,128]{2,1,0:T(8,128)} %get-tuple-element.54), channel_id=1, source_target_pairs={{0,16},{8,24},{16,32},{24,40},{32,48},{40,56},{48,64},{56,72},{64,... | collective-permute-start | bytes 921608 | tf_op jit(solution)/shard_map/ppermute | solution.py:23
  54.2 1.9 %collective-permute-start.5 = (f32[3,200,128]{2,1,0:T(8,128)}, f32[3,200,128]{2,1,0:T(8,128)S(1)}, u32[]{:S(2)}, u32[]{:S(2)}) collective-permute-start(f32[3,200,128]{2,1,0:T(8,128)} %get-tuple-element.53), channel_id=1, source_target_pairs={{0,24},{8,32},{16,40},{24,48},{32,56},{40,64},{48,72},{56,80},{64,... | collective-permute-start | bytes 921608 | tf_op jit(solution)/shard_map/ppermute | solution.py:23
  60.1 10.9 %collective-permute-done.5 = f32[3,200,128]{2,1,0:T(8,128)S(1)} collective-permute-done((f32[3,200,128]{2,1,0:T(8,128)}, f32[3,200,128]{2,1,0:T(8,128)S(1)}, u32[]{:S(2)}, u32[]{:S(2)}) %collective-permute-start.5) | collective-permute-done | bytes 307232 | tf_op jit(solution)/shard_map/ppermute | solution.py:23
  80.1 1.8 %reshape.586 = bf16[64,2048,1]{1,0,2:T(8,128)(2,1)} reshape(bf16[64,16,128]{2,1,0:T(8,128)(2,1)} %copy.143) | data formatting | bytes 524288 | tf_op jit(solution)/shard_map/convert_element_type | solution.py:172
  87.8 6.4 %all-to-all-start = ((f32[8,2,8,2048]{3,2,1,0:T(8,128)}), f32[8,2,8,2048]{3,2,1,0:T(8,128)}, u32[]{:S(2)}, u32[]{:S(2)}) async-start(f32[8,2,8,2048]{3,2,1,0:T(8,128)} %copy.147), calls=%async_computation | async-start | bytes 2097152 | tf_op jit(solution)/shard_map/all_to_all | solution.py:179
  94.2 2.6 %fusion.11 = f32[128,128,16]{1,2,0:T(8,128)} fusion(f32[12,128,128]{2,1,0:T(8,128)S(1)} %fusion.39, f32[12,16]{1,0:T(8,128)S(1)} %gather_fusion.5, pred[12]{0:T(512)(128)(4,1)S(1)} %compare_and_fusion), kind=kOutput, calls=%fused_computation.36 | convolution fusion | flops 37748928 | bytes 1835788 | tf_op jit(solution)/shard_map/kb,kfn->fbn/dot_general | solution.py:71
  97.6 2.5 %copy.154 = f32[128,128,16]{0,1,2:T(8,128)} copy(f32[128,128,16]{1,2,0:T(8,128)} %fusion.11) | data formatting | bytes 2097152 | tf_op jit(solution)/shard_map/kb,kfn->fbn/dot_general | solution.py:71
  102.5 8.4 %all-to-all-done = f32[8,2,8,2048]{3,2,1,0:T(8,128)} async-done(((f32[8,2,8,2048]{3,2,1,0:T(8,128)}), f32[8,2,8,2048]{3,2,1,0:T(8,128)}, u32[]{:S(2)}, u32[]{:S(2)}) %all-to-all-start) | async-done | bytes 1048608 | tf_op jit(solution)/shard_map/all_to_all | solution.py:179
  117.2 6.7 %all-to-all-start.1 = ((f32[64,1,192]{2,1,0:T(1,128)}), f32[64,1,192]{2,1,0:T(1,128)S(1)}, u32[]{:S(2)}, u32[]{:S(2)}) async-start(f32[64,1,192]{2,1,0:T(1,128)} %all_to_all.16), calls=%async_computation.1 | async-start | bytes 131072 | tf_op jit(solution)/shard_map/all_to_all | solution.py:195
  126.0 12.4 %all-to-all-done.1 = f32[64,1,192]{2,1,0:T(1,128)S(1)} async-done(((f32[64,1,192]{2,1,0:T(1,128)}), f32[64,1,192]{2,1,0:T(1,128)S(1)}, u32[]{:S(2)}, u32[]{:S(2)}) %all-to-all-start.1) | async-done | bytes 49184 | tf_op jit(solution)/shard_map/all_to_all | solution.py:195
  138.5 2.2 %collective-permute-start.8 = (bf16[3,8,128]{2,1,0:T(8,128)(2,1)S(1)}, bf16[3,8,128]{2,1,0:T(8,128)(2,1)S(1)}, u32[]{:S(2)}, u32[]{:S(2)}) collective-permute-start(bf16[3,8,128]{2,1,0:T(8,128)(2,1)S(1)} %get-tuple-element.66), channel_id=1, source_target_pairs={{0,488},{8,496},{16,504},{24,0},{32,8},{40,16},{48,24},{56,32},{64... | collective-permute-start | bytes 18440 | tf_op jit(solution)/shard_map/ppermute | solution.py:23
  140.7 2.8 %collective-permute-start.9 = (bf16[3,8,128]{2,1,0:T(8,128)(2,1)S(1)}, bf16[3,8,128]{2,1,0:T(8,128)(2,1)S(1)}, u32[]{:S(2)}, u32[]{:S(2)}) collective-permute-start(bf16[3,8,128]{2,1,0:T(8,128)(2,1)S(1)} %get-tuple-element.65), channel_id=1, source_target_pairs={{0,496},{8,504},{16,0},{24,8},{32,16},{40,24},{48,32},{56,40},{64,... | collective-permute-start | bytes 18440 | tf_op jit(solution)/shard_map/ppermute | solution.py:23
  143.5 2.2 %collective-permute-start.7 = (bf16[3,8,128]{2,1,0:T(8,128)(2,1)S(1)}, bf16[3,8,128]{2,1,0:T(8,128)(2,1)S(1)}, u32[]{:S(2)}, u32[]{:S(2)}) collective-permute-start(bf16[3,8,128]{2,1,0:T(8,128)(2,1)S(1)} %get-tuple-element.67), channel_id=1, source_target_pairs={{0,504},{8,0},{16,8},{24,16},{32,24},{40,32},{48,40},{56,48},{64,5... | collective-permute-start | bytes 18440 | tf_op jit(solution)/shard_map/ppermute | solution.py:23
  145.7 3.3 %collective-permute-start.6 = (bf16[3,8,128]{2,1,0:T(8,128)(2,1)S(1)}, bf16[3,8,128]{2,1,0:T(8,128)(2,1)S(1)}, u32[]{:S(2)}, u32[]{:S(2)}) collective-permute-start(bf16[3,8,128]{2,1,0:T(8,128)(2,1)S(1)} %get-tuple-element.68), channel_id=1, source_target_pairs={{0,8},{8,16},{16,24},{24,32},{32,40},{40,48},{48,56},{56,64},{64,7... | collective-permute-start | bytes 18440 | tf_op jit(solution)/shard_map/ppermute | solution.py:23
  149.1 2.5 %collective-permute-start.10 = (bf16[3,8,128]{2,1,0:T(8,128)(2,1)S(1)}, bf16[3,8,128]{2,1,0:T(8,128)(2,1)S(1)}, u32[]{:S(2)}, u32[]{:S(2)}) collective-permute-start(bf16[3,8,128]{2,1,0:T(8,128)(2,1)S(1)} %get-tuple-element.64), channel_id=1, source_target_pairs={{0,16},{8,24},{16,32},{24,40},{32,48},{40,56},{48,64},{56,72},{64,... | collective-permute-start | bytes 18440 | tf_op jit(solution)/shard_map/ppermute | solution.py:23
  152.3 5.5 %all-to-all-start.2 = ((f32[64,1,192]{2,1,0:T(1,128)}), f32[64,1,192]{2,1,0:T(1,128)S(1)}, u32[]{:S(2)}, u32[]{:S(2)}) async-start(f32[64,1,192]{2,1,0:T(1,128)} %broadcast_in_dim.118), calls=%async_computation.2 | async-start | bytes 131072 | tf_op jit(solution)/shard_map/all_to_all | solution.py:214
  157.8 4.4 %collective-permute-start.11 = (bf16[3,8,128]{2,1,0:T(8,128)(2,1)S(1)}, bf16[3,8,128]{2,1,0:T(8,128)(2,1)S(1)}, u32[]{:S(2)}, u32[]{:S(2)}) collective-permute-start(bf16[3,8,128]{2,1,0:T(8,128)(2,1)S(1)} %get-tuple-element.63), channel_id=1, source_target_pairs={{0,24},{8,32},{16,40},{24,48},{32,56},{40,64},{48,72},{56,80},{64,... | collective-permute-start | bytes 18440 | tf_op jit(solution)/shard_map/ppermute | solution.py:23
  162.3 3.1 %collective-permute-done.11 = bf16[3,8,128]{2,1,0:T(8,128)(2,1)S(1)} collective-permute-done((bf16[3,8,128]{2,1,0:T(8,128)(2,1)S(1)}, bf16[3,8,128]{2,1,0:T(8,128)(2,1)S(1)}, u32[]{:S(2)}, u32[]{:S(2)}) %collective-permute-start.11) | collective-permute-done | bytes 6176 | tf_op jit(solution)/shard_map/ppermute | solution.py:23
  167.6 4.8 %all-to-all-done.2 = f32[64,1,192]{2,1,0:T(1,128)S(1)} async-done(((f32[64,1,192]{2,1,0:T(1,128)}), f32[64,1,192]{2,1,0:T(1,128)S(1)}, u32[]{:S(2)}, u32[]{:S(2)}) %all-to-all-start.2) | async-done | bytes 49184 | tf_op jit(solution)/shard_map/all_to_all | solution.py:214
  (194 shorter events, 61.9 us)
Async XLA Ops:
  0.6 18.0 %copy-start = (bf16[12,128,128]{2,1,0:T(8,128)(2,1)S(1)}, bf16[12,128,128]{2,1,0:T(8,128)(2,1)}, u32[]{:S(2)}) copy-start(bf16[12,128,128]{2,1,0:T(8,128)(2,1)} %param.22) | copy-start | bytes 1179652
  21.7 25.7 %copy-start.23 = (s32[12]{0:T(128)S(1)}, s32[12]{0:T(128)}, u32[]{:S(2)}) copy-start(s32[12]{0:T(128)} %copy-done.22) | copy-start | bytes 148
  22.9 26.1 %copy-start.18 = (s32[12]{0:T(128)S(1)}, s32[12]{0:T(128)}, u32[]{:S(2)}) copy-start(s32[12]{0:T(128)} %get-tuple-element.75) | copy-start | bytes 148
  22.9 26.7 %copy-start.1 = (s32[1,12]{1,0:T(1,128)S(1)}, s32[1,12]{1,0:T(1,128)}, u32[]{:S(2)}) copy-start(s32[1,12]{1,0:T(1,128)} %param.23) | copy-start | bytes 148
  22.9 26.7 %copy-start.19 = (pred[12]{0:T(512)(128)(4,1)S(1)}, pred[12]{0:T(512)(128)(4,1)}, u32[]{:S(2)}) copy-start(pred[12]{0:T(512)(128)(4,1)} %get-tuple-element.80) | copy-start | bytes 40
  22.9 31.2 %collective-permute-start.2 = (f32[3,200,128]{2,1,0:T(8,128)}, f32[3,200,128]{2,1,0:T(8,128)}, u32[]{:S(2)}, u32[]{:S(2)}) collective-permute-start(f32[3,200,128]{2,1,0:T(8,128)} %get-tuple-element.56), channel_id=1, source_target_pairs={{0,488},{8,496},{16,504},{24,0},{32,8},{40,16},{48,24},{56,32},{64... | collective-permute-start | bytes 921608 | tf_op jit(solution)/shard_map/ppermute | solution.py:23
  36.5 20.5 %collective-permute-start.3 = (f32[3,200,128]{2,1,0:T(8,128)}, f32[3,200,128]{2,1,0:T(8,128)}, u32[]{:S(2)}, u32[]{:S(2)}) collective-permute-start(f32[3,200,128]{2,1,0:T(8,128)} %get-tuple-element.55), channel_id=1, source_target_pairs={{0,496},{8,504},{16,0},{24,8},{32,16},{40,24},{48,32},{56,40},{64,... | collective-permute-start | bytes 921608 | tf_op jit(solution)/shard_map/ppermute | solution.py:23
  39.2 18.9 %collective-permute-start.1 = (f32[3,200,128]{2,1,0:T(8,128)}, f32[3,200,128]{2,1,0:T(8,128)S(1)}, u32[]{:S(2)}, u32[]{:S(2)}) collective-permute-start(f32[3,200,128]{2,1,0:T(8,128)} %get-tuple-element.57), channel_id=1, source_target_pairs={{0,504},{8,0},{16,8},{24,16},{32,24},{40,32},{48,40},{56,48},{64,5... | collective-permute-start | bytes 921608 | tf_op jit(solution)/shard_map/ppermute | solution.py:23
  41.6 16.4 %collective-permute-start = (f32[3,200,128]{2,1,0:T(8,128)}, f32[3,200,128]{2,1,0:T(8,128)}, u32[]{:S(2)}, u32[]{:S(2)}) collective-permute-start(f32[3,200,128]{2,1,0:T(8,128)} %get-tuple-element.58), channel_id=1, source_target_pairs={{0,8},{8,16},{16,24},{24,32},{32,40},{40,48},{48,56},{56,64},{64,7... | collective-permute-start | bytes 921608 | tf_op jit(solution)/shard_map/ppermute | solution.py:23
  44.7 14.4 %collective-permute-start.4 = (f32[3,200,128]{2,1,0:T(8,128)}, f32[3,200,128]{2,1,0:T(8,128)}, u32[]{:S(2)}, u32[]{:S(2)}) collective-permute-start(f32[3,200,128]{2,1,0:T(8,128)} %get-tuple-element.54), channel_id=1, source_target_pairs={{0,16},{8,24},{16,32},{24,40},{32,48},{40,56},{48,64},{56,72},{64,... | collective-permute-start | bytes 921608 | tf_op jit(solution)/shard_map/ppermute | solution.py:23
  49.7 22.1 %copy-start.5 = (bf16[12,128,128]{2,1,0:T(8,128)(2,1)}, bf16[12,128,128]{2,1,0:T(8,128)(2,1)S(1)}, u32[]{:S(2)}) copy-start(bf16[12,128,128]{2,1,0:T(8,128)(2,1)S(1)} %gather_fusion.8) | copy-start | bytes 1179652
  54.2 16.8 %collective-permute-start.5 = (f32[3,200,128]{2,1,0:T(8,128)}, f32[3,200,128]{2,1,0:T(8,128)S(1)}, u32[]{:S(2)}, u32[]{:S(2)}) collective-permute-start(f32[3,200,128]{2,1,0:T(8,128)} %get-tuple-element.53), channel_id=1, source_target_pairs={{0,24},{8,32},{16,40},{24,48},{32,56},{40,64},{48,72},{56,80},{64,... | collective-permute-start | bytes 921608 | tf_op jit(solution)/shard_map/ppermute | solution.py:23
  58.0 13.1 %copy-start.10 = (f32[3,200,128]{2,1,0:T(8,128)}, f32[3,200,128]{2,1,0:T(8,128)S(1)}, u32[]{:S(2)}) copy-start(f32[3,200,128]{2,1,0:T(8,128)S(1)} %collective-permute-done.1) | copy-start | bytes 921604
  87.8 23.1 %all-to-all-start = ((f32[8,2,8,2048]{3,2,1,0:T(8,128)}), f32[8,2,8,2048]{3,2,1,0:T(8,128)}, u32[]{:S(2)}, u32[]{:S(2)}) async-start(f32[8,2,8,2048]{3,2,1,0:T(8,128)} %copy.147), calls=%async_computation | async-start | bytes 2097152 | tf_op jit(solution)/shard_map/all_to_all | solution.py:179
  114.1 11.8 %copy-start.17 = (pred[6,3]{1,0:T(8,128)(4,1)S(1)}, pred[6,3]{1,0:T(8,128)(4,1)}, u32[]{:S(2)}) copy-start(pred[6,3]{1,0:T(8,128)(4,1)} %copy-done.16) | copy-start | bytes 58
  115.0 50.4 %copy-start.6 = (bf16[12,128,128]{2,1,0:T(8,128)(2,1)S(1)}, bf16[12,128,128]{2,1,0:T(8,128)(2,1)}, u32[]{:S(2)}) copy-start(bf16[12,128,128]{2,1,0:T(8,128)(2,1)} %copy-done.5) | copy-start | bytes 1179652
  117.2 21.3 %all-to-all-start.1 = ((f32[64,1,192]{2,1,0:T(1,128)}), f32[64,1,192]{2,1,0:T(1,128)S(1)}, u32[]{:S(2)}, u32[]{:S(2)}) async-start(f32[64,1,192]{2,1,0:T(1,128)} %all_to_all.16), calls=%async_computation.1 | async-start | bytes 131072 | tf_op jit(solution)/shard_map/all_to_all | solution.py:195
  138.5 19.3 %collective-permute-start.8 = (bf16[3,8,128]{2,1,0:T(8,128)(2,1)S(1)}, bf16[3,8,128]{2,1,0:T(8,128)(2,1)S(1)}, u32[]{:S(2)}, u32[]{:S(2)}) collective-permute-start(bf16[3,8,128]{2,1,0:T(8,128)(2,1)S(1)} %get-tuple-element.66), channel_id=1, source_target_pairs={{0,488},{8,496},{16,504},{24,0},{32,8},{40,16},{48,24},{56,32},{64... | collective-permute-start | bytes 18440 | tf_op jit(solution)/shard_map/ppermute | solution.py:23
  140.7 21.5 %collective-permute-start.9 = (bf16[3,8,128]{2,1,0:T(8,128)(2,1)S(1)}, bf16[3,8,128]{2,1,0:T(8,128)(2,1)S(1)}, u32[]{:S(2)}, u32[]{:S(2)}) collective-permute-start(bf16[3,8,128]{2,1,0:T(8,128)(2,1)S(1)} %get-tuple-element.65), channel_id=1, source_target_pairs={{0,496},{8,504},{16,0},{24,8},{32,16},{40,24},{48,32},{56,40},{64,... | collective-permute-start | bytes 18440 | tf_op jit(solution)/shard_map/ppermute | solution.py:23
  143.5 18.7 %collective-permute-start.7 = (bf16[3,8,128]{2,1,0:T(8,128)(2,1)S(1)}, bf16[3,8,128]{2,1,0:T(8,128)(2,1)S(1)}, u32[]{:S(2)}, u32[]{:S(2)}) collective-permute-start(bf16[3,8,128]{2,1,0:T(8,128)(2,1)S(1)} %get-tuple-element.67), channel_id=1, source_target_pairs={{0,504},{8,0},{16,8},{24,16},{32,24},{40,32},{48,40},{56,48},{64,5... | collective-permute-start | bytes 18440 | tf_op jit(solution)/shard_map/ppermute | solution.py:23
  145.7 16.5 %collective-permute-start.6 = (bf16[3,8,128]{2,1,0:T(8,128)(2,1)S(1)}, bf16[3,8,128]{2,1,0:T(8,128)(2,1)S(1)}, u32[]{:S(2)}, u32[]{:S(2)}) collective-permute-start(bf16[3,8,128]{2,1,0:T(8,128)(2,1)S(1)} %get-tuple-element.68), channel_id=1, source_target_pairs={{0,8},{8,16},{16,24},{24,32},{32,40},{40,48},{48,56},{56,64},{64,7... | collective-permute-start | bytes 18440 | tf_op jit(solution)/shard_map/ppermute | solution.py:23
  149.1 13.2 %collective-permute-start.10 = (bf16[3,8,128]{2,1,0:T(8,128)(2,1)S(1)}, bf16[3,8,128]{2,1,0:T(8,128)(2,1)S(1)}, u32[]{:S(2)}, u32[]{:S(2)}) collective-permute-start(bf16[3,8,128]{2,1,0:T(8,128)(2,1)S(1)} %get-tuple-element.64), channel_id=1, source_target_pairs={{0,16},{8,24},{16,32},{24,40},{32,48},{40,56},{48,64},{56,72},{64,... | collective-permute-start | bytes 18440 | tf_op jit(solution)/shard_map/ppermute | solution.py:23
  152.3 20.1 %all-to-all-start.2 = ((f32[64,1,192]{2,1,0:T(1,128)}), f32[64,1,192]{2,1,0:T(1,128)S(1)}, u32[]{:S(2)}, u32[]{:S(2)}) async-start(f32[64,1,192]{2,1,0:T(1,128)} %broadcast_in_dim.118), calls=%async_computation.2 | async-start | bytes 131072 | tf_op jit(solution)/shard_map/all_to_all | solution.py:214
  157.8 7.7 %collective-permute-start.11 = (bf16[3,8,128]{2,1,0:T(8,128)(2,1)S(1)}, bf16[3,8,128]{2,1,0:T(8,128)(2,1)S(1)}, u32[]{:S(2)}, u32[]{:S(2)}) collective-permute-start(bf16[3,8,128]{2,1,0:T(8,128)(2,1)S(1)} %get-tuple-element.63), channel_id=1, source_target_pairs={{0,24},{8,32},{16,40},{24,48},{32,56},{40,64},{48,72},{56,80},{64,... | collective-permute-start | bytes 18440 | tf_op jit(solution)/shard_map/ppermute | solution.py:23
  (16 other events, 69.5 us)

commit v10 on v7

--- a/solution.py
+++ b/solution.py
@@ -129,8 +129,12 @@
         preferred_element_type=jnp.float32,
     )
     sg_out = sg_out * jnp.take(live, sending_slot)[:, None, None]
-    sg_edges = jnp.zeros((len(shifts()), 1, c_rows, BLK), jnp.float32)
-    sg_edges = sg_edges.at[up, 0].set(sg_later[:, NB - 1]).at[down, 0].set(sg_prior[:, 0])
+    edge_later = jnp.dot(sg_blocks[:, NB - 1], band_blocks[NB - 1, 2], preferred_element_type=jnp.float32)
+    edge_prior = jnp.dot(sg_blocks[:, 0], band_blocks[0, 0], preferred_element_type=jnp.float32)
+    no_edge = jnp.zeros((c_rows, BLK), jnp.float32)
+    sg_edges = jnp.stack(
+        [edge_later if e == 1 else edge_prior if e == -1 else no_edge for e in shifts()], 0
+    )[:, None]
     sg_send = jnp.concatenate([sg_out.reshape(len(shifts()), 2, c_rows, BLK), sg_edges], 1)
 
     picked = jnp.take(both_blocks.transpose(1, 0, 2), pick, axis=0)

time: 173 us -> 186 us (1.075)
  local copies, waits for them, and re-layouts: 29.7 us -> 37 us
  matrix products: 17.3 us -> 20.9 us
  other arithmetic: 12.6 us -> 14.5 us
    convert_element_type x2, local copies, waits for them, and re-layouts: 0.29 us -> 2.63 us  [local(): hidden_act = jax.nn.silu(hidden_sum).astype(jnp.bfloat16)]
    dot_general x0 -> x2, matrix products: none -> 1.88 us  [the longest x1 0.98 us: local(): jnp.dot(sg_blocks[:, NB - 1], band_blocks[NB - 1, 2], preferred_element_t...]
    unnamed x61 -> x51, local copies, waits for them, and re-layouts: 7.55 us -> 7.05 us
  transfers between devices with their start and end apart: 15 -> 15, of which waited for: 5 -> 5; matrix products, arithmetic and copies ran while one was open for 9% -> 12% of each run, Pallas kernels for 0% -> 0%
where the time goes in v10:
time: 186 us; the launch traced here: 184 us
  starting transfers between devices  64.2 us (35%)
  waiting for transfers between devices  45.8 us (25%)
  local copies, waits for them, and re-layouts  37 us (20%)
  matrix products  20.9 us (11%)
  other arithmetic  14.5 us (8%)
    ppermute x12, starting transfers between devices, send_by(): lax.ppermute(x, axis, [(i, (i + by) % devices) for i in range(devices)])  44.7 us
    all_to_all x1, waiting for transfers between devices, local(): incoming = lax.all_to_all(outgoing, 'col', 0, 0, tiled=True)  14 us
    all_to_all x1, waiting for transfers between devices, local(): lax.all_to_all(flat.reshape(row_devices, -1), 'row', 0, 0, tiled=True)  13.8 us
    ppermute x12, waiting for transfers between devices, send_by(): lax.ppermute(x, axis, [(i, (i + by) % devices) for i in range(devices)])  13.2 us
    unnamed x51, local copies, waits for them, and re-layouts  7.05 us
    all_to_all x1, starting transfers between devices, local(): flat = lax.all_to_all(spread, 'row', 0, 0, tiled=True).reshape(-1)  6.65 us
    all_to_all x1, starting transfers between devices, local(): lax.all_to_all(flat.reshape(row_devices, -1), 'row', 0, 0, tiled=True)  6.51 us
    all_to_all x1, starting transfers between devices, local(): incoming = lax.all_to_all(outgoing, 'col', 0, 0, tiled=True)  6.35 us
  transfers between devices with their start and end apart: 15, of which 5 were waited for; matrix products, arithmetic and copies ran while one was open for 12% of the time, Pallas kernels for 0%

profile of v10, /device:TPU:1, one launch (start us, length us, event | category | flops | bytes accessed | tf_op | source)
XLA Modules:
  0.0 183.9 jit_solution(17000820402486910919)
XLA Ops:
  17.8 1.7 gather_fusion.1
  22.6 13.4 %collective-permute-start.2 = (f32[3,200,128]{2,1,0:T(8,128)}, f32[3,200,128]{2,1,0:T(8,128)}, u32[]{:S(2)}, u32[]{:S(2)}) collective-permute-start(f32[3,200,128]{2,1,0:T(8,128)} %get-tuple-element.32), channel_id=1, source_target_pairs={{0,488},{8,496},{16,504},{24,0},{32,8},{40,16},{48,24},{56,32},{64... | collective-permute-start | bytes 921608 | tf_op jit(solution)/shard_map/ppermute | solution.py:23
  36.0 2.6 %collective-permute-start.3 = (f32[3,200,128]{2,1,0:T(8,128)}, f32[3,200,128]{2,1,0:T(8,128)}, u32[]{:S(2)}, u32[]{:S(2)}) collective-permute-start(f32[3,200,128]{2,1,0:T(8,128)} %get-tuple-element.31), channel_id=1, source_target_pairs={{0,496},{8,504},{16,0},{24,8},{32,16},{40,24},{48,32},{56,40},{64,... | collective-permute-start | bytes 921608 | tf_op jit(solution)/shard_map/ppermute | solution.py:23
  38.6 2.5 %collective-permute-start.1 = (f32[3,200,128]{2,1,0:T(8,128)}, f32[3,200,128]{2,1,0:T(8,128)}, u32[]{:S(2)}, u32[]{:S(2)}) collective-permute-start(f32[3,200,128]{2,1,0:T(8,128)} %get-tuple-element.33), channel_id=1, source_target_pairs={{0,504},{8,0},{16,8},{24,16},{32,24},{40,32},{48,40},{56,48},{64,5... | collective-permute-start | bytes 921608 | tf_op jit(solution)/shard_map/ppermute | solution.py:23
  41.1 3.1 %collective-permute-start = (f32[3,200,128]{2,1,0:T(8,128)}, f32[3,200,128]{2,1,0:T(8,128)}, u32[]{:S(2)}, u32[]{:S(2)}) collective-permute-start(f32[3,200,128]{2,1,0:T(8,128)} %get-tuple-element.34), channel_id=1, source_target_pairs={{0,8},{8,16},{16,24},{24,32},{32,40},{40,48},{48,56},{56,64},{64,7... | collective-permute-start | bytes 921608 | tf_op jit(solution)/shard_map/ppermute | solution.py:23
  44.2 2.6 %collective-permute-start.4 = (f32[3,200,128]{2,1,0:T(8,128)}, f32[3,200,128]{2,1,0:T(8,128)}, u32[]{:S(2)}, u32[]{:S(2)}) collective-permute-start(f32[3,200,128]{2,1,0:T(8,128)} %get-tuple-element.30), channel_id=1, source_target_pairs={{0,16},{8,24},{16,32},{24,40},{32,48},{40,56},{48,64},{56,72},{64,... | collective-permute-start | bytes 921608 | tf_op jit(solution)/shard_map/ppermute | solution.py:23
  49.2 1.6 fusion.26
  58.7 1.9 %collective-permute-start.5 = (f32[3,200,128]{2,1,0:T(8,128)}, f32[3,200,128]{2,1,0:T(8,128)S(1)}, u32[]{:S(2)}, u32[]{:S(2)}) collective-permute-start(f32[3,200,128]{2,1,0:T(8,128)} %get-tuple-element.29), channel_id=1, source_target_pairs={{0,24},{8,32},{16,40},{24,48},{32,56},{40,64},{48,72},{56,80},{64,... | collective-permute-start | bytes 921608 | tf_op jit(solution)/shard_map/ppermute | solution.py:23
  65.4 10.1 %collective-permute-done.5 = f32[3,200,128]{2,1,0:T(8,128)S(1)} collective-permute-done((f32[3,200,128]{2,1,0:T(8,128)}, f32[3,200,128]{2,1,0:T(8,128)S(1)}, u32[]{:S(2)}, u32[]{:S(2)}) %collective-permute-start.5) | collective-permute-done | bytes 307232 | tf_op jit(solution)/shard_map/ppermute | solution.py:23
  76.6 2.4 %fusion.2 = f32[192,128,16]{1,2,0:T(8,128)S(1)} fusion(f32[12,192,128]{2,1,0:T(8,128)S(1)} %fusion.15, f32[12,16]{1,0:T(8,128)S(1)} %gather_fusion.5, pred[12]{0:T(512)(128)(4,1)S(1)} %copy-done.12), kind=kOutput, calls=%fused_computation.16 | convolution fusion | flops 56623296 | bytes 2753292 | tf_op jit(solution)/shard_map/kb,kfn->fbn/dot_general | solution.py:71
  84.8 1.8 reshape.476
  92.5 6.4 %all-to-all-start = ((f32[8,2,8,2048]{3,2,1,0:T(8,128)}), f32[8,2,8,2048]{3,2,1,0:T(8,128)}, u32[]{:S(2)}, u32[]{:S(2)}) async-start(f32[8,2,8,2048]{3,2,1,0:T(8,128)} %copy.126), calls=%async_computation | async-start | bytes 2097152 | tf_op jit(solution)/shard_map/all_to_all | solution.py:176
  101.5 14.0 %all-to-all-done = f32[8,2,8,2048]{3,2,1,0:T(8,128)} async-done(((f32[8,2,8,2048]{3,2,1,0:T(8,128)}), f32[8,2,8,2048]{3,2,1,0:T(8,128)}, u32[]{:S(2)}, u32[]{:S(2)}) %all-to-all-start) | async-done | bytes 1048608 | tf_op jit(solution)/shard_map/all_to_all | solution.py:176
  125.1 6.5 %all-to-all-start.1 = ((f32[64,1,192]{2,1,0:T(1,128)}), f32[64,1,192]{2,1,0:T(1,128)S(1)}, u32[]{:S(2)}, u32[]{:S(2)}) async-start(f32[64,1,192]{2,1,0:T(1,128)} %all_to_all.16), calls=%async_computation.1 | async-start | bytes 131072 | tf_op jit(solution)/shard_map/all_to_all | solution.py:192
  132.4 13.8 %all-to-all-done.1 = f32[64,1,192]{2,1,0:T(1,128)S(1)} async-done(((f32[64,1,192]{2,1,0:T(1,128)}), f32[64,1,192]{2,1,0:T(1,128)S(1)}, u32[]{:S(2)}, u32[]{:S(2)}) %all-to-all-start.1) | async-done | bytes 49184 | tf_op jit(solution)/shard_map/all_to_all | solution.py:192
  146.2 2.2 %collective-permute-start.8 = (bf16[3,8,128]{2,1,0:T(8,128)(2,1)S(1)}, bf16[3,8,128]{2,1,0:T(8,128)(2,1)S(1)}, u32[]{:S(2)}, u32[]{:S(2)}) collective-permute-start(bf16[3,8,128]{2,1,0:T(8,128)(2,1)S(1)} %get-tuple-element.44), channel_id=1, source_target_pairs={{0,488},{8,496},{16,504},{24,0},{32,8},{40,16},{48,24},{56,32},{64... | collective-permute-start | bytes 18440 | tf_op jit(solution)/shard_map/ppermute | solution.py:23
  148.5 3.1 %collective-permute-start.6 = (bf16[3,8,128]{2,1,0:T(8,128)(2,1)S(1)}, bf16[3,8,128]{2,1,0:T(8,128)(2,1)S(1)}, u32[]{:S(2)}, u32[]{:S(2)}) collective-permute-start(bf16[3,8,128]{2,1,0:T(8,128)(2,1)S(1)} %get-tuple-element.46), channel_id=1, source_target_pairs={{0,8},{8,16},{16,24},{24,32},{32,40},{40,48},{48,56},{56,64},{64,7... | collective-permute-start | bytes 18440 | tf_op jit(solution)/shard_map/ppermute | solution.py:23
  151.6 4.9 %collective-permute-start.9 = (bf16[3,8,128]{2,1,0:T(8,128)(2,1)S(1)}, bf16[3,8,128]{2,1,0:T(8,128)(2,1)S(1)}, u32[]{:S(2)}, u32[]{:S(2)}) collective-permute-start(bf16[3,8,128]{2,1,0:T(8,128)(2,1)S(1)} %get-tuple-element.43), channel_id=1, source_target_pairs={{0,496},{8,504},{16,0},{24,8},{32,16},{40,24},{48,32},{56,40},{64,... | collective-permute-start | bytes 18440 | tf_op jit(solution)/shard_map/ppermute | solution.py:23
  156.5 1.9 %collective-permute-start.7 = (bf16[3,8,128]{2,1,0:T(8,128)(2,1)S(1)}, bf16[3,8,128]{2,1,0:T(8,128)(2,1)S(1)}, u32[]{:S(2)}, u32[]{:S(2)}) collective-permute-start(bf16[3,8,128]{2,1,0:T(8,128)(2,1)S(1)} %get-tuple-element.45), channel_id=1, source_target_pairs={{0,504},{8,0},{16,8},{24,16},{32,24},{40,32},{48,40},{56,48},{64,5... | collective-permute-start | bytes 18440 | tf_op jit(solution)/shard_map/ppermute | solution.py:23
  158.4 1.9 %collective-permute-start.10 = (bf16[3,8,128]{2,1,0:T(8,128)(2,1)S(1)}, bf16[3,8,128]{2,1,0:T(8,128)(2,1)S(1)}, u32[]{:S(2)}, u32[]{:S(2)}) collective-permute-start(bf16[3,8,128]{2,1,0:T(8,128)(2,1)S(1)} %get-tuple-element.42), channel_id=1, source_target_pairs={{0,16},{8,24},{16,32},{24,40},{32,48},{40,56},{48,64},{56,72},{64,... | collective-permute-start | bytes 18440 | tf_op jit(solution)/shard_map/ppermute | solution.py:23
  161.1 6.7 %all-to-all-start.2 = ((f32[64,1,192]{2,1,0:T(1,128)}), f32[64,1,192]{2,1,0:T(1,128)S(1)}, u32[]{:S(2)}, u32[]{:S(2)}) async-start(f32[64,1,192]{2,1,0:T(1,128)} %broadcast_in_dim.119), calls=%async_computation.2 | async-start | bytes 131072 | tf_op jit(solution)/shard_map/all_to_all | solution.py:211
  167.7 4.4 %collective-permute-start.11 = (bf16[3,8,128]{2,1,0:T(8,128)(2,1)S(1)}, bf16[3,8,128]{2,1,0:T(8,128)(2,1)S(1)}, u32[]{:S(2)}, u32[]{:S(2)}) collective-permute-start(bf16[3,8,128]{2,1,0:T(8,128)(2,1)S(1)} %get-tuple-element.41), channel_id=1, source_target_pairs={{0,24},{8,32},{16,40},{24,48},{32,56},{40,64},{48,72},{56,80},{64,... | collective-permute-start | bytes 18440 | tf_op jit(solution)/shard_map/ppermute | solution.py:23
  172.3 3.1 %collective-permute-done.11 = bf16[3,8,128]{2,1,0:T(8,128)(2,1)S(1)} collective-permute-done((bf16[3,8,128]{2,1,0:T(8,128)(2,1)S(1)}, bf16[3,8,128]{2,1,0:T(8,128)(2,1)S(1)}, u32[]{:S(2)}, u32[]{:S(2)}) %collective-permute-start.11) | collective-permute-done | bytes 6176 | tf_op jit(solution)/shard_map/ppermute | solution.py:23
  177.5 4.7 %all-to-all-done.2 = f32[64,1,192]{2,1,0:T(1,128)S(1)} async-done(((f32[64,1,192]{2,1,0:T(1,128)}), f32[64,1,192]{2,1,0:T(1,128)S(1)}, u32[]{:S(2)}, u32[]{:S(2)}) %all-to-all-start.2) | async-done | bytes 49184 | tf_op jit(solution)/shard_map/all_to_all | solution.py:211
  (170 shorter events, 65.1 us)
Async XLA Ops:
  0.6 16.5 %copy-start = (bf16[12,128,128]{2,1,0:T(8,128)(2,1)S(1)}, bf16[12,128,128]{2,1,0:T(8,128)(2,1)}, u32[]{:S(2)}) copy-start(bf16[12,128,128]{2,1,0:T(8,128)(2,1)} %param.18) | copy-start | bytes 1179652
  21.2 25.6 %copy-start.2 = (bf16[16,3,128,128]{3,2,1,0:T(8,128)(2,1)S(1)}, bf16[16,3,128,128]{3,2,1,0:T(8,128)(2,1)}, u32[]{:S(2)}) copy-start(bf16[16,3,128,128]{3,2,1,0:T(8,128)(2,1)} %param.17) | copy-start | bytes 4718596
  21.2 25.6 %copy-start.11 = (bf16[8,2048]{1,0:T(8,128)(2,1)S(1)}, bf16[8,2048]{1,0:T(8,128)(2,1)}, u32[]{:S(2)}) copy-start(bf16[8,2048]{1,0:T(8,128)(2,1)} %param.16) | copy-start | bytes 98308
  21.3 27.4 %copy-start.17 = (s32[12]{0:T(128)S(1)}, s32[12]{0:T(128)}, u32[]{:S(2)}) copy-start(s32[12]{0:T(128)} %copy-done.16) | copy-start | bytes 148
  22.6 36.1 %collective-permute-start.2 = (f32[3,200,128]{2,1,0:T(8,128)}, f32[3,200,128]{2,1,0:T(8,128)}, u32[]{:S(2)}, u32[]{:S(2)}) collective-permute-start(f32[3,200,128]{2,1,0:T(8,128)} %get-tuple-element.32), channel_id=1, source_target_pairs={{0,488},{8,496},{16,504},{24,0},{32,8},{40,16},{48,24},{56,32},{64... | collective-permute-start | bytes 921608 | tf_op jit(solution)/shard_map/ppermute | solution.py:23
  36.0 25.6 %collective-permute-start.3 = (f32[3,200,128]{2,1,0:T(8,128)}, f32[3,200,128]{2,1,0:T(8,128)}, u32[]{:S(2)}, u32[]{:S(2)}) collective-permute-start(f32[3,200,128]{2,1,0:T(8,128)} %get-tuple-element.31), channel_id=1, source_target_pairs={{0,496},{8,504},{16,0},{24,8},{32,16},{40,24},{48,32},{56,40},{64,... | collective-permute-start | bytes 921608 | tf_op jit(solution)/shard_map/ppermute | solution.py:23
  38.6 23.9 %collective-permute-start.1 = (f32[3,200,128]{2,1,0:T(8,128)}, f32[3,200,128]{2,1,0:T(8,128)}, u32[]{:S(2)}, u32[]{:S(2)}) collective-permute-start(f32[3,200,128]{2,1,0:T(8,128)} %get-tuple-element.33), channel_id=1, source_target_pairs={{0,504},{8,0},{16,8},{24,16},{32,24},{40,32},{48,40},{56,48},{64,5... | collective-permute-start | bytes 921608 | tf_op jit(solution)/shard_map/ppermute | solution.py:23
  41.1 22.3 %collective-permute-start = (f32[3,200,128]{2,1,0:T(8,128)}, f32[3,200,128]{2,1,0:T(8,128)}, u32[]{:S(2)}, u32[]{:S(2)}) collective-permute-start(f32[3,200,128]{2,1,0:T(8,128)} %get-tuple-element.34), channel_id=1, source_target_pairs={{0,8},{8,16},{16,24},{24,32},{32,40},{40,48},{48,56},{56,64},{64,7... | collective-permute-start | bytes 921608 | tf_op jit(solution)/shard_map/ppermute | solution.py:23
  44.2 20.2 %collective-permute-start.4 = (f32[3,200,128]{2,1,0:T(8,128)}, f32[3,200,128]{2,1,0:T(8,128)}, u32[]{:S(2)}, u32[]{:S(2)}) collective-permute-start(f32[3,200,128]{2,1,0:T(8,128)} %get-tuple-element.30), channel_id=1, source_target_pairs={{0,16},{8,24},{16,32},{24,40},{32,48},{40,56},{48,64},{56,72},{64,... | collective-permute-start | bytes 921608 | tf_op jit(solution)/shard_map/ppermute | solution.py:23
  55.8 20.3 %copy-start.9 = (bf16[12,128,128]{2,1,0:T(8,128)(2,1)}, bf16[12,128,128]{2,1,0:T(8,128)(2,1)S(1)}, u32[]{:S(2)}) copy-start(bf16[12,128,128]{2,1,0:T(8,128)(2,1)S(1)} %gather_fusion.8) | copy-start | bytes 1179652
  58.1 18.0 %copy-start.12 = (pred[12]{0:T(512)(128)(4,1)S(1)}, pred[12]{0:T(512)(128)(4,1)}, u32[]{:S(2)}) copy-start(pred[12]{0:T(512)(128)(4,1)} %compare_and_fusion) | copy-start | bytes 40
  58.7 16.8 %collective-permute-start.5 = (f32[3,200,128]{2,1,0:T(8,128)}, f32[3,200,128]{2,1,0:T(8,128)S(1)}, u32[]{:S(2)}, u32[]{:S(2)}) collective-permute-start(f32[3,200,128]{2,1,0:T(8,128)} %get-tuple-element.29), channel_id=1, source_target_pairs={{0,24},{8,32},{16,40},{24,48},{32,56},{40,64},{48,72},{56,80},{64,... | collective-permute-start | bytes 921608 | tf_op jit(solution)/shard_map/ppermute | solution.py:23
  92.5 23.1 %all-to-all-start = ((f32[8,2,8,2048]{3,2,1,0:T(8,128)}), f32[8,2,8,2048]{3,2,1,0:T(8,128)}, u32[]{:S(2)}, u32[]{:S(2)}) async-start(f32[8,2,8,2048]{3,2,1,0:T(8,128)} %copy.126), calls=%async_computation | async-start | bytes 2097152 | tf_op jit(solution)/shard_map/all_to_all | solution.py:176
  99.9 17.7 %copy-start.8 = (bf16[64,16,128]{2,0,1:T(8,128)(2,1)S(1)}, bf16[64,16,128]{2,0,1:T(8,128)(2,1)}, u32[]{:S(2)}) copy-start(bf16[64,16,128]{2,0,1:T(8,128)(2,1)} %copy-done.7) | copy-start | bytes 786436
  121.1 54.3 %copy-start.10 = (bf16[12,128,128]{2,1,0:T(8,128)(2,1)S(1)}, bf16[12,128,128]{2,1,0:T(8,128)(2,1)}, u32[]{:S(2)}) copy-start(bf16[12,128,128]{2,1,0:T(8,128)(2,1)} %copy-done.9) | copy-start | bytes 1179652
  121.1 54.3 %copy-start.13 = (pred[12]{0:T(512)(128)(4,1)S(1)}, pred[12]{0:T(512)(128)(4,1)}, u32[]{:S(2)}) copy-start(pred[12]{0:T(512)(128)(4,1)} %compare_and_fusion) | copy-start | bytes 40
  125.1 21.1 %all-to-all-start.1 = ((f32[64,1,192]{2,1,0:T(1,128)}), f32[64,1,192]{2,1,0:T(1,128)S(1)}, u32[]{:S(2)}, u32[]{:S(2)}) async-start(f32[64,1,192]{2,1,0:T(1,128)} %all_to_all.16), calls=%async_computation.1 | async-start | bytes 131072 | tf_op jit(solution)/shard_map/all_to_all | solution.py:192
  146.2 21.5 %collective-permute-start.8 = (bf16[3,8,128]{2,1,0:T(8,128)(2,1)S(1)}, bf16[3,8,128]{2,1,0:T(8,128)(2,1)S(1)}, u32[]{:S(2)}, u32[]{:S(2)}) collective-permute-start(bf16[3,8,128]{2,1,0:T(8,128)(2,1)S(1)} %get-tuple-element.44), channel_id=1, source_target_pairs={{0,488},{8,496},{16,504},{24,0},{32,8},{40,16},{48,24},{56,32},{64... | collective-permute-start | bytes 18440 | tf_op jit(solution)/shard_map/ppermute | solution.py:23
  148.5 23.7 %collective-permute-start.6 = (bf16[3,8,128]{2,1,0:T(8,128)(2,1)S(1)}, bf16[3,8,128]{2,1,0:T(8,128)(2,1)S(1)}, u32[]{:S(2)}, u32[]{:S(2)}) collective-permute-start(bf16[3,8,128]{2,1,0:T(8,128)(2,1)S(1)} %get-tuple-element.46), channel_id=1, source_target_pairs={{0,8},{8,16},{16,24},{24,32},{32,40},{40,48},{48,56},{56,64},{64,7... | collective-permute-start | bytes 18440 | tf_op jit(solution)/shard_map/ppermute | solution.py:23
  151.6 20.6 %collective-permute-start.9 = (bf16[3,8,128]{2,1,0:T(8,128)(2,1)S(1)}, bf16[3,8,128]{2,1,0:T(8,128)(2,1)S(1)}, u32[]{:S(2)}, u32[]{:S(2)}) collective-permute-start(bf16[3,8,128]{2,1,0:T(8,128)(2,1)S(1)} %get-tuple-element.43), channel_id=1, source_target_pairs={{0,496},{8,504},{16,0},{24,8},{32,16},{40,24},{48,32},{56,40},{64,... | collective-permute-start | bytes 18440 | tf_op jit(solution)/shard_map/ppermute | solution.py:23
  156.5 15.7 %collective-permute-start.7 = (bf16[3,8,128]{2,1,0:T(8,128)(2,1)S(1)}, bf16[3,8,128]{2,1,0:T(8,128)(2,1)S(1)}, u32[]{:S(2)}, u32[]{:S(2)}) collective-permute-start(bf16[3,8,128]{2,1,0:T(8,128)(2,1)S(1)} %get-tuple-element.45), channel_id=1, source_target_pairs={{0,504},{8,0},{16,8},{24,16},{32,24},{40,32},{48,40},{56,48},{64,5... | collective-permute-start | bytes 18440 | tf_op jit(solution)/shard_map/ppermute | solution.py:23
  158.4 13.8 %collective-permute-start.10 = (bf16[3,8,128]{2,1,0:T(8,128)(2,1)S(1)}, bf16[3,8,128]{2,1,0:T(8,128)(2,1)S(1)}, u32[]{:S(2)}, u32[]{:S(2)}) collective-permute-start(bf16[3,8,128]{2,1,0:T(8,128)(2,1)S(1)} %get-tuple-element.42), channel_id=1, source_target_pairs={{0,16},{8,24},{16,32},{24,40},{32,48},{40,56},{48,64},{56,72},{64,... | collective-permute-start | bytes 18440 | tf_op jit(solution)/shard_map/ppermute | solution.py:23
  161.1 21.2 %all-to-all-start.2 = ((f32[64,1,192]{2,1,0:T(1,128)}), f32[64,1,192]{2,1,0:T(1,128)S(1)}, u32[]{:S(2)}, u32[]{:S(2)}) async-start(f32[64,1,192]{2,1,0:T(1,128)} %broadcast_in_dim.119), calls=%async_computation.2 | async-start | bytes 131072 | tf_op jit(solution)/shard_map/all_to_all | solution.py:211
  167.7 7.7 %collective-permute-start.11 = (bf16[3,8,128]{2,1,0:T(8,128)(2,1)S(1)}, bf16[3,8,128]{2,1,0:T(8,128)(2,1)S(1)}, u32[]{:S(2)}, u32[]{:S(2)}) collective-permute-start(bf16[3,8,128]{2,1,0:T(8,128)(2,1)S(1)} %get-tuple-element.41), channel_id=1, source_target_pairs={{0,24},{8,32},{16,40},{24,48},{32,56},{40,64},{48,72},{56,80},{64,... | collective-permute-start | bytes 18440 | tf_op jit(solution)/shard_map/ppermute | solution.py:23
  (10 other events, 46.9 us)

commit v11 on v6

--- a/solution.py
+++ b/solution.py
@@ -184,6 +184,8 @@
         "in,hn->ih", feat_sum, slope_back.astype(jnp.float32), precision=HI
     )
 
+    flat = jnp.concatenate([first_part.reshape(-1), second_part.reshape(-1)])
+    pieces = lax.all_to_all(flat.reshape(row_devices, -1), "row", 0, 0, tiled=True)
     class_blocks = class_in.reshape(c_rows, NB, BLK)
     class_pick = jnp.take(class_blocks.transpose(1, 0, 2), pick, axis=0)
     class_pick = class_pick.reshape(len(shifts()), 3, c_rows, BLK)
@@ -191,12 +193,20 @@
     for i, e in enumerate(shifts()):
         lanes = lanes.at[e % row_devices].set(class_pick[i])
     doubled = jnp.concatenate([lanes, lanes], 0)
-    outgoing = lax.dynamic_slice_in_dim(doubled, jnp.mod(row_devices - me, row_devices), row_devices, 0)
+    lanes = lax.dynamic_slice_in_dim(doubled, jnp.mod(row_devices - me, row_devices), row_devices, 0)
+
+    flat = jnp.concatenate([first_part.reshape(-1), second_part.reshape(-1)])
+    width = flat.size // row_devices
+    outgoing = jnp.concatenate(
+        [flat.reshape(row_devices, width), lanes.astype(jnp.float32).reshape(row_devices, -1)], 1
+    )
     incoming = lax.all_to_all(outgoing, "row", 0, 0, tiled=True)
-    doubled = jnp.concatenate([incoming, incoming], 0)
+    pieces = incoming[:, :width]
+    from_rows = incoming[:, width:].reshape((row_devices,) + class_pick.shape[1:])
+    doubled = jnp.concatenate([from_rows, from_rows], 0)
     near = lax.dynamic_slice_in_dim(doubled, jnp.mod(me - REACH, row_devices), 2 * REACH + 1, 0)
-    class_arrived = [near[REACH - e] for e in shifts()]
-    class_pairs = jnp.concatenate([a[:2] for a in class_arrived], 0)
+    class_arrived = [near[REACH - e].astype(jnp.bfloat16) for e in shifts()]
+    class_pairs = jnp.concatenate([x[:2] for x in class_arrived], 0)
     scores = forward_sum(
         class_blocks,
         class_arrived[up][2],
@@ -207,8 +217,6 @@
         targets_read,
     ).reshape(c_rows, nodes).astype(jnp.bfloat16)
 
-    flat = jnp.concatenate([first_part.reshape(-1), second_part.reshape(-1)])
-    pieces = lax.all_to_all(flat.reshape(row_devices, -1), "row", 0, 0, tiled=True)
     summed = jnp.sum(pieces, axis=0, keepdims=True)
     spread = jnp.broadcast_to(summed, (row_devices, summed.shape[1]))
     flat = lax.all_to_all(spread, "row", 0, 0, tiled=True).reshape(-1)

time: 190 us -> 192 us (1.011)
  waiting for transfers between devices: 76.2 us -> 80.5 us
    all_to_all x1, waiting for transfers between devices: 25.7 us -> 43 us  [local(): incoming = lax.all_to_all(outgoing, 'row', 0, 0, tiled=True)]
    all_to_all x1 -> x0, waiting for transfers between devices: 14 us -> none  [local(): lax.all_to_all(flat.reshape(row_devices, -1), 'row', 0, 0, tiled=True)]
    all_to_all x1 -> x0, starting transfers between devices: 6.51 us -> none  [local(): lax.all_to_all(flat.reshape(row_devices, -1), 'row', 0, 0, tiled=True)]
    all_to_all x1, starting transfers between devices: 4.61 us -> 8.52 us  [local(): flat = lax.all_to_all(spread, 'row', 0, 0, tiled=True).reshape(-1)]
    scatter x6, local copies, waits for them, and re-layouts: 3.76 us -> 0.1 us  [local(): lanes = lanes.at[e % row_devices].set(class_pick[i])]
    all_to_all x1, starting transfers between devices: 4.45 us -> 6.49 us  [local(): incoming = lax.all_to_all(outgoing, 'row', 0, 0, tiled=True)]
    unnamed x52 -> x56, local copies, waits for them, and re-layouts: 7.5 us -> 8.82 us
  transfers between devices with their start and end apart: 10 -> 9, of which waited for: 5 -> 4; matrix products, arithmetic and copies ran while one was open for 10% -> 8% of each run, Pallas kernels for 0% -> 0%
where the time goes in v11:
time: 192 us; the launch traced here: 191 us
  waiting for transfers between devices  80.5 us (42%)
  starting transfers between devices  47.6 us (25%)
  local copies, waits for them, and re-layouts  31.6 us (16%)
  matrix products  16.8 us (9%)
  other arithmetic  13.2 us (7%)
    all_to_all x1, waiting for transfers between devices, local(): incoming = lax.all_to_all(outgoing, 'row', 0, 0, tiled=True)  43 us
    ppermute x6, starting transfers between devices, send_by(): lax.ppermute(x, axis, [(i, (i + by) % devices) for i in range(devices)])  26.2 us
    all_to_all x1, waiting for transfers between devices, local(): incoming = lax.all_to_all(outgoing, 'col', 0, 0, tiled=True)  14.2 us
    all_to_all x1, waiting for transfers between devices, local(): flat = lax.all_to_all(spread, 'row', 0, 0, tiled=True).reshape(-1)  13.3 us
    ppermute x6, waiting for transfers between devices, send_by(): lax.ppermute(x, axis, [(i, (i + by) % devices) for i in range(devices)])  10.1 us
    unnamed x56, local copies, waits for them, and re-layouts  8.82 us
    all_to_all x1, starting transfers between devices, local(): flat = lax.all_to_all(spread, 'row', 0, 0, tiled=True).reshape(-1)  8.52 us
    all_to_all x1, starting transfers between devices, local(): incoming = lax.all_to_all(outgoing, 'row', 0, 0, tiled=True)  6.49 us
  transfers between devices with their start and end apart: 9, of which 4 were waited for; matrix products, arithmetic and copies ran while one was open for 8% of the time, Pallas kernels for 0%

profile of v11, /device:TPU:1, one launch (start us, length us, event | category | flops | bytes accessed | tf_op | source)
XLA Modules:
  0.0 191.0 jit_solution(6609119492991363890)
XLA Ops:
  0.7 1.4 convolution_bitcast_fusion.3
  2.1 1.3 convolution_bitcast_fusion.2
  15.2 1.7 gather_fusion.1
  16.8 1.3 select_convert_fusion
  19.9 13.4 %collective-permute-start.2 = (f32[3,200,128]{2,1,0:T(8,128)}, f32[3,200,128]{2,1,0:T(8,128)}, u32[]{:S(2)}, u32[]{:S(2)}) collective-permute-start(f32[3,200,128]{2,1,0:T(8,128)} %get-tuple-element.124), channel_id=1, source_target_pairs={{0,488},{8,496},{16,504},{24,0},{32,8},{40,16},{48,24},{56,32},{64... | collective-permute-start | bytes 921608 | tf_op jit(solution)/shard_map/ppermute | solution.py:23
  33.3 2.6 %collective-permute-start.3 = (f32[3,200,128]{2,1,0:T(8,128)}, f32[3,200,128]{2,1,0:T(8,128)}, u32[]{:S(2)}, u32[]{:S(2)}) collective-permute-start(f32[3,200,128]{2,1,0:T(8,128)} %get-tuple-element.123), channel_id=1, source_target_pairs={{0,496},{8,504},{16,0},{24,8},{32,16},{40,24},{48,32},{56,40},{64,... | collective-permute-start | bytes 921608 | tf_op jit(solution)/shard_map/ppermute | solution.py:23
  36.0 2.5 %collective-permute-start.1 = (f32[3,200,128]{2,1,0:T(8,128)}, f32[3,200,128]{2,1,0:T(8,128)}, u32[]{:S(2)}, u32[]{:S(2)}) collective-permute-start(f32[3,200,128]{2,1,0:T(8,128)} %get-tuple-element.125), channel_id=1, source_target_pairs={{0,504},{8,0},{16,8},{24,16},{32,24},{40,32},{48,40},{56,48},{64,5... | collective-permute-start | bytes 921608 | tf_op jit(solution)/shard_map/ppermute | solution.py:23
  38.5 3.1 %collective-permute-start = (f32[3,200,128]{2,1,0:T(8,128)}, f32[3,200,128]{2,1,0:T(8,128)}, u32[]{:S(2)}, u32[]{:S(2)}) collective-permute-start(f32[3,200,128]{2,1,0:T(8,128)} %get-tuple-element.126), channel_id=1, source_target_pairs={{0,8},{8,16},{16,24},{24,32},{32,40},{40,48},{48,56},{56,64},{64,7... | collective-permute-start | bytes 921608 | tf_op jit(solution)/shard_map/ppermute | solution.py:23
  41.6 2.6 %collective-permute-start.4 = (f32[3,200,128]{2,1,0:T(8,128)}, f32[3,200,128]{2,1,0:T(8,128)}, u32[]{:S(2)}, u32[]{:S(2)}) collective-permute-start(f32[3,200,128]{2,1,0:T(8,128)} %get-tuple-element.122), channel_id=1, source_target_pairs={{0,16},{8,24},{16,32},{24,40},{32,48},{40,56},{48,64},{56,72},{64,... | collective-permute-start | bytes 921608 | tf_op jit(solution)/shard_map/ppermute | solution.py:23
  44.3 1.5 fusion.22
  47.8 1.4 gather_fusion.8
  51.5 1.9 %collective-permute-start.5 = (f32[3,200,128]{2,1,0:T(8,128)}, f32[3,200,128]{2,1,0:T(8,128)S(1)}, u32[]{:S(2)}, u32[]{:S(2)}) collective-permute-start(f32[3,200,128]{2,1,0:T(8,128)} %get-tuple-element.121), channel_id=1, source_target_pairs={{0,24},{8,32},{16,40},{24,48},{32,56},{40,64},{48,72},{56,80},{64,... | collective-permute-start | bytes 921608 | tf_op jit(solution)/shard_map/ppermute | solution.py:23
  58.3 10.1 %collective-permute-done.5 = f32[3,200,128]{2,1,0:T(8,128)S(1)} collective-permute-done((f32[3,200,128]{2,1,0:T(8,128)}, f32[3,200,128]{2,1,0:T(8,128)S(1)}, u32[]{:S(2)}, u32[]{:S(2)}) %collective-permute-start.5) | collective-permute-done | bytes 307232 | tf_op jit(solution)/shard_map/ppermute | solution.py:23
  68.9 2.4 %fusion.2 = f32[192,128,16]{1,2,0:T(8,128)S(1)} fusion(f32[12,192,128]{2,1,0:T(8,128)S(1)} %fusion.15, f32[12,16]{1,0:T(8,128)S(1)} %gather_fusion.5, pred[12]{0:T(512)(128)(4,1)S(1)} %compare_and_fusion), kind=kOutput, calls=%fused_computation.16 | convolution fusion | flops 56623296 | bytes 2753292 | tf_op jit(solution)/shard_map/kb,kfn->fbn/dot_general | solution.py:71
  80.9 6.4 %all-to-all-start = ((f32[8,2,8,2048]{3,2,1,0:T(8,128)}), f32[8,2,8,2048]{3,2,1,0:T(8,128)}, u32[]{:S(2)}, u32[]{:S(2)}) async-start(f32[8,2,8,2048]{3,2,1,0:T(8,128)} %copy.126), calls=%async_computation | async-start | bytes 2097152 | tf_op jit(solution)/shard_map/all_to_all | solution.py:172
  88.5 1.3 copy.121
  89.8 14.2 %all-to-all-done = f32[8,2,8,2048]{3,2,1,0:T(8,128)} async-done(((f32[8,2,8,2048]{3,2,1,0:T(8,128)}), f32[8,2,8,2048]{3,2,1,0:T(8,128)}, u32[]{:S(2)}, u32[]{:S(2)}) %all-to-all-start) | async-done | bytes 1048608 | tf_op jit(solution)/shard_map/all_to_all | solution.py:172
  108.7 1.7 fusion.1
  111.6 1.4 pad_maximum_fusion.1
  113.0 1.5 all_to_all.16
  114.5 6.5 %all-to-all-start.1 = ((f32[64,1,3264]{2,1,0:T(1,128)}), f32[64,1,3264]{2,1,0:T(1,128)S(1)}, u32[]{:S(2)}, u32[]{:S(2)}) async-start(f32[64,1,3264]{2,1,0:T(1,128)} %all_to_all.16), calls=%async_computation.1 | async-start | bytes 1703936 | tf_op jit(solution)/shard_map/all_to_all | solution.py:203
  121.0 43.0 %all-to-all-done.1 = f32[64,1,3264]{2,1,0:T(1,128)S(1)} async-done(((f32[64,1,3264]{2,1,0:T(1,128)}), f32[64,1,3264]{2,1,0:T(1,128)S(1)}, u32[]{:S(2)}, u32[]{:S(2)}) %all-to-all-start.1) | async-done | bytes 835616 | tf_op jit(solution)/shard_map/all_to_all | solution.py:203
  166.4 8.5 %all-to-all-start.2 = ((f32[64,1,192]{2,1,0:T(1,128)}), f32[64,1,192]{2,1,0:T(1,128)S(1)}, u32[]{:S(2)}, u32[]{:S(2)}) async-start(f32[64,1,192]{2,1,0:T(1,128)} %broadcast_in_dim.117), calls=%async_computation.2 | async-start | bytes 131072 | tf_op jit(solution)/shard_map/all_to_all | solution.py:222
  176.2 13.3 %all-to-all-done.2 = f32[64,1,192]{2,1,0:T(1,128)S(1)} async-done(((f32[64,1,192]{2,1,0:T(1,128)}), f32[64,1,192]{2,1,0:T(1,128)S(1)}, u32[]{:S(2)}, u32[]{:S(2)}) %all-to-all-start.2) | async-done | bytes 49184 | tf_op jit(solution)/shard_map/all_to_all | solution.py:222
  (176 shorter events, 44.7 us)
Async XLA Ops:
  0.6 13.3 %copy-start = (bf16[12,128,128]{2,1,0:T(8,128)(2,1)S(1)}, bf16[12,128,128]{2,1,0:T(8,128)(2,1)}, u32[]{:S(2)}) copy-start(bf16[12,128,128]{2,1,0:T(8,128)(2,1)} %param.34) | copy-start | bytes 1179652
  0.6 9.2 %copy-start.16 = (s32[6,1]{0,1:T(1,128)S(1)}, s32[6,1]{0,1:T(1,128)}, u32[]{:S(2)}) copy-start(s32[6,1]{0,1:T(1,128)} %constant.448.clone) | copy-start | bytes 76
  0.7 6.6 %copy-start.1 = (s32[1,12]{1,0:T(1,128)S(1)}, s32[1,12]{1,0:T(1,128)}, u32[]{:S(2)}) copy-start(s32[1,12]{1,0:T(1,128)} %param.35) | copy-start | bytes 148
  0.7 9.9 %copy-start.19 = (s32[64]{0:T(128)S(1)}, s32[64]{0:T(128)}, u32[]{:S(2)}) copy-start(s32[64]{0:T(128)} %param.37) | copy-start | bytes 772
  0.7 12.4 %copy-start.5 = (bf16[128,2048]{1,0:T(8,128)(2,1)S(1)}, bf16[128,2048]{1,0:T(8,128)(2,1)}, u32[]{:S(2)}) copy-start(bf16[128,2048]{1,0:T(8,128)(2,1)} %param.29) | copy-start | bytes 1572868
  0.7 12.4 %copy-start.14 = (bf16[128,64]{0,1:T(8,128)(2,1)S(1)}, bf16[128,64]{0,1:T(8,128)(2,1)}, u32[]{:S(2)}) copy-start(bf16[128,64]{0,1:T(8,128)(2,1)} %param.30) | copy-start | bytes 49156
  2.1 42.2 %copy-start.11 = (f32[8,16,128]{2,0,1:T(8,128)}, f32[8,16,128]{2,0,1:T(8,128)S(1)}, u32[]{:S(2)}) copy-start(f32[8,16,128]{2,0,1:T(8,128)S(1)} %convolution_bitcast_fusion.3) | copy-start | bytes 196612
  3.4 40.9 %copy-start.10 = (f32[8,16,128]{2,0,1:T(8,128)}, f32[8,16,128]{2,0,1:T(8,128)S(1)}, u32[]{:S(2)}) copy-start(f32[8,16,128]{2,0,1:T(8,128)S(1)} %convolution_bitcast_fusion.2) | copy-start | bytes 196612
  10.0 34.2 %copy-start.17 = (s32[12]{0:T(128)}, s32[12]{0:T(128)S(1)}, u32[]{:S(2)}) copy-start(s32[12]{0:T(128)S(1)} %select_reduce_fusion) | copy-start | bytes 148
  19.9 31.6 %collective-permute-start.2 = (f32[3,200,128]{2,1,0:T(8,128)}, f32[3,200,128]{2,1,0:T(8,128)}, u32[]{:S(2)}, u32[]{:S(2)}) collective-permute-start(f32[3,200,128]{2,1,0:T(8,128)} %get-tuple-element.124), channel_id=1, source_target_pairs={{0,488},{8,496},{16,504},{24,0},{32,8},{40,16},{48,24},{56,32},{64... | collective-permute-start | bytes 921608 | tf_op jit(solution)/shard_map/ppermute | solution.py:23
  33.3 21.1 %collective-permute-start.3 = (f32[3,200,128]{2,1,0:T(8,128)}, f32[3,200,128]{2,1,0:T(8,128)}, u32[]{:S(2)}, u32[]{:S(2)}) collective-permute-start(f32[3,200,128]{2,1,0:T(8,128)} %get-tuple-element.123), channel_id=1, source_target_pairs={{0,496},{8,504},{16,0},{24,8},{32,16},{40,24},{48,32},{56,40},{64,... | collective-permute-start | bytes 921608 | tf_op jit(solution)/shard_map/ppermute | solution.py:23
  36.0 19.4 %collective-permute-start.1 = (f32[3,200,128]{2,1,0:T(8,128)}, f32[3,200,128]{2,1,0:T(8,128)}, u32[]{:S(2)}, u32[]{:S(2)}) collective-permute-start(f32[3,200,128]{2,1,0:T(8,128)} %get-tuple-element.125), channel_id=1, source_target_pairs={{0,504},{8,0},{16,8},{24,16},{32,24},{40,32},{48,40},{56,48},{64,5... | collective-permute-start | bytes 921608 | tf_op jit(solution)/shard_map/ppermute | solution.py:23
  38.5 17.9 %collective-permute-start = (f32[3,200,128]{2,1,0:T(8,128)}, f32[3,200,128]{2,1,0:T(8,128)}, u32[]{:S(2)}, u32[]{:S(2)}) collective-permute-start(f32[3,200,128]{2,1,0:T(8,128)} %get-tuple-element.126), channel_id=1, source_target_pairs={{0,8},{8,16},{16,24},{24,32},{32,40},{40,48},{48,56},{56,64},{64,7... | collective-permute-start | bytes 921608 | tf_op jit(solution)/shard_map/ppermute | solution.py:23
  41.6 15.7 %collective-permute-start.4 = (f32[3,200,128]{2,1,0:T(8,128)}, f32[3,200,128]{2,1,0:T(8,128)}, u32[]{:S(2)}, u32[]{:S(2)}) collective-permute-start(f32[3,200,128]{2,1,0:T(8,128)} %get-tuple-element.122), channel_id=1, source_target_pairs={{0,16},{8,24},{16,32},{24,40},{32,48},{40,56},{48,64},{56,72},{64,... | collective-permute-start | bytes 921608 | tf_op jit(solution)/shard_map/ppermute | solution.py:23
  51.0 17.4 %copy-start.8 = (bf16[12,128,128]{2,1,0:T(8,128)(2,1)S(1)}, bf16[12,128,128]{2,1,0:T(8,128)(2,1)}, u32[]{:S(2)}) copy-start(bf16[12,128,128]{2,1,0:T(8,128)(2,1)} %gather_fusion.8) | copy-start | bytes 1179652
  51.5 16.8 %collective-permute-start.5 = (f32[3,200,128]{2,1,0:T(8,128)}, f32[3,200,128]{2,1,0:T(8,128)S(1)}, u32[]{:S(2)}, u32[]{:S(2)}) collective-permute-start(f32[3,200,128]{2,1,0:T(8,128)} %get-tuple-element.121), channel_id=1, source_target_pairs={{0,24},{8,32},{16,40},{24,48},{32,56},{40,64},{48,72},{56,80},{64,... | collective-permute-start | bytes 921608 | tf_op jit(solution)/shard_map/ppermute | solution.py:23
  68.8 3.3 %copy-start.3 = (bf16[16,3,128,128]{3,2,1,0:T(8,128)(2,1)S(1)}, bf16[16,3,128,128]{3,2,1,0:T(8,128)(2,1)}, u32[]{:S(2)}) copy-start(bf16[16,3,128,128]{3,2,1,0:T(8,128)(2,1)} %param.33) | copy-start | bytes 4718596
  75.7 3.7 %copy-start.4 = (bf16[16,3,128,128]{3,2,1,0:T(8,128)(2,1)S(1)}, bf16[16,3,128,128]{3,2,1,0:T(8,128)(2,1)}, u32[]{:S(2)}) copy-start(bf16[16,3,128,128]{3,2,1,0:T(8,128)(2,1)} %param.33) | copy-start | bytes 4718596
  75.7 3.7 %slice-start.1 = ((f32[8,16,128]{2,0,1:T(8,128)}), f32[8,15,128]{2,0,1:T(8,128)S(1)}, s32[]{:S(2)}) async-start(f32[8,16,128]{2,0,1:T(8,128)} %copy-done.10), calls=%async_computation.4 | async-start | bytes 122880 | tf_op jit(solution)/shard_map/slice | solution.py:159
  75.7 3.7 %slice-start.2 = ((f32[8,16,128]{2,0,1:T(8,128)}), f32[8,15,128]{2,0,1:T(8,128)S(1)}, s32[]{:S(2)}) async-start(f32[8,16,128]{2,0,1:T(8,128)} %copy-done.11), calls=%async_computation.5 | async-start | bytes 122880 | tf_op jit(solution)/shard_map/slice | solution.py:160
  75.7 3.7 %copy-start.13 = (bf16[8,2048]{1,0:T(8,128)(2,1)S(1)}, bf16[8,2048]{1,0:T(8,128)(2,1)}, u32[]{:S(2)}) copy-start(bf16[8,2048]{1,0:T(8,128)(2,1)} %param.32) | copy-start | bytes 98308
  80.9 23.1 %all-to-all-start = ((f32[8,2,8,2048]{3,2,1,0:T(8,128)}), f32[8,2,8,2048]{3,2,1,0:T(8,128)}, u32[]{:S(2)}, u32[]{:S(2)}) async-start(f32[8,2,8,2048]{3,2,1,0:T(8,128)} %copy.126), calls=%async_computation | async-start | bytes 2097152 | tf_op jit(solution)/shard_map/all_to_all | solution.py:172
  114.5 49.5 %all-to-all-start.1 = ((f32[64,1,3264]{2,1,0:T(1,128)}), f32[64,1,3264]{2,1,0:T(1,128)S(1)}, u32[]{:S(2)}, u32[]{:S(2)}) async-start(f32[64,1,3264]{2,1,0:T(1,128)} %all_to_all.16), calls=%async_computation.1 | async-start | bytes 1703936 | tf_op jit(solution)/shard_map/all_to_all | solution.py:203
  166.4 23.1 %all-to-all-start.2 = ((f32[64,1,192]{2,1,0:T(1,128)}), f32[64,1,192]{2,1,0:T(1,128)S(1)}, u32[]{:S(2)}, u32[]{:S(2)}) async-start(f32[64,1,192]{2,1,0:T(1,128)} %broadcast_in_dim.117), calls=%async_computation.2 | async-start | bytes 131072 | tf_op jit(solution)/shard_map/all_to_all | solution.py:222
  (8 other events, 12.9 us)

commit v12 on v7

--- a/solution.py
+++ b/solution.py
@@ -167,11 +167,15 @@
     my_rows = lax.dynamic_slice_in_dim(weight_out, col_index * hidden_count, hidden_count, 0)
     class_part = jnp.einsum("hc,hn->cn", my_rows, hidden_act, preferred_element_type=jnp.float32)
     part_blocks = class_part.reshape(col_devices, c_rows, nodes)
-    mine = jnp.broadcast_to(class_back.astype(jnp.float32)[None], part_blocks.shape)
-    outgoing = jnp.stack([part_blocks, mine], 1)
+    lead = lax.reduce_precision(part_blocks, exponent_bits=8, mantissa_bits=7)
+    rest = (part_blocks - lead).astype(jnp.bfloat16)
+    mine = jnp.broadcast_to(class_back[None], part_blocks.shape)
+    outgoing = jnp.stack([lead.astype(jnp.bfloat16), rest, mine], 1)
     incoming = lax.all_to_all(outgoing, "col", 0, 0, tiled=True)
-    class_in = jnp.sum(incoming[:, 0], axis=0).astype(jnp.bfloat16)
-    all_back = incoming[:, 1].astype(jnp.bfloat16).reshape(col_devices * c_rows, nodes)
+    class_in = jnp.sum(
+        incoming[:, 0].astype(jnp.float32) + incoming[:, 1].astype(jnp.float32), axis=0
+    ).astype(jnp.bfloat16)
+    all_back = incoming[:, 2].reshape(col_devices * c_rows, nodes)
 
     hidden_back = jnp.einsum("hc,cn->hn", my_rows, all_back, preferred_element_type=jnp.float32)
     second_part = jnp.einsum("hn,cn->hc", hidden_act, all_back, preferred_element_type=jnp.float32)

time: 173 us -> 168 us (0.971)
  waiting for transfers between devices: 45.9 us -> 44 us
  local copies, waits for them, and re-layouts: 29.7 us -> 27.9 us
    all_to_all x1, waiting for transfers between devices: 14.1 us -> 12.2 us  [local(): incoming = lax.all_to_all(outgoing, 'col', 0, 0, tiled=True)]
    unnamed x61 -> x59, local copies, waits for them, and re-layouts: 7.55 us -> 7.5 us
where the time goes in v12:
time: 168 us; the launch traced here: 167 us
  starting transfers between devices  64.6 us (38%)
  waiting for transfers between devices  44 us (26%)
  local copies, waits for them, and re-layouts  27.9 us (17%)
  matrix products  17.2 us (10%)
  other arithmetic  11.5 us (7%)
    ppermute x12, starting transfers between devices, send_by(): lax.ppermute(x, axis, [(i, (i + by) % devices) for i in range(devices)])  44.7 us
    all_to_all x1, waiting for transfers between devices, local(): lax.all_to_all(flat.reshape(row_devices, -1), 'row', 0, 0, tiled=True)  13.8 us
    ppermute x12, waiting for transfers between devices, send_by(): lax.ppermute(x, axis, [(i, (i + by) % devices) for i in range(devices)])  13.2 us
    all_to_all x1, waiting for transfers between devices, local(): incoming = lax.all_to_all(outgoing, 'col', 0, 0, tiled=True)  12.2 us
    unnamed x59, local copies, waits for them, and re-layouts  7.5 us
    all_to_all x1, starting transfers between devices, local(): lax.all_to_all(flat.reshape(row_devices, -1), 'row', 0, 0, tiled=True)  6.8 us
    all_to_all x1, starting transfers between devices, local(): flat = lax.all_to_all(spread, 'row', 0, 0, tiled=True).reshape(-1)  6.65 us
    all_to_all x1, starting transfers between devices, local(): incoming = lax.all_to_all(outgoing, 'col', 0, 0, tiled=True)  6.48 us
  transfers between devices with their start and end apart: 15, of which 5 were waited for; matrix products, arithmetic and copies ran while one was open for 9% of the time, Pallas kernels for 0%

profile of v12, /device:TPU:1, one launch (start us, length us, event | category | flops | bytes accessed | tf_op | source)
XLA Modules:
  0.0 166.7 jit_solution(2423257030391725392)
XLA Ops:
  14.1 1.7 gather_fusion.1
  18.9 13.4 %collective-permute-start.2 = (f32[3,200,128]{2,1,0:T(8,128)}, f32[3,200,128]{2,1,0:T(8,128)}, u32[]{:S(2)}, u32[]{:S(2)}) collective-permute-start(f32[3,200,128]{2,1,0:T(8,128)} %get-tuple-element.56), channel_id=1, source_target_pairs={{0,488},{8,496},{16,504},{24,0},{32,8},{40,16},{48,24},{56,32},{64... | collective-permute-start | bytes 921608 | tf_op jit(solution)/shard_map/ppermute | solution.py:23
  32.3 2.6 %collective-permute-start.3 = (f32[3,200,128]{2,1,0:T(8,128)}, f32[3,200,128]{2,1,0:T(8,128)}, u32[]{:S(2)}, u32[]{:S(2)}) collective-permute-start(f32[3,200,128]{2,1,0:T(8,128)} %get-tuple-element.55), channel_id=1, source_target_pairs={{0,496},{8,504},{16,0},{24,8},{32,16},{40,24},{48,32},{56,40},{64,... | collective-permute-start | bytes 921608 | tf_op jit(solution)/shard_map/ppermute | solution.py:23
  34.9 2.5 %collective-permute-start.1 = (f32[3,200,128]{2,1,0:T(8,128)}, f32[3,200,128]{2,1,0:T(8,128)}, u32[]{:S(2)}, u32[]{:S(2)}) collective-permute-start(f32[3,200,128]{2,1,0:T(8,128)} %get-tuple-element.57), channel_id=1, source_target_pairs={{0,504},{8,0},{16,8},{24,16},{32,24},{40,32},{48,40},{56,48},{64,5... | collective-permute-start | bytes 921608 | tf_op jit(solution)/shard_map/ppermute | solution.py:23
  37.4 3.1 %collective-permute-start = (f32[3,200,128]{2,1,0:T(8,128)}, f32[3,200,128]{2,1,0:T(8,128)}, u32[]{:S(2)}, u32[]{:S(2)}) collective-permute-start(f32[3,200,128]{2,1,0:T(8,128)} %get-tuple-element.58), channel_id=1, source_target_pairs={{0,8},{8,16},{16,24},{24,32},{32,40},{40,48},{48,56},{56,64},{64,7... | collective-permute-start | bytes 921608 | tf_op jit(solution)/shard_map/ppermute | solution.py:23
  40.5 2.6 %collective-permute-start.4 = (f32[3,200,128]{2,1,0:T(8,128)}, f32[3,200,128]{2,1,0:T(8,128)}, u32[]{:S(2)}, u32[]{:S(2)}) collective-permute-start(f32[3,200,128]{2,1,0:T(8,128)} %get-tuple-element.54), channel_id=1, source_target_pairs={{0,16},{8,24},{16,32},{24,40},{32,48},{40,56},{48,64},{56,72},{64,... | collective-permute-start | bytes 921608 | tf_op jit(solution)/shard_map/ppermute | solution.py:23
  43.2 1.5 fusion.24
  48.8 1.9 %collective-permute-start.5 = (f32[3,200,128]{2,1,0:T(8,128)}, f32[3,200,128]{2,1,0:T(8,128)S(1)}, u32[]{:S(2)}, u32[]{:S(2)}) collective-permute-start(f32[3,200,128]{2,1,0:T(8,128)} %get-tuple-element.53), channel_id=1, source_target_pairs={{0,24},{8,32},{16,40},{24,48},{32,56},{40,64},{48,72},{56,80},{64,... | collective-permute-start | bytes 921608 | tf_op jit(solution)/shard_map/ppermute | solution.py:23
  55.5 10.1 %collective-permute-done.5 = f32[3,200,128]{2,1,0:T(8,128)S(1)} collective-permute-done((f32[3,200,128]{2,1,0:T(8,128)}, f32[3,200,128]{2,1,0:T(8,128)S(1)}, u32[]{:S(2)}, u32[]{:S(2)}) %collective-permute-start.5) | collective-permute-done | bytes 307232 | tf_op jit(solution)/shard_map/ppermute | solution.py:23
  66.1 2.4 %fusion.2 = f32[192,128,16]{1,2,0:T(8,128)S(1)} fusion(f32[12,192,128]{2,1,0:T(8,128)S(1)} %fusion.15, f32[12,16]{1,0:T(8,128)S(1)} %gather_fusion.5, pred[12]{0:T(512)(128)(4,1)S(1)} %compare_and_fusion), kind=kOutput, calls=%fused_computation.15 | convolution fusion | flops 56623296 | bytes 2753292 | tf_op jit(solution)/shard_map/kb,kfn->fbn/dot_general | solution.py:71
  78.0 6.5 %all-to-all-start = ((bf16[8,3,8,2048]{3,2,1,0:T(8,128)(2,1)}), bf16[8,3,8,2048]{3,2,1,0:T(8,128)(2,1)}, u32[]{:S(2)}, u32[]{:S(2)}) async-start(bf16[8,3,8,2048]{3,2,1,0:T(8,128)(2,1)} %copy.126), calls=%async_computation | async-start | bytes 1572864 | tf_op jit(solution)/shard_map/all_to_all | solution.py:174
  85.8 12.2 %all-to-all-done = bf16[8,3,8,2048]{3,2,1,0:T(8,128)(2,1)} async-done(((bf16[8,3,8,2048]{3,2,1,0:T(8,128)(2,1)}), bf16[8,3,8,2048]{3,2,1,0:T(8,128)(2,1)}, u32[]{:S(2)}, u32[]{:S(2)}) %all-to-all-start) | async-done | bytes 786464 | tf_op jit(solution)/shard_map/all_to_all | solution.py:174
  103.6 1.6 fusion.130
  107.7 6.8 %all-to-all-start.1 = ((f32[64,1,192]{2,1,0:T(1,128)}), f32[64,1,192]{2,1,0:T(1,128)S(1)}, u32[]{:S(2)}, u32[]{:S(2)}) async-start(f32[64,1,192]{2,1,0:T(1,128)} %all_to_all.16), calls=%async_computation.1 | async-start | bytes 131072 | tf_op jit(solution)/shard_map/all_to_all | solution.py:192
  115.2 13.8 %all-to-all-done.1 = f32[64,1,192]{2,1,0:T(1,128)S(1)} async-done(((f32[64,1,192]{2,1,0:T(1,128)}), f32[64,1,192]{2,1,0:T(1,128)S(1)}, u32[]{:S(2)}, u32[]{:S(2)}) %all-to-all-start.1) | async-done | bytes 49184 | tf_op jit(solution)/shard_map/all_to_all | solution.py:192
  129.1 2.2 %collective-permute-start.8 = (bf16[3,8,128]{2,1,0:T(8,128)(2,1)S(1)}, bf16[3,8,128]{2,1,0:T(8,128)(2,1)S(1)}, u32[]{:S(2)}, u32[]{:S(2)}) collective-permute-start(bf16[3,8,128]{2,1,0:T(8,128)(2,1)S(1)} %get-tuple-element.70), channel_id=1, source_target_pairs={{0,488},{8,496},{16,504},{24,0},{32,8},{40,16},{48,24},{56,32},{64... | collective-permute-start | bytes 18440 | tf_op jit(solution)/shard_map/ppermute | solution.py:23
  131.3 3.1 %collective-permute-start.6 = (bf16[3,8,128]{2,1,0:T(8,128)(2,1)S(1)}, bf16[3,8,128]{2,1,0:T(8,128)(2,1)S(1)}, u32[]{:S(2)}, u32[]{:S(2)}) collective-permute-start(bf16[3,8,128]{2,1,0:T(8,128)(2,1)S(1)} %get-tuple-element.72), channel_id=1, source_target_pairs={{0,8},{8,16},{16,24},{24,32},{32,40},{40,48},{48,56},{56,64},{64,7... | collective-permute-start | bytes 18440 | tf_op jit(solution)/shard_map/ppermute | solution.py:23
  134.4 4.9 %collective-permute-start.9 = (bf16[3,8,128]{2,1,0:T(8,128)(2,1)S(1)}, bf16[3,8,128]{2,1,0:T(8,128)(2,1)S(1)}, u32[]{:S(2)}, u32[]{:S(2)}) collective-permute-start(bf16[3,8,128]{2,1,0:T(8,128)(2,1)S(1)} %get-tuple-element.69), channel_id=1, source_target_pairs={{0,496},{8,504},{16,0},{24,8},{32,16},{40,24},{48,32},{56,40},{64,... | collective-permute-start | bytes 18440 | tf_op jit(solution)/shard_map/ppermute | solution.py:23
  139.3 1.9 %collective-permute-start.7 = (bf16[3,8,128]{2,1,0:T(8,128)(2,1)S(1)}, bf16[3,8,128]{2,1,0:T(8,128)(2,1)S(1)}, u32[]{:S(2)}, u32[]{:S(2)}) collective-permute-start(bf16[3,8,128]{2,1,0:T(8,128)(2,1)S(1)} %get-tuple-element.71), channel_id=1, source_target_pairs={{0,504},{8,0},{16,8},{24,16},{32,24},{40,32},{48,40},{56,48},{64,5... | collective-permute-start | bytes 18440 | tf_op jit(solution)/shard_map/ppermute | solution.py:23
  141.3 1.9 %collective-permute-start.10 = (bf16[3,8,128]{2,1,0:T(8,128)(2,1)S(1)}, bf16[3,8,128]{2,1,0:T(8,128)(2,1)S(1)}, u32[]{:S(2)}, u32[]{:S(2)}) collective-permute-start(bf16[3,8,128]{2,1,0:T(8,128)(2,1)S(1)} %get-tuple-element.68), channel_id=1, source_target_pairs={{0,16},{8,24},{16,32},{24,40},{32,48},{40,56},{48,64},{56,72},{64,... | collective-permute-start | bytes 18440 | tf_op jit(solution)/shard_map/ppermute | solution.py:23
  143.9 6.7 %all-to-all-start.2 = ((f32[64,1,192]{2,1,0:T(1,128)}), f32[64,1,192]{2,1,0:T(1,128)S(1)}, u32[]{:S(2)}, u32[]{:S(2)}) async-start(f32[64,1,192]{2,1,0:T(1,128)} %broadcast_in_dim.116), calls=%async_computation.2 | async-start | bytes 131072 | tf_op jit(solution)/shard_map/all_to_all | solution.py:211
  150.5 4.4 %collective-permute-start.11 = (bf16[3,8,128]{2,1,0:T(8,128)(2,1)S(1)}, bf16[3,8,128]{2,1,0:T(8,128)(2,1)S(1)}, u32[]{:S(2)}, u32[]{:S(2)}) collective-permute-start(bf16[3,8,128]{2,1,0:T(8,128)(2,1)S(1)} %get-tuple-element.67), channel_id=1, source_target_pairs={{0,24},{8,32},{16,40},{24,48},{32,56},{40,64},{48,72},{56,80},{64,... | collective-permute-start | bytes 18440 | tf_op jit(solution)/shard_map/ppermute | solution.py:23
  155.1 3.1 %collective-permute-done.11 = bf16[3,8,128]{2,1,0:T(8,128)(2,1)S(1)} collective-permute-done((bf16[3,8,128]{2,1,0:T(8,128)(2,1)S(1)}, bf16[3,8,128]{2,1,0:T(8,128)(2,1)S(1)}, u32[]{:S(2)}, u32[]{:S(2)}) %collective-permute-start.11) | collective-permute-done | bytes 6176 | tf_op jit(solution)/shard_map/ppermute | solution.py:23
  160.4 4.7 %all-to-all-done.2 = f32[64,1,192]{2,1,0:T(1,128)S(1)} async-done(((f32[64,1,192]{2,1,0:T(1,128)}), f32[64,1,192]{2,1,0:T(1,128)S(1)}, u32[]{:S(2)}, u32[]{:S(2)}) %all-to-all-start.2) | async-done | bytes 49184 | tf_op jit(solution)/shard_map/all_to_all | solution.py:211
  (180 shorter events, 49.4 us)
Async XLA Ops:
  0.6 12.3 %copy-start = (bf16[12,128,128]{2,1,0:T(8,128)(2,1)S(1)}, bf16[12,128,128]{2,1,0:T(8,128)(2,1)}, u32[]{:S(2)}) copy-start(bf16[12,128,128]{2,1,0:T(8,128)(2,1)} %param.22) | copy-start | bytes 1179652
  0.7 11.3 %copy-start.5 = (bf16[128,2048]{1,0:T(8,128)(2,1)S(1)}, bf16[128,2048]{1,0:T(8,128)(2,1)}, u32[]{:S(2)}) copy-start(bf16[128,2048]{1,0:T(8,128)(2,1)} %param.17) | copy-start | bytes 1572868
  2.1 41.1 %copy-start.11 = (f32[8,16,128]{2,0,1:T(8,128)}, f32[8,16,128]{2,0,1:T(8,128)S(1)}, u32[]{:S(2)}) copy-start(f32[8,16,128]{2,0,1:T(8,128)S(1)} %convolution_bitcast_fusion.2) | copy-start | bytes 196612
  3.4 39.8 %copy-start.10 = (f32[8,16,128]{2,0,1:T(8,128)}, f32[8,16,128]{2,0,1:T(8,128)S(1)}, u32[]{:S(2)}) copy-start(f32[8,16,128]{2,0,1:T(8,128)S(1)} %convolution_bitcast_fusion.1) | copy-start | bytes 196612
  9.5 33.7 %copy-start.20 = (s32[12]{0:T(128)}, s32[12]{0:T(128)S(1)}, u32[]{:S(2)}) copy-start(s32[12]{0:T(128)S(1)} %select_reduce_fusion) | copy-start | bytes 148
  18.9 29.9 %collective-permute-start.2 = (f32[3,200,128]{2,1,0:T(8,128)}, f32[3,200,128]{2,1,0:T(8,128)}, u32[]{:S(2)}, u32[]{:S(2)}) collective-permute-start(f32[3,200,128]{2,1,0:T(8,128)} %get-tuple-element.56), channel_id=1, source_target_pairs={{0,488},{8,496},{16,504},{24,0},{32,8},{40,16},{48,24},{56,32},{64... | collective-permute-start | bytes 921608 | tf_op jit(solution)/shard_map/ppermute | solution.py:23
  32.3 19.4 %collective-permute-start.3 = (f32[3,200,128]{2,1,0:T(8,128)}, f32[3,200,128]{2,1,0:T(8,128)}, u32[]{:S(2)}, u32[]{:S(2)}) collective-permute-start(f32[3,200,128]{2,1,0:T(8,128)} %get-tuple-element.55), channel_id=1, source_target_pairs={{0,496},{8,504},{16,0},{24,8},{32,16},{40,24},{48,32},{56,40},{64,... | collective-permute-start | bytes 921608 | tf_op jit(solution)/shard_map/ppermute | solution.py:23
  34.9 17.7 %collective-permute-start.1 = (f32[3,200,128]{2,1,0:T(8,128)}, f32[3,200,128]{2,1,0:T(8,128)}, u32[]{:S(2)}, u32[]{:S(2)}) collective-permute-start(f32[3,200,128]{2,1,0:T(8,128)} %get-tuple-element.57), channel_id=1, source_target_pairs={{0,504},{8,0},{16,8},{24,16},{32,24},{40,32},{48,40},{56,48},{64,5... | collective-permute-start | bytes 921608 | tf_op jit(solution)/shard_map/ppermute | solution.py:23
  37.4 16.2 %collective-permute-start = (f32[3,200,128]{2,1,0:T(8,128)}, f32[3,200,128]{2,1,0:T(8,128)}, u32[]{:S(2)}, u32[]{:S(2)}) collective-permute-start(f32[3,200,128]{2,1,0:T(8,128)} %get-tuple-element.58), channel_id=1, source_target_pairs={{0,8},{8,16},{16,24},{24,32},{32,40},{40,48},{48,56},{56,64},{64,7... | collective-permute-start | bytes 921608 | tf_op jit(solution)/shard_map/ppermute | solution.py:23
  40.5 14.0 %collective-permute-start.4 = (f32[3,200,128]{2,1,0:T(8,128)}, f32[3,200,128]{2,1,0:T(8,128)}, u32[]{:S(2)}, u32[]{:S(2)}) collective-permute-start(f32[3,200,128]{2,1,0:T(8,128)} %get-tuple-element.54), channel_id=1, source_target_pairs={{0,16},{8,24},{16,32},{24,40},{32,48},{40,56},{48,64},{56,72},{64,... | collective-permute-start | bytes 921608 | tf_op jit(solution)/shard_map/ppermute | solution.py:23
  43.2 22.9 %copy-start.16 = (pred[12]{0:T(512)(128)(4,1)}, pred[12]{0:T(512)(128)(4,1)S(1)}, u32[]{:S(2)}) copy-start(pred[12]{0:T(512)(128)(4,1)S(1)} %compare_and_fusion) | copy-start | bytes 40
  48.2 17.4 %copy-start.8 = (bf16[12,128,128]{2,1,0:T(8,128)(2,1)S(1)}, bf16[12,128,128]{2,1,0:T(8,128)(2,1)}, u32[]{:S(2)}) copy-start(bf16[12,128,128]{2,1,0:T(8,128)(2,1)} %gather_fusion.8) | copy-start | bytes 1179652
  48.8 16.8 %collective-permute-start.5 = (f32[3,200,128]{2,1,0:T(8,128)}, f32[3,200,128]{2,1,0:T(8,128)S(1)}, u32[]{:S(2)}, u32[]{:S(2)}) collective-permute-start(f32[3,200,128]{2,1,0:T(8,128)} %get-tuple-element.53), channel_id=1, source_target_pairs={{0,24},{8,32},{16,40},{24,48},{32,56},{40,64},{48,72},{56,80},{64,... | collective-permute-start | bytes 921608 | tf_op jit(solution)/shard_map/ppermute | solution.py:23
  78.0 20.1 %all-to-all-start = ((bf16[8,3,8,2048]{3,2,1,0:T(8,128)(2,1)}), bf16[8,3,8,2048]{3,2,1,0:T(8,128)(2,1)}, u32[]{:S(2)}, u32[]{:S(2)}) async-start(bf16[8,3,8,2048]{3,2,1,0:T(8,128)(2,1)} %copy.126), calls=%async_computation | async-start | bytes 1572864 | tf_op jit(solution)/shard_map/all_to_all | solution.py:174
  103.6 54.6 %copy-start.9 = (bf16[12,128,128]{2,1,0:T(8,128)(2,1)S(1)}, bf16[12,128,128]{2,1,0:T(8,128)(2,1)}, u32[]{:S(2)}) copy-start(bf16[12,128,128]{2,1,0:T(8,128)(2,1)} %gather_fusion.8) | copy-start | bytes 1179652
  103.6 54.6 %copy-start.17 = (pred[12]{0:T(512)(128)(4,1)S(1)}, pred[12]{0:T(512)(128)(4,1)}, u32[]{:S(2)}) copy-start(pred[12]{0:T(512)(128)(4,1)} %copy-done.16) | copy-start | bytes 40
  107.7 21.4 %all-to-all-start.1 = ((f32[64,1,192]{2,1,0:T(1,128)}), f32[64,1,192]{2,1,0:T(1,128)S(1)}, u32[]{:S(2)}, u32[]{:S(2)}) async-start(f32[64,1,192]{2,1,0:T(1,128)} %all_to_all.16), calls=%async_computation.1 | async-start | bytes 131072 | tf_op jit(solution)/shard_map/all_to_all | solution.py:192
  129.1 21.5 %collective-permute-start.8 = (bf16[3,8,128]{2,1,0:T(8,128)(2,1)S(1)}, bf16[3,8,128]{2,1,0:T(8,128)(2,1)S(1)}, u32[]{:S(2)}, u32[]{:S(2)}) collective-permute-start(bf16[3,8,128]{2,1,0:T(8,128)(2,1)S(1)} %get-tuple-element.70), channel_id=1, source_target_pairs={{0,488},{8,496},{16,504},{24,0},{32,8},{40,16},{48,24},{56,32},{64... | collective-permute-start | bytes 18440 | tf_op jit(solution)/shard_map/ppermute | solution.py:23
  131.3 23.7 %collective-permute-start.6 = (bf16[3,8,128]{2,1,0:T(8,128)(2,1)S(1)}, bf16[3,8,128]{2,1,0:T(8,128)(2,1)S(1)}, u32[]{:S(2)}, u32[]{:S(2)}) collective-permute-start(bf16[3,8,128]{2,1,0:T(8,128)(2,1)S(1)} %get-tuple-element.72), channel_id=1, source_target_pairs={{0,8},{8,16},{16,24},{24,32},{32,40},{40,48},{48,56},{56,64},{64,7... | collective-permute-start | bytes 18440 | tf_op jit(solution)/shard_map/ppermute | solution.py:23
  134.4 20.6 %collective-permute-start.9 = (bf16[3,8,128]{2,1,0:T(8,128)(2,1)S(1)}, bf16[3,8,128]{2,1,0:T(8,128)(2,1)S(1)}, u32[]{:S(2)}, u32[]{:S(2)}) collective-permute-start(bf16[3,8,128]{2,1,0:T(8,128)(2,1)S(1)} %get-tuple-element.69), channel_id=1, source_target_pairs={{0,496},{8,504},{16,0},{24,8},{32,16},{40,24},{48,32},{56,40},{64,... | collective-permute-start | bytes 18440 | tf_op jit(solution)/shard_map/ppermute | solution.py:23
  139.3 15.7 %collective-permute-start.7 = (bf16[3,8,128]{2,1,0:T(8,128)(2,1)S(1)}, bf16[3,8,128]{2,1,0:T(8,128)(2,1)S(1)}, u32[]{:S(2)}, u32[]{:S(2)}) collective-permute-start(bf16[3,8,128]{2,1,0:T(8,128)(2,1)S(1)} %get-tuple-element.71), channel_id=1, source_target_pairs={{0,504},{8,0},{16,8},{24,16},{32,24},{40,32},{48,40},{56,48},{64,5... | collective-permute-start | bytes 18440 | tf_op jit(solution)/shard_map/ppermute | solution.py:23
  141.3 13.8 %collective-permute-start.10 = (bf16[3,8,128]{2,1,0:T(8,128)(2,1)S(1)}, bf16[3,8,128]{2,1,0:T(8,128)(2,1)S(1)}, u32[]{:S(2)}, u32[]{:S(2)}) collective-permute-start(bf16[3,8,128]{2,1,0:T(8,128)(2,1)S(1)} %get-tuple-element.68), channel_id=1, source_target_pairs={{0,16},{8,24},{16,32},{24,40},{32,48},{40,56},{48,64},{56,72},{64,... | collective-permute-start | bytes 18440 | tf_op jit(solution)/shard_map/ppermute | solution.py:23
  143.9 21.2 %all-to-all-start.2 = ((f32[64,1,192]{2,1,0:T(1,128)}), f32[64,1,192]{2,1,0:T(1,128)S(1)}, u32[]{:S(2)}, u32[]{:S(2)}) async-start(f32[64,1,192]{2,1,0:T(1,128)} %broadcast_in_dim.116), calls=%async_computation.2 | async-start | bytes 131072 | tf_op jit(solution)/shard_map/all_to_all | solution.py:211
  150.5 7.7 %collective-permute-start.11 = (bf16[3,8,128]{2,1,0:T(8,128)(2,1)S(1)}, bf16[3,8,128]{2,1,0:T(8,128)(2,1)S(1)}, u32[]{:S(2)}, u32[]{:S(2)}) collective-permute-start(bf16[3,8,128]{2,1,0:T(8,128)(2,1)S(1)} %get-tuple-element.67), channel_id=1, source_target_pairs={{0,24},{8,32},{16,40},{24,48},{32,56},{40,64},{48,72},{56,80},{64,... | collective-permute-start | bytes 18440 | tf_op jit(solution)/shard_map/ppermute | solution.py:23
  (17 other events, 78.7 us)

commit v13 on v7

--- a/solution.py
+++ b/solution.py
@@ -167,11 +167,11 @@
     my_rows = lax.dynamic_slice_in_dim(weight_out, col_index * hidden_count, hidden_count, 0)
     class_part = jnp.einsum("hc,hn->cn", my_rows, hidden_act, preferred_element_type=jnp.float32)
     part_blocks = class_part.reshape(col_devices, c_rows, nodes)
-    mine = jnp.broadcast_to(class_back.astype(jnp.float32)[None], part_blocks.shape)
-    outgoing = jnp.stack([part_blocks, mine], 1)
+    mine = jnp.broadcast_to(class_back[None], part_blocks.shape)
+    outgoing = jnp.stack([part_blocks.astype(jnp.bfloat16), mine], 1)
     incoming = lax.all_to_all(outgoing, "col", 0, 0, tiled=True)
-    class_in = jnp.sum(incoming[:, 0], axis=0).astype(jnp.bfloat16)
-    all_back = incoming[:, 1].astype(jnp.bfloat16).reshape(col_devices * c_rows, nodes)
+    class_in = jnp.sum(incoming[:, 0].astype(jnp.float32), axis=0).astype(jnp.bfloat16)
+    all_back = incoming[:, 1].reshape(col_devices * c_rows, nodes)
 
     hidden_back = jnp.einsum("hc,cn->hn", my_rows, all_back, preferred_element_type=jnp.float32)
     second_part = jnp.einsum("hn,cn->hc", hidden_act, all_back, preferred_element_type=jnp.float32)

time: 173 us -> 169 us (0.977)
  waiting for transfers between devices: 45.9 us -> 41.3 us
    all_to_all x1, waiting for transfers between devices: 14.1 us -> 9.45 us  [local(): incoming = lax.all_to_all(outgoing, 'col', 0, 0, tiled=True)]
    unnamed x61 -> x71, local copies, waits for them, and re-layouts: 7.55 us -> 8.22 us
where the time goes in v13:
time: 169 us; the launch traced here: 167 us
  starting transfers between devices  64.6 us (38%)
  waiting for transfers between devices  41.3 us (24%)
  local copies, waits for them, and re-layouts  30.3 us (18%)
  matrix products  18.3 us (11%)
  other arithmetic  11.3 us (7%)
    ppermute x12, starting transfers between devices, send_by(): lax.ppermute(x, axis, [(i, (i + by) % devices) for i in range(devices)])  44.8 us
    all_to_all x1, waiting for transfers between devices, local(): lax.all_to_all(flat.reshape(row_devices, -1), 'row', 0, 0, tiled=True)  13.9 us
    ppermute x12, waiting for transfers between devices, send_by(): lax.ppermute(x, axis, [(i, (i + by) % devices) for i in range(devices)])  13.2 us
    all_to_all x1, waiting for transfers between devices, local(): incoming = lax.all_to_all(outgoing, 'col', 0, 0, tiled=True)  9.45 us
    unnamed x71, local copies, waits for them, and re-layouts  8.22 us
    all_to_all x1, starting transfers between devices, local(): lax.all_to_all(flat.reshape(row_devices, -1), 'row', 0, 0, tiled=True)  6.65 us
    all_to_all x1, starting transfers between devices, local(): flat = lax.all_to_all(spread, 'row', 0, 0, tiled=True).reshape(-1)  6.64 us
    all_to_all x1, starting transfers between devices, local(): incoming = lax.all_to_all(outgoing, 'col', 0, 0, tiled=True)  6.5 us
  transfers between devices with their start and end apart: 15, of which 5 were waited for; matrix products, arithmetic and copies ran while one was open for 9% of the time, Pallas kernels for 0%

profile of v13, /device:TPU:1, one launch (start us, length us, event | category | flops | bytes accessed | tf_op | source)
XLA Modules:
  0.0 167.3 jit_solution(2868456711296554149)
XLA Ops:
  15.2 1.7 gather_fusion.1
  19.9 13.6 %collective-permute-start.2 = (f32[3,200,128]{2,1,0:T(8,128)}, f32[3,200,128]{2,1,0:T(8,128)}, u32[]{:S(2)}, u32[]{:S(2)}) collective-permute-start(f32[3,200,128]{2,1,0:T(8,128)} %get-tuple-element.56), channel_id=1, source_target_pairs={{0,488},{8,496},{16,504},{24,0},{32,8},{40,16},{48,24},{56,32},{64... | collective-permute-start | bytes 921608 | tf_op jit(solution)/shard_map/ppermute | solution.py:23
  33.4 2.6 %collective-permute-start.3 = (f32[3,200,128]{2,1,0:T(8,128)}, f32[3,200,128]{2,1,0:T(8,128)}, u32[]{:S(2)}, u32[]{:S(2)}) collective-permute-start(f32[3,200,128]{2,1,0:T(8,128)} %get-tuple-element.55), channel_id=1, source_target_pairs={{0,496},{8,504},{16,0},{24,8},{32,16},{40,24},{48,32},{56,40},{64,... | collective-permute-start | bytes 921608 | tf_op jit(solution)/shard_map/ppermute | solution.py:23
  36.1 2.5 %collective-permute-start.1 = (f32[3,200,128]{2,1,0:T(8,128)}, f32[3,200,128]{2,1,0:T(8,128)}, u32[]{:S(2)}, u32[]{:S(2)}) collective-permute-start(f32[3,200,128]{2,1,0:T(8,128)} %get-tuple-element.57), channel_id=1, source_target_pairs={{0,504},{8,0},{16,8},{24,16},{32,24},{40,32},{48,40},{56,48},{64,5... | collective-permute-start | bytes 921608 | tf_op jit(solution)/shard_map/ppermute | solution.py:23
  38.6 3.1 %collective-permute-start = (f32[3,200,128]{2,1,0:T(8,128)}, f32[3,200,128]{2,1,0:T(8,128)}, u32[]{:S(2)}, u32[]{:S(2)}) collective-permute-start(f32[3,200,128]{2,1,0:T(8,128)} %get-tuple-element.58), channel_id=1, source_target_pairs={{0,8},{8,16},{16,24},{24,32},{32,40},{40,48},{48,56},{56,64},{64,7... | collective-permute-start | bytes 921608 | tf_op jit(solution)/shard_map/ppermute | solution.py:23
  41.7 2.6 %collective-permute-start.4 = (f32[3,200,128]{2,1,0:T(8,128)}, f32[3,200,128]{2,1,0:T(8,128)}, u32[]{:S(2)}, u32[]{:S(2)}) collective-permute-start(f32[3,200,128]{2,1,0:T(8,128)} %get-tuple-element.54), channel_id=1, source_target_pairs={{0,16},{8,24},{16,32},{24,40},{32,48},{40,56},{48,64},{56,72},{64,... | collective-permute-start | bytes 921608 | tf_op jit(solution)/shard_map/ppermute | solution.py:23
  50.3 1.9 %collective-permute-start.5 = (f32[3,200,128]{2,1,0:T(8,128)}, f32[3,200,128]{2,1,0:T(8,128)S(1)}, u32[]{:S(2)}, u32[]{:S(2)}) collective-permute-start(f32[3,200,128]{2,1,0:T(8,128)} %get-tuple-element.53), channel_id=1, source_target_pairs={{0,24},{8,32},{16,40},{24,48},{32,56},{40,64},{48,72},{56,80},{64,... | collective-permute-start | bytes 921608 | tf_op jit(solution)/shard_map/ppermute | solution.py:23
  57.0 10.1 %collective-permute-done.5 = f32[3,200,128]{2,1,0:T(8,128)S(1)} collective-permute-done((f32[3,200,128]{2,1,0:T(8,128)}, f32[3,200,128]{2,1,0:T(8,128)S(1)}, u32[]{:S(2)}, u32[]{:S(2)}) %collective-permute-start.5) | collective-permute-done | bytes 307232 | tf_op jit(solution)/shard_map/ppermute | solution.py:23
  67.6 2.4 %fusion.3 = f32[192,128,16]{1,2,0:T(8,128)S(1)} fusion(f32[12,192,128]{2,1,0:T(8,128)S(1)} %fusion.16, f32[12,16]{1,0:T(8,128)S(1)} %gather_fusion.5, pred[12]{0:T(512)(128)(4,1)S(1)} %copy-done.20), kind=kOutput, calls=%fused_computation.17 | convolution fusion | flops 56623296 | bytes 2753292 | tf_op jit(solution)/shard_map/kb,kfn->fbn/dot_general | solution.py:71
  80.1 6.5 %all-to-all-start = ((bf16[8,2,8,2048]{3,2,1,0:T(8,128)(2,1)}), bf16[8,2,8,2048]{3,2,1,0:T(8,128)(2,1)S(1)}, u32[]{:S(2)}, u32[]{:S(2)}) async-start(bf16[8,2,8,2048]{3,2,1,0:T(8,128)(2,1)} %copy.126), calls=%async_computation | async-start | bytes 1048576 | tf_op jit(solution)/shard_map/all_to_all | solution.py:172
  87.9 9.4 %all-to-all-done = bf16[8,2,8,2048]{3,2,1,0:T(8,128)(2,1)S(1)} async-done(((bf16[8,2,8,2048]{3,2,1,0:T(8,128)(2,1)}), bf16[8,2,8,2048]{3,2,1,0:T(8,128)(2,1)S(1)}, u32[]{:S(2)}, u32[]{:S(2)}) %all-to-all-start) | async-done | bytes 524320 | tf_op jit(solution)/shard_map/all_to_all | solution.py:172
  99.6 1.8 %fusion.43 = f32[64,64]{1,0:T(8,128)} fusion(bf16[8,2,8,2048]{3,2,1,0:T(8,128)(2,1)S(1)} %all-to-all-done, bf16[64,16,128]{2,0,1:T(8,128)(2,1)} %copy-done.10), kind=kOutput, calls=%fused_computation.79 | convolution fusion | flops 16777216 | bytes 540672 | tf_op jit(solution)/shard_map/hn,cn->hc/dot_general | solution.py:177
  104.4 1.6 fusion.125
  108.4 6.6 %all-to-all-start.1 = ((f32[64,1,192]{2,1,0:T(1,128)}), f32[64,1,192]{2,1,0:T(1,128)S(1)}, u32[]{:S(2)}, u32[]{:S(2)}) async-start(f32[64,1,192]{2,1,0:T(1,128)} %all_to_all.16), calls=%async_computation.1 | async-start | bytes 131072 | tf_op jit(solution)/shard_map/all_to_all | solution.py:188
  115.8 13.9 %all-to-all-done.1 = f32[64,1,192]{2,1,0:T(1,128)S(1)} async-done(((f32[64,1,192]{2,1,0:T(1,128)}), f32[64,1,192]{2,1,0:T(1,128)S(1)}, u32[]{:S(2)}, u32[]{:S(2)}) %all-to-all-start.1) | async-done | bytes 49184 | tf_op jit(solution)/shard_map/all_to_all | solution.py:188
  129.7 2.2 %collective-permute-start.8 = (bf16[3,8,128]{2,1,0:T(8,128)(2,1)S(1)}, bf16[3,8,128]{2,1,0:T(8,128)(2,1)S(1)}, u32[]{:S(2)}, u32[]{:S(2)}) collective-permute-start(bf16[3,8,128]{2,1,0:T(8,128)(2,1)S(1)} %get-tuple-element.68), channel_id=1, source_target_pairs={{0,488},{8,496},{16,504},{24,0},{32,8},{40,16},{48,24},{56,32},{64... | collective-permute-start | bytes 18440 | tf_op jit(solution)/shard_map/ppermute | solution.py:23
  131.9 3.1 %collective-permute-start.6 = (bf16[3,8,128]{2,1,0:T(8,128)(2,1)S(1)}, bf16[3,8,128]{2,1,0:T(8,128)(2,1)S(1)}, u32[]{:S(2)}, u32[]{:S(2)}) collective-permute-start(bf16[3,8,128]{2,1,0:T(8,128)(2,1)S(1)} %get-tuple-element.70), channel_id=1, source_target_pairs={{0,8},{8,16},{16,24},{24,32},{32,40},{40,48},{48,56},{56,64},{64,7... | collective-permute-start | bytes 18440 | tf_op jit(solution)/shard_map/ppermute | solution.py:23
  135.0 4.9 %collective-permute-start.9 = (bf16[3,8,128]{2,1,0:T(8,128)(2,1)S(1)}, bf16[3,8,128]{2,1,0:T(8,128)(2,1)S(1)}, u32[]{:S(2)}, u32[]{:S(2)}) collective-permute-start(bf16[3,8,128]{2,1,0:T(8,128)(2,1)S(1)} %get-tuple-element.67), channel_id=1, source_target_pairs={{0,496},{8,504},{16,0},{24,8},{32,16},{40,24},{48,32},{56,40},{64,... | collective-permute-start | bytes 18440 | tf_op jit(solution)/shard_map/ppermute | solution.py:23
  140.0 1.9 %collective-permute-start.7 = (bf16[3,8,128]{2,1,0:T(8,128)(2,1)S(1)}, bf16[3,8,128]{2,1,0:T(8,128)(2,1)S(1)}, u32[]{:S(2)}, u32[]{:S(2)}) collective-permute-start(bf16[3,8,128]{2,1,0:T(8,128)(2,1)S(1)} %get-tuple-element.69), channel_id=1, source_target_pairs={{0,504},{8,0},{16,8},{24,16},{32,24},{40,32},{48,40},{56,48},{64,5... | collective-permute-start | bytes 18440 | tf_op jit(solution)/shard_map/ppermute | solution.py:23
  141.9 1.9 %collective-permute-start.10 = (bf16[3,8,128]{2,1,0:T(8,128)(2,1)S(1)}, bf16[3,8,128]{2,1,0:T(8,128)(2,1)S(1)}, u32[]{:S(2)}, u32[]{:S(2)}) collective-permute-start(bf16[3,8,128]{2,1,0:T(8,128)(2,1)S(1)} %get-tuple-element.66), channel_id=1, source_target_pairs={{0,16},{8,24},{16,32},{24,40},{32,48},{40,56},{48,64},{56,72},{64,... | collective-permute-start | bytes 18440 | tf_op jit(solution)/shard_map/ppermute | solution.py:23
  144.5 6.6 %all-to-all-start.2 = ((f32[64,1,192]{2,1,0:T(1,128)}), f32[64,1,192]{2,1,0:T(1,128)S(1)}, u32[]{:S(2)}, u32[]{:S(2)}) async-start(f32[64,1,192]{2,1,0:T(1,128)} %broadcast_in_dim.116), calls=%async_computation.2 | async-start | bytes 131072 | tf_op jit(solution)/shard_map/all_to_all | solution.py:207
  151.2 4.4 %collective-permute-start.11 = (bf16[3,8,128]{2,1,0:T(8,128)(2,1)S(1)}, bf16[3,8,128]{2,1,0:T(8,128)(2,1)S(1)}, u32[]{:S(2)}, u32[]{:S(2)}) collective-permute-start(bf16[3,8,128]{2,1,0:T(8,128)(2,1)S(1)} %get-tuple-element.65), channel_id=1, source_target_pairs={{0,24},{8,32},{16,40},{24,48},{32,56},{40,64},{48,72},{56,80},{64,... | collective-permute-start | bytes 18440 | tf_op jit(solution)/shard_map/ppermute | solution.py:23
  155.7 3.1 %collective-permute-done.11 = bf16[3,8,128]{2,1,0:T(8,128)(2,1)S(1)} collective-permute-done((bf16[3,8,128]{2,1,0:T(8,128)(2,1)S(1)}, bf16[3,8,128]{2,1,0:T(8,128)(2,1)S(1)}, u32[]{:S(2)}, u32[]{:S(2)}) %collective-permute-start.11) | collective-permute-done | bytes 6176 | tf_op jit(solution)/shard_map/ppermute | solution.py:23
  161.0 4.7 %all-to-all-done.2 = f32[64,1,192]{2,1,0:T(1,128)S(1)} async-done(((f32[64,1,192]{2,1,0:T(1,128)}), f32[64,1,192]{2,1,0:T(1,128)S(1)}, u32[]{:S(2)}, u32[]{:S(2)}) %all-to-all-start.2) | async-done | bytes 49184 | tf_op jit(solution)/shard_map/all_to_all | solution.py:207
  (192 shorter events, 52.5 us)
Async XLA Ops:
  2.1 42.3 %copy-start.16 = (f32[8,16,128]{2,0,1:T(8,128)}, f32[8,16,128]{2,0,1:T(8,128)S(1)}, u32[]{:S(2)}) copy-start(f32[8,16,128]{2,0,1:T(8,128)S(1)} %convolution_bitcast_fusion.2) | copy-start | bytes 196612
  3.4 41.0 %copy-start.15 = (f32[8,16,128]{2,0,1:T(8,128)}, f32[8,16,128]{2,0,1:T(8,128)S(1)}, u32[]{:S(2)}) copy-start(f32[8,16,128]{2,0,1:T(8,128)S(1)} %convolution_bitcast_fusion.1) | copy-start | bytes 196612
  10.0 34.3 %copy-start.26 = (s32[12]{0:T(128)}, s32[12]{0:T(128)S(1)}, u32[]{:S(2)}) copy-start(s32[12]{0:T(128)S(1)} %select_reduce_fusion) | copy-start | bytes 148
  19.9 26.5 %copy-start.23 = (s32[6,2]{0,1:T(2,128)S(1)}, s32[6,2]{0,1:T(2,128)}, u32[]{:S(2)}) copy-start(s32[6,2]{0,1:T(2,128)} %get-tuple-element.73) | copy-start | bytes 148
  19.9 30.4 %collective-permute-start.2 = (f32[3,200,128]{2,1,0:T(8,128)}, f32[3,200,128]{2,1,0:T(8,128)}, u32[]{:S(2)}, u32[]{:S(2)}) collective-permute-start(f32[3,200,128]{2,1,0:T(8,128)} %get-tuple-element.56), channel_id=1, source_target_pairs={{0,488},{8,496},{16,504},{24,0},{32,8},{40,16},{48,24},{56,32},{64... | collective-permute-start | bytes 921608 | tf_op jit(solution)/shard_map/ppermute | solution.py:23
  33.4 19.7 %collective-permute-start.3 = (f32[3,200,128]{2,1,0:T(8,128)}, f32[3,200,128]{2,1,0:T(8,128)}, u32[]{:S(2)}, u32[]{:S(2)}) collective-permute-start(f32[3,200,128]{2,1,0:T(8,128)} %get-tuple-element.55), channel_id=1, source_target_pairs={{0,496},{8,504},{16,0},{24,8},{32,16},{40,24},{48,32},{56,40},{64,... | collective-permute-start | bytes 921608 | tf_op jit(solution)/shard_map/ppermute | solution.py:23
  36.1 18.0 %collective-permute-start.1 = (f32[3,200,128]{2,1,0:T(8,128)}, f32[3,200,128]{2,1,0:T(8,128)}, u32[]{:S(2)}, u32[]{:S(2)}) collective-permute-start(f32[3,200,128]{2,1,0:T(8,128)} %get-tuple-element.57), channel_id=1, source_target_pairs={{0,504},{8,0},{16,8},{24,16},{32,24},{40,32},{48,40},{56,48},{64,5... | collective-permute-start | bytes 921608 | tf_op jit(solution)/shard_map/ppermute | solution.py:23
  38.6 16.5 %collective-permute-start = (f32[3,200,128]{2,1,0:T(8,128)}, f32[3,200,128]{2,1,0:T(8,128)}, u32[]{:S(2)}, u32[]{:S(2)}) collective-permute-start(f32[3,200,128]{2,1,0:T(8,128)} %get-tuple-element.58), channel_id=1, source_target_pairs={{0,8},{8,16},{16,24},{24,32},{32,40},{40,48},{48,56},{56,64},{64,7... | collective-permute-start | bytes 921608 | tf_op jit(solution)/shard_map/ppermute | solution.py:23
  41.7 14.4 %collective-permute-start.4 = (f32[3,200,128]{2,1,0:T(8,128)}, f32[3,200,128]{2,1,0:T(8,128)}, u32[]{:S(2)}, u32[]{:S(2)}) collective-permute-start(f32[3,200,128]{2,1,0:T(8,128)} %get-tuple-element.54), channel_id=1, source_target_pairs={{0,16},{8,24},{16,32},{24,40},{32,48},{40,56},{48,64},{56,72},{64,... | collective-permute-start | bytes 921608 | tf_op jit(solution)/shard_map/ppermute | solution.py:23
  49.7 17.4 %copy-start.20 = (pred[12]{0:T(512)(128)(4,1)S(1)}, pred[12]{0:T(512)(128)(4,1)}, u32[]{:S(2)}) copy-start(pred[12]{0:T(512)(128)(4,1)} %compare_and_fusion) | copy-start | bytes 40
  50.3 16.8 %collective-permute-start.5 = (f32[3,200,128]{2,1,0:T(8,128)}, f32[3,200,128]{2,1,0:T(8,128)S(1)}, u32[]{:S(2)}, u32[]{:S(2)}) collective-permute-start(f32[3,200,128]{2,1,0:T(8,128)} %get-tuple-element.53), channel_id=1, source_target_pairs={{0,24},{8,32},{16,40},{24,48},{32,56},{40,64},{48,72},{56,80},{64,... | collective-permute-start | bytes 921608 | tf_op jit(solution)/shard_map/ppermute | solution.py:23
  80.1 17.3 %all-to-all-start = ((bf16[8,2,8,2048]{3,2,1,0:T(8,128)(2,1)}), bf16[8,2,8,2048]{3,2,1,0:T(8,128)(2,1)S(1)}, u32[]{:S(2)}, u32[]{:S(2)}) async-start(bf16[8,2,8,2048]{3,2,1,0:T(8,128)(2,1)} %copy.126), calls=%async_computation | async-start | bytes 1048576 | tf_op jit(solution)/shard_map/all_to_all | solution.py:172
  104.4 27.6 %copy-start.12 = (bf16[8,2048]{1,0:T(8,128)(2,1)S(1)}, bf16[8,2048]{1,0:T(8,128)(2,1)}, u32[]{:S(2)}) copy-start(bf16[8,2048]{1,0:T(8,128)(2,1)} %copy-done.11) | copy-start | bytes 98308
  104.4 54.5 %copy-start.9 = (bf16[12,128,128]{2,1,0:T(8,128)(2,1)S(1)}, bf16[12,128,128]{2,1,0:T(8,128)(2,1)}, u32[]{:S(2)}) copy-start(bf16[12,128,128]{2,1,0:T(8,128)(2,1)} %gather_fusion.8) | copy-start | bytes 1179652
  104.4 54.5 %copy-start.21 = (pred[12]{0:T(512)(128)(4,1)S(1)}, pred[12]{0:T(512)(128)(4,1)}, u32[]{:S(2)}) copy-start(pred[12]{0:T(512)(128)(4,1)} %compare_and_fusion) | copy-start | bytes 40
  104.4 55.2 %copy-start.13 = (f32[16,8,128]{2,1,0:T(8,128)S(1)}, f32[16,8,128]{2,1,0:T(8,128)}, u32[]{:S(2)}) copy-start(f32[16,8,128]{2,1,0:T(8,128)} %fusion.21) | copy-start | bytes 196612
  108.4 21.3 %all-to-all-start.1 = ((f32[64,1,192]{2,1,0:T(1,128)}), f32[64,1,192]{2,1,0:T(1,128)S(1)}, u32[]{:S(2)}, u32[]{:S(2)}) async-start(f32[64,1,192]{2,1,0:T(1,128)} %all_to_all.16), calls=%async_computation.1 | async-start | bytes 131072 | tf_op jit(solution)/shard_map/all_to_all | solution.py:188
  129.7 21.5 %collective-permute-start.8 = (bf16[3,8,128]{2,1,0:T(8,128)(2,1)S(1)}, bf16[3,8,128]{2,1,0:T(8,128)(2,1)S(1)}, u32[]{:S(2)}, u32[]{:S(2)}) collective-permute-start(bf16[3,8,128]{2,1,0:T(8,128)(2,1)S(1)} %get-tuple-element.68), channel_id=1, source_target_pairs={{0,488},{8,496},{16,504},{24,0},{32,8},{40,16},{48,24},{56,32},{64... | collective-permute-start | bytes 18440 | tf_op jit(solution)/shard_map/ppermute | solution.py:23
  131.9 23.7 %collective-permute-start.6 = (bf16[3,8,128]{2,1,0:T(8,128)(2,1)S(1)}, bf16[3,8,128]{2,1,0:T(8,128)(2,1)S(1)}, u32[]{:S(2)}, u32[]{:S(2)}) collective-permute-start(bf16[3,8,128]{2,1,0:T(8,128)(2,1)S(1)} %get-tuple-element.70), channel_id=1, source_target_pairs={{0,8},{8,16},{16,24},{24,32},{32,40},{40,48},{48,56},{56,64},{64,7... | collective-permute-start | bytes 18440 | tf_op jit(solution)/shard_map/ppermute | solution.py:23
  135.0 20.6 %collective-permute-start.9 = (bf16[3,8,128]{2,1,0:T(8,128)(2,1)S(1)}, bf16[3,8,128]{2,1,0:T(8,128)(2,1)S(1)}, u32[]{:S(2)}, u32[]{:S(2)}) collective-permute-start(bf16[3,8,128]{2,1,0:T(8,128)(2,1)S(1)} %get-tuple-element.67), channel_id=1, source_target_pairs={{0,496},{8,504},{16,0},{24,8},{32,16},{40,24},{48,32},{56,40},{64,... | collective-permute-start | bytes 18440 | tf_op jit(solution)/shard_map/ppermute | solution.py:23
  140.0 15.7 %collective-permute-start.7 = (bf16[3,8,128]{2,1,0:T(8,128)(2,1)S(1)}, bf16[3,8,128]{2,1,0:T(8,128)(2,1)S(1)}, u32[]{:S(2)}, u32[]{:S(2)}) collective-permute-start(bf16[3,8,128]{2,1,0:T(8,128)(2,1)S(1)} %get-tuple-element.69), channel_id=1, source_target_pairs={{0,504},{8,0},{16,8},{24,16},{32,24},{40,32},{48,40},{56,48},{64,5... | collective-permute-start | bytes 18440 | tf_op jit(solution)/shard_map/ppermute | solution.py:23
  141.9 13.8 %collective-permute-start.10 = (bf16[3,8,128]{2,1,0:T(8,128)(2,1)S(1)}, bf16[3,8,128]{2,1,0:T(8,128)(2,1)S(1)}, u32[]{:S(2)}, u32[]{:S(2)}) collective-permute-start(bf16[3,8,128]{2,1,0:T(8,128)(2,1)S(1)} %get-tuple-element.66), channel_id=1, source_target_pairs={{0,16},{8,24},{16,32},{24,40},{32,48},{40,56},{48,64},{56,72},{64,... | collective-permute-start | bytes 18440 | tf_op jit(solution)/shard_map/ppermute | solution.py:23
  144.5 21.2 %all-to-all-start.2 = ((f32[64,1,192]{2,1,0:T(1,128)}), f32[64,1,192]{2,1,0:T(1,128)S(1)}, u32[]{:S(2)}, u32[]{:S(2)}) async-start(f32[64,1,192]{2,1,0:T(1,128)} %broadcast_in_dim.116), calls=%async_computation.2 | async-start | bytes 131072 | tf_op jit(solution)/shard_map/all_to_all | solution.py:207
  151.2 7.7 %collective-permute-start.11 = (bf16[3,8,128]{2,1,0:T(8,128)(2,1)S(1)}, bf16[3,8,128]{2,1,0:T(8,128)(2,1)S(1)}, u32[]{:S(2)}, u32[]{:S(2)}) collective-permute-start(bf16[3,8,128]{2,1,0:T(8,128)(2,1)S(1)} %get-tuple-element.65), channel_id=1, source_target_pairs={{0,24},{8,32},{16,40},{24,48},{32,56},{40,64},{48,72},{56,80},{64,... | collective-permute-start | bytes 18440 | tf_op jit(solution)/shard_map/ppermute | solution.py:23
  (23 other events, 142.1 us)

commit v14 on v12

--- a/solution.py
+++ b/solution.py
@@ -189,7 +189,11 @@
     )
 
     flat = jnp.concatenate([first_part.reshape(-1), second_part.reshape(-1)])
-    pieces = lax.all_to_all(flat.reshape(row_devices, -1), "row", 0, 0, tiled=True)
+    flat = flat + swap_with(flat, "row", 1)
+    halves = flat.reshape(row_devices, 2, -1)
+    own_half = lax.dynamic_index_in_dim(halves, me % 2, 1, keepdims=False)
+    arrived_halves = lax.all_to_all(own_half, "row", 0, 0, tiled=True)
+    pieces = arrived_halves.reshape(row_devices // 2, -1)
     class_blocks = class_in.reshape(c_rows, NB, BLK)
     class_pick = jnp.take(class_blocks.transpose(1, 0, 2), pick, axis=0)
     class_pick = class_pick.reshape(len(shifts()), 3, c_rows, BLK)

time: 168 us -> 170 us (1.012)
  starting transfers between devices: 64.6 us -> 66.4 us
    ppermute x0 -> x1, starting transfers between devices: none -> 3.76 us  [swap_with(): return lax.ppermute(x, axis, [(i, i ^ mask) for i in range(devices)])]
    all_to_all x1, starting transfers between devices: 6.8 us -> 5.05 us  [local(): arrived_halves = lax.all_to_all(own_half, 'row', 0, 0, tiled=True)]
    unnamed x59 -> x53, local copies, waits for them, and re-layouts: 7.5 us -> 7.49 us
  transfers between devices with their start and end apart: 15 -> 16, of which waited for: 5 -> 5; matrix products, arithmetic and copies ran while one was open for 9% -> 11% of each run, Pallas kernels for 0% -> 0%
where the time goes in v14:
time: 170 us; the launch traced here: 168 us
  starting transfers between devices  66.4 us (39%)
  waiting for transfers between devices  43.4 us (26%)
  local copies, waits for them, and re-layouts  28.7 us (17%)
  matrix products  16.6 us (10%)
  other arithmetic  12 us (7%)
    ppermute x12, starting transfers between devices, send_by(): lax.ppermute(x, axis, [(i, (i + by) % devices) for i in range(devices)])  44.4 us
    ppermute x12, waiting for transfers between devices, send_by(): lax.ppermute(x, axis, [(i, (i + by) % devices) for i in range(devices)])  13.2 us
    all_to_all x1, waiting for transfers between devices, local(): arrived_halves = lax.all_to_all(own_half, 'row', 0, 0, tiled=True)  13.1 us
    all_to_all x1, waiting for transfers between devices, local(): incoming = lax.all_to_all(outgoing, 'col', 0, 0, tiled=True)  12.3 us
    unnamed x53, local copies, waits for them, and re-layouts  7.49 us
    all_to_all x1, starting transfers between devices, local(): flat = lax.all_to_all(spread, 'row', 0, 0, tiled=True).reshape(-1)  6.73 us
    all_to_all x1, starting transfers between devices, local(): incoming = lax.all_to_all(outgoing, 'col', 0, 0, tiled=True)  6.48 us
    all_to_all x1, starting transfers between devices, local(): arrived_halves = lax.all_to_all(own_half, 'row', 0, 0, tiled=True)  5.05 us
  transfers between devices with their start and end apart: 16, of which 5 were waited for; matrix products, arithmetic and copies ran while one was open for 11% of the time, Pallas kernels for 0%

profile of v14, /device:TPU:1, one launch (start us, length us, event | category | flops | bytes accessed | tf_op | source)
XLA Modules:
  0.0 168.3 jit_solution(174818670335371731)
XLA Ops:
  15.2 1.7 gather_fusion.1
  19.9 13.4 %collective-permute-start.2 = (f32[3,200,128]{2,1,0:T(8,128)}, f32[3,200,128]{2,1,0:T(8,128)}, u32[]{:S(2)}, u32[]{:S(2)}) collective-permute-start(f32[3,200,128]{2,1,0:T(8,128)} %get-tuple-element.56), channel_id=1, source_target_pairs={{0,488},{8,496},{16,504},{24,0},{32,8},{40,16},{48,24},{56,32},{64... | collective-permute-start | bytes 921608 | tf_op jit(solution)/shard_map/ppermute | solution.py:23
  33.4 2.6 %collective-permute-start.3 = (f32[3,200,128]{2,1,0:T(8,128)}, f32[3,200,128]{2,1,0:T(8,128)}, u32[]{:S(2)}, u32[]{:S(2)}) collective-permute-start(f32[3,200,128]{2,1,0:T(8,128)} %get-tuple-element.55), channel_id=1, source_target_pairs={{0,496},{8,504},{16,0},{24,8},{32,16},{40,24},{48,32},{56,40},{64,... | collective-permute-start | bytes 921608 | tf_op jit(solution)/shard_map/ppermute | solution.py:23
  36.0 2.5 %collective-permute-start.1 = (f32[3,200,128]{2,1,0:T(8,128)}, f32[3,200,128]{2,1,0:T(8,128)}, u32[]{:S(2)}, u32[]{:S(2)}) collective-permute-start(f32[3,200,128]{2,1,0:T(8,128)} %get-tuple-element.57), channel_id=1, source_target_pairs={{0,504},{8,0},{16,8},{24,16},{32,24},{40,32},{48,40},{56,48},{64,5... | collective-permute-start | bytes 921608 | tf_op jit(solution)/shard_map/ppermute | solution.py:23
  38.5 3.1 %collective-permute-start = (f32[3,200,128]{2,1,0:T(8,128)}, f32[3,200,128]{2,1,0:T(8,128)}, u32[]{:S(2)}, u32[]{:S(2)}) collective-permute-start(f32[3,200,128]{2,1,0:T(8,128)} %get-tuple-element.58), channel_id=1, source_target_pairs={{0,8},{8,16},{16,24},{24,32},{32,40},{40,48},{48,56},{56,64},{64,7... | collective-permute-start | bytes 921608 | tf_op jit(solution)/shard_map/ppermute | solution.py:23
  41.6 2.6 %collective-permute-start.4 = (f32[3,200,128]{2,1,0:T(8,128)}, f32[3,200,128]{2,1,0:T(8,128)}, u32[]{:S(2)}, u32[]{:S(2)}) collective-permute-start(f32[3,200,128]{2,1,0:T(8,128)} %get-tuple-element.54), channel_id=1, source_target_pairs={{0,16},{8,24},{16,32},{24,40},{32,48},{40,56},{48,64},{56,72},{64,... | collective-permute-start | bytes 921608 | tf_op jit(solution)/shard_map/ppermute | solution.py:23
  44.3 1.5 fusion.24
  51.5 1.9 %collective-permute-start.5 = (f32[3,200,128]{2,1,0:T(8,128)}, f32[3,200,128]{2,1,0:T(8,128)S(1)}, u32[]{:S(2)}, u32[]{:S(2)}) collective-permute-start(f32[3,200,128]{2,1,0:T(8,128)} %get-tuple-element.53), channel_id=1, source_target_pairs={{0,24},{8,32},{16,40},{24,48},{32,56},{40,64},{48,72},{56,80},{64,... | collective-permute-start | bytes 921608 | tf_op jit(solution)/shard_map/ppermute | solution.py:23
  58.3 10.1 %collective-permute-done.5 = f32[3,200,128]{2,1,0:T(8,128)S(1)} collective-permute-done((f32[3,200,128]{2,1,0:T(8,128)}, f32[3,200,128]{2,1,0:T(8,128)S(1)}, u32[]{:S(2)}, u32[]{:S(2)}) %collective-permute-start.5) | collective-permute-done | bytes 307232 | tf_op jit(solution)/shard_map/ppermute | solution.py:23
  68.9 2.4 %fusion.2 = f32[192,128,16]{1,2,0:T(8,128)S(1)} fusion(f32[12,192,128]{2,1,0:T(8,128)S(1)} %fusion.15, f32[12,16]{1,0:T(8,128)S(1)} %gather_fusion.5, pred[12]{0:T(512)(128)(4,1)S(1)} %compare_and_fusion), kind=kOutput, calls=%fused_computation.15 | convolution fusion | flops 56623296 | bytes 2753292 | tf_op jit(solution)/shard_map/kb,kfn->fbn/dot_general | solution.py:71
  80.8 6.5 %all-to-all-start = ((bf16[8,3,8,2048]{3,2,1,0:T(8,128)(2,1)}), bf16[8,3,8,2048]{3,2,1,0:T(8,128)(2,1)}, u32[]{:S(2)}, u32[]{:S(2)}) async-start(bf16[8,3,8,2048]{3,2,1,0:T(8,128)(2,1)} %copy.126), calls=%async_computation | async-start | bytes 1572864 | tf_op jit(solution)/shard_map/all_to_all | solution.py:174
  88.6 12.3 %all-to-all-done = bf16[8,3,8,2048]{3,2,1,0:T(8,128)(2,1)} async-done(((bf16[8,3,8,2048]{3,2,1,0:T(8,128)(2,1)}), bf16[8,3,8,2048]{3,2,1,0:T(8,128)(2,1)}, u32[]{:S(2)}, u32[]{:S(2)}) %all-to-all-start) | async-done | bytes 786464 | tf_op jit(solution)/shard_map/all_to_all | solution.py:174
  104.8 3.8 %collective-permute-start.6 = (f32[12288]{0:T(1024)S(1)}, f32[12288]{0:T(1024)S(1)}, u32[]{:S(2)}, u32[]{:S(2)}) collective-permute-start(f32[12288]{0:T(1024)S(1)} %constant_dynamic-update-slice_fusion.7), channel_id=1, source_target_pairs={{0,8},{8,0},{16,24},{24,16},{32,40},{40,32},{48,56},{56,48},{64,72... | collective-permute-start | bytes 147464 | tf_op jit(solution)/shard_map/ppermute | solution.py:28
  111.4 5.0 %all-to-all-start.1 = ((f32[64,1,96]{2,1,0:T(1,128)}), f32[64,1,96]{2,1,0:T(1,128)S(1)}, u32[]{:S(2)}, u32[]{:S(2)}) async-start(f32[64,1,96]{2,1,0:T(1,128)} %constant_dynamic-slice_fusion), calls=%async_computation.1 | async-start | bytes 65536 | tf_op jit(solution)/shard_map/all_to_all | solution.py:195
  116.6 13.1 %all-to-all-done.1 = f32[64,1,96]{2,1,0:T(1,128)S(1)} async-done(((f32[64,1,96]{2,1,0:T(1,128)}), f32[64,1,96]{2,1,0:T(1,128)S(1)}, u32[]{:S(2)}, u32[]{:S(2)}) %all-to-all-start.1) | async-done | bytes 24608 | tf_op jit(solution)/shard_map/all_to_all | solution.py:195
  131.0 2.5 %collective-permute-start.9 = (bf16[3,8,128]{2,1,0:T(8,128)(2,1)S(1)}, bf16[3,8,128]{2,1,0:T(8,128)(2,1)S(1)}, u32[]{:S(2)}, u32[]{:S(2)}) collective-permute-start(bf16[3,8,128]{2,1,0:T(8,128)(2,1)S(1)} %get-tuple-element.70), channel_id=1, source_target_pairs={{0,488},{8,496},{16,504},{24,0},{32,8},{40,16},{48,24},{56,32},{64... | collective-permute-start | bytes 18440 | tf_op jit(solution)/shard_map/ppermute | solution.py:23
  133.6 2.8 %collective-permute-start.7 = (bf16[3,8,128]{2,1,0:T(8,128)(2,1)S(1)}, bf16[3,8,128]{2,1,0:T(8,128)(2,1)S(1)}, u32[]{:S(2)}, u32[]{:S(2)}) collective-permute-start(bf16[3,8,128]{2,1,0:T(8,128)(2,1)S(1)} %get-tuple-element.72), channel_id=1, source_target_pairs={{0,8},{8,16},{16,24},{24,32},{32,40},{40,48},{48,56},{56,64},{64,7... | collective-permute-start | bytes 18440 | tf_op jit(solution)/shard_map/ppermute | solution.py:23
  136.4 4.5 %collective-permute-start.10 = (bf16[3,8,128]{2,1,0:T(8,128)(2,1)S(1)}, bf16[3,8,128]{2,1,0:T(8,128)(2,1)S(1)}, u32[]{:S(2)}, u32[]{:S(2)}) collective-permute-start(bf16[3,8,128]{2,1,0:T(8,128)(2,1)S(1)} %get-tuple-element.69), channel_id=1, source_target_pairs={{0,496},{8,504},{16,0},{24,8},{32,16},{40,24},{48,32},{56,40},{64,... | collective-permute-start | bytes 18440 | tf_op jit(solution)/shard_map/ppermute | solution.py:23
  140.9 1.9 %collective-permute-start.8 = (bf16[3,8,128]{2,1,0:T(8,128)(2,1)S(1)}, bf16[3,8,128]{2,1,0:T(8,128)(2,1)S(1)}, u32[]{:S(2)}, u32[]{:S(2)}) collective-permute-start(bf16[3,8,128]{2,1,0:T(8,128)(2,1)S(1)} %get-tuple-element.71), channel_id=1, source_target_pairs={{0,504},{8,0},{16,8},{24,16},{32,24},{40,32},{48,40},{56,48},{64,5... | collective-permute-start | bytes 18440 | tf_op jit(solution)/shard_map/ppermute | solution.py:23
  142.8 1.9 %collective-permute-start.11 = (bf16[3,8,128]{2,1,0:T(8,128)(2,1)S(1)}, bf16[3,8,128]{2,1,0:T(8,128)(2,1)S(1)}, u32[]{:S(2)}, u32[]{:S(2)}) collective-permute-start(bf16[3,8,128]{2,1,0:T(8,128)(2,1)S(1)} %get-tuple-element.68), channel_id=1, source_target_pairs={{0,16},{8,24},{16,32},{24,40},{32,48},{40,56},{48,64},{56,72},{64,... | collective-permute-start | bytes 18440 | tf_op jit(solution)/shard_map/ppermute | solution.py:23
  145.5 6.7 %all-to-all-start.2 = ((f32[64,1,192]{2,1,0:T(1,128)}), f32[64,1,192]{2,1,0:T(1,128)S(1)}, u32[]{:S(2)}, u32[]{:S(2)}) async-start(f32[64,1,192]{2,1,0:T(1,128)} %broadcast_in_dim.116), calls=%async_computation.2 | async-start | bytes 131072 | tf_op jit(solution)/shard_map/all_to_all | solution.py:215
  152.2 4.4 %collective-permute-start.12 = (bf16[3,8,128]{2,1,0:T(8,128)(2,1)S(1)}, bf16[3,8,128]{2,1,0:T(8,128)(2,1)S(1)}, u32[]{:S(2)}, u32[]{:S(2)}) collective-permute-start(bf16[3,8,128]{2,1,0:T(8,128)(2,1)S(1)} %get-tuple-element.67), channel_id=1, source_target_pairs={{0,24},{8,32},{16,40},{24,48},{32,56},{40,64},{48,72},{56,80},{64,... | collective-permute-start | bytes 18440 | tf_op jit(solution)/shard_map/ppermute | solution.py:23
  156.7 3.1 %collective-permute-done.12 = bf16[3,8,128]{2,1,0:T(8,128)(2,1)S(1)} collective-permute-done((bf16[3,8,128]{2,1,0:T(8,128)(2,1)S(1)}, bf16[3,8,128]{2,1,0:T(8,128)(2,1)S(1)}, u32[]{:S(2)}, u32[]{:S(2)}) %collective-permute-start.12) | collective-permute-done | bytes 6176 | tf_op jit(solution)/shard_map/ppermute | solution.py:23
  162.0 4.8 %all-to-all-done.2 = f32[64,1,192]{2,1,0:T(1,128)S(1)} async-done(((f32[64,1,192]{2,1,0:T(1,128)}), f32[64,1,192]{2,1,0:T(1,128)S(1)}, u32[]{:S(2)}, u32[]{:S(2)}) %all-to-all-start.2) | async-done | bytes 49184 | tf_op jit(solution)/shard_map/all_to_all | solution.py:215
  (181 shorter events, 51.7 us)
Async XLA Ops:
  0.6 13.3 %copy-start = (bf16[12,128,128]{2,1,0:T(8,128)(2,1)S(1)}, bf16[12,128,128]{2,1,0:T(8,128)(2,1)}, u32[]{:S(2)}) copy-start(bf16[12,128,128]{2,1,0:T(8,128)(2,1)} %param.22) | copy-start | bytes 1179652
  0.7 12.3 %copy-start.5 = (bf16[128,2048]{1,0:T(8,128)(2,1)S(1)}, bf16[128,2048]{1,0:T(8,128)(2,1)}, u32[]{:S(2)}) copy-start(bf16[128,2048]{1,0:T(8,128)(2,1)} %param.17) | copy-start | bytes 1572868
  2.1 42.2 %copy-start.11 = (f32[8,16,128]{2,0,1:T(8,128)}, f32[8,16,128]{2,0,1:T(8,128)S(1)}, u32[]{:S(2)}) copy-start(f32[8,16,128]{2,0,1:T(8,128)S(1)} %convolution_bitcast_fusion.2) | copy-start | bytes 196612
  3.4 40.9 %copy-start.10 = (f32[8,16,128]{2,0,1:T(8,128)}, f32[8,16,128]{2,0,1:T(8,128)S(1)}, u32[]{:S(2)}) copy-start(f32[8,16,128]{2,0,1:T(8,128)S(1)} %convolution_bitcast_fusion.1) | copy-start | bytes 196612
  10.0 34.2 %copy-start.17 = (s32[12]{0:T(128)}, s32[12]{0:T(128)S(1)}, u32[]{:S(2)}) copy-start(s32[12]{0:T(128)S(1)} %select_reduce_fusion) | copy-start | bytes 148
  19.9 31.6 %collective-permute-start.2 = (f32[3,200,128]{2,1,0:T(8,128)}, f32[3,200,128]{2,1,0:T(8,128)}, u32[]{:S(2)}, u32[]{:S(2)}) collective-permute-start(f32[3,200,128]{2,1,0:T(8,128)} %get-tuple-element.56), channel_id=1, source_target_pairs={{0,488},{8,496},{16,504},{24,0},{32,8},{40,16},{48,24},{56,32},{64... | collective-permute-start | bytes 921608 | tf_op jit(solution)/shard_map/ppermute | solution.py:23
  33.4 21.1 %collective-permute-start.3 = (f32[3,200,128]{2,1,0:T(8,128)}, f32[3,200,128]{2,1,0:T(8,128)}, u32[]{:S(2)}, u32[]{:S(2)}) collective-permute-start(f32[3,200,128]{2,1,0:T(8,128)} %get-tuple-element.55), channel_id=1, source_target_pairs={{0,496},{8,504},{16,0},{24,8},{32,16},{40,24},{48,32},{56,40},{64,... | collective-permute-start | bytes 921608 | tf_op jit(solution)/shard_map/ppermute | solution.py:23
  36.0 19.4 %collective-permute-start.1 = (f32[3,200,128]{2,1,0:T(8,128)}, f32[3,200,128]{2,1,0:T(8,128)}, u32[]{:S(2)}, u32[]{:S(2)}) collective-permute-start(f32[3,200,128]{2,1,0:T(8,128)} %get-tuple-element.57), channel_id=1, source_target_pairs={{0,504},{8,0},{16,8},{24,16},{32,24},{40,32},{48,40},{56,48},{64,5... | collective-permute-start | bytes 921608 | tf_op jit(solution)/shard_map/ppermute | solution.py:23
  38.5 17.9 %collective-permute-start = (f32[3,200,128]{2,1,0:T(8,128)}, f32[3,200,128]{2,1,0:T(8,128)}, u32[]{:S(2)}, u32[]{:S(2)}) collective-permute-start(f32[3,200,128]{2,1,0:T(8,128)} %get-tuple-element.58), channel_id=1, source_target_pairs={{0,8},{8,16},{16,24},{24,32},{32,40},{40,48},{48,56},{56,64},{64,7... | collective-permute-start | bytes 921608 | tf_op jit(solution)/shard_map/ppermute | solution.py:23
  41.6 15.7 %collective-permute-start.4 = (f32[3,200,128]{2,1,0:T(8,128)}, f32[3,200,128]{2,1,0:T(8,128)}, u32[]{:S(2)}, u32[]{:S(2)}) collective-permute-start(f32[3,200,128]{2,1,0:T(8,128)} %get-tuple-element.54), channel_id=1, source_target_pairs={{0,16},{8,24},{16,32},{24,40},{32,48},{40,56},{48,64},{56,72},{64,... | collective-permute-start | bytes 921608 | tf_op jit(solution)/shard_map/ppermute | solution.py:23
  51.0 17.4 %copy-start.8 = (bf16[12,128,128]{2,1,0:T(8,128)(2,1)S(1)}, bf16[12,128,128]{2,1,0:T(8,128)(2,1)}, u32[]{:S(2)}) copy-start(bf16[12,128,128]{2,1,0:T(8,128)(2,1)} %gather_fusion.8) | copy-start | bytes 1179652
  51.5 16.8 %collective-permute-start.5 = (f32[3,200,128]{2,1,0:T(8,128)}, f32[3,200,128]{2,1,0:T(8,128)S(1)}, u32[]{:S(2)}, u32[]{:S(2)}) collective-permute-start(f32[3,200,128]{2,1,0:T(8,128)} %get-tuple-element.53), channel_id=1, source_target_pairs={{0,24},{8,32},{16,40},{24,48},{32,56},{40,64},{48,72},{56,80},{64,... | collective-permute-start | bytes 921608 | tf_op jit(solution)/shard_map/ppermute | solution.py:23
  80.8 20.1 %all-to-all-start = ((bf16[8,3,8,2048]{3,2,1,0:T(8,128)(2,1)}), bf16[8,3,8,2048]{3,2,1,0:T(8,128)(2,1)}, u32[]{:S(2)}, u32[]{:S(2)}) async-start(bf16[8,3,8,2048]{3,2,1,0:T(8,128)(2,1)} %copy.126), calls=%async_computation | async-start | bytes 1572864 | tf_op jit(solution)/shard_map/all_to_all | solution.py:174
  88.6 13.8 %copy-start.6 = (f32[128,16,128]{0,2,1:T(8,128)S(1)}, f32[128,16,128]{0,2,1:T(8,128)}, u32[]{:S(2)}) copy-start(f32[128,16,128]{0,2,1:T(8,128)} %copy.127) | copy-start | bytes 3145732
  103.5 56.4 %copy-start.9 = (bf16[12,128,128]{2,1,0:T(8,128)(2,1)S(1)}, bf16[12,128,128]{2,1,0:T(8,128)(2,1)}, u32[]{:S(2)}) copy-start(bf16[12,128,128]{2,1,0:T(8,128)(2,1)} %gather_fusion.8) | copy-start | bytes 1179652
  104.8 5.8 %collective-permute-start.6 = (f32[12288]{0:T(1024)S(1)}, f32[12288]{0:T(1024)S(1)}, u32[]{:S(2)}, u32[]{:S(2)}) collective-permute-start(f32[12288]{0:T(1024)S(1)} %constant_dynamic-update-slice_fusion.7), channel_id=1, source_target_pairs={{0,8},{8,0},{16,24},{24,16},{32,40},{40,32},{48,56},{56,48},{64,72... | collective-permute-start | bytes 147464 | tf_op jit(solution)/shard_map/ppermute | solution.py:28
  111.4 18.2 %all-to-all-start.1 = ((f32[64,1,96]{2,1,0:T(1,128)}), f32[64,1,96]{2,1,0:T(1,128)S(1)}, u32[]{:S(2)}, u32[]{:S(2)}) async-start(f32[64,1,96]{2,1,0:T(1,128)} %constant_dynamic-slice_fusion), calls=%async_computation.1 | async-start | bytes 65536 | tf_op jit(solution)/shard_map/all_to_all | solution.py:195
  131.0 21.2 %collective-permute-start.9 = (bf16[3,8,128]{2,1,0:T(8,128)(2,1)S(1)}, bf16[3,8,128]{2,1,0:T(8,128)(2,1)S(1)}, u32[]{:S(2)}, u32[]{:S(2)}) collective-permute-start(bf16[3,8,128]{2,1,0:T(8,128)(2,1)S(1)} %get-tuple-element.70), channel_id=1, source_target_pairs={{0,488},{8,496},{16,504},{24,0},{32,8},{40,16},{48,24},{56,32},{64... | collective-permute-start | bytes 18440 | tf_op jit(solution)/shard_map/ppermute | solution.py:23
  133.6 23.1 %collective-permute-start.7 = (bf16[3,8,128]{2,1,0:T(8,128)(2,1)S(1)}, bf16[3,8,128]{2,1,0:T(8,128)(2,1)S(1)}, u32[]{:S(2)}, u32[]{:S(2)}) collective-permute-start(bf16[3,8,128]{2,1,0:T(8,128)(2,1)S(1)} %get-tuple-element.72), channel_id=1, source_target_pairs={{0,8},{8,16},{16,24},{24,32},{32,40},{40,48},{48,56},{56,64},{64,7... | collective-permute-start | bytes 18440 | tf_op jit(solution)/shard_map/ppermute | solution.py:23
  136.4 20.3 %collective-permute-start.10 = (bf16[3,8,128]{2,1,0:T(8,128)(2,1)S(1)}, bf16[3,8,128]{2,1,0:T(8,128)(2,1)S(1)}, u32[]{:S(2)}, u32[]{:S(2)}) collective-permute-start(bf16[3,8,128]{2,1,0:T(8,128)(2,1)S(1)} %get-tuple-element.69), channel_id=1, source_target_pairs={{0,496},{8,504},{16,0},{24,8},{32,16},{40,24},{48,32},{56,40},{64,... | collective-permute-start | bytes 18440 | tf_op jit(solution)/shard_map/ppermute | solution.py:23
  140.9 15.8 %collective-permute-start.8 = (bf16[3,8,128]{2,1,0:T(8,128)(2,1)S(1)}, bf16[3,8,128]{2,1,0:T(8,128)(2,1)S(1)}, u32[]{:S(2)}, u32[]{:S(2)}) collective-permute-start(bf16[3,8,128]{2,1,0:T(8,128)(2,1)S(1)} %get-tuple-element.71), channel_id=1, source_target_pairs={{0,504},{8,0},{16,8},{24,16},{32,24},{40,32},{48,40},{56,48},{64,5... | collective-permute-start | bytes 18440 | tf_op jit(solution)/shard_map/ppermute | solution.py:23
  142.8 13.9 %collective-permute-start.11 = (bf16[3,8,128]{2,1,0:T(8,128)(2,1)S(1)}, bf16[3,8,128]{2,1,0:T(8,128)(2,1)S(1)}, u32[]{:S(2)}, u32[]{:S(2)}) collective-permute-start(bf16[3,8,128]{2,1,0:T(8,128)(2,1)S(1)} %get-tuple-element.68), channel_id=1, source_target_pairs={{0,16},{8,24},{16,32},{24,40},{32,48},{40,56},{48,64},{56,72},{64,... | collective-permute-start | bytes 18440 | tf_op jit(solution)/shard_map/ppermute | solution.py:23
  145.5 21.3 %all-to-all-start.2 = ((f32[64,1,192]{2,1,0:T(1,128)}), f32[64,1,192]{2,1,0:T(1,128)S(1)}, u32[]{:S(2)}, u32[]{:S(2)}) async-start(f32[64,1,192]{2,1,0:T(1,128)} %broadcast_in_dim.116), calls=%async_computation.2 | async-start | bytes 131072 | tf_op jit(solution)/shard_map/all_to_all | solution.py:215
  152.2 7.7 %collective-permute-start.12 = (bf16[3,8,128]{2,1,0:T(8,128)(2,1)S(1)}, bf16[3,8,128]{2,1,0:T(8,128)(2,1)S(1)}, u32[]{:S(2)}, u32[]{:S(2)}) collective-permute-start(bf16[3,8,128]{2,1,0:T(8,128)(2,1)S(1)} %get-tuple-element.67), channel_id=1, source_target_pairs={{0,24},{8,32},{16,40},{24,48},{32,56},{40,64},{48,72},{56,80},{64,... | collective-permute-start | bytes 18440 | tf_op jit(solution)/shard_map/ppermute | solution.py:23
  (15 other events, 71.7 us)

commit v15 on v12

--- a/solution.py
+++ b/solution.py
@@ -136,7 +136,10 @@
     picked = jnp.take(both_blocks.transpose(1, 0, 2), pick, axis=0)
     picked = picked.reshape(len(shifts()), 3, hf_rows, BLK).astype(jnp.float32)
     send_all = jnp.concatenate([picked, sg_send], 2)
-    arrived = [send_by(send_all[i], "row", e) for i, e in enumerate(shifts())]
+    arrived = [
+        send_by(send_all[i] if abs(e) == 1 else send_all[i, :2], "row", e)
+        for i, e in enumerate(shifts())
+    ]
     pairs_in = jnp.concatenate([a[:2] for a in arrived], 0)
 
     both_sum = forward_sum(

time: 168 us -> 179 us (1.065)
  local copies, waits for them, and re-layouts: 27.9 us -> 36.1 us
  waiting for transfers between devices: 44 us -> 39.3 us
  other arithmetic: 11.5 us -> 15.2 us
  matrix products: 17.2 us -> 20.6 us
    ppermute x12, waiting for transfers between devices: 13.2 us -> 9.73 us  [send_by(): lax.ppermute(x, axis, [(i, (i + by) % devices) for i in range(devices)])]
    convert_element_type x2, local copies, waits for them, and re-layouts: 0.29 us -> 2.67 us  [local(): hidden_act = jax.nn.silu(hidden_sum).astype(jnp.bfloat16)]
    unnamed x59 -> x69, local copies, waits for them, and re-layouts: 7.5 us -> 7.14 us
  transfers between devices with their start and end apart: 15 -> 15, of which waited for: 5 -> 5; matrix products, arithmetic and copies ran while one was open for 9% -> 10% of each run, Pallas kernels for 0% -> 0%
where the time goes in v15:
time: 179 us; the launch traced here: 177 us
  starting transfers between devices  64.7 us (36%)
  waiting for transfers between devices  39.3 us (22%)
  local copies, waits for them, and re-layouts  36.1 us (20%)
  matrix products  20.6 us (12%)
  other arithmetic  15.2 us (8%)
    ppermute x12, starting transfers between devices, send_by(): lax.ppermute(x, axis, [(i, (i + by) % devices) for i in range(devices)])  45 us
    all_to_all x1, waiting for transfers between devices, local(): lax.all_to_all(flat.reshape(row_devices, -1), 'row', 0, 0, tiled=True)  13.9 us
    all_to_all x1, waiting for transfers between devices, local(): incoming = lax.all_to_all(outgoing, 'col', 0, 0, tiled=True)  10.9 us
    ppermute x12, waiting for transfers between devices, send_by(): lax.ppermute(x, axis, [(i, (i + by) % devices) for i in range(devices)])  9.73 us
    unnamed x69, local copies, waits for them, and re-layouts  7.14 us
    all_to_all x1, starting transfers between devices, local(): lax.all_to_all(flat.reshape(row_devices, -1), 'row', 0, 0, tiled=True)  6.75 us
    all_to_all x1, starting transfers between devices, local(): flat = lax.all_to_all(spread, 'row', 0, 0, tiled=True).reshape(-1)  6.65 us
    all_to_all x1, starting transfers between devices, local(): incoming = lax.all_to_all(outgoing, 'col', 0, 0, tiled=True)  6.37 us
  transfers between devices with their start and end apart: 15, of which 5 were waited for; matrix products, arithmetic and copies ran while one was open for 10% of the time, Pallas kernels for 0%

profile of v15, /device:TPU:1, one launch (start us, length us, event | category | flops | bytes accessed | tf_op | source)
XLA Modules:
  0.0 177.4 jit_solution(10700272241637261580)
XLA Ops:
  11.0 2.0 %convolution_bitcast_fusion.1 = f32[8,16,128]{2,0,1:T(8,128)} fusion(bf16[16,3,128,128]{3,2,1,0:T(8,128)(2,1)} %param.21, bf16[8,2048]{1,0:T(8,128)(2,1)} %param.20), kind=kOutput, calls=%fused_computation.22 | convolution fusion | flops 4194304 | bytes 622592 | tf_op jit(solution)/shard_map/fbn,bnm->fbm/dot_general | solution.py:123
  17.9 1.6 gather_fusion.1
  26.6 13.4 %collective-permute-start.2 = (f32[2,200,128]{2,1,0:T(8,128)}, f32[2,200,128]{2,1,0:T(8,128)}, u32[]{:S(2)}, u32[]{:S(2)}) collective-permute-start(f32[2,200,128]{2,1,0:T(8,128)} %get-tuple-element.56), channel_id=1, source_target_pairs={{0,488},{8,496},{16,504},{24,0},{32,8},{40,16},{48,24},{56,32},{64... | collective-permute-start | bytes 614408 | tf_op jit(solution)/shard_map/ppermute | solution.py:23
  40.1 2.8 %collective-permute-start.3 = (f32[2,200,128]{2,1,0:T(8,128)}, f32[2,200,128]{2,1,0:T(8,128)}, u32[]{:S(2)}, u32[]{:S(2)}) collective-permute-start(f32[2,200,128]{2,1,0:T(8,128)} %get-tuple-element.55), channel_id=1, source_target_pairs={{0,496},{8,504},{16,0},{24,8},{32,16},{40,24},{48,32},{56,40},{64,... | collective-permute-start | bytes 614408 | tf_op jit(solution)/shard_map/ppermute | solution.py:23
  43.9 2.6 %collective-permute-start.1 = (f32[3,200,128]{2,1,0:T(8,128)}, f32[3,200,128]{2,1,0:T(8,128)}, u32[]{:S(2)}, u32[]{:S(2)}) collective-permute-start(f32[3,200,128]{2,1,0:T(8,128)} %get-tuple-element.58), channel_id=1, source_target_pairs={{0,504},{8,0},{16,8},{24,16},{32,24},{40,32},{48,40},{56,48},{64,5... | collective-permute-start | bytes 921608 | tf_op jit(solution)/shard_map/ppermute | solution.py:23
  46.5 3.1 %collective-permute-start = (f32[3,200,128]{2,1,0:T(8,128)}, f32[3,200,128]{2,1,0:T(8,128)}, u32[]{:S(2)}, u32[]{:S(2)}) collective-permute-start(f32[3,200,128]{2,1,0:T(8,128)} %get-tuple-element.57), channel_id=1, source_target_pairs={{0,8},{8,16},{16,24},{24,32},{32,40},{40,48},{48,56},{56,64},{64,7... | collective-permute-start | bytes 921608 | tf_op jit(solution)/shard_map/ppermute | solution.py:23
  49.6 2.6 %collective-permute-start.4 = (f32[2,200,128]{2,1,0:T(8,128)}, f32[2,200,128]{2,1,0:T(8,128)}, u32[]{:S(2)}, u32[]{:S(2)}) collective-permute-start(f32[2,200,128]{2,1,0:T(8,128)} %get-tuple-element.54), channel_id=1, source_target_pairs={{0,16},{8,24},{16,32},{24,40},{32,48},{40,56},{48,64},{56,72},{64,... | collective-permute-start | bytes 614408 | tf_op jit(solution)/shard_map/ppermute | solution.py:23
  58.6 1.9 %collective-permute-start.5 = (f32[2,200,128]{2,1,0:T(8,128)S(1)}, f32[2,200,128]{2,1,0:T(8,128)S(1)}, u32[]{:S(2)}, u32[]{:S(2)}) collective-permute-start(f32[2,200,128]{2,1,0:T(8,128)S(1)} %copy-done.13), channel_id=1, source_target_pairs={{0,24},{8,32},{16,40},{24,48},{32,56},{40,64},{48,72},{56,80},{64,... | collective-permute-start | bytes 614408 | tf_op jit(solution)/shard_map/ppermute | solution.py:23
  65.3 6.6 %collective-permute-done.5 = f32[2,200,128]{2,1,0:T(8,128)S(1)} collective-permute-done((f32[2,200,128]{2,1,0:T(8,128)S(1)}, f32[2,200,128]{2,1,0:T(8,128)S(1)}, u32[]{:S(2)}, u32[]{:S(2)}) %collective-permute-start.5) | collective-permute-done | bytes 204832 | tf_op jit(solution)/shard_map/ppermute | solution.py:23
  73.0 2.4 %fusion.2 = f32[192,128,16]{1,2,0:T(8,128)S(1)} fusion(f32[12,192,128]{2,1,0:T(8,128)S(1)} %fusion.15, f32[12,16]{1,0:T(8,128)S(1)} %gather_fusion.5, pred[12]{0:T(512)(128)(4,1)S(1)} %compare_and_fusion), kind=kOutput, calls=%fused_computation.15 | convolution fusion | flops 56623296 | bytes 2753292 | tf_op jit(solution)/shard_map/kb,kfn->fbn/dot_general | solution.py:71
  81.2 1.8 reshape.553
  88.8 6.4 %all-to-all-start = ((bf16[8,3,8,2048]{3,2,1,0:T(8,128)(2,1)}), bf16[8,3,8,2048]{3,2,1,0:T(8,128)(2,1)}, u32[]{:S(2)}, u32[]{:S(2)}) async-start(bf16[8,3,8,2048]{3,2,1,0:T(8,128)(2,1)} %copy.126), calls=%async_computation | async-start | bytes 1572864 | tf_op jit(solution)/shard_map/all_to_all | solution.py:177
  97.9 10.9 %all-to-all-done = bf16[8,3,8,2048]{3,2,1,0:T(8,128)(2,1)} async-done(((bf16[8,3,8,2048]{3,2,1,0:T(8,128)(2,1)}), bf16[8,3,8,2048]{3,2,1,0:T(8,128)(2,1)}, u32[]{:S(2)}, u32[]{:S(2)}) %all-to-all-start) | async-done | bytes 786464 | tf_op jit(solution)/shard_map/all_to_all | solution.py:177
  118.4 6.7 %all-to-all-start.1 = ((f32[64,1,192]{2,1,0:T(1,128)}), f32[64,1,192]{2,1,0:T(1,128)S(1)}, u32[]{:S(2)}, u32[]{:S(2)}) async-start(f32[64,1,192]{2,1,0:T(1,128)} %all_to_all.16), calls=%async_computation.1 | async-start | bytes 131072 | tf_op jit(solution)/shard_map/all_to_all | solution.py:195
  125.9 13.9 %all-to-all-done.1 = f32[64,1,192]{2,1,0:T(1,128)S(1)} async-done(((f32[64,1,192]{2,1,0:T(1,128)}), f32[64,1,192]{2,1,0:T(1,128)S(1)}, u32[]{:S(2)}, u32[]{:S(2)}) %all-to-all-start.1) | async-done | bytes 49184 | tf_op jit(solution)/shard_map/all_to_all | solution.py:195
  139.8 2.2 %collective-permute-start.8 = (bf16[3,8,128]{2,1,0:T(8,128)(2,1)S(1)}, bf16[3,8,128]{2,1,0:T(8,128)(2,1)S(1)}, u32[]{:S(2)}, u32[]{:S(2)}) collective-permute-start(bf16[3,8,128]{2,1,0:T(8,128)(2,1)S(1)} %get-tuple-element.70), channel_id=1, source_target_pairs={{0,488},{8,496},{16,504},{24,0},{32,8},{40,16},{48,24},{56,32},{64... | collective-permute-start | bytes 18440 | tf_op jit(solution)/shard_map/ppermute | solution.py:23
  142.0 3.1 %collective-permute-start.6 = (bf16[3,8,128]{2,1,0:T(8,128)(2,1)S(1)}, bf16[3,8,128]{2,1,0:T(8,128)(2,1)S(1)}, u32[]{:S(2)}, u32[]{:S(2)}) collective-permute-start(bf16[3,8,128]{2,1,0:T(8,128)(2,1)S(1)} %get-tuple-element.72), channel_id=1, source_target_pairs={{0,8},{8,16},{16,24},{24,32},{32,40},{40,48},{48,56},{56,64},{64,7... | collective-permute-start | bytes 18440 | tf_op jit(solution)/shard_map/ppermute | solution.py:23
  145.1 4.9 %collective-permute-start.9 = (bf16[3,8,128]{2,1,0:T(8,128)(2,1)S(1)}, bf16[3,8,128]{2,1,0:T(8,128)(2,1)S(1)}, u32[]{:S(2)}, u32[]{:S(2)}) collective-permute-start(bf16[3,8,128]{2,1,0:T(8,128)(2,1)S(1)} %get-tuple-element.69), channel_id=1, source_target_pairs={{0,496},{8,504},{16,0},{24,8},{32,16},{40,24},{48,32},{56,40},{64,... | collective-permute-start | bytes 18440 | tf_op jit(solution)/shard_map/ppermute | solution.py:23
  150.0 1.9 %collective-permute-start.7 = (bf16[3,8,128]{2,1,0:T(8,128)(2,1)S(1)}, bf16[3,8,128]{2,1,0:T(8,128)(2,1)S(1)}, u32[]{:S(2)}, u32[]{:S(2)}) collective-permute-start(bf16[3,8,128]{2,1,0:T(8,128)(2,1)S(1)} %get-tuple-element.71), channel_id=1, source_target_pairs={{0,504},{8,0},{16,8},{24,16},{32,24},{40,32},{48,40},{56,48},{64,5... | collective-permute-start | bytes 18440 | tf_op jit(solution)/shard_map/ppermute | solution.py:23
  152.0 1.9 %collective-permute-start.10 = (bf16[3,8,128]{2,1,0:T(8,128)(2,1)S(1)}, bf16[3,8,128]{2,1,0:T(8,128)(2,1)S(1)}, u32[]{:S(2)}, u32[]{:S(2)}) collective-permute-start(bf16[3,8,128]{2,1,0:T(8,128)(2,1)S(1)} %get-tuple-element.68), channel_id=1, source_target_pairs={{0,16},{8,24},{16,32},{24,40},{32,48},{40,56},{48,64},{56,72},{64,... | collective-permute-start | bytes 18440 | tf_op jit(solution)/shard_map/ppermute | solution.py:23
  154.6 6.7 %all-to-all-start.2 = ((f32[64,1,192]{2,1,0:T(1,128)}), f32[64,1,192]{2,1,0:T(1,128)S(1)}, u32[]{:S(2)}, u32[]{:S(2)}) async-start(f32[64,1,192]{2,1,0:T(1,128)} %broadcast_in_dim.116), calls=%async_computation.2 | async-start | bytes 131072 | tf_op jit(solution)/shard_map/all_to_all | solution.py:214
  161.2 4.4 %collective-permute-start.11 = (bf16[3,8,128]{2,1,0:T(8,128)(2,1)S(1)}, bf16[3,8,128]{2,1,0:T(8,128)(2,1)S(1)}, u32[]{:S(2)}, u32[]{:S(2)}) collective-permute-start(bf16[3,8,128]{2,1,0:T(8,128)(2,1)S(1)} %get-tuple-element.67), channel_id=1, source_target_pairs={{0,24},{8,32},{16,40},{24,48},{32,56},{40,64},{48,72},{56,80},{64,... | collective-permute-start | bytes 18440 | tf_op jit(solution)/shard_map/ppermute | solution.py:23
  165.8 3.1 %collective-permute-done.11 = bf16[3,8,128]{2,1,0:T(8,128)(2,1)S(1)} collective-permute-done((bf16[3,8,128]{2,1,0:T(8,128)(2,1)S(1)}, bf16[3,8,128]{2,1,0:T(8,128)(2,1)S(1)}, u32[]{:S(2)}, u32[]{:S(2)}) %collective-permute-start.11) | collective-permute-done | bytes 6176 | tf_op jit(solution)/shard_map/ppermute | solution.py:23
  171.1 4.8 %all-to-all-done.2 = f32[64,1,192]{2,1,0:T(1,128)S(1)} async-done(((f32[64,1,192]{2,1,0:T(1,128)}), f32[64,1,192]{2,1,0:T(1,128)S(1)}, u32[]{:S(2)}, u32[]{:S(2)}) %all-to-all-start.2) | async-done | bytes 49184 | tf_op jit(solution)/shard_map/all_to_all | solution.py:214
  (188 shorter events, 64.2 us)
Async XLA Ops:
  0.6 21.1 %copy-start = (bf16[12,128,128]{2,1,0:T(8,128)(2,1)S(1)}, bf16[12,128,128]{2,1,0:T(8,128)(2,1)}, u32[]{:S(2)}) copy-start(bf16[12,128,128]{2,1,0:T(8,128)(2,1)} %param.22) | copy-start | bytes 1179652
  0.6 12.3 %copy-start.4 = (bf16[128,2048]{1,0:T(8,128)(2,1)S(1)}, bf16[128,2048]{1,0:T(8,128)(2,1)}, u32[]{:S(2)}) copy-start(bf16[128,2048]{1,0:T(8,128)(2,1)} %param.17) | copy-start | bytes 1572868
  0.7 12.3 %copy-start.18 = (bf16[128,64]{0,1:T(8,128)(2,1)S(1)}, bf16[128,64]{0,1:T(8,128)(2,1)}, u32[]{:S(2)}) copy-start(bf16[128,64]{0,1:T(8,128)(2,1)} %param.18) | copy-start | bytes 49156
  26.6 32.0 %collective-permute-start.2 = (f32[2,200,128]{2,1,0:T(8,128)}, f32[2,200,128]{2,1,0:T(8,128)}, u32[]{:S(2)}, u32[]{:S(2)}) collective-permute-start(f32[2,200,128]{2,1,0:T(8,128)} %get-tuple-element.56), channel_id=1, source_target_pairs={{0,488},{8,496},{16,504},{24,0},{32,8},{40,16},{48,24},{56,32},{64... | collective-permute-start | bytes 614408 | tf_op jit(solution)/shard_map/ppermute | solution.py:23
  40.1 12.2 %copy-start.16 = (f32[8,16,128]{2,0,1:T(8,128)S(1)}, f32[8,16,128]{2,0,1:T(8,128)}, u32[]{:S(2)}) copy-start(f32[8,16,128]{2,0,1:T(8,128)} %copy-done.15) | copy-start | bytes 196612
  40.1 12.8 %copy-start.14 = (f32[8,16,128]{2,0,1:T(8,128)S(1)}, f32[8,16,128]{2,0,1:T(8,128)}, u32[]{:S(2)}) copy-start(f32[8,16,128]{2,0,1:T(8,128)} %convolution_bitcast_fusion.1) | copy-start | bytes 196612
  40.1 13.4 %copy-start.26 = (s32[12]{0:T(128)S(1)}, s32[12]{0:T(128)}, u32[]{:S(2)}) copy-start(s32[12]{0:T(128)} %copy-done.25) | copy-start | bytes 148
  40.1 21.4 %collective-permute-start.3 = (f32[2,200,128]{2,1,0:T(8,128)}, f32[2,200,128]{2,1,0:T(8,128)}, u32[]{:S(2)}, u32[]{:S(2)}) collective-permute-start(f32[2,200,128]{2,1,0:T(8,128)} %get-tuple-element.55), channel_id=1, source_target_pairs={{0,496},{8,504},{16,0},{24,8},{32,16},{40,24},{48,32},{56,40},{64,... | collective-permute-start | bytes 614408 | tf_op jit(solution)/shard_map/ppermute | solution.py:23
  43.9 18.5 %collective-permute-start.1 = (f32[3,200,128]{2,1,0:T(8,128)}, f32[3,200,128]{2,1,0:T(8,128)}, u32[]{:S(2)}, u32[]{:S(2)}) collective-permute-start(f32[3,200,128]{2,1,0:T(8,128)} %get-tuple-element.58), channel_id=1, source_target_pairs={{0,504},{8,0},{16,8},{24,16},{32,24},{40,32},{48,40},{56,48},{64,5... | collective-permute-start | bytes 921608 | tf_op jit(solution)/shard_map/ppermute | solution.py:23
  46.5 16.9 %collective-permute-start = (f32[3,200,128]{2,1,0:T(8,128)}, f32[3,200,128]{2,1,0:T(8,128)}, u32[]{:S(2)}, u32[]{:S(2)}) collective-permute-start(f32[3,200,128]{2,1,0:T(8,128)} %get-tuple-element.57), channel_id=1, source_target_pairs={{0,8},{8,16},{16,24},{24,32},{32,40},{40,48},{48,56},{56,64},{64,7... | collective-permute-start | bytes 921608 | tf_op jit(solution)/shard_map/ppermute | solution.py:23
  49.6 14.7 %collective-permute-start.4 = (f32[2,200,128]{2,1,0:T(8,128)}, f32[2,200,128]{2,1,0:T(8,128)}, u32[]{:S(2)}, u32[]{:S(2)}) collective-permute-start(f32[2,200,128]{2,1,0:T(8,128)} %get-tuple-element.54), channel_id=1, source_target_pairs={{0,16},{8,24},{16,32},{24,40},{32,48},{40,56},{48,64},{56,72},{64,... | collective-permute-start | bytes 614408 | tf_op jit(solution)/shard_map/ppermute | solution.py:23
  58.0 15.0 %copy-start.9 = (bf16[12,128,128]{2,1,0:T(8,128)(2,1)}, bf16[12,128,128]{2,1,0:T(8,128)(2,1)S(1)}, u32[]{:S(2)}) copy-start(bf16[12,128,128]{2,1,0:T(8,128)(2,1)S(1)} %gather_fusion.8) | copy-start | bytes 1179652
  58.6 13.3 %collective-permute-start.5 = (f32[2,200,128]{2,1,0:T(8,128)S(1)}, f32[2,200,128]{2,1,0:T(8,128)S(1)}, u32[]{:S(2)}, u32[]{:S(2)}) collective-permute-start(f32[2,200,128]{2,1,0:T(8,128)S(1)} %copy-done.13), channel_id=1, source_target_pairs={{0,24},{8,32},{16,40},{24,48},{32,56},{40,64},{48,72},{56,80},{64,... | collective-permute-start | bytes 614408 | tf_op jit(solution)/shard_map/ppermute | solution.py:23
  88.8 20.0 %all-to-all-start = ((bf16[8,3,8,2048]{3,2,1,0:T(8,128)(2,1)}), bf16[8,3,8,2048]{3,2,1,0:T(8,128)(2,1)}, u32[]{:S(2)}, u32[]{:S(2)}) async-start(bf16[8,3,8,2048]{3,2,1,0:T(8,128)(2,1)} %copy.126), calls=%async_computation | async-start | bytes 1572864 | tf_op jit(solution)/shard_map/all_to_all | solution.py:177
  96.3 14.7 %copy-start.12 = (bf16[64,16,128]{2,0,1:T(8,128)(2,1)S(1)}, bf16[64,16,128]{2,0,1:T(8,128)(2,1)}, u32[]{:S(2)}) copy-start(bf16[64,16,128]{2,0,1:T(8,128)(2,1)} %copy-done.11) | copy-start | bytes 786436
  114.4 54.5 %copy-start.10 = (bf16[12,128,128]{2,1,0:T(8,128)(2,1)S(1)}, bf16[12,128,128]{2,1,0:T(8,128)(2,1)}, u32[]{:S(2)}) copy-start(bf16[12,128,128]{2,1,0:T(8,128)(2,1)} %copy-done.9) | copy-start | bytes 1179652
  118.4 21.3 %all-to-all-start.1 = ((f32[64,1,192]{2,1,0:T(1,128)}), f32[64,1,192]{2,1,0:T(1,128)S(1)}, u32[]{:S(2)}, u32[]{:S(2)}) async-start(f32[64,1,192]{2,1,0:T(1,128)} %all_to_all.16), calls=%async_computation.1 | async-start | bytes 131072 | tf_op jit(solution)/shard_map/all_to_all | solution.py:195
  139.8 21.5 %collective-permute-start.8 = (bf16[3,8,128]{2,1,0:T(8,128)(2,1)S(1)}, bf16[3,8,128]{2,1,0:T(8,128)(2,1)S(1)}, u32[]{:S(2)}, u32[]{:S(2)}) collective-permute-start(bf16[3,8,128]{2,1,0:T(8,128)(2,1)S(1)} %get-tuple-element.70), channel_id=1, source_target_pairs={{0,488},{8,496},{16,504},{24,0},{32,8},{40,16},{48,24},{56,32},{64... | collective-permute-start | bytes 18440 | tf_op jit(solution)/shard_map/ppermute | solution.py:23
  142.0 23.7 %collective-permute-start.6 = (bf16[3,8,128]{2,1,0:T(8,128)(2,1)S(1)}, bf16[3,8,128]{2,1,0:T(8,128)(2,1)S(1)}, u32[]{:S(2)}, u32[]{:S(2)}) collective-permute-start(bf16[3,8,128]{2,1,0:T(8,128)(2,1)S(1)} %get-tuple-element.72), channel_id=1, source_target_pairs={{0,8},{8,16},{16,24},{24,32},{32,40},{40,48},{48,56},{56,64},{64,7... | collective-permute-start | bytes 18440 | tf_op jit(solution)/shard_map/ppermute | solution.py:23
  145.1 20.6 %collective-permute-start.9 = (bf16[3,8,128]{2,1,0:T(8,128)(2,1)S(1)}, bf16[3,8,128]{2,1,0:T(8,128)(2,1)S(1)}, u32[]{:S(2)}, u32[]{:S(2)}) collective-permute-start(bf16[3,8,128]{2,1,0:T(8,128)(2,1)S(1)} %get-tuple-element.69), channel_id=1, source_target_pairs={{0,496},{8,504},{16,0},{24,8},{32,16},{40,24},{48,32},{56,40},{64,... | collective-permute-start | bytes 18440 | tf_op jit(solution)/shard_map/ppermute | solution.py:23
  150.0 15.7 %collective-permute-start.7 = (bf16[3,8,128]{2,1,0:T(8,128)(2,1)S(1)}, bf16[3,8,128]{2,1,0:T(8,128)(2,1)S(1)}, u32[]{:S(2)}, u32[]{:S(2)}) collective-permute-start(bf16[3,8,128]{2,1,0:T(8,128)(2,1)S(1)} %get-tuple-element.71), channel_id=1, source_target_pairs={{0,504},{8,0},{16,8},{24,16},{32,24},{40,32},{48,40},{56,48},{64,5... | collective-permute-start | bytes 18440 | tf_op jit(solution)/shard_map/ppermute | solution.py:23
  152.0 13.8 %collective-permute-start.10 = (bf16[3,8,128]{2,1,0:T(8,128)(2,1)S(1)}, bf16[3,8,128]{2,1,0:T(8,128)(2,1)S(1)}, u32[]{:S(2)}, u32[]{:S(2)}) collective-permute-start(bf16[3,8,128]{2,1,0:T(8,128)(2,1)S(1)} %get-tuple-element.68), channel_id=1, source_target_pairs={{0,16},{8,24},{16,32},{24,40},{32,48},{40,56},{48,64},{56,72},{64,... | collective-permute-start | bytes 18440 | tf_op jit(solution)/shard_map/ppermute | solution.py:23
  154.6 21.2 %all-to-all-start.2 = ((f32[64,1,192]{2,1,0:T(1,128)}), f32[64,1,192]{2,1,0:T(1,128)S(1)}, u32[]{:S(2)}, u32[]{:S(2)}) async-start(f32[64,1,192]{2,1,0:T(1,128)} %broadcast_in_dim.116), calls=%async_computation.2 | async-start | bytes 131072 | tf_op jit(solution)/shard_map/all_to_all | solution.py:214
  161.2 7.7 %collective-permute-start.11 = (bf16[3,8,128]{2,1,0:T(8,128)(2,1)S(1)}, bf16[3,8,128]{2,1,0:T(8,128)(2,1)S(1)}, u32[]{:S(2)}, u32[]{:S(2)}) collective-permute-start(bf16[3,8,128]{2,1,0:T(8,128)(2,1)S(1)} %get-tuple-element.67), channel_id=1, source_target_pairs={{0,24},{8,32},{16,40},{24,48},{32,56},{40,64},{48,72},{56,80},{64,... | collective-permute-start | bytes 18440 | tf_op jit(solution)/shard_map/ppermute | solution.py:23
  (19 other events, 93.2 us)
